TPU v7x, 32 devices: a whole 2x2x4 slice. The times are simulated.
32 devices in a mesh: row: 4 (over z), col: 8 (over y, x, core).
Axes of the slice: x: 2, y: 2, z: 4, core: 2. Of those that a mesh axis runs over, the one named last changes fastest.
Arguments:
- layer_input: bfloat16 [8192, 2048], P(('col', 'row')), may hold values from -6 to 6
- w_query: bfloat16 [2048, 2048], P('col', 'row'), may hold values from -0.125 to 0.125
- w_key: bfloat16 [2048, 2048], P('col', 'row'), may hold values from -0.125 to 0.125
- w_value: bfloat16 [2048, 2048], P('col', 'row'), may hold values from -0.125 to 0.125
- w_output: bfloat16 [2048, 2048], P('row', 'col'), may hold values from -1.5 to 1.5
- w_gate: bfloat16 [2048, 8192], P('col', 'row'), may hold values from -0.125 to 0.125
- w_up: bfloat16 [2048, 8192], P('col', 'row'), may hold values from -0.125 to 0.125
- w_down: bfloat16 [8192, 2048], P('row', 'col'), may hold values from -0.0625 to 0.0625
- piece_starts: int32 [8, 2], P('col'), may hold values from 0 to 768, as said below
- cotangent: bfloat16 [8192, 2048], P(('col', 'row')), may hold values from -6 to 6
Outputs:
- output: bfloat16 [8192, 2048], P(('col', 'row'))
- input_grad: float32 [8192, 2048], P(('col', 'row'))
- grad_w_query: float32 [2048, 2048], P('col', 'row')
- grad_w_key: float32 [2048, 2048], P('col', 'row')
- grad_w_value: float32 [2048, 2048], P('col', 'row')
- grad_w_output: float32 [2048, 2048], P('row', 'col')
- grad_w_gate: float32 [2048, 8192], P('col', 'row')
- grad_w_up: float32 [2048, 8192], P('col', 'row')
- grad_w_down: float32 [8192, 2048], P('row', 'col')
Inputs may be any that keep to these rules, and one draw needn't show every extreme that they name: `piece_starts`: piece p of a sequence starts at p * 512 or later and ends by (p + 1) * 512, so the pieces of one sequence do not intersect.
All inputs are finite; a program needn't handle non-finite values.
Results may differ from a plain program's by a relative error of at most 0.019.
Values may be sent and summed in bfloat16 or wider, within the bound.
No kernel may reach another device: no remote copies, remote signals or barrier semaphores. Data moves between devices by JAX's collectives and lax.ppermute only.
A program may use at most 256 MiB of HBM per device.

v0:
```python
import math

import jax
import jax.numpy as jnp
from jax import lax
from jax.sharding import PartitionSpec as P

HD = 128
LENGTH = 1024
PIECE = 256


EPSILON = 1e-05
NEGATIVE = -1e30


def product(left, right):
    return jnp.dot(left, right, preferred_element_type=jnp.float32)


def contract_rows(left, right):
    return lax.dot_general(
        left, right, (((0,), (0,)), ((), ())), preferred_element_type=jnp.float32
    )


def times_transpose(left, right):
    return lax.dot_general(
        left, right, (((1,), (1,)), ((), ())), preferred_element_type=jnp.float32
    )


def layer_norm(inputs):
    center = inputs - jnp.mean(inputs, axis=-1, keepdims=True)
    spread = jnp.mean(center * center, axis=-1, keepdims=True)
    return center * lax.rsqrt(spread + EPSILON)


def norm_back(inputs, grad):
    center = inputs - jnp.mean(inputs, axis=-1, keepdims=True)
    inverse = lax.rsqrt(jnp.mean(center * center, axis=-1, keepdims=True) + EPSILON)
    normed = center * inverse
    return inverse * (
        grad
        - jnp.mean(grad, axis=-1, keepdims=True)
        - normed * jnp.mean(grad * normed, axis=-1, keepdims=True)
    )


def rope_tables():
    positions = jnp.arange(LENGTH, dtype=jnp.float32)
    freqs = jnp.power(jnp.float32(10000.0), -jnp.arange(HD // 2, dtype=jnp.float32) * (2.0 / HD))
    angles = positions[:, None] * freqs[None, :]
    return (jnp.cos(angles)[:, None, :], jnp.sin(angles)[:, None, :])


def rotate(field, cosine, sine):
    half_size = field.shape[-1] // 2
    first_half = field[..., :half_size]
    second_half = field[..., half_size:]
    return jnp.concatenate(
        [first_half * cosine - second_half * sine, second_half * cosine + first_half * sine],
        axis=-1,
    )


def unrotate(field, cosine, sine):
    half_size = field.shape[-1] // 2
    first_half = field[..., :half_size]
    second_half = field[..., half_size:]
    return jnp.concatenate(
        [first_half * cosine + second_half * sine, second_half * cosine - first_half * sine],
        axis=-1,
    )


def piece_mask(starts):
    positions = jnp.arange(LENGTH, dtype=jnp.int32)
    inside = (positions[None, :] >= starts[:, None]) & (
        positions[None, :] < starts[:, None] + PIECE
    )
    shared = jnp.any(inside[:, :, None] & inside[:, None, :], axis=0)
    causal = positions[None, :] <= positions[:, None]
    return causal | shared


def masked_scores(queries, keys_rot, starts):
    scale = 1.0 / math.sqrt(HD)
    scores = (
        jnp.einsum("qhd,khd->hqk", queries, keys_rot, preferred_element_type=jnp.float32) * scale
    )
    return jnp.where(piece_mask(starts)[None], scores, NEGATIVE)


def attend_forward(operands):
    queries, keys_rot, values, starts = operands
    scores = masked_scores(queries, keys_rot, starts)
    row_top = jnp.max(scores, axis=-1, keepdims=True)
    shifted = jnp.exp(scores - row_top)
    row_total = jnp.sum(shifted, axis=-1, keepdims=True)
    probs = (shifted / row_total).astype(jnp.bfloat16)
    mixed = jnp.einsum("hqk,khd->qhd", probs, values, preferred_element_type=jnp.float32)
    return (mixed, row_top + jnp.log(row_total))


def attend_backward(operands):
    queries, keys_rot, values, starts, log_total, grad_mixed = operands
    scale = 1.0 / math.sqrt(HD)
    scores = masked_scores(queries, keys_rot, starts)
    probs = jnp.exp(scores - log_total)
    probs_low = probs.astype(jnp.bfloat16)
    grad_values = jnp.einsum(
        "hqk,qhd->khd", probs_low, grad_mixed, preferred_element_type=jnp.float32
    )
    grad_probs = jnp.einsum("qhd,khd->hqk", grad_mixed, values, preferred_element_type=jnp.float32)
    inner = jnp.sum(probs * grad_probs, axis=-1, keepdims=True)
    grad_scores = (probs * (grad_probs - inner)).astype(jnp.bfloat16)
    grad_queries = (
        jnp.einsum("hqk,khd->qhd", grad_scores, keys_rot, preferred_element_type=jnp.float32)
        * scale
    )
    grad_keys = (
        jnp.einsum("hqk,qhd->khd", grad_scores, queries, preferred_element_type=jnp.float32) * scale
    )
    return (grad_queries, grad_keys, grad_values)


def per_device(
    layer_input, w_query, w_key, w_value, w_output, w_gate, w_up, w_down, piece_starts, cotangent
):
    seq_count = piece_starts.shape[0]
    group_rows = seq_count * LENGTH
    heads_local = w_query.shape[1] // HD
    gathered = (
        lax.all_gather(w_query, "col", axis=0, tiled=True),
        lax.all_gather(w_key, "col", axis=0, tiled=True),
        lax.all_gather(w_value, "col", axis=0, tiled=True),
        lax.all_gather(w_output, "col", axis=1, tiled=True),
        lax.all_gather(w_gate, "col", axis=0, tiled=True),
        lax.all_gather(w_up, "col", axis=0, tiled=True),
        lax.all_gather(w_down, "col", axis=1, tiled=True),
    )
    full_query, full_key, full_value, full_output, full_gate, full_up, full_down = gathered
    cosine, sine = rope_tables()
    inputs = layer_input.astype(jnp.float32)
    normed_first = layer_norm(inputs).astype(jnp.bfloat16)
    first_rows = lax.all_gather(normed_first, "row", axis=0, tiled=True)

    def split_heads(matrix):
        return matrix.reshape(seq_count, LENGTH, heads_local, HD)

    def merge_heads(field):
        return field.reshape(group_rows, heads_local * HD)

    queries = rotate(split_heads(product(first_rows, full_query)), cosine, sine).astype(
        jnp.bfloat16
    )
    keys_rot = rotate(split_heads(product(first_rows, full_key)), cosine, sine).astype(jnp.bfloat16)
    values = split_heads(product(first_rows, full_value)).astype(jnp.bfloat16)
    mixed, log_total = lax.map(attend_forward, (queries, keys_rot, values, piece_starts))
    attended = merge_heads(mixed.astype(jnp.bfloat16))
    attention_sum = lax.psum_scatter(
        product(attended, full_output), "row", scatter_dimension=0, tiled=True
    )
    middle = inputs + attention_sum
    normed_second = layer_norm(middle).astype(jnp.bfloat16)
    second_rows = lax.all_gather(normed_second, "row", axis=0, tiled=True)
    gate_lin = product(second_rows, full_gate)
    up_lin = product(second_rows, full_up)
    activation = (jax.nn.silu(gate_lin) * up_lin).astype(jnp.bfloat16)
    ffn_sum = lax.psum_scatter(
        product(activation, full_down).astype(jnp.bfloat16), "row", scatter_dimension=0, tiled=True
    ).astype(jnp.float32)
    output = (middle + ffn_sum).astype(jnp.bfloat16)
    back_query, back_key, back_value, back_output = (full_query, full_key, full_value, full_output)
    back_gate, back_up, back_down = (full_gate, full_up, full_down)
    grad_rows = lax.all_gather(cotangent, "row", axis=0, tiled=True)
    grad_activation = times_transpose(grad_rows, back_down)
    sigma = jax.nn.sigmoid(gate_lin)
    grad_gate = (grad_activation * up_lin * sigma * (1.0 + gate_lin * (1.0 - sigma))).astype(
        jnp.bfloat16
    )
    grad_up = (grad_activation * gate_lin * sigma).astype(jnp.bfloat16)
    grad_second = lax.psum_scatter(
        (times_transpose(grad_gate, back_gate) + times_transpose(grad_up, back_up)).astype(
            jnp.bfloat16
        ),
        "row",
        scatter_dimension=0,
        tiled=True,
    ).astype(jnp.float32)
    grad_middle = cotangent.astype(jnp.float32) + norm_back(middle, grad_second)
    grad_branch = lax.all_gather(grad_middle.astype(jnp.bfloat16), "row", axis=0, tiled=True)
    grad_mixed = split_heads(times_transpose(grad_branch, back_output).astype(jnp.bfloat16))
    grad_q_rot, grad_k_rot, grad_values = lax.map(
        attend_backward, (queries, keys_rot, values, piece_starts, log_total, grad_mixed)
    )
    grad_query = merge_heads(unrotate(grad_q_rot, cosine, sine)).astype(jnp.bfloat16)
    grad_key = merge_heads(unrotate(grad_k_rot, cosine, sine)).astype(jnp.bfloat16)
    grad_value = merge_heads(grad_values).astype(jnp.bfloat16)
    grad_first = lax.psum_scatter(
        (
            times_transpose(grad_query, back_query)
            + times_transpose(grad_key, back_key)
            + times_transpose(grad_value, back_value)
        ).astype(jnp.bfloat16),
        "row",
        scatter_dimension=0,
        tiled=True,
    ).astype(jnp.float32)
    grad_input = grad_middle + norm_back(inputs, grad_first)
    grad_query_w = contract_rows(first_rows, grad_query)
    grad_key_w = contract_rows(first_rows, grad_key)
    grad_value_w = contract_rows(first_rows, grad_value)
    grad_output_w = contract_rows(attended, grad_branch)
    grad_gate_w = contract_rows(second_rows, grad_gate)
    grad_up_w = contract_rows(second_rows, grad_up)
    grad_down_w = contract_rows(activation, grad_rows)
    summed = (
        lax.psum_scatter(
            grad_query_w.astype(jnp.bfloat16), "col", scatter_dimension=0, tiled=True
        ).astype(jnp.float32),
        lax.psum_scatter(
            grad_key_w.astype(jnp.bfloat16), "col", scatter_dimension=0, tiled=True
        ).astype(jnp.float32),
        lax.psum_scatter(
            grad_value_w.astype(jnp.bfloat16), "col", scatter_dimension=0, tiled=True
        ).astype(jnp.float32),
        lax.psum_scatter(
            grad_output_w.astype(jnp.bfloat16), "col", scatter_dimension=1, tiled=True
        ).astype(jnp.float32),
        lax.psum_scatter(
            grad_gate_w.astype(jnp.bfloat16), "col", scatter_dimension=0, tiled=True
        ).astype(jnp.float32),
        lax.psum_scatter(
            grad_up_w.astype(jnp.bfloat16), "col", scatter_dimension=0, tiled=True
        ).astype(jnp.float32),
        lax.psum_scatter(
            grad_down_w.astype(jnp.bfloat16), "col", scatter_dimension=1, tiled=True
        ).astype(jnp.float32),
    )
    results = tuple(summed)
    return (
        output,
        grad_input,
        results[0],
        results[1],
        results[2],
        results[3],
        results[4],
        results[5],
        results[6],
    )


def solution(mesh):
    in_specs = (
        P(("col", "row"), None),
        P("col", "row"),
        P("col", "row"),
        P("col", "row"),
        P("row", "col"),
        P("col", "row"),
        P("col", "row"),
        P("row", "col"),
        P("col", None),
        P(("col", "row"), None),
    )
    out_specs = (
        P(("col", "row"), None),
        P(("col", "row"), None),
        P("col", "row"),
        P("col", "row"),
        P("col", "row"),
        P("row", "col"),
        P("col", "row"),
        P("col", "row"),
        P("row", "col"),
    )
    return jax.shard_map(
        per_device, mesh=mesh, in_specs=in_specs, out_specs=out_specs, check_vma=False
    )
```

profile of v0, /device:TPU:0, one launch (start us, length us, event | category | flops | bytes accessed | tf_op | source)
XLA Modules:
  0.0 1477.7 jit_solution(13351820157895669522)
XLA Ops:
  22.8 17.7 %all-gather.18.cloned.1.call-done = bf16[2048,512]{1,0:T(8,128)(2,1)} async-done(((bf16[256,512]{1,0:T(8,128)(2,1)}), bf16[2048,512]{1,0:T(8,128)(2,1)}) %all-gather.18.cloned.1.call-update) | async-done | bytes 2097168 | tf_op jit(solution)/shard_map/all_gather | solution.py:136
  40.4 82.9 %all-gather.12.cloned.1.call-done = bf16[1024,2048]{1,0:T(8,128)(2,1)} async-done(((bf16[256,2048]{1,0:T(8,128)(2,1)}), bf16[1024,2048]{1,0:T(8,128)(2,1)}) %all-gather.12.cloned.1.call-update) | async-done | bytes 4194320 | tf_op jit(solution)/shard_map/all_gather | solution.py:147
  135.2 16.4 %all-gather.16.cloned.1.call-done = bf16[2048,512]{1,0:T(8,128)(2,1)} async-done(((bf16[256,512]{1,0:T(8,128)(2,1)}), bf16[2048,512]{1,0:T(8,128)(2,1)}) %all-gather.16.cloned.1.call-update) | async-done | bytes 2097168 | tf_op jit(solution)/shard_map/all_gather | solution.py:135
  219.0 144.0 %reduce-scatter.12.cloned.1.call-done = f32[256,2048]{1,0:T(8,128)} async-done(((f32[1024,2048]{1,0:T(8,128)}), f32[256,2048]{1,0:T(8,128)}) %reduce-scatter.12.cloned.1.call-update) | async-done | bytes 2097168 | tf_op jit(solution)/shard_map/reduce_scatter | solution.py:162
  368.6 51.1 %all-gather.26.cloned.1.call-done = bf16[2048,2048]{1,0:T(8,128)(2,1)} async-done(((bf16[256,2048]{1,0:T(8,128)(2,1)}), bf16[2048,2048]{1,0:T(8,128)(2,1)}) %all-gather.26.cloned.1.call-update) | async-done | bytes 8388624 | tf_op jit(solution)/shard_map/all_gather | solution.py:140
  419.7 82.9 %all-gather.22.cloned.1.call-done = bf16[1024,2048]{1,0:T(8,128)(2,1)} async-done(((bf16[256,2048]{1,0:T(8,128)(2,1)}), bf16[1024,2048]{1,0:T(8,128)(2,1)}) %all-gather.22.cloned.1.call-update) | async-done | bytes 4194320 | tf_op jit(solution)/shard_map/all_gather | solution.py:167
  502.6 14.6 fusion.44
  517.3 40.0 %all-gather.24.cloned.1.call-done = bf16[2048,2048]{1,0:T(8,128)(2,1)} async-done(((bf16[256,2048]{1,0:T(8,128)(2,1)}), bf16[2048,2048]{1,0:T(8,128)(2,1)}) %all-gather.24.cloned.1.call-update) | async-done | bytes 8388624 | tf_op jit(solution)/shard_map/all_gather | solution.py:139
  557.3 14.5 fusion.43
  571.8 67.7 %all-gather.30.cloned.1.call-done = bf16[1024,2048]{1,0:T(8,128)(2,1)} async-done(((bf16[256,2048]{1,0:T(8,128)(2,1)}), bf16[1024,2048]{1,0:T(8,128)(2,1)}) %all-gather.30.cloned.1.call-update) | async-done | bytes 4194320 | tf_op jit(solution)/shard_map/all_gather | solution.py:177
  639.5 56.3 %all-gather.28.cloned.1.call-done = bf16[2048,2048]{1,0:T(8,128)(2,1)} async-done(((bf16[2048,256]{1,0:T(8,128)(2,1)}), bf16[2048,2048]{1,0:T(8,128)(2,1)}) %all-gather.28.cloned.1.call-update) | async-done | bytes 8388624 | tf_op jit(solution)/shard_map/all_gather | solution.py:141
  695.8 21.8 %multiply_convert_fusion.1 = (bf16[1024,2048]{1,0:T(8,128)(2,1)}, bf16[1024,2048]{1,0:T(8,128)(2,1)}, bf16[1024,2048]{1,0:T(8,128)(2,1)}) fusion(f32[1024,2048]{1,0:T(8,128)} %fusion.43, f32[1024,2048]{1,0:T(8,128)} %fusion.44, bf16[1024,2048]{1,0:T(8,128)(2,1)} %all-gather.30.cloned.1.call-done, bf16[2048,2048]{1,0:T(8,128)(2,1)} %all-gather.28.cloned.1.call-done), kind=kOutput, calls=%fused_computation.12 | convolution fusion | flops 8623489024 | bytes 41943040 | tf_op jit(solution)/shard_map/dot_general | solution.py:28
  757.9 62.5 %reduce-scatter.16.cloned.1.call-done = bf16[256,2048]{1,0:T(8,128)(2,1)} async-done(((bf16[1024,2048]{1,0:T(8,128)(2,1)}), bf16[256,2048]{1,0:T(8,128)(2,1)}) %reduce-scatter.16.cloned.1.call-update) | async-done | bytes 1048592 | tf_op jit(solution)/shard_map/reduce_scatter | solution.py:184
  822.3 77.8 %reduce-scatter.14.cloned.1.call-done = bf16[256,2048]{1,0:T(8,128)(2,1)} async-done(((bf16[1024,2048]{1,0:T(8,128)(2,1)}), bf16[256,2048]{1,0:T(8,128)(2,1)}) %reduce-scatter.14.cloned.1.call-update) | async-done | bytes 1048592 | tf_op jit(solution)/shard_map/reduce_scatter | solution.py:171
  904.8 14.1 convolution_convert_fusion.1
  918.9 14.1 convolution_convert_fusion.2
  948.1 38.0 %all-gather.32.cloned.1.call-done = bf16[1024,2048]{1,0:T(8,128)(2,1)} async-done(((bf16[256,2048]{1,0:T(8,128)(2,1)}), bf16[1024,2048]{1,0:T(8,128)(2,1)}) %all-gather.32.cloned.1.call-update) | async-done | bytes 4194320 | tf_op jit(solution)/shard_map/all_gather | solution.py:193
  1077.8 56.5 %reduce-scatter.28.cloned.1.call-done = bf16[256,2048]{1,0:T(8,128)(2,1)} async-done(((bf16[2048,2048]{1,0:T(8,128)(2,1)}), bf16[256,2048]{1,0:T(8,128)(2,1)}) %reduce-scatter.28.cloned.1.call-update) | async-done | bytes 1048592 | tf_op jit(solution)/shard_map/reduce_scatter | solution.py:232
  1137.0 71.8 %reduce-scatter.32.cloned.1.call-done = bf16[2048,256]{1,0:T(8,128)(2,1)} async-done(((bf16[2048,2048]{1,0:T(8,128)(2,1)}), bf16[2048,256]{1,0:T(8,128)(2,1)}) %reduce-scatter.32.cloned.1.call-update) | async-done | bytes 1048592 | tf_op jit(solution)/shard_map/reduce_scatter | solution.py:238
  1211.6 41.6 %reduce-scatter.26.cloned.1.call-done = bf16[512,256]{1,0:T(8,128)(2,1)} async-done(((bf16[512,2048]{1,0:T(8,128)(2,1)}), bf16[512,256]{1,0:T(8,128)(2,1)}) %reduce-scatter.26.cloned.1.call-update) | async-done | bytes 262160 | tf_op jit(solution)/shard_map/reduce_scatter | solution.py:229
  1255.0 42.7 %reduce-scatter.24.cloned.1.call-done = bf16[256,512]{1,0:T(8,128)(2,1)} async-done(((bf16[2048,512]{1,0:T(8,128)(2,1)}), bf16[256,512]{1,0:T(8,128)(2,1)}) %reduce-scatter.24.cloned.1.call-update) | async-done | bytes 262160 | tf_op jit(solution)/shard_map/reduce_scatter | solution.py:226
  1299.4 42.5 %reduce-scatter.20.cloned.1.call-done = bf16[256,512]{1,0:T(8,128)(2,1)} async-done(((bf16[2048,512]{1,0:T(8,128)(2,1)}), bf16[256,512]{1,0:T(8,128)(2,1)}) %reduce-scatter.20.cloned.1.call-update) | async-done | bytes 262160 | tf_op jit(solution)/shard_map/reduce_scatter | solution.py:220
  1343.7 42.6 %reduce-scatter.22.cloned.1.call-done = bf16[256,512]{1,0:T(8,128)(2,1)} async-done(((bf16[2048,512]{1,0:T(8,128)(2,1)}), bf16[256,512]{1,0:T(8,128)(2,1)}) %reduce-scatter.22.cloned.1.call-update) | async-done | bytes 262160 | tf_op jit(solution)/shard_map/reduce_scatter | solution.py:223
  1388.1 77.3 %reduce-scatter.18.cloned.1.call-done = bf16[256,2048]{1,0:T(8,128)(2,1)} async-done(((bf16[1024,2048]{1,0:T(8,128)(2,1)}), bf16[256,2048]{1,0:T(8,128)(2,1)}) %reduce-scatter.18.cloned.1.call-update) | async-done | bytes 1048592 | tf_op jit(solution)/shard_map/reduce_scatter | solution.py:201
  (189 shorter events, 271.3 us)
Async XLA Ops:
  7.2 33.2 %all-gather.18.cloned.1.call-start = ((), (), s32[]{:S(2)}) async-start(), calls=%async_computation.14 | async-start | bytes 2359296 | tf_op jit(solution)/shard_map/all_gather | solution.py:136
  7.9 115.4 %all-gather.12.cloned.1.call-start = ((), (), s32[]{:S(2)}) async-start(), calls=%async_computation.11 | async-start | bytes 5242880 | tf_op jit(solution)/shard_map/all_gather | solution.py:147
  14.2 137.3 %all-gather.16.cloned.1.call-start = ((), (), s32[]{:S(2)}) async-start(), calls=%async_computation.13 | async-start | bytes 2359296 | tf_op jit(solution)/shard_map/all_gather | solution.py:135
  15.0 166.1 %all-gather.14.cloned.1.call-start = ((), (), s32[]{:S(2)}) async-start(), calls=%async_computation.12 | async-start | bytes 2359296 | tf_op jit(solution)/shard_map/all_gather | solution.py:137
  15.5 195.4 %all-gather.20.cloned.1.call-start = ((), (), s32[]{:S(2)}) async-start(), calls=%async_computation.15 | async-start | bytes 2359296 | tf_op jit(solution)/shard_map/all_gather | solution.py:138
  16.1 346.8 %reduce-scatter.12.cloned.1.call-start = ((), (), s32[]{:S(2)}) async-start(), calls=%async_computation.16 | async-start | bytes 10485760 | tf_op jit(solution)/shard_map/reduce_scatter | solution.py:162
  218.2 201.6 %all-gather.26.cloned.1.call-start = ((), (), s32[]{:S(2)}) async-start(), calls=%async_computation.19 | async-start | bytes 9437184 | tf_op jit(solution)/shard_map/all_gather | solution.py:140
  218.9 283.7 %all-gather.22.cloned.1.call-start = ((), (), s32[]{:S(2)}) async-start(), calls=%async_computation.17 | async-start | bytes 5242880 | tf_op jit(solution)/shard_map/all_gather | solution.py:167
  366.5 190.8 %all-gather.24.cloned.1.call-start = ((), (), s32[]{:S(2)}) async-start(), calls=%async_computation.18 | async-start | bytes 9437184 | tf_op jit(solution)/shard_map/all_gather | solution.py:139
  367.2 272.3 %all-gather.30.cloned.1.call-start = ((), (), s32[]{:S(2)}) async-start(), calls=%async_computation.22 | async-start | bytes 5242880 | tf_op jit(solution)/shard_map/all_gather | solution.py:177
  367.8 327.9 %all-gather.28.cloned.1.call-start = ((), (), s32[]{:S(2)}) async-start(), calls=%async_computation.20 | async-start | bytes 9437184 | tf_op jit(solution)/shard_map/all_gather | solution.py:141
  368.6 451.9 %reduce-scatter.16.cloned.1.call-start = ((), (), s32[]{:S(2)}) async-start(), calls=%async_computation.23 | async-start | bytes 5242880 | tf_op jit(solution)/shard_map/reduce_scatter | solution.py:184
  743.5 156.6 %reduce-scatter.14.cloned.1.call-start = ((), (), s32[]{:S(2)}) async-start(), calls=%async_computation.21 | async-start | bytes 5242880 | tf_op jit(solution)/shard_map/reduce_scatter | solution.py:171
  757.4 228.7 %all-gather.32.cloned.1.call-start = ((), (), s32[]{:S(2)}) async-start(), calls=%async_computation.24 | async-start | bytes 5242880 | tf_op jit(solution)/shard_map/all_gather | solution.py:193
  904.7 170.1 %reduce-scatter.30.cloned.1.call-start = ((), (), s32[]{:S(2)}) async-start(), calls=%async_computation.31 | async-start | bytes 9437184 | tf_op jit(solution)/shard_map/reduce_scatter | solution.py:235
  918.8 215.4 %reduce-scatter.28.cloned.1.call-start = ((), (), s32[]{:S(2)}) async-start(), calls=%async_computation.30 | async-start | bytes 9437184 | tf_op jit(solution)/shard_map/reduce_scatter | solution.py:232
  933.0 275.9 %reduce-scatter.32.cloned.1.call-start = ((), (), s32[]{:S(2)}) async-start(), calls=%async_computation.32 | async-start | bytes 9437184 | tf_op jit(solution)/shard_map/reduce_scatter | solution.py:238
  947.3 305.8 %reduce-scatter.26.cloned.1.call-start = ((), (), s32[]{:S(2)}) async-start(), calls=%async_computation.29 | async-start | bytes 2359296 | tf_op jit(solution)/shard_map/reduce_scatter | solution.py:229
  992.0 305.6 %reduce-scatter.24.cloned.1.call-start = ((), (), s32[]{:S(2)}) async-start(), calls=%async_computation.28 | async-start | bytes 2359296 | tf_op jit(solution)/shard_map/reduce_scatter | solution.py:226
  1025.0 317.0 %reduce-scatter.20.cloned.1.call-start = ((), (), s32[]{:S(2)}) async-start(), calls=%async_computation.26 | async-start | bytes 2359296 | tf_op jit(solution)/shard_map/reduce_scatter | solution.py:220
  1053.6 332.8 %reduce-scatter.22.cloned.1.call-start = ((), (), s32[]{:S(2)}) async-start(), calls=%async_computation.27 | async-start | bytes 2359296 | tf_op jit(solution)/shard_map/reduce_scatter | solution.py:223
  1061.4 404.1 %reduce-scatter.18.cloned.1.call-start = ((), (), s32[]{:S(2)}) async-start(), calls=%async_computation.25 | async-start | bytes 5242880 | tf_op jit(solution)/shard_map/reduce_scatter | solution.py:201
  1077.8 387.7 %copy-start.28 = (f32[256]{0:T(256)S(1)}, f32[256]{0:T(256)}, u32[]{:S(2)}) copy-start(f32[256]{0:T(256)} %copy-done.27) | copy-start | bytes 3076
  1077.8 387.7 %copy-start.30 = (f32[256]{0:T(256)S(1)}, f32[256]{0:T(256)}, u32[]{:S(2)}) copy-start(f32[256]{0:T(256)} %copy-done.29) | copy-start | bytes 3076
  (35 other events, 1477.1 us)
Sparse Core Ops, SparseCore 0:
  9.9 30.4 all-gather.17
  42.6 80.7 all-gather.11
  125.2 26.2 all-gather.15
  153.3 27.7 all-gather.13
  182.8 28.0 all-gather.19
  218.3 144.6 reduce-scatter.11
  364.8 54.8 all-gather.25
  421.9 80.7 all-gather.21
  504.5 52.7 all-gather.23
  558.7 80.7 all-gather.29
  641.4 54.3 all-gather.27
  743.6 76.7 reduce-scatter.15
  822.7 77.2 reduce-scatter.13
  904.8 81.2 all-gather.31
  989.4 69.9 reduce-scatter.29
  1062.7 71.4 reduce-scatter.27
  1137.6 71.2 reduce-scatter.31
  1212.0 41.1 reduce-scatter.25
  1256.5 41.1 reduce-scatter.23
  1300.8 41.1 reduce-scatter.19
  1345.2 41.0 reduce-scatter.21
  1388.6 76.7 reduce-scatter.17
where the time goes:
time: 1490 us; the launch traced here: 1480 us
  waiting for transfers between devices  1130 us (76%)
  matrix products  241 us (16%)
  other arithmetic  68.2 us (5%)
  local copies, waits for them, and re-layouts  23.8 us (2%)
  between operations  15.1 us (1%)
    reduce_scatter x1, waiting for transfers between devices, per_device(): lax.psum_scatter(product(attended, full_output), 'row', scatter_dimension...  144 us
    all_gather x1, waiting for transfers between devices, per_device(): first_rows = lax.all_gather(normed_first, 'row', axis=0, tiled=True)  82.9 us
    all_gather x1, waiting for transfers between devices, per_device(): second_rows = lax.all_gather(normed_second, 'row', axis=0, tiled=True)  82.9 us
    reduce_scatter x1, waiting for transfers between devices, per_device(): lax.psum_scatter(product(activation, full_down).astype(jnp.bfloat16), 'ro...  77.8 us
    reduce_scatter x1, waiting for transfers between devices, per_device(): lax.psum_scatter((times_transpose(grad_query, back_query) + times_transpo...  77.3 us
    reduce_scatter x1, waiting for transfers between devices, per_device(): lax.psum_scatter(grad_down_w.astype(jnp.bfloat16), 'col', scatter_dimensi...  71.8 us
    all_gather x1, waiting for transfers between devices, per_device(): grad_rows = lax.all_gather(cotangent, 'row', axis=0, tiled=True)  67.7 us
    dot_general x7, matrix products, times_transpose(): lax.dot_general(left, right, (((1,), (1,)), ((), ())), preferred_element_...  66.8 us
  transfers between devices with their start and end apart: 22, of which 21 were waited for; matrix products, arithmetic and copies ran while one was open for 18% of the time, Pallas kernels for 0%

commit v1 on v0

--- a/solution.py
+++ b/solution.py
@@ -28,6 +28,53 @@
     return lax.dot_general(
         left, right, (((1,), (1,)), ((), ())), preferred_element_type=jnp.float32
     )
+
+
+def line_all_gather(shard, axis):
+    n = lax.psum(1, axis)
+    if n == 1:
+        return shard
+    me = lax.axis_index(axis)
+    rows = shard.shape[0]
+    buf = jnp.zeros(((3 * n - 2) * rows,) + shard.shape[1:], shard.dtype)
+    buf = lax.dynamic_update_slice_in_dim(buf, shard, (me + n - 1) * rows, 0)
+    from_left = shard
+    from_right = shard
+    for step in range(1, n):
+        right_pairs = [(j, j + 1) for j in range(step - 1, n - 1)]
+        left_pairs = [(j, j - 1) for j in range(1, n - step + 1)]
+        from_left = lax.ppermute(from_left, axis, right_pairs)
+        from_right = lax.ppermute(from_right, axis, left_pairs)
+        buf = lax.dynamic_update_slice_in_dim(buf, from_left, (me - step + n - 1) * rows, 0)
+        buf = lax.dynamic_update_slice_in_dim(buf, from_right, (me + step + n - 1) * rows, 0)
+    return buf[(n - 1) * rows : (2 * n - 1) * rows]
+
+
+def line_reduce_scatter(partial, axis, send_dtype):
+    n = lax.psum(1, axis)
+    if n == 1:
+        return partial
+    me = lax.axis_index(axis)
+    rows = partial.shape[0] // n
+
+    def block(k):
+        return lax.dynamic_slice_in_dim(partial, jnp.clip(k, 0, n - 1) * rows, rows, 0)
+
+    recv_right = None
+    recv_left = None
+    for step in range(1, n):
+        send_right = block(n - step + me)
+        send_left = block(me + step - n)
+        if recv_right is not None:
+            send_right = send_right + recv_right
+            send_left = send_left + recv_left
+        recv_right = lax.ppermute(
+            send_right.astype(send_dtype), axis, [(j, j + 1) for j in range(0, step)]
+        ).astype(jnp.float32)
+        recv_left = lax.ppermute(
+            send_left.astype(send_dtype), axis, [(j, j - 1) for j in range(n - step, n)]
+        ).astype(jnp.float32)
+    return block(me) + recv_right + recv_left
 
 
 def layer_norm(inputs):
@@ -144,7 +191,7 @@
     cosine, sine = rope_tables()
     inputs = layer_input.astype(jnp.float32)
     normed_first = layer_norm(inputs).astype(jnp.bfloat16)
-    first_rows = lax.all_gather(normed_first, "row", axis=0, tiled=True)
+    first_rows = line_all_gather(normed_first, "row")
 
     def split_heads(matrix):
         return matrix.reshape(seq_count, LENGTH, heads_local, HD)
@@ -159,38 +206,31 @@
     values = split_heads(product(first_rows, full_value)).astype(jnp.bfloat16)
     mixed, log_total = lax.map(attend_forward, (queries, keys_rot, values, piece_starts))
     attended = merge_heads(mixed.astype(jnp.bfloat16))
-    attention_sum = lax.psum_scatter(
-        product(attended, full_output), "row", scatter_dimension=0, tiled=True
-    )
+    attention_sum = line_reduce_scatter(product(attended, full_output), "row", jnp.float32)
     middle = inputs + attention_sum
     normed_second = layer_norm(middle).astype(jnp.bfloat16)
-    second_rows = lax.all_gather(normed_second, "row", axis=0, tiled=True)
+    second_rows = line_all_gather(normed_second, "row")
     gate_lin = product(second_rows, full_gate)
     up_lin = product(second_rows, full_up)
     activation = (jax.nn.silu(gate_lin) * up_lin).astype(jnp.bfloat16)
-    ffn_sum = lax.psum_scatter(
-        product(activation, full_down).astype(jnp.bfloat16), "row", scatter_dimension=0, tiled=True
-    ).astype(jnp.float32)
+    ffn_sum = line_reduce_scatter(product(activation, full_down), "row", jnp.bfloat16)
     output = (middle + ffn_sum).astype(jnp.bfloat16)
     back_query, back_key, back_value, back_output = (full_query, full_key, full_value, full_output)
     back_gate, back_up, back_down = (full_gate, full_up, full_down)
-    grad_rows = lax.all_gather(cotangent, "row", axis=0, tiled=True)
+    grad_rows = line_all_gather(cotangent, "row")
     grad_activation = times_transpose(grad_rows, back_down)
     sigma = jax.nn.sigmoid(gate_lin)
     grad_gate = (grad_activation * up_lin * sigma * (1.0 + gate_lin * (1.0 - sigma))).astype(
         jnp.bfloat16
     )
     grad_up = (grad_activation * gate_lin * sigma).astype(jnp.bfloat16)
-    grad_second = lax.psum_scatter(
-        (times_transpose(grad_gate, back_gate) + times_transpose(grad_up, back_up)).astype(
-            jnp.bfloat16
-        ),
+    grad_second = line_reduce_scatter(
+        times_transpose(grad_gate, back_gate) + times_transpose(grad_up, back_up),
         "row",
-        scatter_dimension=0,
-        tiled=True,
-    ).astype(jnp.float32)
+        jnp.bfloat16,
+    )
     grad_middle = cotangent.astype(jnp.float32) + norm_back(middle, grad_second)
-    grad_branch = lax.all_gather(grad_middle.astype(jnp.bfloat16), "row", axis=0, tiled=True)
+    grad_branch = line_all_gather(grad_middle.astype(jnp.bfloat16), "row")
     grad_mixed = split_heads(times_transpose(grad_branch, back_output).astype(jnp.bfloat16))
     grad_q_rot, grad_k_rot, grad_values = lax.map(
         attend_backward, (queries, keys_rot, values, piece_starts, log_total, grad_mixed)
@@ -198,16 +238,13 @@
     grad_query = merge_heads(unrotate(grad_q_rot, cosine, sine)).astype(jnp.bfloat16)
     grad_key = merge_heads(unrotate(grad_k_rot, cosine, sine)).astype(jnp.bfloat16)
     grad_value = merge_heads(grad_values).astype(jnp.bfloat16)
-    grad_first = lax.psum_scatter(
-        (
-            times_transpose(grad_query, back_query)
-            + times_transpose(grad_key, back_key)
-            + times_transpose(grad_value, back_value)
-        ).astype(jnp.bfloat16),
+    grad_first = line_reduce_scatter(
+        times_transpose(grad_query, back_query)
+        + times_transpose(grad_key, back_key)
+        + times_transpose(grad_value, back_value),
         "row",
-        scatter_dimension=0,
-        tiled=True,
-    ).astype(jnp.float32)
+        jnp.bfloat16,
+    )
     grad_input = grad_middle + norm_back(inputs, grad_first)
     grad_query_w = contract_rows(first_rows, grad_query)
     grad_key_w = contract_rows(first_rows, grad_key)

time: 1490 us -> 1280 us (0.86)
  waiting for transfers between devices: 1130 us -> 646 us
  starting transfers between devices: 2.25 us -> 203 us
  local copies, waits for them, and re-layouts: 23.8 us -> 77.9 us
  other arithmetic: 68.2 us -> 94.5 us
    ppermute x0 -> x48, waiting for transfers between devices: none -> 475 us  [the longest x12 198 us: line_reduce_scatter(): lax.ppermute(send_right.astype(send_dtype), axis, [(j, j + 1) for j in ra...]
    reduce_scatter x4 -> x0, waiting for transfers between devices: 362 us -> none  [the longest x1 144 us: per_device(): lax.psum_scatter(product(attended, full_output), 'row', scatter_dimension...]
    all_gather x4 -> x0, waiting for transfers between devices: 272 us -> none  [the longest x1 82.9 us: per_device(): first_rows = lax.all_gather(normed_first, 'row', axis=0, tiled=True)]
    ppermute x0 -> x48, starting transfers between devices: none -> 202 us  [the longest x12 128 us: line_all_gather(): from_left = lax.ppermute(from_left, axis, right_pairs)]
    all_gather x1, waiting for transfers between devices: 56.3 us -> 0.01 us  [per_device(): lax.all_gather(w_down, 'col', axis=1, tiled=True)]
    all_gather x1, waiting for transfers between devices: 51.1 us -> 0.01 us  [per_device(): lax.all_gather(w_up, 'col', axis=0, tiled=True)]
    reduce_scatter x1, waiting for transfers between devices: 42.7 us -> 0.01 us  [per_device(): lax.psum_scatter(grad_value_w.astype(jnp.bfloat16), 'col', scatter_dimens...]
    reduce_scatter x1, waiting for transfers between devices: 42.6 us -> 0.01 us  [per_device(): lax.psum_scatter(grad_key_w.astype(jnp.bfloat16), 'col', scatter_dimensio...]
  transfers between devices with their start and end apart: 22 -> 62, of which waited for: 21 -> 31; matrix products, arithmetic and copies ran while one was open for 18% -> 28% of each run, Pallas kernels for 0% -> 0%
where the time goes in v1:
time: 1280 us
  waiting for transfers between devices  646 us (50%)
  matrix products  241 us (19%)
  starting transfers between devices  203 us (16%)
  other arithmetic  94.5 us (7%)
  local copies, waits for them, and re-layouts  77.9 us (6%)
  between operations  15.3 us (1%)
    ppermute x12, waiting for transfers between devices, line_reduce_scatter(): lax.ppermute(send_right.astype(send_dtype), axis, [(j, j + 1) for j in ra...  198 us
    ppermute x12, waiting for transfers between devices, line_all_gather(): from_right = lax.ppermute(from_right, axis, left_pairs)  187 us
    ppermute x12, starting transfers between devices, line_all_gather(): from_left = lax.ppermute(from_left, axis, right_pairs)  128 us
    reduce_scatter x1, waiting for transfers between devices, per_device(): lax.psum_scatter(grad_gate_w.astype(jnp.bfloat16), 'col', scatter_dimensi...  72.2 us
    reduce_scatter x1, waiting for transfers between devices, per_device(): lax.psum_scatter(grad_down_w.astype(jnp.bfloat16), 'col', scatter_dimensi...  71.9 us
    dot_general x7, matrix products, times_transpose(): lax.dot_general(left, right, (((1,), (1,)), ((), ())), preferred_element_...  71.3 us
    dot_general x7, matrix products, contract_rows(): lax.dot_general(left, right, (((0,), (0,)), ((), ())), preferred_element_...  64.9 us
    dot_general x7, matrix products, product(): return jnp.dot(left, right, preferred_element_type=jnp.float32)  62.6 us
  transfers between devices with their start and end apart: 62, of which 31 were waited for; matrix products, arithmetic and copies ran while one was open for 28% of the time, Pallas kernels for 0%

profile of v1, /device:TPU:0, one launch (start us, length us, event | category | flops | bytes accessed | tf_op | source)
XLA Modules:
  0.0 1278.6 jit_solution(11315879451042629948)
XLA Ops:
  26.7 20.9 %collective-permute-done = bf16[256,2048]{1,0:T(8,128)(2,1)S(1)} collective-permute-done((bf16[256,2048]{1,0:T(8,128)(2,1)S(1)}, bf16[256,2048]{1,0:T(8,128)(2,1)S(1)}, u32[]{:S(2)}, u32[]{:S(2)}) %collective-permute-start) | collective-permute-done | bytes 1048608 | tf_op jit(solution)/shard_map/ppermute | solution.py:46
  62.2 16.7 %collective-permute-done.3 = bf16[256,2048]{1,0:T(8,128)(2,1)} collective-permute-done((bf16[256,2048]{1,0:T(8,128)(2,1)}, bf16[256,2048]{1,0:T(8,128)(2,1)}, u32[]{:S(2)}, u32[]{:S(2)}) %collective-permute-start.3) | collective-permute-done | bytes 1048608 | tf_op jit(solution)/shard_map/ppermute | solution.py:47
  180.4 41.5 %collective-permute-done.6 = f32[256,2048]{1,0:T(8,128)} collective-permute-done((f32[256,2048]{1,0:T(8,128)S(1)}, f32[256,2048]{1,0:T(8,128)}, u32[]{:S(2)}, u32[]{:S(2)}) %collective-permute-start.6) | collective-permute-done | bytes 2097184 | tf_op jit(solution)/shard_map/ppermute | solution.py:71
  230.3 40.6 %collective-permute-done.7 = f32[256,2048]{1,0:T(8,128)} collective-permute-done((f32[256,2048]{1,0:T(8,128)S(1)}, f32[256,2048]{1,0:T(8,128)}, u32[]{:S(2)}, u32[]{:S(2)}) %collective-permute-start.7) | collective-permute-done | bytes 2097184 | tf_op jit(solution)/shard_map/ppermute | solution.py:71
  293.1 87.6 %collective-permute-start.24 = (bf16[256,2048]{1,0:T(8,128)(2,1)S(1)}, bf16[256,2048]{1,0:T(8,128)(2,1)}, u32[]{:S(2)}, u32[]{:S(2)}) collective-permute-start(bf16[256,2048]{1,0:T(8,128)(2,1)S(1)} %copy-done.9), channel_id=1, source_target_pairs={{0,8},{8,16},{16,24},{1,9},{9,17},{17,25},{2,10},{10,18},{18,26},{... | collective-permute-start | bytes 3145736 | tf_op jit(solution)/shard_map/ppermute | solution.py:46
  382.0 15.1 %collective-permute-done.24 = bf16[256,2048]{1,0:T(8,128)(2,1)} collective-permute-done((bf16[256,2048]{1,0:T(8,128)(2,1)S(1)}, bf16[256,2048]{1,0:T(8,128)(2,1)}, u32[]{:S(2)}, u32[]{:S(2)}) %collective-permute-start.24) | collective-permute-done | bytes 1048608 | tf_op jit(solution)/shard_map/ppermute | solution.py:46
  397.9 44.2 %collective-permute-done.25 = bf16[256,2048]{1,0:T(8,128)(2,1)} collective-permute-done((bf16[256,2048]{1,0:T(8,128)(2,1)S(1)}, bf16[256,2048]{1,0:T(8,128)(2,1)}, u32[]{:S(2)}, u32[]{:S(2)}) %collective-permute-start.25) | collective-permute-done | bytes 1048608 | tf_op jit(solution)/shard_map/ppermute | solution.py:47
  477.1 15.6 %collective-permute-done.13 = bf16[256,2048]{1,0:T(8,128)(2,1)S(1)} collective-permute-done((bf16[256,2048]{1,0:T(8,128)(2,1)S(1)}, bf16[256,2048]{1,0:T(8,128)(2,1)S(1)}, u32[]{:S(2)}, u32[]{:S(2)}) %collective-permute-start.13) | collective-permute-done | bytes 1048608 | tf_op jit(solution)/shard_map/ppermute | solution.py:47
  516.2 16.8 %collective-permute-done.15 = bf16[256,2048]{1,0:T(8,128)(2,1)S(1)} collective-permute-done((bf16[256,2048]{1,0:T(8,128)(2,1)S(1)}, bf16[256,2048]{1,0:T(8,128)(2,1)S(1)}, u32[]{:S(2)}, u32[]{:S(2)}) %collective-permute-start.15) | collective-permute-done | bytes 1048608 | tf_op jit(solution)/shard_map/ppermute | solution.py:47
  583.4 21.9 %multiply_convert_fusion.1 = (bf16[1024,2048]{1,0:T(8,128)(2,1)}, bf16[1024,2048]{1,0:T(8,128)(2,1)}, bf16[1024,2048]{1,0:T(8,128)(2,1)}) fusion(f32[1024,2048]{1,0:T(8,128)} %fusion.21, f32[1024,2048]{1,0:T(8,128)} %fusion.19, bf16[2048,2048]{1,0:T(8,128)(2,1)} %all-gather.20.cloned.1.call-done, bf16[2560,2048]{1,0:T(8,128)(2,1)} %constant_dynamic-update-slice_fusion.7), kind=kOutput, calls=%fused_computation.11 | convolution fusion | flops 8623489024 | bytes 41943040 | tf_op jit(solution)/shard_map/dot_general | solution.py:28
  633.3 15.7 %convolution_add_fusion = f32[1024,2048]{1,0:T(8,128)} fusion(f32[1024,2048]{1,0:T(8,128)} %fusion.72, bf16[1024,2048]{1,0:T(8,128)(2,1)} %get-tuple-element.75, bf16[2048,2048]{1,0:T(8,128)(2,1)} %all-gather.18.cloned.1.call-done), kind=kOutput, calls=%fused_computation.22 | convolution fusion | flops 8592031744 | bytes 29360128 | tf_op jit(solution)/shard_map/dot_general | solution.py:28
  657.1 19.9 %collective-permute-done.30 = bf16[256,2048]{1,0:T(8,128)(2,1)S(1)} collective-permute-done((bf16[256,2048]{1,0:T(8,128)(2,1)S(1)}, bf16[256,2048]{1,0:T(8,128)(2,1)S(1)}, u32[]{:S(2)}, u32[]{:S(2)}) %collective-permute-start.30) | collective-permute-done | bytes 1048608 | tf_op jit(solution)/shard_map/ppermute | solution.py:71
  681.8 17.7 %collective-permute-done.19 = bf16[256,2048]{1,0:T(8,128)(2,1)S(1)} collective-permute-done((bf16[256,2048]{1,0:T(8,128)(2,1)S(1)}, bf16[256,2048]{1,0:T(8,128)(2,1)S(1)}, u32[]{:S(2)}, u32[]{:S(2)}) %collective-permute-start.19) | collective-permute-done | bytes 1048608 | tf_op jit(solution)/shard_map/ppermute | solution.py:71
  729.6 15.7 %collective-permute-done.20 = bf16[256,2048]{1,0:T(8,128)(2,1)S(1)} collective-permute-done((bf16[256,2048]{1,0:T(8,128)(2,1)S(1)}, bf16[256,2048]{1,0:T(8,128)(2,1)S(1)}, u32[]{:S(2)}, u32[]{:S(2)}) %collective-permute-start.20) | collective-permute-done | bytes 1048608 | tf_op jit(solution)/shard_map/ppermute | solution.py:71
  773.6 22.9 %collective-permute-start.36 = (bf16[256,2048]{1,0:T(8,128)(2,1)S(1)}, bf16[256,2048]{1,0:T(8,128)(2,1)S(1)}, u32[]{:S(2)}, u32[]{:S(2)}) collective-permute-start(bf16[256,2048]{1,0:T(8,128)(2,1)S(1)} %get-tuple-element.56), channel_id=1, source_target_pairs={{0,8},{8,16},{16,24},{1,9},{9,17},{17,25},{2,10},{10,18},{18,26},{... | collective-permute-start | bytes 3145736 | tf_op jit(solution)/shard_map/ppermute | solution.py:46
  797.9 15.2 %collective-permute-done.36 = bf16[256,2048]{1,0:T(8,128)(2,1)S(1)} collective-permute-done((bf16[256,2048]{1,0:T(8,128)(2,1)S(1)}, bf16[256,2048]{1,0:T(8,128)(2,1)S(1)}, u32[]{:S(2)}, u32[]{:S(2)}) %collective-permute-start.36) | collective-permute-done | bytes 1048608 | tf_op jit(solution)/shard_map/ppermute | solution.py:46
  822.0 21.2 %collective-permute-done.39 = bf16[256,2048]{1,0:T(8,128)(2,1)S(1)} collective-permute-done((bf16[256,2048]{1,0:T(8,128)(2,1)S(1)}, bf16[256,2048]{1,0:T(8,128)(2,1)S(1)}, u32[]{:S(2)}, u32[]{:S(2)}) %collective-permute-start.39) | collective-permute-done | bytes 1048608 | tf_op jit(solution)/shard_map/ppermute | solution.py:47
  845.2 17.0 %collective-permute-done.41 = bf16[256,2048]{1,0:T(8,128)(2,1)S(1)} collective-permute-done((bf16[256,2048]{1,0:T(8,128)(2,1)S(1)}, bf16[256,2048]{1,0:T(8,128)(2,1)S(1)}, u32[]{:S(2)}, u32[]{:S(2)}) %collective-permute-start.41) | collective-permute-done | bytes 1048608 | tf_op jit(solution)/shard_map/ppermute | solution.py:47
  1002.8 17.6 %collective-permute-done.42 = bf16[256,2048]{1,0:T(8,128)(2,1)S(1)} collective-permute-done((bf16[256,2048]{1,0:T(8,128)(2,1)S(1)}, bf16[256,2048]{1,0:T(8,128)(2,1)S(1)}, u32[]{:S(2)}, u32[]{:S(2)}) %collective-permute-start.42) | collective-permute-done | bytes 1048608 | tf_op jit(solution)/shard_map/ppermute | solution.py:71
  1025.2 16.3 %collective-permute-done.43 = bf16[256,2048]{1,0:T(8,128)(2,1)S(1)} collective-permute-done((bf16[256,2048]{1,0:T(8,128)(2,1)S(1)}, bf16[256,2048]{1,0:T(8,128)(2,1)S(1)}, u32[]{:S(2)}, u32[]{:S(2)}) %collective-permute-start.43) | collective-permute-done | bytes 1048608 | tf_op jit(solution)/shard_map/ppermute | solution.py:71
  1061.7 28.3 %collective-permute-done.47 = bf16[256,2048]{1,0:T(8,128)(2,1)} collective-permute-done((bf16[256,2048]{1,0:T(8,128)(2,1)}, bf16[256,2048]{1,0:T(8,128)(2,1)}, u32[]{:S(2)}, u32[]{:S(2)}) %collective-permute-start.47) | collective-permute-done | bytes 1048608 | tf_op jit(solution)/shard_map/ppermute | solution.py:74
  1095.2 24.3 %reduce-scatter.18.cloned.1.call-done = bf16[256,2048]{1,0:T(8,128)(2,1)} async-done(((bf16[2048,2048]{1,0:T(8,128)(2,1)}), bf16[256,2048]{1,0:T(8,128)(2,1)}) %reduce-scatter.18.cloned.1.call-update) | async-done | bytes 1048592 | tf_op jit(solution)/shard_map/reduce_scatter | solution.py:272
  1122.3 72.2 %reduce-scatter.16.cloned.1.call-done = bf16[256,2048]{1,0:T(8,128)(2,1)} async-done(((bf16[2048,2048]{1,0:T(8,128)(2,1)}), bf16[256,2048]{1,0:T(8,128)(2,1)}) %reduce-scatter.16.cloned.1.call-update) | async-done | bytes 1048592 | tf_op jit(solution)/shard_map/reduce_scatter | solution.py:269
  1197.3 71.9 %reduce-scatter.20.cloned.1.call-done = bf16[2048,256]{1,0:T(8,128)(2,1)} async-done(((bf16[2048,2048]{1,0:T(8,128)(2,1)}), bf16[2048,256]{1,0:T(8,128)(2,1)}) %reduce-scatter.20.cloned.1.call-update) | async-done | bytes 1048592 | tf_op jit(solution)/shard_map/reduce_scatter | solution.py:275
  (309 shorter events, 566.4 us)
Async XLA Ops:
  7.2 99.2 %all-gather.10.cloned.1.call-start = ((), (), s32[]{:S(2)}) async-start(), calls=%async_computation.8 | async-start | bytes 2359296 | tf_op jit(solution)/shard_map/all_gather | solution.py:182
  7.9 110.4 %all-gather.12.cloned.1.call-start = ((), (), s32[]{:S(2)}) async-start(), calls=%async_computation.9 | async-start | bytes 2359296 | tf_op jit(solution)/shard_map/all_gather | solution.py:183
  8.7 129.1 %all-gather.8.cloned.1.call-start = ((), (), s32[]{:S(2)}) async-start(), calls=%async_computation.7 | async-start | bytes 2359296 | tf_op jit(solution)/shard_map/all_gather | solution.py:184
  9.4 159.7 %all-gather.14.cloned.1.call-start = ((), (), s32[]{:S(2)}) async-start(), calls=%async_computation.10 | async-start | bytes 2359296 | tf_op jit(solution)/shard_map/all_gather | solution.py:185
  10.0 544.5 %all-gather.18.cloned.1.call-start = ((), (), s32[]{:S(2)}) async-start(), calls=%async_computation.12 | async-start | bytes 9437184 | tf_op jit(solution)/shard_map/all_gather | solution.py:187
  10.6 558.4 %all-gather.16.cloned.1.call-start = ((), (), s32[]{:S(2)}) async-start(), calls=%async_computation.11 | async-start | bytes 9437184 | tf_op jit(solution)/shard_map/all_gather | solution.py:186
  26.6 556.7 %all-gather.20.cloned.1.call-start = ((), (), s32[]{:S(2)}) async-start(), calls=%async_computation.13 | async-start | bytes 9437184 | tf_op jit(solution)/shard_map/all_gather | solution.py:188
  177.5 44.4 %collective-permute-start.6 = (f32[256,2048]{1,0:T(8,128)S(1)}, f32[256,2048]{1,0:T(8,128)}, u32[]{:S(2)}, u32[]{:S(2)}) collective-permute-start(f32[256,2048]{1,0:T(8,128)S(1)} %constant_dynamic-slice_fusion.1), channel_id=1, source_target_pairs={{0,8},{1,9},{2,10},{3,11},{4,12},{5,13},{6,14},{7,15}} | collective-permute-start | bytes 6291464 | tf_op jit(solution)/shard_map/ppermute | solution.py:71
  224.4 46.5 %collective-permute-start.7 = (f32[256,2048]{1,0:T(8,128)S(1)}, f32[256,2048]{1,0:T(8,128)}, u32[]{:S(2)}, u32[]{:S(2)}) collective-permute-start(f32[256,2048]{1,0:T(8,128)S(1)} %dynamic-slice_add_fusion.2), channel_id=1, source_target_pairs={{0,8},{8,16},{1,9},{9,17},{2,10},{10,18},{3,11},{11,19},{4,12},{12... | collective-permute-start | bytes 6291464 | tf_op jit(solution)/shard_map/ppermute | solution.py:71
  277.3 775.4 %reduce-scatter.14.cloned.1.call-start = ((), (), s32[]{:S(2)}) async-start(), calls=%async_computation.17 | async-start | bytes 2359296 | tf_op jit(solution)/shard_map/reduce_scatter | solution.py:266
  282.6 160.8 %collective-permute-start.8 = (f32[256,2048]{1,0:T(8,128)}, f32[256,2048]{1,0:T(8,128)}, u32[]{:S(2)}, u32[]{:S(2)}) collective-permute-start(f32[256,2048]{1,0:T(8,128)} %get-tuple-element.90), channel_id=1, source_target_pairs={{0,8},{8,16},{16,24},{1,9},{9,17},{17,25},{2,10},{10,18},{18,26},{... | collective-permute-start | bytes 6291464 | tf_op jit(solution)/shard_map/ppermute | solution.py:71
  291.8 151.6 %collective-permute-start.11 = (f32[256,2048]{1,0:T(8,128)}, f32[256,2048]{1,0:T(8,128)}, u32[]{:S(2)}, u32[]{:S(2)}) collective-permute-start(f32[256,2048]{1,0:T(8,128)} %dynamic-slice_add_fusion.1), channel_id=1, source_target_pairs={{8,0},{16,8},{24,16},{9,1},{17,9},{25,17},{10,2},{18,10},{26,18},{... | collective-permute-start | bytes 6291464 | tf_op jit(solution)/shard_map/ppermute | solution.py:74
  293.1 104.0 %collective-permute-start.24 = (bf16[256,2048]{1,0:T(8,128)(2,1)S(1)}, bf16[256,2048]{1,0:T(8,128)(2,1)}, u32[]{:S(2)}, u32[]{:S(2)}) collective-permute-start(bf16[256,2048]{1,0:T(8,128)(2,1)S(1)} %copy-done.9), channel_id=1, source_target_pairs={{0,8},{8,16},{16,24},{1,9},{9,17},{17,25},{2,10},{10,18},{18,26},{... | collective-permute-start | bytes 3145736 | tf_op jit(solution)/shard_map/ppermute | solution.py:46
  380.7 61.4 %collective-permute-start.25 = (bf16[256,2048]{1,0:T(8,128)(2,1)S(1)}, bf16[256,2048]{1,0:T(8,128)(2,1)}, u32[]{:S(2)}, u32[]{:S(2)}) collective-permute-start(bf16[256,2048]{1,0:T(8,128)(2,1)S(1)} %copy-done.9), channel_id=1, source_target_pairs={{8,0},{16,8},{24,16},{9,1},{17,9},{25,17},{10,2},{18,10},{26,18},{... | collective-permute-start | bytes 3145736 | tf_op jit(solution)/shard_map/ppermute | solution.py:47
  397.2 62.5 %collective-permute-start.26 = (bf16[256,2048]{1,0:T(8,128)(2,1)}, bf16[256,2048]{1,0:T(8,128)(2,1)S(1)}, u32[]{:S(2)}, u32[]{:S(2)}) collective-permute-start(bf16[256,2048]{1,0:T(8,128)(2,1)} %collective-permute-done.24), channel_id=1, source_target_pairs={{8,16},{16,24},{9,17},{17,25},{10,18},{18,26},{11,19},{19,27},{12,... | collective-permute-start | bytes 3145736 | tf_op jit(solution)/shard_map/ppermute | solution.py:46
  470.3 44.9 %collective-permute-start.29 = (bf16[256,2048]{1,0:T(8,128)(2,1)S(1)}, bf16[256,2048]{1,0:T(8,128)(2,1)S(1)}, u32[]{:S(2)}, u32[]{:S(2)}) collective-permute-start(bf16[256,2048]{1,0:T(8,128)(2,1)S(1)} %collective-permute-done.27), channel_id=1, source_target_pairs={{8,0},{9,1},{10,2},{11,3},{12,4},{13,5},{14,6},{15,7}} | collective-permute-start | bytes 3145736 | tf_op jit(solution)/shard_map/ppermute | solution.py:47
  654.6 44.9 %collective-permute-start.19 = (bf16[256,2048]{1,0:T(8,128)(2,1)S(1)}, bf16[256,2048]{1,0:T(8,128)(2,1)S(1)}, u32[]{:S(2)}, u32[]{:S(2)}) collective-permute-start(bf16[256,2048]{1,0:T(8,128)(2,1)S(1)} %add_convert_fusion.14), channel_id=1, source_target_pairs={{0,8},{8,16},{1,9},{9,17},{2,10},{10,18},{3,11},{11,19},{4,12},{12... | collective-permute-start | bytes 3145736 | tf_op jit(solution)/shard_map/ppermute | solution.py:71
  655.9 45.0 %collective-permute-start.33 = (bf16[256,2048]{1,0:T(8,128)(2,1)S(1)}, bf16[256,2048]{1,0:T(8,128)(2,1)S(1)}, u32[]{:S(2)}, u32[]{:S(2)}) collective-permute-start(bf16[256,2048]{1,0:T(8,128)(2,1)S(1)} %get-tuple-element.85), channel_id=1, source_target_pairs={{24,16},{25,17},{26,18},{27,19},{28,20},{29,21},{30,22},{31,23}} | collective-permute-start | bytes 3145736 | tf_op jit(solution)/shard_map/ppermute | solution.py:74
  870.0 184.5 %reduce-scatter.12.cloned.1.call-start = ((), (), s32[]{:S(2)}) async-start(), calls=%async_computation.16 | async-start | bytes 2359296 | tf_op jit(solution)/shard_map/reduce_scatter | solution.py:263
  901.2 155.1 %reduce-scatter.10.cloned.1.call-start = ((), (), s32[]{:S(2)}) async-start(), calls=%async_computation.15 | async-start | bytes 2359296 | tf_op jit(solution)/shard_map/reduce_scatter | solution.py:260
  930.8 127.4 %reduce-scatter.8.cloned.1.call-start = ((), (), s32[]{:S(2)}) async-start(), calls=%async_computation.14 | async-start | bytes 2359296 | tf_op jit(solution)/shard_map/reduce_scatter | solution.py:257
  939.9 179.6 %reduce-scatter.18.cloned.1.call-start = ((), (), s32[]{:S(2)}) async-start(), calls=%async_computation.19 | async-start | bytes 9437184 | tf_op jit(solution)/shard_map/reduce_scatter | solution.py:272
  954.1 240.4 %reduce-scatter.16.cloned.1.call-start = ((), (), s32[]{:S(2)}) async-start(), calls=%async_computation.18 | async-start | bytes 9437184 | tf_op jit(solution)/shard_map/reduce_scatter | solution.py:269
  968.2 301.0 %reduce-scatter.20.cloned.1.call-start = ((), (), s32[]{:S(2)}) async-start(), calls=%async_computation.20 | async-start | bytes 9437184 | tf_op jit(solution)/shard_map/reduce_scatter | solution.py:275
  (76 other events, 1543.5 us)
Sparse Core Ops, SparseCore 0:
  9.9 30.4 all-gather.9
  42.3 27.7 all-gather.11
  72.0 27.7 all-gather.7
  101.5 28.0 all-gather.13
  131.4 54.2 all-gather.17
  187.4 54.2 all-gather.15
  277.4 58.4 all-gather.19
  870.1 39.6 reduce-scatter.13
  913.7 41.0 reduce-scatter.11
  958.5 41.1 reduce-scatter.9
  1003.5 41.0 reduce-scatter.7
  1048.0 71.4 reduce-scatter.17
  1123.0 71.4 reduce-scatter.15
  1197.8 71.2 reduce-scatter.19

commit v2 on v1

--- a/solution.py
+++ b/solution.py
@@ -3,7 +3,7 @@
 import jax
 import jax.numpy as jnp
 from jax import lax
-from jax.sharding import PartitionSpec as P
+from jax.sharding import Mesh, PartitionSpec as P
 
 HD = 128
 LENGTH = 1024
@@ -77,6 +77,34 @@
     return block(me) + recv_right + recv_left
 
 
+COL = ("chip", "core")
+
+
+def col_gather(block, axis):
+    part = lax.all_gather(block, "chip", axis=axis, tiled=True)
+    both = lax.all_gather(part, "core", axis=axis, tiled=False)
+    shape = both.shape
+    chips = lax.psum(1, "chip")
+    size = block.shape[axis]
+    split = shape[:axis] + (2, chips, size) + shape[axis + 2 :]
+    order = list(range(len(split)))
+    order[axis], order[axis + 1] = axis + 1, axis
+    merged = shape[:axis] + (2 * chips * size,) + shape[axis + 2 :]
+    return both.reshape(split).transpose(order).reshape(merged)
+
+
+def col_scatter(partial, axis):
+    chips = lax.psum(1, "chip")
+    shape = partial.shape
+    size = shape[axis] // (2 * chips)
+    split = shape[:axis] + (chips, 2, size) + shape[axis + 1 :]
+    order = list(range(len(split)))
+    order[axis], order[axis + 1] = axis + 1, axis
+    low_part = partial.reshape(split).transpose(order).reshape(shape).astype(jnp.bfloat16)
+    half = lax.psum_scatter(low_part, "core", scatter_dimension=axis, tiled=True)
+    return lax.psum_scatter(half, "chip", scatter_dimension=axis, tiled=True).astype(jnp.float32)
+
+
 def layer_norm(inputs):
     center = inputs - jnp.mean(inputs, axis=-1, keepdims=True)
     spread = jnp.mean(center * center, axis=-1, keepdims=True)
@@ -179,13 +207,13 @@
     group_rows = seq_count * LENGTH
     heads_local = w_query.shape[1] // HD
     gathered = (
-        lax.all_gather(w_query, "col", axis=0, tiled=True),
-        lax.all_gather(w_key, "col", axis=0, tiled=True),
-        lax.all_gather(w_value, "col", axis=0, tiled=True),
-        lax.all_gather(w_output, "col", axis=1, tiled=True),
-        lax.all_gather(w_gate, "col", axis=0, tiled=True),
-        lax.all_gather(w_up, "col", axis=0, tiled=True),
-        lax.all_gather(w_down, "col", axis=1, tiled=True),
+        col_gather(w_query, 0),
+        col_gather(w_key, 0),
+        col_gather(w_value, 0),
+        col_gather(w_output, 1),
+        col_gather(w_gate, 0),
+        col_gather(w_up, 0),
+        col_gather(w_down, 1),
     )
     full_query, full_key, full_value, full_output, full_gate, full_up, full_down = gathered
     cosine, sine = rope_tables()
@@ -206,7 +234,7 @@
     values = split_heads(product(first_rows, full_value)).astype(jnp.bfloat16)
     mixed, log_total = lax.map(attend_forward, (queries, keys_rot, values, piece_starts))
     attended = merge_heads(mixed.astype(jnp.bfloat16))
-    attention_sum = line_reduce_scatter(product(attended, full_output), "row", jnp.float32)
+    attention_sum = line_reduce_scatter(product(attended, full_output), "row", jnp.bfloat16)
     middle = inputs + attention_sum
     normed_second = layer_norm(middle).astype(jnp.bfloat16)
     second_rows = line_all_gather(normed_second, "row")
@@ -254,27 +282,13 @@
     grad_up_w = contract_rows(second_rows, grad_up)
     grad_down_w = contract_rows(activation, grad_rows)
     summed = (
-        lax.psum_scatter(
-            grad_query_w.astype(jnp.bfloat16), "col", scatter_dimension=0, tiled=True
-        ).astype(jnp.float32),
-        lax.psum_scatter(
-            grad_key_w.astype(jnp.bfloat16), "col", scatter_dimension=0, tiled=True
-        ).astype(jnp.float32),
-        lax.psum_scatter(
-            grad_value_w.astype(jnp.bfloat16), "col", scatter_dimension=0, tiled=True
-        ).astype(jnp.float32),
-        lax.psum_scatter(
-            grad_output_w.astype(jnp.bfloat16), "col", scatter_dimension=1, tiled=True
-        ).astype(jnp.float32),
-        lax.psum_scatter(
-            grad_gate_w.astype(jnp.bfloat16), "col", scatter_dimension=0, tiled=True
-        ).astype(jnp.float32),
-        lax.psum_scatter(
-            grad_up_w.astype(jnp.bfloat16), "col", scatter_dimension=0, tiled=True
-        ).astype(jnp.float32),
-        lax.psum_scatter(
-            grad_down_w.astype(jnp.bfloat16), "col", scatter_dimension=1, tiled=True
-        ).astype(jnp.float32),
+        col_scatter(grad_query_w, 0),
+        col_scatter(grad_key_w, 0),
+        col_scatter(grad_value_w, 0),
+        col_scatter(grad_output_w, 1),
+        col_scatter(grad_gate_w, 0),
+        col_scatter(grad_up_w, 0),
+        col_scatter(grad_down_w, 1),
     )
     results = tuple(summed)
     return (
@@ -292,28 +306,32 @@
 
 def solution(mesh):
     in_specs = (
-        P(("col", "row"), None),
-        P("col", "row"),
-        P("col", "row"),
-        P("col", "row"),
-        P("row", "col"),
-        P("col", "row"),
-        P("col", "row"),
-        P("row", "col"),
-        P("col", None),
-        P(("col", "row"), None),
+        P(("chip", "core", "row"), None),
+        P(COL, "row"),
+        P(COL, "row"),
+        P(COL, "row"),
+        P("row", COL),
+        P(COL, "row"),
+        P(COL, "row"),
+        P("row", COL),
+        P(COL, None),
+        P(("chip", "core", "row"), None),
     )
     out_specs = (
-        P(("col", "row"), None),
-        P(("col", "row"), None),
-        P("col", "row"),
-        P("col", "row"),
-        P("col", "row"),
-        P("row", "col"),
-        P("col", "row"),
-        P("col", "row"),
-        P("row", "col"),
+        P(("chip", "core", "row"), None),
+        P(("chip", "core", "row"), None),
+        P(COL, "row"),
+        P(COL, "row"),
+        P(COL, "row"),
+        P("row", COL),
+        P(COL, "row"),
+        P(COL, "row"),
+        P("row", COL),
+    )
+    devices = mesh.devices
+    sub_mesh = Mesh(
+        devices.reshape(devices.shape[0], devices.shape[1] // 2, 2), ("row", "chip", "core")
     )
     return jax.shard_map(
-        per_device, mesh=mesh, in_specs=in_specs, out_specs=out_specs, check_vma=False
-    )
+        per_device, mesh=sub_mesh, in_specs=in_specs, out_specs=out_specs, check_vma=False
+    )

time: 1280 us -> 1410 us (1.10)
  local copies, waits for them, and re-layouts: 77.9 us -> 200 us
  waiting for transfers between devices: 646 us -> 750 us
  starting transfers between devices: 203 us -> 131 us
  other arithmetic: 94.5 us -> 70.5 us
    all_gather x7 -> x14, waiting for transfers between devices: 0.04 us -> 164 us  [the longest x7 164 us: col_gather(): part = lax.all_gather(block, 'chip', axis=axis, tiled=True)]
    ppermute x12, starting transfers between devices: 128 us -> 54.2 us  [line_all_gather(): from_left = lax.ppermute(from_left, axis, right_pairs)]
    convert_element_type x0 -> x8, local copies, waits for them, and re-layouts: none -> 51.7 us  [col_scatter(): partial.reshape(split).transpose(order).reshape(shape).astype(jnp.bfloat16)]
    ppermute x12, waiting for transfers between devices: 187 us -> 140 us  [line_all_gather(): from_right = lax.ppermute(from_right, axis, left_pairs)]
    transpose x0 -> x7, local copies, waits for them, and re-layouts: none -> 45.4 us  [col_gather(): return both.reshape(split).transpose(order).reshape(merged)]
    ppermute x12, waiting for transfers between devices: 198 us -> 174 us  [line_reduce_scatter(): lax.ppermute(send_right.astype(send_dtype), axis, [(j, j + 1) for j in ra...]
    dot_general x0 -> x4, local copies, waits for them, and re-layouts: none -> 20.1 us  [contract_rows(): lax.dot_general(left, right, (((0,), (0,)), ((), ())), preferred_element_...]
    add x4 -> x0, other arithmetic: 15.3 us -> none  [the longest x2 8.03 us: line_reduce_scatter(): send_right = send_right + recv_right]
  transfers between devices with their start and end apart: 62 -> 76, of which waited for: 31 -> 38; matrix products, arithmetic and copies ran while one was open for 28% -> 30% of each run, Pallas kernels for 0% -> 0%
where the time goes in v2:
time: 1410 us; the launch traced here: 1400 us
  waiting for transfers between devices  750 us (53%)
  matrix products  234 us (17%)
  local copies, waits for them, and re-layouts  200 us (14%)
  starting transfers between devices  131 us (9%)
  other arithmetic  70.5 us (5%)
  between operations  16.1 us (1%)
    reduce_scatter x7, waiting for transfers between devices, col_scatter(): lax.psum_scatter(half, 'chip', scatter_dimension=axis, tiled=True)  176 us
    ppermute x12, waiting for transfers between devices, line_reduce_scatter(): lax.ppermute(send_right.astype(send_dtype), axis, [(j, j + 1) for j in ra...  174 us
    all_gather x7, waiting for transfers between devices, col_gather(): part = lax.all_gather(block, 'chip', axis=axis, tiled=True)  164 us
    ppermute x12, waiting for transfers between devices, line_all_gather(): from_right = lax.ppermute(from_right, axis, left_pairs)  140 us
    dot_general x7, matrix products, times_transpose(): lax.dot_general(left, right, (((1,), (1,)), ((), ())), preferred_element_...  79.2 us
    dot_general x7, matrix products, product(): return jnp.dot(left, right, preferred_element_type=jnp.float32)  58.7 us
    dot_general x7, matrix products, contract_rows(): lax.dot_general(left, right, (((0,), (0,)), ((), ())), preferred_element_...  58.6 us
    ppermute x12, starting transfers between devices, line_all_gather(): from_left = lax.ppermute(from_left, axis, right_pairs)  54.2 us
  transfers between devices with their start and end apart: 76, of which 38 were waited for; matrix products, arithmetic and copies ran while one was open for 30% of the time, Pallas kernels for 0%

profile of v2, /device:TPU:0, one launch (start us, length us, event | category | flops | bytes accessed | tf_op | source)
XLA Modules:
  0.0 1401.1 jit_solution(3543992335280637462)
XLA Ops:
  11.9 27.2 %all-gather.24.cloned.1.call-done = bf16[1024,512]{1,0:T(8,128)(2,1)} async-done(((bf16[256,512]{1,0:T(8,128)(2,1)}), bf16[1024,512]{1,0:T(8,128)(2,1)}) %all-gather.24.cloned.1.call-update) | async-done | bytes 1048592 | tf_op jit(solution)/shard_map/all_gather | solution.py:84
  39.2 28.3 %all-gather.26.cloned.1.call-done = bf16[1024,512]{1,0:T(8,128)(2,1)} async-done(((bf16[256,512]{1,0:T(8,128)(2,1)}), bf16[1024,512]{1,0:T(8,128)(2,1)}) %all-gather.26.cloned.1.call-update) | async-done | bytes 1048592 | tf_op jit(solution)/shard_map/all_gather | solution.py:84
  67.5 28.3 %all-gather.22.cloned.1.call-done = bf16[1024,512]{1,0:T(8,128)(2,1)} async-done(((bf16[256,512]{1,0:T(8,128)(2,1)}), bf16[1024,512]{1,0:T(8,128)(2,1)}) %all-gather.22.cloned.1.call-update) | async-done | bytes 1048592 | tf_op jit(solution)/shard_map/all_gather | solution.py:84
  95.9 28.7 %all-gather.28.cloned.1.call-done = bf16[512,1024]{0,1:T(8,128)(2,1)} async-done(((bf16[512,256]{0,1:T(8,128)(2,1)}), bf16[512,1024]{0,1:T(8,128)(2,1)}) %all-gather.28.cloned.1.call-update) | async-done | bytes 1048592 | tf_op jit(solution)/shard_map/all_gather | solution.py:84
  127.5 51.5 %all-gather.32.cloned.1.call-done = bf16[1024,2048]{1,0:T(8,128)(2,1)} async-done(((bf16[256,2048]{1,0:T(8,128)(2,1)}), bf16[1024,2048]{1,0:T(8,128)(2,1)}) %all-gather.32.cloned.1.call-update) | async-done | bytes 4194320 | tf_op jit(solution)/shard_map/all_gather | solution.py:84
  190.4 20.9 %collective-permute-done = bf16[256,2048]{1,0:T(8,128)(2,1)S(1)} collective-permute-done((bf16[256,2048]{1,0:T(8,128)(2,1)S(1)}, bf16[256,2048]{1,0:T(8,128)(2,1)S(1)}, u32[]{:S(2)}, u32[]{:S(2)}) %collective-permute-start) | collective-permute-done | bytes 1048608 | tf_op jit(solution)/shard_map/ppermute | solution.py:46
  224.8 17.5 %collective-permute-done.3 = bf16[256,2048]{1,0:T(8,128)(2,1)} collective-permute-done((bf16[256,2048]{1,0:T(8,128)(2,1)}, bf16[256,2048]{1,0:T(8,128)(2,1)}, u32[]{:S(2)}, u32[]{:S(2)}) %collective-permute-start.3) | collective-permute-done | bytes 1048608 | tf_op jit(solution)/shard_map/ppermute | solution.py:47
  350.1 17.3 %collective-permute-done.6 = bf16[256,2048]{1,0:T(8,128)(2,1)} collective-permute-done((bf16[256,2048]{1,0:T(8,128)(2,1)S(1)}, bf16[256,2048]{1,0:T(8,128)(2,1)}, u32[]{:S(2)}, u32[]{:S(2)}) %collective-permute-start.6) | collective-permute-done | bytes 1048608 | tf_op jit(solution)/shard_map/ppermute | solution.py:71
  376.0 18.4 %collective-permute-done.7 = bf16[256,2048]{1,0:T(8,128)(2,1)} collective-permute-done((bf16[256,2048]{1,0:T(8,128)(2,1)}, bf16[256,2048]{1,0:T(8,128)(2,1)}, u32[]{:S(2)}, u32[]{:S(2)}) %collective-permute-start.7) | collective-permute-done | bytes 1048608 | tf_op jit(solution)/shard_map/ppermute | solution.py:71
  467.6 18.6 %collective-permute-start.12 = (bf16[256,2048]{1,0:T(8,128)(2,1)S(1)}, bf16[256,2048]{1,0:T(8,128)(2,1)S(1)}, u32[]{:S(2)}, u32[]{:S(2)}) collective-permute-start(bf16[256,2048]{1,0:T(8,128)(2,1)S(1)} %get-tuple-element.97), channel_id=1, source_target_pairs={{0,8},{8,16},{16,24},{1,9},{9,17},{17,25},{2,10},{10,18},{18,26},{... | collective-permute-start | bytes 3145736 | tf_op jit(solution)/shard_map/ppermute | solution.py:46
  537.7 16.8 %collective-permute-done.15 = bf16[256,2048]{1,0:T(8,128)(2,1)S(1)} collective-permute-done((bf16[256,2048]{1,0:T(8,128)(2,1)S(1)}, bf16[256,2048]{1,0:T(8,128)(2,1)S(1)}, u32[]{:S(2)}, u32[]{:S(2)}) %collective-permute-start.15) | collective-permute-done | bytes 1048608 | tf_op jit(solution)/shard_map/ppermute | solution.py:47
  625.1 22.1 %multiply_convert_fusion.1 = (bf16[1024,2048]{1,0:T(8,128)(2,1)}, bf16[1024,2048]{1,0:T(8,128)(2,1)}, bf16[1024,2048]{1,0:T(8,128)(2,1)}) fusion(f32[1024,2048]{1,0:T(8,128)} %fusion.22, f32[1024,2048]{1,0:T(8,128)} %fusion.20, bf16[2048,2048]{0,1:T(8,128)(2,1)} %bitcast.171, bf16[2560,2048]{1,0:T(8,128)(2,1)} %constant_dynamic-update-slice_fusion.7), kind=kOutput, calls=%fused_computation.11 | convolution fusion | flops 8623489024 | bytes 41943040 | tf_op jit(solution)/shard_map/dot_general | solution.py:28
  675.5 15.8 %convolution_add_fusion = f32[1024,2048]{1,0:T(8,128)} fusion(f32[1024,2048]{1,0:T(8,128)} %fusion.71, bf16[1024,2048]{1,0:T(8,128)(2,1)} %get-tuple-element.102, bf16[2048,2048]{1,0:T(8,128)(2,1)} %bitcast.168), kind=kOutput, calls=%fused_computation.28 | convolution fusion | flops 8592031744 | bytes 29360128 | tf_op jit(solution)/shard_map/dot_general | solution.py:28
  699.2 20.1 %collective-permute-done.30 = bf16[256,2048]{1,0:T(8,128)(2,1)S(1)} collective-permute-done((bf16[256,2048]{1,0:T(8,128)(2,1)S(1)}, bf16[256,2048]{1,0:T(8,128)(2,1)S(1)}, u32[]{:S(2)}, u32[]{:S(2)}) %collective-permute-start.30) | collective-permute-done | bytes 1048608 | tf_op jit(solution)/shard_map/ppermute | solution.py:71
  724.1 16.5 %collective-permute-done.19 = bf16[256,2048]{1,0:T(8,128)(2,1)S(1)} collective-permute-done((bf16[256,2048]{1,0:T(8,128)(2,1)S(1)}, bf16[256,2048]{1,0:T(8,128)(2,1)S(1)}, u32[]{:S(2)}, u32[]{:S(2)}) %collective-permute-start.19) | collective-permute-done | bytes 1048608 | tf_op jit(solution)/shard_map/ppermute | solution.py:71
  817.0 18.6 %collective-permute-start.36 = (bf16[256,2048]{1,0:T(8,128)(2,1)S(1)}, bf16[256,2048]{1,0:T(8,128)(2,1)S(1)}, u32[]{:S(2)}, u32[]{:S(2)}) collective-permute-start(bf16[256,2048]{1,0:T(8,128)(2,1)S(1)} %get-tuple-element.93), channel_id=1, source_target_pairs={{0,8},{8,16},{16,24},{1,9},{9,17},{17,25},{2,10},{10,18},{18,26},{... | collective-permute-start | bytes 3145736 | tf_op jit(solution)/shard_map/ppermute | solution.py:46
  864.5 25.9 %collective-permute-done.39 = bf16[256,2048]{1,0:T(8,128)(2,1)S(1)} collective-permute-done((bf16[256,2048]{1,0:T(8,128)(2,1)S(1)}, bf16[256,2048]{1,0:T(8,128)(2,1)S(1)}, u32[]{:S(2)}, u32[]{:S(2)}) %collective-permute-start.39) | collective-permute-done | bytes 1048608 | tf_op jit(solution)/shard_map/ppermute | solution.py:47
  1119.2 17.7 %collective-permute-done.42 = bf16[256,2048]{1,0:T(8,128)(2,1)S(1)} collective-permute-done((bf16[256,2048]{1,0:T(8,128)(2,1)S(1)}, bf16[256,2048]{1,0:T(8,128)(2,1)S(1)}, u32[]{:S(2)}, u32[]{:S(2)}) %collective-permute-start.42) | collective-permute-done | bytes 1048608 | tf_op jit(solution)/shard_map/ppermute | solution.py:71
  1141.6 16.7 %collective-permute-done.43 = bf16[256,2048]{1,0:T(8,128)(2,1)S(1)} collective-permute-done((bf16[256,2048]{1,0:T(8,128)(2,1)S(1)}, bf16[256,2048]{1,0:T(8,128)(2,1)S(1)}, u32[]{:S(2)}, u32[]{:S(2)}) %collective-permute-start.43) | collective-permute-done | bytes 1048608 | tf_op jit(solution)/shard_map/ppermute | solution.py:71
  1180.5 19.2 %collective-permute-done.47 = bf16[256,2048]{1,0:T(8,128)(2,1)S(1)} collective-permute-done((bf16[256,2048]{1,0:T(8,128)(2,1)S(1)}, bf16[256,2048]{1,0:T(8,128)(2,1)S(1)}, u32[]{:S(2)}, u32[]{:S(2)}) %collective-permute-start.47) | collective-permute-done | bytes 1048608 | tf_op jit(solution)/shard_map/ppermute | solution.py:74
  1208.1 16.8 %reduce-scatter.17.cloned.1.call-done = bf16[256,512]{1,0:T(8,128)(2,1)} async-done(((bf16[1024,512]{1,0:T(8,128)(2,1)}), bf16[256,512]{1,0:T(8,128)(2,1)}) %reduce-scatter.17.cloned.1.call-update) | async-done | bytes 262160 | tf_op jit(solution)/shard_map/reduce_scatter | solution.py:105
  1226.7 53.7 %reduce-scatter.33.cloned.1.call-done = bf16[256,2048]{1,0:T(8,128)(2,1)} async-done(((bf16[1024,2048]{1,0:T(8,128)(2,1)}), bf16[256,2048]{1,0:T(8,128)(2,1)}) %reduce-scatter.33.cloned.1.call-update) | async-done | bytes 1048592 | tf_op jit(solution)/shard_map/reduce_scatter | solution.py:105
  1283.1 52.7 %reduce-scatter.37.cloned.1.call-done = bf16[256,2048]{1,0:T(8,128)(2,1)} async-done(((bf16[1024,2048]{1,0:T(8,128)(2,1)}), bf16[256,2048]{1,0:T(8,128)(2,1)}) %reduce-scatter.37.cloned.1.call-update) | async-done | bytes 1048592 | tf_op jit(solution)/shard_map/reduce_scatter | solution.py:105
  1338.6 52.8 %reduce-scatter.41.cloned.1.call-done = bf16[2048,256]{1,0:T(8,128)(2,1)} async-done(((bf16[2048,1024]{1,0:T(8,128)(2,1)}), bf16[2048,256]{1,0:T(8,128)(2,1)}) %reduce-scatter.41.cloned.1.call-update) | async-done | bytes 1048592 | tf_op jit(solution)/shard_map/reduce_scatter | solution.py:105
  (405 shorter events, 763.0 us)
Async XLA Ops:
  8.7 87.2 %all-gather.22.cloned.1.call-start = ((), (), s32[]{:S(2)}) async-start(), calls=%async_computation.14 | async-start | bytes 1310720 | tf_op jit(solution)/shard_map/all_gather | solution.py:84
  9.4 115.2 %all-gather.28.cloned.1.call-start = ((), (), s32[]{:S(2)}) async-start(), calls=%async_computation.17 | async-start | bytes 1310720 | tf_op jit(solution)/shard_map/all_gather | solution.py:84
  11.3 167.7 %all-gather.32.cloned.1.call-start = ((), (), s32[]{:S(2)}) async-start(), calls=%async_computation.19 | async-start | bytes 5242880 | tf_op jit(solution)/shard_map/all_gather | solution.py:84
  11.9 256.7 %all-gather.38.cloned.1.call-start = ((), (), s32[]{:S(2)}) async-start(), calls=%async_computation.36 | async-start | bytes 3145728 | tf_op jit(solution)/shard_map/all_gather | solution.py:85
  39.1 237.3 %all-gather.40.cloned.1.call-start = ((), (), s32[]{:S(2)}) async-start(), calls=%async_computation.37 | async-start | bytes 3145728 | tf_op jit(solution)/shard_map/all_gather | solution.py:85
  67.5 216.7 %all-gather.36.cloned.1.call-start = ((), (), s32[]{:S(2)}) async-start(), calls=%async_computation.35 | async-start | bytes 3145728 | tf_op jit(solution)/shard_map/all_gather | solution.py:85
  95.9 197.9 %all-gather.42.cloned.1.call-start = ((), (), s32[]{:S(2)}) async-start(), calls=%async_computation.38 | async-start | bytes 3145728 | tf_op jit(solution)/shard_map/all_gather | solution.py:85
  124.7 205.7 %all-gather.30.cloned.1.call-start = ((), (), s32[]{:S(2)}) async-start(), calls=%async_computation.18 | async-start | bytes 5242880 | tf_op jit(solution)/shard_map/all_gather | solution.py:84
  125.3 306.7 %all-gather.34.cloned.1.call-start = ((), (), s32[]{:S(2)}) async-start(), calls=%async_computation.20 | async-start | bytes 5242880 | tf_op jit(solution)/shard_map/all_gather | solution.py:84
  126.8 445.4 %all-gather.46.cloned.1.call-start = ((), (), s32[]{:S(2)}) async-start(), calls=%async_computation.40 | async-start | bytes 12582912 | tf_op jit(solution)/shard_map/all_gather | solution.py:85
  179.0 401.6 %all-gather.44.cloned.1.call-start = ((), (), s32[]{:S(2)}) async-start(), calls=%async_computation.39 | async-start | bytes 12582912 | tf_op jit(solution)/shard_map/all_gather | solution.py:85
  330.4 286.4 %all-gather.48.cloned.1.call-start = ((), (), s32[]{:S(2)}) async-start(), calls=%async_computation.41 | async-start | bytes 12582912 | tf_op jit(solution)/shard_map/all_gather | solution.py:85
  432.0 654.1 %reduce-scatter.27.cloned.1.call-start = ((), (), s32[]{:S(2)}) async-start(), calls=%async_computation.27 | async-start | bytes 3145728 | tf_op jit(solution)/shard_map/reduce_scatter | solution.py:104
  925.9 160.9 %reduce-scatter.23.cloned.1.call-start = ((), (), s32[]{:S(2)}) async-start(), calls=%async_computation.25 | async-start | bytes 3145728 | tf_op jit(solution)/shard_map/reduce_scatter | solution.py:104
  966.9 120.7 %reduce-scatter.19.cloned.1.call-start = ((), (), s32[]{:S(2)}) async-start(), calls=%async_computation.23 | async-start | bytes 3145728 | tf_op jit(solution)/shard_map/reduce_scatter | solution.py:104
  991.1 97.0 %reduce-scatter.15.cloned.1.call-start = ((), (), s32[]{:S(2)}) async-start(), calls=%async_computation.21 | async-start | bytes 3145728 | tf_op jit(solution)/shard_map/reduce_scatter | solution.py:104
  997.7 91.2 %reduce-scatter.31.cloned.1.call-start = ((), (), s32[]{:S(2)}) async-start(), calls=%async_computation.29 | async-start | bytes 12582912 | tf_op jit(solution)/shard_map/reduce_scatter | solution.py:104
  1086.0 116.6 %reduce-scatter.29.cloned.1.call-start = ((), (), s32[]{:S(2)}) async-start(), calls=%async_computation.28 | async-start | bytes 1310720 | tf_op jit(solution)/shard_map/reduce_scatter | solution.py:105
  1086.8 117.7 %reduce-scatter.25.cloned.1.call-start = ((), (), s32[]{:S(2)}) async-start(), calls=%async_computation.26 | async-start | bytes 1310720 | tf_op jit(solution)/shard_map/reduce_scatter | solution.py:105
  1087.5 118.8 %reduce-scatter.21.cloned.1.call-start = ((), (), s32[]{:S(2)}) async-start(), calls=%async_computation.24 | async-start | bytes 1310720 | tf_op jit(solution)/shard_map/reduce_scatter | solution.py:105
  1088.1 136.8 %reduce-scatter.17.cloned.1.call-start = ((), (), s32[]{:S(2)}) async-start(), calls=%async_computation.22 | async-start | bytes 1310720 | tf_op jit(solution)/shard_map/reduce_scatter | solution.py:105
  1088.8 191.5 %reduce-scatter.33.cloned.1.call-start = ((), (), s32[]{:S(2)}) async-start(), calls=%async_computation.30 | async-start | bytes 5242880 | tf_op jit(solution)/shard_map/reduce_scatter | solution.py:105
  1089.4 246.4 %reduce-scatter.37.cloned.1.call-start = ((), (), s32[]{:S(2)}) async-start(), calls=%async_computation.32 | async-start | bytes 5242880 | tf_op jit(solution)/shard_map/reduce_scatter | solution.py:105
  1090.0 301.4 %reduce-scatter.41.cloned.1.call-start = ((), (), s32[]{:S(2)}) async-start(), calls=%async_computation.34 | async-start | bytes 5242880 | tf_op jit(solution)/shard_map/reduce_scatter | solution.py:105
  (109 other events, 2621.5 us)
Sparse Core Ops, SparseCore 0:
  9.8 29.2 all-gather.23
  40.9 26.4 all-gather.25
  69.3 26.4 all-gather.21
  98.1 26.4 all-gather.27
  126.3 52.5 all-gather.31
  192.5 11.7 all-gather.39
  205.8 11.7 all-gather.35
  219.1 11.7 all-gather.41
  232.6 53.7 all-gather.29
  288.8 52.5 all-gather.33
  342.8 19.8 all-gather.45
  364.2 21.0 all-gather.43
  432.1 40.9 all-gather.47
  1000.9 11.0 reduce-scatter.14
  1020.7 13.7 reduce-scatter.30
  1043.2 13.9 reduce-scatter.34
  1086.1 14.1 reduce-scatter.38
  1103.2 29.2 reduce-scatter.28
  1135.3 27.9 reduce-scatter.24
  1166.0 27.9 reduce-scatter.20
  1196.9 27.9 reduce-scatter.16
  1227.7 52.5 reduce-scatter.32
  1283.1 52.5 reduce-scatter.36
  1338.7 52.5 reduce-scatter.40
  (4 shorter events, 31.3 us)

commit v3 on v2

--- a/solution.py
+++ b/solution.py
@@ -4,6 +4,7 @@
 import jax.numpy as jnp
 from jax import lax
 from jax.sharding import Mesh, PartitionSpec as P
+
 
 HD = 128
 LENGTH = 1024
@@ -81,28 +82,12 @@
 
 
 def col_gather(block, axis):
-    part = lax.all_gather(block, "chip", axis=axis, tiled=True)
-    both = lax.all_gather(part, "core", axis=axis, tiled=False)
-    shape = both.shape
-    chips = lax.psum(1, "chip")
-    size = block.shape[axis]
-    split = shape[:axis] + (2, chips, size) + shape[axis + 2 :]
-    order = list(range(len(split)))
-    order[axis], order[axis + 1] = axis + 1, axis
-    merged = shape[:axis] + (2 * chips * size,) + shape[axis + 2 :]
-    return both.reshape(split).transpose(order).reshape(merged)
+    return lax.all_gather(block, COL, axis=axis, tiled=True)
 
 
 def col_scatter(partial, axis):
-    chips = lax.psum(1, "chip")
-    shape = partial.shape
-    size = shape[axis] // (2 * chips)
-    split = shape[:axis] + (chips, 2, size) + shape[axis + 1 :]
-    order = list(range(len(split)))
-    order[axis], order[axis + 1] = axis + 1, axis
-    low_part = partial.reshape(split).transpose(order).reshape(shape).astype(jnp.bfloat16)
-    half = lax.psum_scatter(low_part, "core", scatter_dimension=axis, tiled=True)
-    return lax.psum_scatter(half, "chip", scatter_dimension=axis, tiled=True).astype(jnp.float32)
+    low_part = partial.astype(jnp.bfloat16)
+    return lax.psum_scatter(low_part, COL, scatter_dimension=axis, tiled=True).astype(jnp.float32)
 
 
 def layer_norm(inputs):
@@ -200,7 +185,7 @@
     return (grad_queries, grad_keys, grad_values)
 
 
-def per_device(
+def per_device_body(
     layer_input, w_query, w_key, w_value, w_output, w_gate, w_up, w_down, piece_starts, cotangent
 ):
     seq_count = piece_starts.shape[0]
@@ -333,5 +318,5 @@
         devices.reshape(devices.shape[0], devices.shape[1] // 2, 2), ("row", "chip", "core")
     )
     return jax.shard_map(
-        per_device, mesh=sub_mesh, in_specs=in_specs, out_specs=out_specs, check_vma=False
-    )
+        per_device_body, mesh=sub_mesh, in_specs=in_specs, out_specs=out_specs, check_vma=False
+    )

time: 1410 us -> 1140 us (0.81)
  waiting for transfers between devices: 750 us -> 575 us
  local copies, waits for them, and re-layouts: 200 us -> 78 us
  other arithmetic: 70.5 us -> 88 us
    all_gather x14 -> x7, waiting for transfers between devices: 164 us -> 0.04 us  [col_gather(): return lax.all_gather(block, COL, axis=axis, tiled=True)]
    convert_element_type x8 -> x0, local copies, waits for them, and re-layouts: 51.7 us -> none  [col_scatter(): partial.reshape(split).transpose(order).reshape(shape).astype(jnp.bfloat16)]
    transpose x7 -> x0, local copies, waits for them, and re-layouts: 45.4 us -> none  [col_gather(): return both.reshape(split).transpose(order).reshape(merged)]
    dot_general x4 -> x0, local copies, waits for them, and re-layouts: 20.1 us -> none  [contract_rows(): lax.dot_general(left, right, (((0,), (0,)), ((), ())), preferred_element_...]
    reduce_scatter x14 -> x7, waiting for transfers between devices: 176 us -> 169 us  [col_scatter(): lax.psum_scatter(low_part, COL, scatter_dimension=axis, tiled=True)]
  transfers between devices with their start and end apart: 76 -> 62, of which waited for: 38 -> 32; matrix products, arithmetic and copies ran while one was open for 30% -> 31% of each run, Pallas kernels for 0% -> 0%
where the time goes in v3:
time: 1140 us; the launch traced here: 1130 us
  waiting for transfers between devices  575 us (50%)
  matrix products  240 us (21%)
  starting transfers between devices  134 us (12%)
  other arithmetic  88 us (8%)
  local copies, waits for them, and re-layouts  78 us (7%)
  between operations  15.3 us (1%)
    ppermute x12, waiting for transfers between devices, line_reduce_scatter(): lax.ppermute(send_right.astype(send_dtype), axis, [(j, j + 1) for j in ra...  174 us
    reduce_scatter x7, waiting for transfers between devices, col_scatter(): lax.psum_scatter(low_part, COL, scatter_dimension=axis, tiled=True)  169 us
    ppermute x12, waiting for transfers between devices, line_all_gather(): from_right = lax.ppermute(from_right, axis, left_pairs)  141 us
    dot_general x7, matrix products, times_transpose(): lax.dot_general(left, right, (((1,), (1,)), ((), ())), preferred_element_...  71.4 us
    dot_general x7, matrix products, contract_rows(): lax.dot_general(left, right, (((0,), (0,)), ((), ())), preferred_element_...  64.5 us
    dot_general x7, matrix products, product(): return jnp.dot(left, right, preferred_element_type=jnp.float32)  62.5 us
    ppermute x12, starting transfers between devices, line_all_gather(): from_left = lax.ppermute(from_left, axis, right_pairs)  57.4 us
    ppermute x12, waiting for transfers between devices, line_all_gather(): from_left = lax.ppermute(from_left, axis, right_pairs)  47.4 us
  transfers between devices with their start and end apart: 62, of which 32 were waited for; matrix products, arithmetic and copies ran while one was open for 31% of the time, Pallas kernels for 0%

profile of v3, /device:TPU:0, one launch (start us, length us, event | category | flops | bytes accessed | tf_op | source)
XLA Modules:
  0.0 1130.9 jit_solution(16351415300923217913)
XLA Ops:
  26.0 21.0 %collective-permute-done = bf16[256,2048]{1,0:T(8,128)(2,1)S(1)} collective-permute-done((bf16[256,2048]{1,0:T(8,128)(2,1)S(1)}, bf16[256,2048]{1,0:T(8,128)(2,1)S(1)}, u32[]{:S(2)}, u32[]{:S(2)}) %collective-permute-start) | collective-permute-done | bytes 1048608 | tf_op jit(solution)/shard_map/ppermute | solution.py:47
  61.6 16.7 %collective-permute-done.3 = bf16[256,2048]{1,0:T(8,128)(2,1)} collective-permute-done((bf16[256,2048]{1,0:T(8,128)(2,1)}, bf16[256,2048]{1,0:T(8,128)(2,1)}, u32[]{:S(2)}, u32[]{:S(2)}) %collective-permute-start.3) | collective-permute-done | bytes 1048608 | tf_op jit(solution)/shard_map/ppermute | solution.py:48
  181.0 17.6 %collective-permute-done.6 = bf16[256,2048]{1,0:T(8,128)(2,1)} collective-permute-done((bf16[256,2048]{1,0:T(8,128)(2,1)S(1)}, bf16[256,2048]{1,0:T(8,128)(2,1)}, u32[]{:S(2)}, u32[]{:S(2)}) %collective-permute-start.6) | collective-permute-done | bytes 1048608 | tf_op jit(solution)/shard_map/ppermute | solution.py:72
  207.2 19.0 %collective-permute-done.7 = bf16[256,2048]{1,0:T(8,128)(2,1)} collective-permute-done((bf16[256,2048]{1,0:T(8,128)(2,1)}, bf16[256,2048]{1,0:T(8,128)(2,1)}, u32[]{:S(2)}, u32[]{:S(2)}) %collective-permute-start.7) | collective-permute-done | bytes 1048608 | tf_op jit(solution)/shard_map/ppermute | solution.py:72
  297.9 20.3 %collective-permute-start.12 = (bf16[256,2048]{1,0:T(8,128)(2,1)S(1)}, bf16[256,2048]{1,0:T(8,128)(2,1)S(1)}, u32[]{:S(2)}, u32[]{:S(2)}) collective-permute-start(bf16[256,2048]{1,0:T(8,128)(2,1)S(1)} %get-tuple-element.70), channel_id=1, source_target_pairs={{0,8},{8,16},{16,24},{1,9},{9,17},{17,25},{2,10},{10,18},{18,26},{... | collective-permute-start | bytes 3145736 | tf_op jit(solution)/shard_map/ppermute | solution.py:47
  353.6 15.0 %collective-permute-done.29 = bf16[256,2048]{1,0:T(8,128)(2,1)S(1)} collective-permute-done((bf16[256,2048]{1,0:T(8,128)(2,1)S(1)}, bf16[256,2048]{1,0:T(8,128)(2,1)S(1)}, u32[]{:S(2)}, u32[]{:S(2)}) %collective-permute-start.29) | collective-permute-done | bytes 1048608 | tf_op jit(solution)/shard_map/ppermute | solution.py:48
  369.6 16.8 %collective-permute-done.15 = bf16[256,2048]{1,0:T(8,128)(2,1)S(1)} collective-permute-done((bf16[256,2048]{1,0:T(8,128)(2,1)S(1)}, bf16[256,2048]{1,0:T(8,128)(2,1)S(1)}, u32[]{:S(2)}, u32[]{:S(2)}) %collective-permute-start.15) | collective-permute-done | bytes 1048608 | tf_op jit(solution)/shard_map/ppermute | solution.py:48
  404.6 14.5 %fusion.19 = f32[1024,2048]{1,0:T(8,128)} fusion(bf16[2048,2048]{1,0:T(8,128)(2,1)} %all-gather.18.cloned.1.call-done, bf16[2560,2048]{1,0:T(8,128)(2,1)} %constant_dynamic-update-slice_fusion.14), kind=kOutput, calls=%fused_computation.39 | convolution fusion | flops 8589934592 | bytes 20971520 | tf_op jit(solution)/shard_map/dot_general | solution.py:19
  419.1 14.6 %fusion.21 = f32[1024,2048]{1,0:T(8,128)} fusion(bf16[2048,2048]{1,0:T(8,128)(2,1)} %all-gather.16.cloned.1.call-done, bf16[2560,2048]{1,0:T(8,128)(2,1)} %constant_dynamic-update-slice_fusion.14), kind=kOutput, calls=%fused_computation.41 | convolution fusion | flops 8589934592 | bytes 20971520 | tf_op jit(solution)/shard_map/dot_general | solution.py:19
  433.7 21.8 %multiply_convert_fusion.1 = (bf16[1024,2048]{1,0:T(8,128)(2,1)}, bf16[1024,2048]{1,0:T(8,128)(2,1)}, bf16[1024,2048]{1,0:T(8,128)(2,1)}) fusion(f32[1024,2048]{1,0:T(8,128)} %fusion.21, f32[1024,2048]{1,0:T(8,128)} %fusion.19, bf16[2048,2048]{1,0:T(8,128)(2,1)} %all-gather.20.cloned.1.call-done, bf16[2560,2048]{1,0:T(8,128)(2,1)} %constant_dynamic-update-slice_fusion.7), kind=kOutput, calls=%fused_computation.11 | convolution fusion | flops 8623489024 | bytes 41943040 | tf_op jit(solution)/shard_map/dot_general | solution.py:29
  483.6 15.8 %convolution_add_fusion = f32[1024,2048]{1,0:T(8,128)} fusion(f32[1024,2048]{1,0:T(8,128)} %fusion.72, bf16[1024,2048]{1,0:T(8,128)(2,1)} %get-tuple-element.75, bf16[2048,2048]{1,0:T(8,128)(2,1)} %all-gather.18.cloned.1.call-done), kind=kOutput, calls=%fused_computation.22 | convolution fusion | flops 8592031744 | bytes 29360128 | tf_op jit(solution)/shard_map/dot_general | solution.py:29
  507.3 20.1 %collective-permute-done.30 = bf16[256,2048]{1,0:T(8,128)(2,1)S(1)} collective-permute-done((bf16[256,2048]{1,0:T(8,128)(2,1)S(1)}, bf16[256,2048]{1,0:T(8,128)(2,1)S(1)}, u32[]{:S(2)}, u32[]{:S(2)}) %collective-permute-start.30) | collective-permute-done | bytes 1048608 | tf_op jit(solution)/shard_map/ppermute | solution.py:72
  532.2 17.4 %collective-permute-done.19 = bf16[256,2048]{1,0:T(8,128)(2,1)S(1)} collective-permute-done((bf16[256,2048]{1,0:T(8,128)(2,1)S(1)}, bf16[256,2048]{1,0:T(8,128)(2,1)S(1)}, u32[]{:S(2)}, u32[]{:S(2)}) %collective-permute-start.19) | collective-permute-done | bytes 1048608 | tf_op jit(solution)/shard_map/ppermute | solution.py:72
  551.0 14.7 %collective-permute-done.31 = bf16[256,2048]{1,0:T(8,128)(2,1)S(1)} collective-permute-done((bf16[256,2048]{1,0:T(8,128)(2,1)S(1)}, bf16[256,2048]{1,0:T(8,128)(2,1)S(1)}, u32[]{:S(2)}, u32[]{:S(2)}) %collective-permute-start.31) | collective-permute-done | bytes 1048608 | tf_op jit(solution)/shard_map/ppermute | solution.py:72
  580.0 14.5 %collective-permute-done.20 = bf16[256,2048]{1,0:T(8,128)(2,1)S(1)} collective-permute-done((bf16[256,2048]{1,0:T(8,128)(2,1)S(1)}, bf16[256,2048]{1,0:T(8,128)(2,1)S(1)}, u32[]{:S(2)}, u32[]{:S(2)}) %collective-permute-start.20) | collective-permute-done | bytes 1048608 | tf_op jit(solution)/shard_map/ppermute | solution.py:72
  626.0 19.5 %collective-permute-start.36 = (bf16[256,2048]{1,0:T(8,128)(2,1)S(1)}, bf16[256,2048]{1,0:T(8,128)(2,1)S(1)}, u32[]{:S(2)}, u32[]{:S(2)}) collective-permute-start(bf16[256,2048]{1,0:T(8,128)(2,1)S(1)} %get-tuple-element.56), channel_id=1, source_target_pairs={{0,8},{8,16},{16,24},{1,9},{9,17},{17,25},{2,10},{10,18},{18,26},{... | collective-permute-start | bytes 3145736 | tf_op jit(solution)/shard_map/ppermute | solution.py:47
  673.5 25.0 %collective-permute-done.39 = bf16[256,2048]{1,0:T(8,128)(2,1)S(1)} collective-permute-done((bf16[256,2048]{1,0:T(8,128)(2,1)S(1)}, bf16[256,2048]{1,0:T(8,128)(2,1)S(1)}, u32[]{:S(2)}, u32[]{:S(2)}) %collective-permute-start.39) | collective-permute-done | bytes 1048608 | tf_op jit(solution)/shard_map/ppermute | solution.py:48
  700.5 14.7 %collective-permute-done.41 = bf16[256,2048]{1,0:T(8,128)(2,1)S(1)} collective-permute-done((bf16[256,2048]{1,0:T(8,128)(2,1)S(1)}, bf16[256,2048]{1,0:T(8,128)(2,1)S(1)}, u32[]{:S(2)}, u32[]{:S(2)}) %collective-permute-start.41) | collective-permute-done | bytes 1048608 | tf_op jit(solution)/shard_map/ppermute | solution.py:48
  855.8 21.8 %collective-permute-done.42 = bf16[256,2048]{1,0:T(8,128)(2,1)S(1)} collective-permute-done((bf16[256,2048]{1,0:T(8,128)(2,1)S(1)}, bf16[256,2048]{1,0:T(8,128)(2,1)S(1)}, u32[]{:S(2)}, u32[]{:S(2)}) %collective-permute-start.42) | collective-permute-done | bytes 1048608 | tf_op jit(solution)/shard_map/ppermute | solution.py:72
  882.4 22.0 %collective-permute-done.43 = bf16[256,2048]{1,0:T(8,128)(2,1)S(1)} collective-permute-done((bf16[256,2048]{1,0:T(8,128)(2,1)S(1)}, bf16[256,2048]{1,0:T(8,128)(2,1)S(1)}, u32[]{:S(2)}, u32[]{:S(2)}) %collective-permute-start.43) | collective-permute-done | bytes 1048608 | tf_op jit(solution)/shard_map/ppermute | solution.py:72
  924.6 17.5 %collective-permute-done.47 = bf16[256,2048]{1,0:T(8,128)(2,1)} collective-permute-done((bf16[256,2048]{1,0:T(8,128)(2,1)}, bf16[256,2048]{1,0:T(8,128)(2,1)}, u32[]{:S(2)}, u32[]{:S(2)}) %collective-permute-start.47) | collective-permute-done | bytes 1048608 | tf_op jit(solution)/shard_map/ppermute | solution.py:75
  947.4 24.5 %reduce-scatter.18.cloned.1.call-done = bf16[256,2048]{1,0:T(8,128)(2,1)} async-done(((bf16[2048,2048]{1,0:T(8,128)(2,1)}), bf16[256,2048]{1,0:T(8,128)(2,1)}) %reduce-scatter.18.cloned.1.call-update) | async-done | bytes 1048592 | tf_op jit(solution)/shard_map/reduce_scatter | solution.py:90
  974.7 72.2 %reduce-scatter.16.cloned.1.call-done = bf16[256,2048]{1,0:T(8,128)(2,1)} async-done(((bf16[2048,2048]{1,0:T(8,128)(2,1)}), bf16[256,2048]{1,0:T(8,128)(2,1)}) %reduce-scatter.16.cloned.1.call-update) | async-done | bytes 1048592 | tf_op jit(solution)/shard_map/reduce_scatter | solution.py:90
  1049.6 71.9 %reduce-scatter.20.cloned.1.call-done = bf16[2048,256]{1,0:T(8,128)(2,1)} async-done(((bf16[2048,2048]{1,0:T(8,128)(2,1)}), bf16[2048,256]{1,0:T(8,128)(2,1)}) %reduce-scatter.20.cloned.1.call-update) | async-done | bytes 1048592 | tf_op jit(solution)/shard_map/reduce_scatter | solution.py:90
  (308 shorter events, 566.7 us)
Async XLA Ops:
  7.2 98.5 %all-gather.10.cloned.1.call-start = ((), (), s32[]{:S(2)}) async-start(), calls=%async_computation.8 | async-start | bytes 2359296 | tf_op jit(solution)/shard_map/all_gather | solution.py:85
  7.9 109.7 %all-gather.12.cloned.1.call-start = ((), (), s32[]{:S(2)}) async-start(), calls=%async_computation.9 | async-start | bytes 2359296 | tf_op jit(solution)/shard_map/all_gather | solution.py:85
  8.7 128.3 %all-gather.8.cloned.1.call-start = ((), (), s32[]{:S(2)}) async-start(), calls=%async_computation.7 | async-start | bytes 2359296 | tf_op jit(solution)/shard_map/all_gather | solution.py:85
  9.4 158.4 %all-gather.14.cloned.1.call-start = ((), (), s32[]{:S(2)}) async-start(), calls=%async_computation.10 | async-start | bytes 2359296 | tf_op jit(solution)/shard_map/all_gather | solution.py:85
  10.0 394.6 %all-gather.18.cloned.1.call-start = ((), (), s32[]{:S(2)}) async-start(), calls=%async_computation.12 | async-start | bytes 9437184 | tf_op jit(solution)/shard_map/all_gather | solution.py:85
  10.6 408.5 %all-gather.16.cloned.1.call-start = ((), (), s32[]{:S(2)}) async-start(), calls=%async_computation.11 | async-start | bytes 9437184 | tf_op jit(solution)/shard_map/all_gather | solution.py:85
  11.1 422.5 %all-gather.20.cloned.1.call-start = ((), (), s32[]{:S(2)}) async-start(), calls=%async_computation.13 | async-start | bytes 9437184 | tf_op jit(solution)/shard_map/all_gather | solution.py:85
  179.3 736.3 %reduce-scatter.14.cloned.1.call-start = ((), (), s32[]{:S(2)}) async-start(), calls=%async_computation.17 | async-start | bytes 2359296 | tf_op jit(solution)/shard_map/reduce_scatter | solution.py:90
  238.7 39.0 %collective-permute-start.8 = (bf16[256,2048]{1,0:T(8,128)(2,1)S(1)}, bf16[256,2048]{1,0:T(8,128)(2,1)}, u32[]{:S(2)}, u32[]{:S(2)}) collective-permute-start(bf16[256,2048]{1,0:T(8,128)(2,1)S(1)} %get-tuple-element.90), channel_id=1, source_target_pairs={{0,8},{8,16},{16,24},{1,9},{9,17},{17,25},{2,10},{10,18},{18,26},{... | collective-permute-start | bytes 3145736 | tf_op jit(solution)/shard_map/ppermute | solution.py:72
  247.5 40.7 %collective-permute-start.11 = (bf16[256,2048]{1,0:T(8,128)(2,1)}, bf16[256,2048]{1,0:T(8,128)(2,1)}, u32[]{:S(2)}, u32[]{:S(2)}) collective-permute-start(bf16[256,2048]{1,0:T(8,128)(2,1)} %add_convert_fusion.15), channel_id=1, source_target_pairs={{8,0},{16,8},{24,16},{9,1},{17,9},{25,17},{10,2},{18,10},{26,18},{... | collective-permute-start | bytes 3145736 | tf_op jit(solution)/shard_map/ppermute | solution.py:75
  260.0 59.5 %collective-permute-start.26 = (bf16[256,2048]{1,0:T(8,128)(2,1)}, bf16[256,2048]{1,0:T(8,128)(2,1)S(1)}, u32[]{:S(2)}, u32[]{:S(2)}) collective-permute-start(bf16[256,2048]{1,0:T(8,128)(2,1)} %collective-permute-done.24), channel_id=1, source_target_pairs={{8,16},{16,24},{9,17},{17,25},{10,18},{18,26},{11,19},{19,27},{12,... | collective-permute-start | bytes 3145736 | tf_op jit(solution)/shard_map/ppermute | solution.py:47
  262.2 64.3 %collective-permute-start.27 = (bf16[256,2048]{1,0:T(8,128)(2,1)}, bf16[256,2048]{1,0:T(8,128)(2,1)S(1)}, u32[]{:S(2)}, u32[]{:S(2)}) collective-permute-start(bf16[256,2048]{1,0:T(8,128)(2,1)} %collective-permute-done.25), channel_id=1, source_target_pairs={{8,0},{16,8},{9,1},{17,9},{10,2},{18,10},{11,3},{19,11},{12,4},{20... | collective-permute-start | bytes 3145736 | tf_op jit(solution)/shard_map/ppermute | solution.py:48
  326.5 42.1 %collective-permute-start.29 = (bf16[256,2048]{1,0:T(8,128)(2,1)S(1)}, bf16[256,2048]{1,0:T(8,128)(2,1)S(1)}, u32[]{:S(2)}, u32[]{:S(2)}) collective-permute-start(bf16[256,2048]{1,0:T(8,128)(2,1)S(1)} %collective-permute-done.27), channel_id=1, source_target_pairs={{8,0},{9,1},{10,2},{11,3},{12,4},{13,5},{14,6},{15,7}} | collective-permute-start | bytes 3145736 | tf_op jit(solution)/shard_map/ppermute | solution.py:48
  346.1 40.4 %collective-permute-start.15 = (bf16[256,2048]{1,0:T(8,128)(2,1)S(1)}, bf16[256,2048]{1,0:T(8,128)(2,1)S(1)}, u32[]{:S(2)}, u32[]{:S(2)}) collective-permute-start(bf16[256,2048]{1,0:T(8,128)(2,1)S(1)} %collective-permute-done.13), channel_id=1, source_target_pairs={{8,0},{16,8},{9,1},{17,9},{10,2},{18,10},{11,3},{19,11},{12,4},{20... | collective-permute-start | bytes 3145736 | tf_op jit(solution)/shard_map/ppermute | solution.py:48
  352.8 39.5 %collective-permute-start.16 = (bf16[256,2048]{1,0:T(8,128)(2,1)S(1)}, bf16[256,2048]{1,0:T(8,128)(2,1)S(1)}, u32[]{:S(2)}, u32[]{:S(2)}) collective-permute-start(bf16[256,2048]{1,0:T(8,128)(2,1)S(1)} %collective-permute-done.14), channel_id=1, source_target_pairs={{16,24},{17,25},{18,26},{19,27},{20,28},{21,29},{22,30},{23,31}} | collective-permute-start | bytes 3145736 | tf_op jit(solution)/shard_map/ppermute | solution.py:47
  505.0 44.6 %collective-permute-start.19 = (bf16[256,2048]{1,0:T(8,128)(2,1)S(1)}, bf16[256,2048]{1,0:T(8,128)(2,1)S(1)}, u32[]{:S(2)}, u32[]{:S(2)}) collective-permute-start(bf16[256,2048]{1,0:T(8,128)(2,1)S(1)} %add_convert_fusion.14), channel_id=1, source_target_pairs={{0,8},{8,16},{1,9},{9,17},{2,10},{10,18},{3,11},{11,19},{4,12},{12... | collective-permute-start | bytes 3145736 | tf_op jit(solution)/shard_map/ppermute | solution.py:72
  506.3 44.7 %collective-permute-start.33 = (bf16[256,2048]{1,0:T(8,128)(2,1)S(1)}, bf16[256,2048]{1,0:T(8,128)(2,1)S(1)}, u32[]{:S(2)}, u32[]{:S(2)}) collective-permute-start(bf16[256,2048]{1,0:T(8,128)(2,1)S(1)} %get-tuple-element.85), channel_id=1, source_target_pairs={{24,16},{25,17},{26,18},{27,19},{28,20},{29,21},{30,22},{31,23}} | collective-permute-start | bytes 3145736 | tf_op jit(solution)/shard_map/ppermute | solution.py:75
  578.7 39.4 %collective-permute-start.35 = (bf16[256,2048]{1,0:T(8,128)(2,1)S(1)}, bf16[256,2048]{1,0:T(8,128)(2,1)S(1)}, u32[]{:S(2)}, u32[]{:S(2)}) collective-permute-start(bf16[256,2048]{1,0:T(8,128)(2,1)S(1)} %add_convert_fusion.6), channel_id=1, source_target_pairs={{8,0},{16,8},{24,16},{9,1},{17,9},{25,17},{10,2},{18,10},{26,18},{... | collective-permute-start | bytes 3145736 | tf_op jit(solution)/shard_map/ppermute | solution.py:75
  723.0 194.4 %reduce-scatter.12.cloned.1.call-start = ((), (), s32[]{:S(2)}) async-start(), calls=%async_computation.16 | async-start | bytes 2359296 | tf_op jit(solution)/shard_map/reduce_scatter | solution.py:90
  754.2 165.0 %reduce-scatter.10.cloned.1.call-start = ((), (), s32[]{:S(2)}) async-start(), calls=%async_computation.15 | async-start | bytes 2359296 | tf_op jit(solution)/shard_map/reduce_scatter | solution.py:90
  783.8 137.3 %reduce-scatter.8.cloned.1.call-start = ((), (), s32[]{:S(2)}) async-start(), calls=%async_computation.14 | async-start | bytes 2359296 | tf_op jit(solution)/shard_map/reduce_scatter | solution.py:90
  792.5 179.3 %reduce-scatter.18.cloned.1.call-start = ((), (), s32[]{:S(2)}) async-start(), calls=%async_computation.19 | async-start | bytes 9437184 | tf_op jit(solution)/shard_map/reduce_scatter | solution.py:90
  806.7 240.1 %reduce-scatter.16.cloned.1.call-start = ((), (), s32[]{:S(2)}) async-start(), calls=%async_computation.18 | async-start | bytes 9437184 | tf_op jit(solution)/shard_map/reduce_scatter | solution.py:90
  820.8 300.7 %reduce-scatter.20.cloned.1.call-start = ((), (), s32[]{:S(2)}) async-start(), calls=%async_computation.20 | async-start | bytes 9437184 | tf_op jit(solution)/shard_map/reduce_scatter | solution.py:90
  (76 other events, 1522.7 us)
Sparse Core Ops, SparseCore 0:
  9.9 30.4 all-gather.9
  42.3 27.7 all-gather.11
  72.0 27.7 all-gather.7
  101.5 28.0 all-gather.13
  131.4 54.2 all-gather.17
  187.4 54.2 all-gather.15
  243.6 55.8 all-gather.19
  723.1 38.9 reduce-scatter.13
  766.0 41.1 reduce-scatter.11
  810.9 41.1 reduce-scatter.9
  855.9 41.1 reduce-scatter.7
  900.3 71.4 reduce-scatter.17
  975.3 71.4 reduce-scatter.15
  1050.2 71.2 reduce-scatter.19

commit v4 on v3

--- a/solution.py
+++ b/solution.py
@@ -78,6 +78,98 @@
     return block(me) + recv_right + recv_left
 
 
+class GatherSteps:
+    def __init__(self, shard, axis):
+        self.axis = axis
+        self.n = lax.psum(1, axis)
+        self.me = lax.axis_index(axis)
+        self.rows = shard.shape[0]
+        buf = jnp.zeros(((3 * self.n - 2) * self.rows,) + shard.shape[1:], shard.dtype)
+        self.buf = lax.dynamic_update_slice_in_dim(buf, shard, (self.me + self.n - 1) * self.rows, 0)
+        self.pending = (shard, shard)
+        self.step = 0
+
+    def steps(self):
+        return self.n - 1
+
+    def send(self):
+        n, step = self.n, self.step + 1
+        from_left, from_right = self.pending
+        from_left = lax.ppermute(from_left, self.axis, [(j, j + 1) for j in range(step - 1, n - 1)])
+        from_right = lax.ppermute(from_right, self.axis, [(j, j - 1) for j in range(1, n - step + 1)])
+        self.pending = (from_left, from_right)
+        self.step = step
+
+    def land(self):
+        n, step, rows = self.n, self.step, self.rows
+        from_left, from_right = self.pending
+        self.buf = lax.dynamic_update_slice_in_dim(self.buf, from_left, (self.me - step + n - 1) * rows, 0)
+        self.buf = lax.dynamic_update_slice_in_dim(self.buf, from_right, (self.me + step + n - 1) * rows, 0)
+
+    def result(self):
+        return self.buf[(self.n - 1) * self.rows : (2 * self.n - 1) * self.rows]
+
+
+class ScatterSteps:
+    def __init__(self, partial, axis, send_dtype):
+        self.axis = axis
+        self.n = lax.psum(1, axis)
+        self.me = lax.axis_index(axis)
+        self.rows = partial.shape[0] // self.n
+        self.partial = partial
+        self.send_dtype = send_dtype
+        self.pending = None
+        self.step = 0
+
+    def steps(self):
+        return self.n - 1
+
+    def block(self, k):
+        return lax.dynamic_slice_in_dim(
+            self.partial, jnp.clip(k, 0, self.n - 1) * self.rows, self.rows, 0
+        )
+
+    def send(self):
+        n, me, step = self.n, self.me, self.step + 1
+        send_right = self.block(n - step + me)
+        send_left = self.block(me + step - n)
+        if self.pending is not None:
+            send_right = send_right + self.pending[0].astype(jnp.float32)
+            send_left = send_left + self.pending[1].astype(jnp.float32)
+        recv_right = lax.ppermute(
+            send_right.astype(self.send_dtype), self.axis, [(j, j + 1) for j in range(0, step)]
+        )
+        recv_left = lax.ppermute(
+            send_left.astype(self.send_dtype), self.axis, [(j, j - 1) for j in range(n - step, n)]
+        )
+        self.pending = (recv_right, recv_left)
+        self.step = step
+
+    def land(self):
+        pass
+
+    def result(self):
+        return (
+            self.block(self.me)
+            + self.pending[0].astype(jnp.float32)
+            + self.pending[1].astype(jnp.float32)
+        )
+
+
+def overlap(chain, pieces):
+    value = ()
+    count = chain.steps()
+    for index in range(count):
+        chain.send()
+        if index < len(pieces):
+            value = pieces[index](value)
+        chain.pending, value = lax.optimization_barrier((chain.pending, value))
+        chain.land()
+    for piece in pieces[count:]:
+        value = piece(value)
+    return value
+
+
 COL = ("chip", "core")
 
 
@@ -190,17 +282,13 @@
 ):
     seq_count = piece_starts.shape[0]
     group_rows = seq_count * LENGTH
-    heads_local = w_query.shape[1] // HD
-    gathered = (
-        col_gather(w_query, 0),
-        col_gather(w_key, 0),
-        col_gather(w_value, 0),
-        col_gather(w_output, 1),
-        col_gather(w_gate, 0),
-        col_gather(w_up, 0),
-        col_gather(w_down, 1),
-    )
-    full_query, full_key, full_value, full_output, full_gate, full_up, full_down = gathered
+    width = w_query.shape[1]
+    hidden = w_gate.shape[1]
+    heads_local = width // HD
+    full_qkv = col_gather(jnp.concatenate([w_query, w_key, w_value], axis=1), 0)
+    full_output = col_gather(w_output, 1)
+    full_gu = col_gather(jnp.concatenate([w_gate, w_up], axis=1), 0)
+    full_down = col_gather(w_down, 1)
     cosine, sine = rope_tables()
     inputs = layer_input.astype(jnp.float32)
     normed_first = layer_norm(inputs).astype(jnp.bfloat16)
@@ -212,80 +300,94 @@
     def merge_heads(field):
         return field.reshape(group_rows, heads_local * HD)
 
-    queries = rotate(split_heads(product(first_rows, full_query)), cosine, sine).astype(
-        jnp.bfloat16
-    )
-    keys_rot = rotate(split_heads(product(first_rows, full_key)), cosine, sine).astype(jnp.bfloat16)
-    values = split_heads(product(first_rows, full_value)).astype(jnp.bfloat16)
-    mixed, log_total = lax.map(attend_forward, (queries, keys_rot, values, piece_starts))
-    attended = merge_heads(mixed.astype(jnp.bfloat16))
-    attention_sum = line_reduce_scatter(product(attended, full_output), "row", jnp.bfloat16)
+    def project(_):
+        qkv_lin = product(first_rows, full_qkv)
+        queries = rotate(split_heads(qkv_lin[:, :width]), cosine, sine).astype(jnp.bfloat16)
+        keys_rot = rotate(split_heads(qkv_lin[:, width : 2 * width]), cosine, sine).astype(
+            jnp.bfloat16
+        )
+        values = split_heads(qkv_lin[:, 2 * width :]).astype(jnp.bfloat16)
+        return dict(queries=queries, keys_rot=keys_rot, values=values)
+
+    def attend(state):
+        mixed, log_total = lax.map(
+            attend_forward, (state["queries"], state["keys_rot"], state["values"], piece_starts)
+        )
+        return dict(state, mixed=mixed, log_total=log_total)
+
+    def out_project(state):
+        attended = merge_heads(state.pop("mixed").astype(jnp.bfloat16))
+        return dict(state, attended=attended, attn_partial=product(attended, full_output))
+
+    cot_chain = GatherSteps(cotangent, "row")
+    fwd = overlap(cot_chain, [project, attend, out_project])
+    grad_rows = cot_chain.result()
+    queries, keys_rot, values = fwd["queries"], fwd["keys_rot"], fwd["values"]
+    log_total, attended = fwd["log_total"], fwd["attended"]
+    attention_sum = line_reduce_scatter(fwd["attn_partial"], "row", jnp.bfloat16)
     middle = inputs + attention_sum
     normed_second = layer_norm(middle).astype(jnp.bfloat16)
     second_rows = line_all_gather(normed_second, "row")
-    gate_lin = product(second_rows, full_gate)
-    up_lin = product(second_rows, full_up)
+    gu_lin = product(second_rows, full_gu)
+    gate_lin = gu_lin[:, :hidden]
+    up_lin = gu_lin[:, hidden:]
     activation = (jax.nn.silu(gate_lin) * up_lin).astype(jnp.bfloat16)
-    ffn_sum = line_reduce_scatter(product(activation, full_down), "row", jnp.bfloat16)
+    ffn_chain = ScatterSteps(product(activation, full_down), "row", jnp.bfloat16)
+
+    def gate_up_grads(_):
+        grad_activation = times_transpose(grad_rows, full_down)
+        sigma = jax.nn.sigmoid(gate_lin)
+        grad_gate = grad_activation * up_lin * sigma * (1.0 + gate_lin * (1.0 - sigma))
+        grad_up = grad_activation * gate_lin * sigma
+        return dict(grad_gu=jnp.concatenate([grad_gate, grad_up], axis=1).astype(jnp.bfloat16))
+
+    def second_partial(state):
+        return dict(state, second_partial=times_transpose(state["grad_gu"], full_gu))
+
+    def down_weight_grad(state):
+        return dict(state, grad_down_w=contract_rows(activation, grad_rows))
+
+    bwd = overlap(ffn_chain, [gate_up_grads, second_partial, down_weight_grad])
+    ffn_sum = ffn_chain.result()
     output = (middle + ffn_sum).astype(jnp.bfloat16)
-    back_query, back_key, back_value, back_output = (full_query, full_key, full_value, full_output)
-    back_gate, back_up, back_down = (full_gate, full_up, full_down)
-    grad_rows = line_all_gather(cotangent, "row")
-    grad_activation = times_transpose(grad_rows, back_down)
-    sigma = jax.nn.sigmoid(gate_lin)
-    grad_gate = (grad_activation * up_lin * sigma * (1.0 + gate_lin * (1.0 - sigma))).astype(
-        jnp.bfloat16
-    )
-    grad_up = (grad_activation * gate_lin * sigma).astype(jnp.bfloat16)
-    grad_second = line_reduce_scatter(
-        times_transpose(grad_gate, back_gate) + times_transpose(grad_up, back_up),
-        "row",
-        jnp.bfloat16,
-    )
+    grad_gu = bwd["grad_gu"]
+    down_sum = col_scatter(bwd["grad_down_w"], 1)
+    second_chain = ScatterSteps(bwd["second_partial"], "row", jnp.bfloat16)
+
+    def gate_up_weight_grad(_):
+        return contract_rows(second_rows, grad_gu)
+
+    grad_gu_w = overlap(second_chain, [gate_up_weight_grad])
+    grad_second = second_chain.result()
+    gu_sum = col_scatter(grad_gu_w, 0)
     grad_middle = cotangent.astype(jnp.float32) + norm_back(middle, grad_second)
     grad_branch = line_all_gather(grad_middle.astype(jnp.bfloat16), "row")
-    grad_mixed = split_heads(times_transpose(grad_branch, back_output).astype(jnp.bfloat16))
+    output_sum = col_scatter(contract_rows(attended, grad_branch), 1)
+    grad_mixed = split_heads(times_transpose(grad_branch, full_output).astype(jnp.bfloat16))
     grad_q_rot, grad_k_rot, grad_values = lax.map(
         attend_backward, (queries, keys_rot, values, piece_starts, log_total, grad_mixed)
     )
-    grad_query = merge_heads(unrotate(grad_q_rot, cosine, sine)).astype(jnp.bfloat16)
-    grad_key = merge_heads(unrotate(grad_k_rot, cosine, sine)).astype(jnp.bfloat16)
-    grad_value = merge_heads(grad_values).astype(jnp.bfloat16)
-    grad_first = line_reduce_scatter(
-        times_transpose(grad_query, back_query)
-        + times_transpose(grad_key, back_key)
-        + times_transpose(grad_value, back_value),
-        "row",
-        jnp.bfloat16,
-    )
+    grad_qkv = jnp.concatenate(
+        [
+            merge_heads(unrotate(grad_q_rot, cosine, sine)),
+            merge_heads(unrotate(grad_k_rot, cosine, sine)),
+            merge_heads(grad_values),
+        ],
+        axis=1,
+    ).astype(jnp.bfloat16)
+    qkv_sum = col_scatter(contract_rows(first_rows, grad_qkv), 0)
+    grad_first = line_reduce_scatter(times_transpose(grad_qkv, full_qkv), "row", jnp.bfloat16)
     grad_input = grad_middle + norm_back(inputs, grad_first)
-    grad_query_w = contract_rows(first_rows, grad_query)
-    grad_key_w = contract_rows(first_rows, grad_key)
-    grad_value_w = contract_rows(first_rows, grad_value)
-    grad_output_w = contract_rows(attended, grad_branch)
-    grad_gate_w = contract_rows(second_rows, grad_gate)
-    grad_up_w = contract_rows(second_rows, grad_up)
-    grad_down_w = contract_rows(activation, grad_rows)
-    summed = (
-        col_scatter(grad_query_w, 0),
-        col_scatter(grad_key_w, 0),
-        col_scatter(grad_value_w, 0),
-        col_scatter(grad_output_w, 1),
-        col_scatter(grad_gate_w, 0),
-        col_scatter(grad_up_w, 0),
-        col_scatter(grad_down_w, 1),
-    )
-    results = tuple(summed)
     return (
         output,
         grad_input,
-        results[0],
-        results[1],
-        results[2],
-        results[3],
-        results[4],
-        results[5],
-        results[6],
+        qkv_sum[:, :width],
+        qkv_sum[:, width : 2 * width],
+        qkv_sum[:, 2 * width :],
+        output_sum,
+        gu_sum[:, :hidden],
+        gu_sum[:, hidden:],
+        down_sum,
     )
 
 

time: 1140 us -> 1020 us (0.89)
  waiting for transfers between devices: 575 us -> 496 us
  matrix products: 240 us -> 209 us
  starting transfers between devices: 134 us -> 110 us
    ppermute x12 -> x6, waiting for transfers between devices: 174 us -> 98.3 us  [line_reduce_scatter(): lax.ppermute(send_right.astype(send_dtype), axis, [(j, j + 1) for j in ra...]
    ppermute x0 -> x18, waiting for transfers between devices: none -> 70.4 us  [the longest x6 33.6 us: send(): lax.ppermute(send_right.astype(self.send_dtype), self.axis, [(j, j + 1) f...]
    reduce_scatter x7 -> x4, waiting for transfers between devices: 169 us -> 127 us  [col_scatter(): lax.psum_scatter(low_part, COL, scatter_dimension=axis, tiled=True)]
    ppermute x0 -> x18, starting transfers between devices: none -> 41.5 us  [the longest x6 22.2 us: send(): lax.ppermute(send_right.astype(self.send_dtype), self.axis, [(j, j + 1) f...]
    ppermute x12 -> x9, starting transfers between devices: 57.4 us -> 16.8 us  [line_all_gather(): from_left = lax.ppermute(from_left, axis, right_pairs)]
    ppermute x12 -> x6, starting transfers between devices: 45.2 us -> 24.9 us  [line_reduce_scatter(): lax.ppermute(send_right.astype(send_dtype), axis, [(j, j + 1) for j in ra...]
    ppermute x12 -> x9, waiting for transfers between devices: 141 us -> 122 us  [line_all_gather(): from_right = lax.ppermute(from_right, axis, left_pairs)]
    dynamic_update_slice x1 -> x7, local copies, waits for them, and re-layouts: 1.03 us -> 15 us  [the longest x3 6.95 us: land(): lax.dynamic_update_slice_in_dim(self.buf, from_right, (self.me + step + n...]
  transfers between devices with their start and end apart: 62 -> 56, of which waited for: 32 -> 29; matrix products, arithmetic and copies ran while one was open for 31% -> 30% of each run, Pallas kernels for 0% -> 0%
where the time goes in v4:
time: 1020 us; the launch traced here: 1010 us
  waiting for transfers between devices  496 us (49%)
  matrix products  209 us (20%)
  starting transfers between devices  110 us (11%)
  local copies, waits for them, and re-layouts  88.8 us (9%)
  other arithmetic  87.6 us (9%)
  between operations  15.7 us (2%)
    reduce_scatter x4, waiting for transfers between devices, col_scatter(): lax.psum_scatter(low_part, COL, scatter_dimension=axis, tiled=True)  127 us
    ppermute x9, waiting for transfers between devices, line_all_gather(): from_right = lax.ppermute(from_right, axis, left_pairs)  122 us
    ppermute x6, waiting for transfers between devices, line_reduce_scatter(): lax.ppermute(send_right.astype(send_dtype), axis, [(j, j + 1) for j in ra...  98.3 us
    dot_general x4, matrix products, times_transpose(): lax.dot_general(left, right, (((1,), (1,)), ((), ())), preferred_element_...  57.7 us
    dot_general x4, matrix products, contract_rows(): lax.dot_general(left, right, (((0,), (0,)), ((), ())), preferred_element_...  55.7 us
    dot_general x4, matrix products, product(): return jnp.dot(left, right, preferred_element_type=jnp.float32)  49.9 us
    ppermute x6, waiting for transfers between devices, line_reduce_scatter(): lax.ppermute(send_left.astype(send_dtype), axis, [(j, j - 1) for j in ran...  41.7 us
    ppermute x9, waiting for transfers between devices, line_all_gather(): from_left = lax.ppermute(from_left, axis, right_pairs)  34.2 us
  transfers between devices with their start and end apart: 56, of which 29 were waited for; matrix products, arithmetic and copies ran while one was open for 30% of the time, Pallas kernels for 0%

profile of v4, /device:TPU:0, one launch (start us, length us, event | category | flops | bytes accessed | tf_op | source)
XLA Modules:
  0.0 1006.6 jit_solution(11611628071942725395)
XLA Ops:
  33.8 15.3 %collective-permute-done.2 = bf16[256,2048]{1,0:T(8,128)(2,1)S(1)} collective-permute-done((bf16[256,2048]{1,0:T(8,128)(2,1)S(1)}, bf16[256,2048]{1,0:T(8,128)(2,1)S(1)}, u32[]{:S(2)}, u32[]{:S(2)}) %collective-permute-start.2) | collective-permute-done | bytes 1048608 | tf_op jit(solution)/shard_map/ppermute | solution.py:47
  62.4 34.8 %collective-permute-done.5 = bf16[256,2048]{1,0:T(8,128)(2,1)} collective-permute-done((bf16[256,2048]{1,0:T(8,128)(2,1)}, bf16[256,2048]{1,0:T(8,128)(2,1)}, u32[]{:S(2)}, u32[]{:S(2)}) %collective-permute-start.5) | collective-permute-done | bytes 1048608 | tf_op jit(solution)/shard_map/ppermute | solution.py:48
  110.4 13.1 %collective-permute-done.7 = bf16[256,2048]{1,0:T(8,128)(2,1)S(1)} collective-permute-done((bf16[256,2048]{1,0:T(8,128)(2,1)}, bf16[256,2048]{1,0:T(8,128)(2,1)S(1)}, u32[]{:S(2)}, u32[]{:S(2)}) %collective-permute-start.7) | collective-permute-done | bytes 1048608 | tf_op jit(solution)/shard_map/ppermute | solution.py:48
  186.8 19.4 %collective-permute-done.11 = bf16[256,2048]{1,0:T(8,128)(2,1)} collective-permute-done((bf16[256,2048]{1,0:T(8,128)(2,1)}, bf16[256,2048]{1,0:T(8,128)(2,1)}, u32[]{:S(2)}, u32[]{:S(2)}) %collective-permute-start.11) | collective-permute-done | bytes 1048608 | tf_op jit(solution)/shard_map/ppermute | solution.py:99
  210.8 18.9 %collective-permute-done.12 = bf16[256,2048]{1,0:T(8,128)(2,1)} collective-permute-done((bf16[256,2048]{1,0:T(8,128)(2,1)}, bf16[256,2048]{1,0:T(8,128)(2,1)}, u32[]{:S(2)}, u32[]{:S(2)}) %collective-permute-start.12) | collective-permute-done | bytes 1048608 | tf_op jit(solution)/shard_map/ppermute | solution.py:72
  238.2 18.8 %collective-permute-done.13 = bf16[256,2048]{1,0:T(8,128)(2,1)} collective-permute-done((bf16[256,2048]{1,0:T(8,128)(2,1)}, bf16[256,2048]{1,0:T(8,128)(2,1)}, u32[]{:S(2)}, u32[]{:S(2)}) %collective-permute-start.13) | collective-permute-done | bytes 1048608 | tf_op jit(solution)/shard_map/ppermute | solution.py:72
  271.4 14.1 %collective-permute-done.14 = bf16[256,2048]{1,0:T(8,128)(2,1)} collective-permute-done((bf16[256,2048]{1,0:T(8,128)(2,1)S(1)}, bf16[256,2048]{1,0:T(8,128)(2,1)}, u32[]{:S(2)}, u32[]{:S(2)}) %collective-permute-start.14) | collective-permute-done | bytes 1048608 | tf_op jit(solution)/shard_map/ppermute | solution.py:72
  285.6 24.3 %collective-permute-done.17 = bf16[256,2048]{1,0:T(8,128)(2,1)} collective-permute-done((bf16[256,2048]{1,0:T(8,128)(2,1)S(1)}, bf16[256,2048]{1,0:T(8,128)(2,1)}, u32[]{:S(2)}, u32[]{:S(2)}) %collective-permute-start.17) | collective-permute-done | bytes 1048608 | tf_op jit(solution)/shard_map/ppermute | solution.py:75
  356.6 14.4 %collective-permute-done.21 = bf16[256,2048]{1,0:T(8,128)(2,1)S(1)} collective-permute-done((bf16[256,2048]{1,0:T(8,128)(2,1)S(1)}, bf16[256,2048]{1,0:T(8,128)(2,1)S(1)}, u32[]{:S(2)}, u32[]{:S(2)}) %collective-permute-start.21) | collective-permute-done | bytes 1048608 | tf_op jit(solution)/shard_map/ppermute | solution.py:48
  390.3 23.4 %fusion.18 = f32[1024,4096]{1,0:T(8,128)} fusion(bf16[2048,4096]{1,0:T(8,128)(2,1)} %all-gather.9.cloned.1.call-done, bf16[2560,2048]{1,0:T(8,128)(2,1)} %constant_dynamic-update-slice_fusion.14), kind=kOutput, calls=%fused_computation.31 | convolution fusion | flops 17179869184 | bytes 37748736 | tf_op jit(solution)/shard_map/dot_general | solution.py:19
  413.7 21.9 %multiply_convert_fusion.2 = (bf16[1024,2048]{1,0:T(8,128)(2,1)}, bf16[1024,2048]{1,0:T(8,128)(2,1)}, bf16[1024,2048]{1,0:T(8,128)(2,1)}) fusion(f32[1024,4096]{1,0:T(8,128)} %fusion.18, bf16[2048,2048]{1,0:T(8,128)(2,1)} %all-gather.11.cloned.1.call-done, bf16[2560,2048]{1,0:T(8,128)(2,1)} %constant_dynamic-update-slice_fusion.7), kind=kOutput, calls=%fused_computation.11 | convolution fusion | flops 8623489024 | bytes 41943040 | tf_op jit(solution)/shard_map/dot_general | solution.py:29
  479.0 22.1 %fusion.75 = f32[1024,2048]{1,0:T(8,128)} fusion(bf16[1024,4096]{1,0:T(8,128)(2,1)S(1)} %copy-done.14, bf16[2048,4096]{1,0:T(8,128)(2,1)} %all-gather.9.cloned.1.call-done), kind=kOutput, calls=%fused_computation.173 | convolution fusion | flops 17179869184 | bytes 33554432 | tf_op jit(solution)/shard_map/dot_general | solution.py:29
  507.0 13.5 %fusion.12 = bf16[2048,2048]{1,0:T(8,128)(2,1)} fusion(bf16[1024,2048]{1,0:T(8,128)(2,1)S(1)} %copy-done.36, bf16[2560,2048]{1,0:T(8,128)(2,1)} %constant_dynamic-update-slice_fusion.7), kind=kOutput, calls=%fused_computation.25 | convolution fusion | flops 8589934592 | bytes 16777216 | tf_op jit(solution)/shard_map/dot_general | solution.py:23
  532.1 25.3 %fusion.16 = bf16[2048,4096]{1,0:T(8,128)(2,1)} fusion(bf16[1024,4096]{1,0:T(8,128)(2,1)} %pad_maximum_fusion, bf16[2560,2048]{1,0:T(8,128)(2,1)} %constant_dynamic-update-slice_fusion.14), kind=kOutput, calls=%fused_computation.29 | convolution fusion | flops 17179869184 | bytes 29360128 | tf_op jit(solution)/shard_map/dot_general | solution.py:23
  562.9 15.5 %collective-permute-done.32 = bf16[256,2048]{1,0:T(8,128)(2,1)S(1)} collective-permute-done((bf16[256,2048]{1,0:T(8,128)(2,1)S(1)}, bf16[256,2048]{1,0:T(8,128)(2,1)S(1)}, u32[]{:S(2)}, u32[]{:S(2)}) %collective-permute-start.32) | collective-permute-done | bytes 1048608 | tf_op jit(solution)/shard_map/ppermute | solution.py:139
  630.9 14.0 %collective-permute-done.37 = bf16[256,2048]{1,0:T(8,128)(2,1)S(1)} collective-permute-done((bf16[256,2048]{1,0:T(8,128)(2,1)S(1)}, bf16[256,2048]{1,0:T(8,128)(2,1)S(1)}, u32[]{:S(2)}, u32[]{:S(2)}) %collective-permute-start.37) | collective-permute-done | bytes 1048608 | tf_op jit(solution)/shard_map/ppermute | solution.py:48
  646.9 24.1 %collective-permute-done.39 = bf16[256,2048]{1,0:T(8,128)(2,1)S(1)} collective-permute-done((bf16[256,2048]{1,0:T(8,128)(2,1)S(1)}, bf16[256,2048]{1,0:T(8,128)(2,1)S(1)}, u32[]{:S(2)}, u32[]{:S(2)}) %collective-permute-start.39) | collective-permute-done | bytes 1048608 | tf_op jit(solution)/shard_map/ppermute | solution.py:48
  673.0 14.7 %collective-permute-done.41 = bf16[256,2048]{1,0:T(8,128)(2,1)S(1)} collective-permute-done((bf16[256,2048]{1,0:T(8,128)(2,1)S(1)}, bf16[256,2048]{1,0:T(8,128)(2,1)S(1)}, u32[]{:S(2)}, u32[]{:S(2)}) %collective-permute-start.41) | collective-permute-done | bytes 1048608 | tf_op jit(solution)/shard_map/ppermute | solution.py:48
  710.6 12.8 %multiply_reduce_fusion = (f32[4,1024]{1,0:T(4,128)S(1)}, f32[4,1024,1024]{1,2,0:T(8,128)}) fusion(f32[4,1024,1024]{1,2,0:T(8,128)} %fusion.48, f32[4,1024]{1,0:T(4,128)S(1)} %bitcast.82, pred[1024,1024]{0,1:T(8,128)(4,1)S(1)} %copy-done.3, bf16[1024,4,128]{0,2,1:T(8,128)(2,1)S(1)} %bitcast.76, bf16[1,1024,4,128]{3,2,1,0:T(4,128)(2,1)S(1)} %copy-done.12), kind=kOutput, calls=%fused_computation.1 | convolution fusion | flops 1094709248 | bytes 36732928 | tf_op jit(solution)/shard_map/while/body/eval_jaxpr/qhd,khd->hqk/dot_general | solution.py:267
  750.7 13.2 %convolution_convert_fusion = bf16[2048,1536]{1,0:T(8,128)(2,1)} fusion(bf16[2560,2048]{1,0:T(8,128)(2,1)} %constant_dynamic-update-slice_fusion.21, bf16[1024,512]{0,1:T(8,128)(2,1)S(1)} %bitcast.88, bf16[1024,512]{0,1:T(8,128)(2,1)S(1)} %bitcast.80, bf16[1024,512]{0,1:T(8,128)(2,1)S(1)} %bitcast.78), kind=kOutput, calls=%fused_computation.18 | convolution fusion | flops 6455033856 | bytes 13631488 | tf_op jit(solution)/shard_map/dot_general | solution.py:23
  776.0 18.3 %collective-permute-done.42 = bf16[256,2048]{1,0:T(8,128)(2,1)S(1)} collective-permute-done((bf16[256,2048]{1,0:T(8,128)(2,1)S(1)}, bf16[256,2048]{1,0:T(8,128)(2,1)S(1)}, u32[]{:S(2)}, u32[]{:S(2)}) %collective-permute-start.42) | collective-permute-done | bytes 1048608 | tf_op jit(solution)/shard_map/ppermute | solution.py:72
  799.2 21.0 %collective-permute-done.43 = bf16[256,2048]{1,0:T(8,128)(2,1)S(1)} collective-permute-done((bf16[256,2048]{1,0:T(8,128)(2,1)S(1)}, bf16[256,2048]{1,0:T(8,128)(2,1)S(1)}, u32[]{:S(2)}, u32[]{:S(2)}) %collective-permute-start.43) | collective-permute-done | bytes 1048608 | tf_op jit(solution)/shard_map/ppermute | solution.py:72
  840.4 17.5 %collective-permute-done.47 = bf16[256,2048]{1,0:T(8,128)(2,1)} collective-permute-done((bf16[256,2048]{1,0:T(8,128)(2,1)}, bf16[256,2048]{1,0:T(8,128)(2,1)}, u32[]{:S(2)}, u32[]{:S(2)}) %collective-permute-start.47) | collective-permute-done | bytes 1048608 | tf_op jit(solution)/shard_map/ppermute | solution.py:75
  877.8 117.5 %reduce-scatter.9.cloned.1.call-done = bf16[256,4096]{1,0:T(8,128)(2,1)} async-done(((bf16[2048,4096]{1,0:T(8,128)(2,1)}), bf16[256,4096]{1,0:T(8,128)(2,1)}) %reduce-scatter.9.cloned.1.call-update) | async-done | bytes 2097168 | tf_op jit(solution)/shard_map/reduce_scatter | solution.py:182
  (283 shorter events, 443.2 us)
Async XLA Ops:
  7.2 117.4 %all-gather.5.cloned.1.call-start = ((), (), s32[]{:S(2)}) async-start(), calls=%async_computation.4 | async-start | bytes 7077888 | tf_op jit(solution)/shard_map/all_gather | solution.py:177
  9.4 172.4 %all-gather.7.cloned.1.call-start = ((), (), s32[]{:S(2)}) async-start(), calls=%async_computation.5 | async-start | bytes 2359296 | tf_op jit(solution)/shard_map/all_gather | solution.py:177
  10.1 380.2 %all-gather.9.cloned.1.call-start = ((), (), s32[]{:S(2)}) async-start(), calls=%async_computation.6 | async-start | bytes 18874368 | tf_op jit(solution)/shard_map/all_gather | solution.py:177
  13.3 400.4 %all-gather.11.cloned.1.call-start = ((), (), s32[]{:S(2)}) async-start(), calls=%async_computation.7 | async-start | bytes 9437184 | tf_op jit(solution)/shard_map/all_gather | solution.py:177
  20.6 28.5 %collective-permute-start.2 = (bf16[256,2048]{1,0:T(8,128)(2,1)S(1)}, bf16[256,2048]{1,0:T(8,128)(2,1)S(1)}, u32[]{:S(2)}, u32[]{:S(2)}) collective-permute-start(bf16[256,2048]{1,0:T(8,128)(2,1)S(1)} %get-tuple-element.156), channel_id=1, source_target_pairs={{0,8},{8,16},{16,24},{1,9},{9,17},{17,25},{2,10},{10,18},{18,26},{... | collective-permute-start | bytes 3145736 | tf_op jit(solution)/shard_map/ppermute | solution.py:47
  25.6 28.0 %collective-permute-start.3 = (bf16[256,2048]{1,0:T(8,128)(2,1)S(1)}, bf16[256,2048]{1,0:T(8,128)(2,1)}, u32[]{:S(2)}, u32[]{:S(2)}) collective-permute-start(bf16[256,2048]{1,0:T(8,128)(2,1)S(1)} %get-tuple-element.156), channel_id=1, source_target_pairs={{8,0},{16,8},{24,16},{9,1},{17,9},{25,17},{10,2},{18,10},{26,18},{... | collective-permute-start | bytes 3145736 | tf_op jit(solution)/shard_map/ppermute | solution.py:48
  26.9 121.5 %collective-permute-start = (bf16[256,2048]{1,0:T(8,128)(2,1)}, bf16[256,2048]{1,0:T(8,128)(2,1)}, u32[]{:S(2)}, u32[]{:S(2)}) collective-permute-start(bf16[256,2048]{1,0:T(8,128)(2,1)} %param.19), channel_id=1, source_target_pairs={{0,8},{8,16},{16,24},{1,9},{9,17},{17,25},{2,10},{10,18},{18,26},{... | collective-permute-start | bytes 3145736 | tf_op jit(solution)/shard_map/ppermute | solution.py:98
  32.5 115.9 %collective-permute-start.1 = (bf16[256,2048]{1,0:T(8,128)(2,1)}, bf16[256,2048]{1,0:T(8,128)(2,1)}, u32[]{:S(2)}, u32[]{:S(2)}) collective-permute-start(bf16[256,2048]{1,0:T(8,128)(2,1)} %param.19), channel_id=1, source_target_pairs={{8,0},{16,8},{24,16},{9,1},{17,9},{25,17},{10,2},{18,10},{26,18},{... | collective-permute-start | bytes 3145736 | tf_op jit(solution)/shard_map/ppermute | solution.py:99
  53.7 43.5 %collective-permute-start.5 = (bf16[256,2048]{1,0:T(8,128)(2,1)}, bf16[256,2048]{1,0:T(8,128)(2,1)}, u32[]{:S(2)}, u32[]{:S(2)}) collective-permute-start(bf16[256,2048]{1,0:T(8,128)(2,1)} %collective-permute-done.3), channel_id=1, source_target_pairs={{8,0},{16,8},{9,1},{17,9},{10,2},{18,10},{11,3},{19,11},{12,4},{20... | collective-permute-start | bytes 3145736 | tf_op jit(solution)/shard_map/ppermute | solution.py:48
  57.0 51.1 %collective-permute-start.6 = (bf16[256,2048]{1,0:T(8,128)(2,1)}, bf16[256,2048]{1,0:T(8,128)(2,1)}, u32[]{:S(2)}, u32[]{:S(2)}) collective-permute-start(bf16[256,2048]{1,0:T(8,128)(2,1)} %collective-permute-done.4), channel_id=1, source_target_pairs={{16,24},{17,25},{18,26},{19,27},{20,28},{21,29},{22,30},{23,31}} | collective-permute-start | bytes 3145736 | tf_op jit(solution)/shard_map/ppermute | solution.py:47
  152.8 26.9 %collective-permute-start.9 = (bf16[256,2048]{1,0:T(8,128)(2,1)}, bf16[256,2048]{1,0:T(8,128)(2,1)}, u32[]{:S(2)}, u32[]{:S(2)}) collective-permute-start(bf16[256,2048]{1,0:T(8,128)(2,1)} %collective-permute-done.1), channel_id=1, source_target_pairs={{8,0},{16,8},{9,1},{17,9},{10,2},{18,10},{11,3},{19,11},{12,4},{20... | collective-permute-start | bytes 3145736 | tf_op jit(solution)/shard_map/ppermute | solution.py:99
  210.0 621.4 %reduce-scatter.7.cloned.1.call-start = ((), (), s32[]{:S(2)}) async-start(), calls=%async_computation.9 | async-start | bytes 2359296 | tf_op jit(solution)/shard_map/reduce_scatter | solution.py:182
  210.0 28.2 %collective-permute-start.15 = (bf16[256,2048]{1,0:T(8,128)(2,1)S(1)}, bf16[256,2048]{1,0:T(8,128)(2,1)S(1)}, u32[]{:S(2)}, u32[]{:S(2)}) collective-permute-start(bf16[256,2048]{1,0:T(8,128)(2,1)S(1)} %get-tuple-element.179), channel_id=1, source_target_pairs={{24,16},{25,17},{26,18},{27,19},{28,20},{29,21},{30,22},{31,23}} | collective-permute-start | bytes 3145736 | tf_op jit(solution)/shard_map/ppermute | solution.py:75
  270.1 39.7 %collective-permute-start.17 = (bf16[256,2048]{1,0:T(8,128)(2,1)S(1)}, bf16[256,2048]{1,0:T(8,128)(2,1)}, u32[]{:S(2)}, u32[]{:S(2)}) collective-permute-start(bf16[256,2048]{1,0:T(8,128)(2,1)S(1)} %add_convert_fusion.13), channel_id=1, source_target_pairs={{8,0},{16,8},{24,16},{9,1},{17,9},{25,17},{10,2},{18,10},{26,18},{... | collective-permute-start | bytes 3145736 | tf_op jit(solution)/shard_map/ppermute | solution.py:75
  344.3 26.7 %collective-permute-start.21 = (bf16[256,2048]{1,0:T(8,128)(2,1)S(1)}, bf16[256,2048]{1,0:T(8,128)(2,1)S(1)}, u32[]{:S(2)}, u32[]{:S(2)}) collective-permute-start(bf16[256,2048]{1,0:T(8,128)(2,1)S(1)} %collective-permute-done.19), channel_id=1, source_target_pairs={{8,0},{16,8},{9,1},{17,9},{10,2},{18,10},{11,3},{19,11},{12,4},{20... | collective-permute-start | bytes 3145736 | tf_op jit(solution)/shard_map/ppermute | solution.py:48
  353.6 31.7 %collective-permute-start.22 = (bf16[256,2048]{1,0:T(8,128)(2,1)S(1)}, bf16[256,2048]{1,0:T(8,128)(2,1)S(1)}, u32[]{:S(2)}, u32[]{:S(2)}) collective-permute-start(bf16[256,2048]{1,0:T(8,128)(2,1)S(1)} %collective-permute-done.20), channel_id=1, source_target_pairs={{16,24},{17,25},{18,26},{19,27},{20,28},{21,29},{22,30},{23,31}} | collective-permute-start | bytes 3145736 | tf_op jit(solution)/shard_map/ppermute | solution.py:47
  473.7 27.4 %collective-permute-start.26 = (bf16[256,2048]{1,0:T(8,128)(2,1)S(1)}, bf16[256,2048]{1,0:T(8,128)(2,1)S(1)}, u32[]{:S(2)}, u32[]{:S(2)}) collective-permute-start(bf16[256,2048]{1,0:T(8,128)(2,1)S(1)} %get-tuple-element.173), channel_id=1, source_target_pairs={{0,8},{8,16},{1,9},{9,17},{2,10},{10,18},{3,11},{11,19},{4,12},{12... | collective-permute-start | bytes 3145736 | tf_op jit(solution)/shard_map/ppermute | solution.py:139
  526.2 31.1 %collective-permute-start.30 = (bf16[256,2048]{1,0:T(8,128)(2,1)}, bf16[256,2048]{1,0:T(8,128)(2,1)S(1)}, u32[]{:S(2)}, u32[]{:S(2)}) collective-permute-start(bf16[256,2048]{1,0:T(8,128)(2,1)} %get-tuple-element.169), channel_id=1, source_target_pairs={{0,8},{1,9},{2,10},{3,11},{4,12},{5,13},{6,14},{7,15}} | collective-permute-start | bytes 3145736 | tf_op jit(solution)/shard_map/ppermute | solution.py:139
  530.0 27.3 %collective-permute-start.31 = (bf16[256,2048]{1,0:T(8,128)(2,1)}, bf16[256,2048]{1,0:T(8,128)(2,1)}, u32[]{:S(2)}, u32[]{:S(2)}) collective-permute-start(bf16[256,2048]{1,0:T(8,128)(2,1)} %get-tuple-element.168), channel_id=1, source_target_pairs={{24,16},{25,17},{26,18},{27,19},{28,20},{29,21},{30,22},{31,23}} | collective-permute-start | bytes 3145736 | tf_op jit(solution)/shard_map/ppermute | solution.py:142
  617.9 27.0 %collective-permute-start.37 = (bf16[256,2048]{1,0:T(8,128)(2,1)S(1)}, bf16[256,2048]{1,0:T(8,128)(2,1)S(1)}, u32[]{:S(2)}, u32[]{:S(2)}) collective-permute-start(bf16[256,2048]{1,0:T(8,128)(2,1)S(1)} %get-tuple-element.148), channel_id=1, source_target_pairs={{8,0},{16,8},{24,16},{9,1},{17,9},{25,17},{10,2},{18,10},{26,18},{... | collective-permute-start | bytes 3145736 | tf_op jit(solution)/shard_map/ppermute | solution.py:48
  695.4 167.6 %reduce-scatter.11.cloned.1.call-start = ((), (), s32[]{:S(2)}) async-start(), calls=%async_computation.11 | async-start | bytes 9437184 | tf_op jit(solution)/shard_map/reduce_scatter | solution.py:182
  696.0 179.5 %reduce-scatter.5.cloned.1.call-start = ((), (), s32[]{:S(2)}) async-start(), calls=%async_computation.8 | async-start | bytes 7077888 | tf_op jit(solution)/shard_map/reduce_scatter | solution.py:182
  763.9 231.4 %reduce-scatter.9.cloned.1.call-start = ((), (), s32[]{:S(2)}) async-start(), calls=%async_computation.10 | async-start | bytes 18874368 | tf_op jit(solution)/shard_map/reduce_scatter | solution.py:182
  830.1 27.8 %collective-permute-start.47 = (bf16[256,2048]{1,0:T(8,128)(2,1)}, bf16[256,2048]{1,0:T(8,128)(2,1)}, u32[]{:S(2)}, u32[]{:S(2)}) collective-permute-start(bf16[256,2048]{1,0:T(8,128)(2,1)} %add_convert_fusion), channel_id=1, source_target_pairs={{8,0},{16,8},{24,16},{9,1},{17,9},{25,17},{10,2},{18,10},{26,18},{... | collective-permute-start | bytes 3145736 | tf_op jit(solution)/shard_map/ppermute | solution.py:75
  (71 other events, 1474.5 us)
Sparse Core Ops, SparseCore 0:
  10.5 48.1 all-gather.4
  60.5 28.0 all-gather.6
  91.1 89.7 all-gather.8
  210.1 54.2 all-gather.10
  695.5 40.0 reduce-scatter.6
  739.0 71.2 reduce-scatter.10
  813.7 61.7 reduce-scatter.4
  879.0 116.1 reduce-scatter.8

commit v5 on v4

--- a/solution.py
+++ b/solution.py
@@ -319,7 +319,8 @@
         attended = merge_heads(state.pop("mixed").astype(jnp.bfloat16))
         return dict(state, attended=attended, attn_partial=product(attended, full_output))
 
-    cot_chain = GatherSteps(cotangent, "row")
+    cot_later, first_rows = lax.optimization_barrier((cotangent, first_rows))
+    cot_chain = GatherSteps(cot_later, "row")
     fwd = overlap(cot_chain, [project, attend, out_project])
     grad_rows = cot_chain.result()
     queries, keys_rot, values = fwd["queries"], fwd["keys_rot"], fwd["values"]
@@ -357,7 +358,12 @@
     def gate_up_weight_grad(_):
         return contract_rows(second_rows, grad_gu)
 
-    grad_gu_w = overlap(second_chain, [gate_up_weight_grad])
+    def keep_down_sum(grad_gu_w):
+        return (grad_gu_w, down_sum)
+
+    grad_gu_w, down_sum = overlap(
+        second_chain, [gate_up_weight_grad, lambda value: value, keep_down_sum]
+    )
     grad_second = second_chain.result()
     gu_sum = col_scatter(grad_gu_w, 0)
     grad_middle = cotangent.astype(jnp.float32) + norm_back(middle, grad_second)

time: 1020 us -> 969 us (0.950)
  waiting for transfers between devices: 496 us -> 446 us
  local copies, waits for them, and re-layouts: 88.8 us -> 100 us
    reduce_scatter x4, waiting for transfers between devices: 127 us -> 98.2 us  [col_scatter(): lax.psum_scatter(low_part, COL, scatter_dimension=axis, tiled=True)]
    ppermute x9, waiting for transfers between devices: 122 us -> 95.2 us  [line_all_gather(): from_right = lax.ppermute(from_right, axis, left_pairs)]
  transfers between devices with their start and end apart: 56 -> 56, of which waited for: 29 -> 28; matrix products, arithmetic and copies ran while one was open for 30% -> 30% of each run, Pallas kernels for 0% -> 0%
where the time goes in v5:
time: 969 us; the launch traced here: 962 us
  waiting for transfers between devices  446 us (46%)
  matrix products  209 us (22%)
  local copies, waits for them, and re-layouts  100 us (10%)
  starting transfers between devices  100 us (10%)
  other arithmetic  91 us (9%)
  between operations  15.4 us (2%)
    reduce_scatter x4, waiting for transfers between devices, col_scatter(): lax.psum_scatter(low_part, COL, scatter_dimension=axis, tiled=True)  98.2 us
    ppermute x9, waiting for transfers between devices, line_all_gather(): from_right = lax.ppermute(from_right, axis, left_pairs)  95.2 us
    ppermute x6, waiting for transfers between devices, line_reduce_scatter(): lax.ppermute(send_right.astype(send_dtype), axis, [(j, j + 1) for j in ra...  94.4 us
    dot_general x4, matrix products, times_transpose(): lax.dot_general(left, right, (((1,), (1,)), ((), ())), preferred_element_...  57.7 us
    dot_general x4, matrix products, contract_rows(): lax.dot_general(left, right, (((0,), (0,)), ((), ())), preferred_element_...  56.5 us
    dot_general x4, matrix products, product(): return jnp.dot(left, right, preferred_element_type=jnp.float32)  49.9 us
    ppermute x6, waiting for transfers between devices, line_reduce_scatter(): lax.ppermute(send_left.astype(send_dtype), axis, [(j, j - 1) for j in ran...  48.1 us
    ppermute x9, waiting for transfers between devices, line_all_gather(): from_left = lax.ppermute(from_left, axis, right_pairs)  39.2 us
  transfers between devices with their start and end apart: 56, of which 28 were waited for; matrix products, arithmetic and copies ran while one was open for 30% of the time, Pallas kernels for 0%

profile of v5, /device:TPU:0, one launch (start us, length us, event | category | flops | bytes accessed | tf_op | source)
XLA Modules:
  0.0 961.9 jit_solution(8580125073156225393)
XLA Ops:
  27.0 21.0 %collective-permute-done = bf16[256,2048]{1,0:T(8,128)(2,1)S(1)} collective-permute-done((bf16[256,2048]{1,0:T(8,128)(2,1)S(1)}, bf16[256,2048]{1,0:T(8,128)(2,1)S(1)}, u32[]{:S(2)}, u32[]{:S(2)}) %collective-permute-start) | collective-permute-done | bytes 1048608 | tf_op jit(solution)/shard_map/ppermute | solution.py:47
  61.0 18.3 %collective-permute-done.3 = bf16[256,2048]{1,0:T(8,128)(2,1)} collective-permute-done((bf16[256,2048]{1,0:T(8,128)(2,1)}, bf16[256,2048]{1,0:T(8,128)(2,1)}, u32[]{:S(2)}, u32[]{:S(2)}) %collective-permute-start.3) | collective-permute-done | bytes 1048608 | tf_op jit(solution)/shard_map/ppermute | solution.py:48
  92.2 12.5 %collective-permute-done.5 = bf16[256,2048]{1,0:T(8,128)(2,1)S(1)} collective-permute-done((bf16[256,2048]{1,0:T(8,128)(2,1)}, bf16[256,2048]{1,0:T(8,128)(2,1)S(1)}, u32[]{:S(2)}, u32[]{:S(2)}) %collective-permute-start.5) | collective-permute-done | bytes 1048608 | tf_op jit(solution)/shard_map/ppermute | solution.py:48
  159.4 12.4 %collective-permute-done.9 = bf16[256,2048]{1,0:T(8,128)(2,1)} collective-permute-done((bf16[256,2048]{1,0:T(8,128)(2,1)}, bf16[256,2048]{1,0:T(8,128)(2,1)}, u32[]{:S(2)}, u32[]{:S(2)}) %collective-permute-start.9) | collective-permute-done | bytes 1048608 | tf_op jit(solution)/shard_map/ppermute | solution.py:99
  178.9 18.7 %collective-permute-done.11 = bf16[256,2048]{1,0:T(8,128)(2,1)} collective-permute-done((bf16[256,2048]{1,0:T(8,128)(2,1)}, bf16[256,2048]{1,0:T(8,128)(2,1)}, u32[]{:S(2)}, u32[]{:S(2)}) %collective-permute-start.11) | collective-permute-done | bytes 1048608 | tf_op jit(solution)/shard_map/ppermute | solution.py:99
  202.2 17.9 %collective-permute-done.12 = bf16[256,2048]{1,0:T(8,128)(2,1)} collective-permute-done((bf16[256,2048]{1,0:T(8,128)(2,1)}, bf16[256,2048]{1,0:T(8,128)(2,1)}, u32[]{:S(2)}, u32[]{:S(2)}) %collective-permute-start.12) | collective-permute-done | bytes 1048608 | tf_op jit(solution)/shard_map/ppermute | solution.py:72
  228.7 18.1 %collective-permute-done.13 = bf16[256,2048]{1,0:T(8,128)(2,1)} collective-permute-done((bf16[256,2048]{1,0:T(8,128)(2,1)}, bf16[256,2048]{1,0:T(8,128)(2,1)}, u32[]{:S(2)}, u32[]{:S(2)}) %collective-permute-start.13) | collective-permute-done | bytes 1048608 | tf_op jit(solution)/shard_map/ppermute | solution.py:72
  261.2 13.4 %collective-permute-done.14 = bf16[256,2048]{1,0:T(8,128)(2,1)} collective-permute-done((bf16[256,2048]{1,0:T(8,128)(2,1)S(1)}, bf16[256,2048]{1,0:T(8,128)(2,1)}, u32[]{:S(2)}, u32[]{:S(2)}) %collective-permute-start.14) | collective-permute-done | bytes 1048608 | tf_op jit(solution)/shard_map/ppermute | solution.py:72
  274.6 23.5 %collective-permute-done.17 = bf16[256,2048]{1,0:T(8,128)(2,1)} collective-permute-done((bf16[256,2048]{1,0:T(8,128)(2,1)S(1)}, bf16[256,2048]{1,0:T(8,128)(2,1)}, u32[]{:S(2)}, u32[]{:S(2)}) %collective-permute-start.17) | collective-permute-done | bytes 1048608 | tf_op jit(solution)/shard_map/ppermute | solution.py:75
  344.9 14.4 %collective-permute-done.21 = bf16[256,2048]{1,0:T(8,128)(2,1)S(1)} collective-permute-done((bf16[256,2048]{1,0:T(8,128)(2,1)S(1)}, bf16[256,2048]{1,0:T(8,128)(2,1)S(1)}, u32[]{:S(2)}, u32[]{:S(2)}) %collective-permute-start.21) | collective-permute-done | bytes 1048608 | tf_op jit(solution)/shard_map/ppermute | solution.py:48
  377.9 23.4 %fusion.18 = f32[1024,4096]{1,0:T(8,128)} fusion(bf16[2048,4096]{1,0:T(8,128)(2,1)} %all-gather.9.cloned.1.call-done, bf16[2560,2048]{1,0:T(8,128)(2,1)} %constant_dynamic-update-slice_fusion.14), kind=kOutput, calls=%fused_computation.31 | convolution fusion | flops 17179869184 | bytes 37748736 | tf_op jit(solution)/shard_map/dot_general | solution.py:19
  401.3 21.9 %multiply_convert_fusion.2 = (bf16[1024,2048]{1,0:T(8,128)(2,1)}, bf16[1024,2048]{1,0:T(8,128)(2,1)}, bf16[1024,2048]{1,0:T(8,128)(2,1)}) fusion(f32[1024,4096]{1,0:T(8,128)} %fusion.18, bf16[2048,2048]{1,0:T(8,128)(2,1)} %all-gather.11.cloned.1.call-done, bf16[2560,2048]{1,0:T(8,128)(2,1)} %constant_dynamic-update-slice_fusion.7), kind=kOutput, calls=%fused_computation.11 | convolution fusion | flops 8623489024 | bytes 41943040 | tf_op jit(solution)/shard_map/dot_general | solution.py:29
  423.2 12.5 %fusion.72 = f32[1024,2048]{1,0:T(8,128)S(1)} fusion(bf16[1024,2048]{1,0:T(8,128)(2,1)} %get-tuple-element.165, bf16[2048,2048]{1,0:T(8,128)(2,1)} %all-gather.11.cloned.1.call-done), kind=kOutput, calls=%fused_computation.170 | convolution fusion | flops 8589934592 | bytes 20971520 | tf_op jit(solution)/shard_map/dot_general | solution.py:19
  466.2 22.1 %fusion.73 = f32[1024,2048]{1,0:T(8,128)} fusion(bf16[1024,4096]{1,0:T(8,128)(2,1)S(1)} %copy-done.13, bf16[2048,4096]{1,0:T(8,128)(2,1)} %all-gather.9.cloned.1.call-done), kind=kOutput, calls=%fused_computation.171 | convolution fusion | flops 17179869184 | bytes 33554432 | tf_op jit(solution)/shard_map/dot_general | solution.py:29
  494.2 13.4 %fusion.12 = bf16[2048,2048]{1,0:T(8,128)(2,1)} fusion(bf16[1024,2048]{1,0:T(8,128)(2,1)S(1)} %copy-done.40, bf16[2560,2048]{1,0:T(8,128)(2,1)} %constant_dynamic-update-slice_fusion.7), kind=kOutput, calls=%fused_computation.25 | convolution fusion | flops 8589934592 | bytes 16777216 | tf_op jit(solution)/shard_map/dot_general | solution.py:23
  519.1 27.2 %fusion.16 = bf16[2048,4096]{1,0:T(8,128)(2,1)} fusion(bf16[1024,4096]{1,0:T(8,128)(2,1)} %pad_maximum_fusion, bf16[2560,2048]{1,0:T(8,128)(2,1)} %constant_dynamic-update-slice_fusion.14), kind=kOutput, calls=%fused_computation.29 | convolution fusion | flops 17179869184 | bytes 29360128 | tf_op jit(solution)/shard_map/dot_general | solution.py:23
  551.9 15.8 %collective-permute-done.32 = bf16[256,2048]{1,0:T(8,128)(2,1)S(1)} collective-permute-done((bf16[256,2048]{1,0:T(8,128)(2,1)S(1)}, bf16[256,2048]{1,0:T(8,128)(2,1)S(1)}, u32[]{:S(2)}, u32[]{:S(2)}) %collective-permute-start.32) | collective-permute-done | bytes 1048608 | tf_op jit(solution)/shard_map/ppermute | solution.py:139
  649.3 13.2 %collective-permute-done.39 = bf16[256,2048]{1,0:T(8,128)(2,1)S(1)} collective-permute-done((bf16[256,2048]{1,0:T(8,128)(2,1)S(1)}, bf16[256,2048]{1,0:T(8,128)(2,1)S(1)}, u32[]{:S(2)}, u32[]{:S(2)}) %collective-permute-start.39) | collective-permute-done | bytes 1048608 | tf_op jit(solution)/shard_map/ppermute | solution.py:48
  685.1 12.9 %multiply_reduce_fusion = (f32[4,1024]{1,0:T(4,128)S(1)}, f32[4,1024,1024]{1,2,0:T(8,128)}) fusion(f32[4,1024,1024]{1,2,0:T(8,128)} %fusion.45, f32[4,1024]{1,0:T(4,128)S(1)} %bitcast.84, pred[1024,1024]{0,1:T(8,128)(4,1)S(1)} %copy-done.3, bf16[1024,4,128]{0,2,1:T(8,128)(2,1)S(1)} %bitcast.78, bf16[1,1024,4,128]{3,2,1,0:T(4,128)(2,1)S(1)} %copy-done.12), kind=kOutput, calls=%fused_computation.1 | convolution fusion | flops 1094709248 | bytes 36732928 | tf_op jit(solution)/shard_map/while/body/eval_jaxpr/qhd,khd->hqk/dot_general | solution.py:267
  698.0 12.1 %multiply_convert_fusion = bf16[4,1024,1024]{1,2,0:T(8,128)(2,1)S(1)} fusion(f32[4,1024,1024]{1,2,0:T(8,128)} %get-tuple-element.211, f32[4,1024,1024]{1,2,0:T(8,128)} %fusion.45, f32[4,1024]{1,0:T(4,128)S(1)} %get-tuple-element.210, f32[4,1024]{1,0:T(4,128)S(1)} %bitcast.85, pred[1024,1024]{0,1:T(8,128)(4,1)S(1)} %copy-done.3), kind=kLoop, calls=%fused_computation | loop fusion | flops 25165824 | bytes 43024384 | tf_op jit(solution)/shard_map/while/body/eval_jaxpr/convert_element_type | solution.py:269
  756.7 19.5 %collective-permute-done.42 = bf16[256,2048]{1,0:T(8,128)(2,1)S(1)} collective-permute-done((bf16[256,2048]{1,0:T(8,128)(2,1)S(1)}, bf16[256,2048]{1,0:T(8,128)(2,1)S(1)}, u32[]{:S(2)}, u32[]{:S(2)}) %collective-permute-start.42) | collective-permute-done | bytes 1048608 | tf_op jit(solution)/shard_map/ppermute | solution.py:72
  781.4 18.2 %collective-permute-done.43 = bf16[256,2048]{1,0:T(8,128)(2,1)S(1)} collective-permute-done((bf16[256,2048]{1,0:T(8,128)(2,1)S(1)}, bf16[256,2048]{1,0:T(8,128)(2,1)S(1)}, u32[]{:S(2)}, u32[]{:S(2)}) %collective-permute-start.43) | collective-permute-done | bytes 1048608 | tf_op jit(solution)/shard_map/ppermute | solution.py:72
  819.7 24.6 %collective-permute-done.47 = bf16[256,2048]{1,0:T(8,128)(2,1)} collective-permute-done((bf16[256,2048]{1,0:T(8,128)(2,1)}, bf16[256,2048]{1,0:T(8,128)(2,1)}, u32[]{:S(2)}, u32[]{:S(2)}) %collective-permute-start.47) | collective-permute-done | bytes 1048608 | tf_op jit(solution)/shard_map/ppermute | solution.py:75
  852.6 98.2 %reduce-scatter.11.cloned.1.call-done = bf16[256,4096]{1,0:T(8,128)(2,1)} async-done(((bf16[2048,4096]{1,0:T(8,128)(2,1)}), bf16[256,4096]{1,0:T(8,128)(2,1)}) %reduce-scatter.11.cloned.1.call-update) | async-done | bytes 2097168 | tf_op jit(solution)/shard_map/reduce_scatter | solution.py:182
  (292 shorter events, 441.2 us)
Async XLA Ops:
  7.2 107.9 %all-gather.5.cloned.1.call-start = ((), (), s32[]{:S(2)}) async-start(), calls=%async_computation.4 | async-start | bytes 7077888 | tf_op jit(solution)/shard_map/all_gather | solution.py:177
  9.4 164.4 %all-gather.7.cloned.1.call-start = ((), (), s32[]{:S(2)}) async-start(), calls=%async_computation.5 | async-start | bytes 2359296 | tf_op jit(solution)/shard_map/all_gather | solution.py:177
  10.1 367.8 %all-gather.9.cloned.1.call-start = ((), (), s32[]{:S(2)}) async-start(), calls=%async_computation.6 | async-start | bytes 18874368 | tf_op jit(solution)/shard_map/all_gather | solution.py:177
  13.3 388.0 %all-gather.11.cloned.1.call-start = ((), (), s32[]{:S(2)}) async-start(), calls=%async_computation.7 | async-start | bytes 9437184 | tf_op jit(solution)/shard_map/all_gather | solution.py:177
  20.7 27.3 %collective-permute-start = (bf16[256,2048]{1,0:T(8,128)(2,1)S(1)}, bf16[256,2048]{1,0:T(8,128)(2,1)S(1)}, u32[]{:S(2)}, u32[]{:S(2)}) collective-permute-start(bf16[256,2048]{1,0:T(8,128)(2,1)S(1)} %get-tuple-element.162), channel_id=1, source_target_pairs={{0,8},{8,16},{16,24},{1,9},{9,17},{17,25},{2,10},{10,18},{18,26},{... | collective-permute-start | bytes 3145736 | tf_op jit(solution)/shard_map/ppermute | solution.py:47
  25.7 26.6 %collective-permute-start.1 = (bf16[256,2048]{1,0:T(8,128)(2,1)S(1)}, bf16[256,2048]{1,0:T(8,128)(2,1)}, u32[]{:S(2)}, u32[]{:S(2)}) collective-permute-start(bf16[256,2048]{1,0:T(8,128)(2,1)S(1)} %get-tuple-element.162), channel_id=1, source_target_pairs={{8,0},{16,8},{24,16},{9,1},{17,9},{25,17},{10,2},{18,10},{26,18},{... | collective-permute-start | bytes 3145736 | tf_op jit(solution)/shard_map/ppermute | solution.py:48
  52.3 27.0 %collective-permute-start.3 = (bf16[256,2048]{1,0:T(8,128)(2,1)}, bf16[256,2048]{1,0:T(8,128)(2,1)}, u32[]{:S(2)}, u32[]{:S(2)}) collective-permute-start(bf16[256,2048]{1,0:T(8,128)(2,1)} %collective-permute-done.1), channel_id=1, source_target_pairs={{8,0},{16,8},{9,1},{17,9},{10,2},{18,10},{11,3},{19,11},{12,4},{20... | collective-permute-start | bytes 3145736 | tf_op jit(solution)/shard_map/ppermute | solution.py:48
  55.6 34.3 %collective-permute-start.4 = (bf16[256,2048]{1,0:T(8,128)(2,1)}, bf16[256,2048]{1,0:T(8,128)(2,1)}, u32[]{:S(2)}, u32[]{:S(2)}) collective-permute-start(bf16[256,2048]{1,0:T(8,128)(2,1)} %collective-permute-done.2), channel_id=1, source_target_pairs={{16,24},{17,25},{18,26},{19,27},{20,28},{21,29},{22,30},{23,31}} | collective-permute-start | bytes 3145736 | tf_op jit(solution)/shard_map/ppermute | solution.py:47
  110.7 28.6 %collective-permute-start.6 = (bf16[256,2048]{1,0:T(8,128)(2,1)}, bf16[256,2048]{1,0:T(8,128)(2,1)}, u32[]{:S(2)}, u32[]{:S(2)}) collective-permute-start(bf16[256,2048]{1,0:T(8,128)(2,1)} %param.19), channel_id=1, source_target_pairs={{0,8},{8,16},{16,24},{1,9},{9,17},{17,25},{2,10},{10,18},{18,26},{... | collective-permute-start | bytes 3145736 | tf_op jit(solution)/shard_map/ppermute | solution.py:98
  113.2 26.1 %collective-permute-start.7 = (bf16[256,2048]{1,0:T(8,128)(2,1)}, bf16[256,2048]{1,0:T(8,128)(2,1)}, u32[]{:S(2)}, u32[]{:S(2)}) collective-permute-start(bf16[256,2048]{1,0:T(8,128)(2,1)} %param.19), channel_id=1, source_target_pairs={{8,0},{16,8},{24,16},{9,1},{17,9},{25,17},{10,2},{18,10},{26,18},{... | collective-permute-start | bytes 3145736 | tf_op jit(solution)/shard_map/ppermute | solution.py:99
  143.8 28.0 %collective-permute-start.9 = (bf16[256,2048]{1,0:T(8,128)(2,1)}, bf16[256,2048]{1,0:T(8,128)(2,1)}, u32[]{:S(2)}, u32[]{:S(2)}) collective-permute-start(bf16[256,2048]{1,0:T(8,128)(2,1)} %collective-permute-done.7), channel_id=1, source_target_pairs={{8,0},{16,8},{9,1},{17,9},{10,2},{18,10},{11,3},{19,11},{12,4},{20... | collective-permute-start | bytes 3145736 | tf_op jit(solution)/shard_map/ppermute | solution.py:99
  201.3 381.3 %reduce-scatter.5.cloned.1.call-start = ((), (), s32[]{:S(2)}) async-start(), calls=%async_computation.8 | async-start | bytes 9437184 | tf_op jit(solution)/shard_map/reduce_scatter | solution.py:182
  201.5 27.2 %collective-permute-start.15 = (bf16[256,2048]{1,0:T(8,128)(2,1)S(1)}, bf16[256,2048]{1,0:T(8,128)(2,1)S(1)}, u32[]{:S(2)}, u32[]{:S(2)}) collective-permute-start(bf16[256,2048]{1,0:T(8,128)(2,1)S(1)} %get-tuple-element.185), channel_id=1, source_target_pairs={{24,16},{25,17},{26,18},{27,19},{28,20},{29,21},{30,22},{31,23}} | collective-permute-start | bytes 3145736 | tf_op jit(solution)/shard_map/ppermute | solution.py:75
  259.9 38.2 %collective-permute-start.17 = (bf16[256,2048]{1,0:T(8,128)(2,1)S(1)}, bf16[256,2048]{1,0:T(8,128)(2,1)}, u32[]{:S(2)}, u32[]{:S(2)}) collective-permute-start(bf16[256,2048]{1,0:T(8,128)(2,1)S(1)} %add_convert_fusion.13), channel_id=1, source_target_pairs={{8,0},{16,8},{24,16},{9,1},{17,9},{25,17},{10,2},{18,10},{26,18},{... | collective-permute-start | bytes 3145736 | tf_op jit(solution)/shard_map/ppermute | solution.py:75
  332.6 26.7 %collective-permute-start.21 = (bf16[256,2048]{1,0:T(8,128)(2,1)S(1)}, bf16[256,2048]{1,0:T(8,128)(2,1)S(1)}, u32[]{:S(2)}, u32[]{:S(2)}) collective-permute-start(bf16[256,2048]{1,0:T(8,128)(2,1)S(1)} %collective-permute-done.19), channel_id=1, source_target_pairs={{8,0},{16,8},{9,1},{17,9},{10,2},{18,10},{11,3},{19,11},{12,4},{20... | collective-permute-start | bytes 3145736 | tf_op jit(solution)/shard_map/ppermute | solution.py:48
  460.9 27.4 %collective-permute-start.26 = (bf16[256,2048]{1,0:T(8,128)(2,1)S(1)}, bf16[256,2048]{1,0:T(8,128)(2,1)S(1)}, u32[]{:S(2)}, u32[]{:S(2)}) collective-permute-start(bf16[256,2048]{1,0:T(8,128)(2,1)S(1)} %get-tuple-element.179), channel_id=1, source_target_pairs={{0,8},{8,16},{1,9},{9,17},{2,10},{10,18},{3,11},{11,19},{4,12},{12... | collective-permute-start | bytes 3145736 | tf_op jit(solution)/shard_map/ppermute | solution.py:139
  509.6 301.0 %reduce-scatter.9.cloned.1.call-start = ((), (), s32[]{:S(2)}) async-start(), calls=%async_computation.10 | async-start | bytes 2359296 | tf_op jit(solution)/shard_map/reduce_scatter | solution.py:182
  513.5 32.8 %collective-permute-start.30 = (bf16[256,2048]{1,0:T(8,128)(2,1)}, bf16[256,2048]{1,0:T(8,128)(2,1)S(1)}, u32[]{:S(2)}, u32[]{:S(2)}) collective-permute-start(bf16[256,2048]{1,0:T(8,128)(2,1)} %get-tuple-element.175), channel_id=1, source_target_pairs={{0,8},{1,9},{2,10},{3,11},{4,12},{5,13},{6,14},{7,15}} | collective-permute-start | bytes 3145736 | tf_op jit(solution)/shard_map/ppermute | solution.py:139
  517.3 29.0 %collective-permute-start.31 = (bf16[256,2048]{1,0:T(8,128)(2,1)S(1)}, bf16[256,2048]{1,0:T(8,128)(2,1)}, u32[]{:S(2)}, u32[]{:S(2)}) collective-permute-start(bf16[256,2048]{1,0:T(8,128)(2,1)S(1)} %get-tuple-element.174), channel_id=1, source_target_pairs={{24,16},{25,17},{26,18},{27,19},{28,20},{29,21},{30,22},{31,23}} | collective-permute-start | bytes 3145736 | tf_op jit(solution)/shard_map/ppermute | solution.py:142
  640.4 28.1 %collective-permute-start.40 = (bf16[256,2048]{1,0:T(8,128)(2,1)S(1)}, bf16[256,2048]{1,0:T(8,128)(2,1)S(1)}, u32[]{:S(2)}, u32[]{:S(2)}) collective-permute-start(bf16[256,2048]{1,0:T(8,128)(2,1)S(1)} %collective-permute-done.38), channel_id=1, source_target_pairs={{16,24},{17,25},{18,26},{19,27},{20,28},{21,29},{22,30},{23,31}} | collective-permute-start | bytes 3145736 | tf_op jit(solution)/shard_map/ppermute | solution.py:47
  721.6 128.5 %reduce-scatter.7.cloned.1.call-start = ((), (), s32[]{:S(2)}) async-start(), calls=%async_computation.9 | async-start | bytes 7077888 | tf_op jit(solution)/shard_map/reduce_scatter | solution.py:182
  744.1 206.7 %reduce-scatter.11.cloned.1.call-start = ((), (), s32[]{:S(2)}) async-start(), calls=%async_computation.11 | async-start | bytes 18874368 | tf_op jit(solution)/shard_map/reduce_scatter | solution.py:182
  755.9 25.4 %collective-permute-start.45 = (bf16[256,2048]{1,0:T(8,128)(2,1)S(1)}, bf16[256,2048]{1,0:T(8,128)(2,1)S(1)}, u32[]{:S(2)}, u32[]{:S(2)}) collective-permute-start(bf16[256,2048]{1,0:T(8,128)(2,1)S(1)} %get-tuple-element.169), channel_id=1, source_target_pairs={{24,16},{25,17},{26,18},{27,19},{28,20},{29,21},{30,22},{31,23}} | collective-permute-start | bytes 3145736 | tf_op jit(solution)/shard_map/ppermute | solution.py:75
  809.3 35.0 %collective-permute-start.47 = (bf16[256,2048]{1,0:T(8,128)(2,1)}, bf16[256,2048]{1,0:T(8,128)(2,1)}, u32[]{:S(2)}, u32[]{:S(2)}) collective-permute-start(bf16[256,2048]{1,0:T(8,128)(2,1)} %add_convert_fusion), channel_id=1, source_target_pairs={{8,0},{16,8},{24,16},{9,1},{17,9},{25,17},{10,2},{18,10},{26,18},{... | collective-permute-start | bytes 3145736 | tf_op jit(solution)/shard_map/ppermute | solution.py:75
  (75 other events, 1557.5 us)
Sparse Core Ops, SparseCore 0:
  10.5 48.1 all-gather.4
  60.5 28.0 all-gather.6
  91.1 89.7 all-gather.8
  201.4 54.0 all-gather.10
  509.7 72.7 reduce-scatter.4
  721.7 44.0 reduce-scatter.8
  769.2 61.7 reduce-scatter.6
  834.6 116.1 reduce-scatter.10

commit v6 on v4

--- a/solution.py
+++ b/solution.py
@@ -156,6 +156,53 @@
         )
 
 
+class RingGather:
+    def __init__(self, shard, axis):
+        self.axis = axis
+        self.n = lax.psum(1, axis)
+        self.slots = [shard]
+        self.pending = shard
+
+    def steps(self):
+        return self.n - 1
+
+    def send(self):
+        n = self.n
+        self.pending = lax.ppermute(self.pending, self.axis, [(j, (j + 1) % n) for j in range(n)])
+
+    def land(self):
+        self.slots.append(self.pending)
+
+
+class RingScatter:
+    def __init__(self, slots, axis, send_dtype):
+        self.axis = axis
+        self.n = lax.psum(1, axis)
+        self.slots = slots
+        self.send_dtype = send_dtype
+        self.pending = None
+        self.step = 0
+
+    def steps(self):
+        return self.n - 1
+
+    def send(self):
+        n, step = self.n, self.step + 1
+        value = self.slots[step]
+        if self.pending is not None:
+            value = value + self.pending.astype(jnp.float32)
+        self.pending = lax.ppermute(
+            value.astype(self.send_dtype), self.axis, [(j, (j + 1) % n) for j in range(n)]
+        )
+        self.step = step
+
+    def land(self):
+        pass
+
+    def result(self):
+        return self.slots[0] + self.pending.astype(jnp.float32)
+
+
 def overlap(chain, pieces):
     value = ()
     count = chain.steps()
@@ -319,49 +366,71 @@
         attended = merge_heads(state.pop("mixed").astype(jnp.bfloat16))
         return dict(state, attended=attended, attn_partial=product(attended, full_output))
 
-    cot_chain = GatherSteps(cotangent, "row")
-    fwd = overlap(cot_chain, [project, attend, out_project])
-    grad_rows = cot_chain.result()
+    cot_later, first_rows = lax.optimization_barrier((cotangent, first_rows))
+    cot_ring = RingGather(cot_later, "row")
+    fwd = overlap(cot_ring, [project, attend, out_project])
+    cot_slots = cot_ring.slots
     queries, keys_rot, values = fwd["queries"], fwd["keys_rot"], fwd["values"]
     log_total, attended = fwd["log_total"], fwd["attended"]
     attention_sum = line_reduce_scatter(fwd["attn_partial"], "row", jnp.bfloat16)
     middle = inputs + attention_sum
     normed_second = layer_norm(middle).astype(jnp.bfloat16)
-    second_rows = line_all_gather(normed_second, "row")
-    gu_lin = product(second_rows, full_gu)
-    gate_lin = gu_lin[:, :hidden]
-    up_lin = gu_lin[:, hidden:]
-    activation = (jax.nn.silu(gate_lin) * up_lin).astype(jnp.bfloat16)
-    ffn_chain = ScatterSteps(product(activation, full_down), "row", jnp.bfloat16)
-
-    def gate_up_grads(_):
-        grad_activation = times_transpose(grad_rows, full_down)
-        sigma = jax.nn.sigmoid(gate_lin)
-        grad_gate = grad_activation * up_lin * sigma * (1.0 + gate_lin * (1.0 - sigma))
-        grad_up = grad_activation * gate_lin * sigma
-        return dict(grad_gu=jnp.concatenate([grad_gate, grad_up], axis=1).astype(jnp.bfloat16))
-
-    def second_partial(state):
-        return dict(state, second_partial=times_transpose(state["grad_gu"], full_gu))
-
-    def down_weight_grad(state):
-        return dict(state, grad_down_w=contract_rows(activation, grad_rows))
-
-    bwd = overlap(ffn_chain, [gate_up_grads, second_partial, down_weight_grad])
-    ffn_sum = ffn_chain.result()
+    second_ring = RingGather(normed_second, "row")
+    slots = second_ring.n
+
+    def ffn_forward(slot):
+        def piece(done):
+            gu_lin = product(second_ring.slots[slot], full_gu)
+            gate_lin = gu_lin[:, :hidden]
+            up_lin = gu_lin[:, hidden:]
+            activation = (jax.nn.silu(gate_lin) * up_lin).astype(jnp.bfloat16)
+            part = product(activation, full_down)
+            return done + ((gate_lin, up_lin, activation, part),)
+
+        return piece
+
+    ffn = overlap(second_ring, [ffn_forward(slot) for slot in range(slots)])
+    second_slots = second_ring.slots
+    gate_slots = [item[0] for item in ffn]
+    up_slots = [item[1] for item in ffn]
+    act_slots = [item[2] for item in ffn]
+    ffn_ring = RingScatter([item[3] for item in ffn], "row", jnp.bfloat16)
+
+    def ffn_backward(slot):
+        def piece(done):
+            gate_lin, up_lin = gate_slots[slot], up_slots[slot]
+            grad_activation = times_transpose(cot_slots[slot], full_down)
+            sigma = jax.nn.sigmoid(gate_lin)
+            grad_gate = grad_activation * up_lin * sigma * (1.0 + gate_lin * (1.0 - sigma))
+            grad_up = grad_activation * gate_lin * sigma
+            grad_gu = jnp.concatenate([grad_gate, grad_up], axis=1).astype(jnp.bfloat16)
+            return done + ((grad_gu, times_transpose(grad_gu, full_gu)),)
+
+        return piece
+
+    order = list(range(1, slots)) + [0]
+    bwd = overlap(ffn_ring, [ffn_backward(slot) for slot in order])
+    ffn_sum = ffn_ring.result()
     output = (middle + ffn_sum).astype(jnp.bfloat16)
-    grad_gu = bwd["grad_gu"]
-    down_sum = col_scatter(bwd["grad_down_w"], 1)
-    second_chain = ScatterSteps(bwd["second_partial"], "row", jnp.bfloat16)
-
-    def gate_up_weight_grad(_):
-        return contract_rows(second_rows, grad_gu)
-
-    grad_gu_w = overlap(second_chain, [gate_up_weight_grad])
-    grad_second = second_chain.result()
+    by_slot = dict(zip(order, bwd))
+    grad_gu = jnp.concatenate([by_slot[slot][0] for slot in range(slots)], axis=0)
+    second_ring_back = RingScatter([by_slot[slot][1] for slot in range(slots)], "row", jnp.bfloat16)
+    rows_second = jnp.concatenate(second_slots, axis=0)
+
+    def down_weight_grad(_):
+        return contract_rows(jnp.concatenate(act_slots, axis=0), jnp.concatenate(cot_slots, axis=0))
+
+    def gate_up_weight_grad(grad_down_w):
+        return (grad_down_w, contract_rows(rows_second, grad_gu))
+
+    grad_down_w, grad_gu_w = overlap(second_ring_back, [down_weight_grad, gate_up_weight_grad])
+    grad_second = second_ring_back.result()
+    down_sum = col_scatter(grad_down_w, 1)
     gu_sum = col_scatter(grad_gu_w, 0)
     grad_middle = cotangent.astype(jnp.float32) + norm_back(middle, grad_second)
-    grad_branch = line_all_gather(grad_middle.astype(jnp.bfloat16), "row")
+    branch_chain = GatherSteps(grad_middle.astype(jnp.bfloat16), "row")
+    down_sum = overlap(branch_chain, [lambda value: value] * (branch_chain.steps() - 1) + [lambda value: down_sum])
+    grad_branch = branch_chain.result()
     output_sum = col_scatter(contract_rows(attended, grad_branch), 1)
     grad_mixed = split_heads(times_transpose(grad_branch, full_output).astype(jnp.bfloat16))
     grad_q_rot, grad_k_rot, grad_values = lax.map(

time: 1020 us -> 919 us (0.901)
  waiting for transfers between devices: 496 us -> 415 us
  matrix products: 209 us -> 260 us
  starting transfers between devices: 110 us -> 62.1 us
  local copies, waits for them, and re-layouts: 88.8 us -> 66 us
    ppermute x9 -> x3, waiting for transfers between devices: 122 us -> 33.5 us  [line_all_gather(): from_right = lax.ppermute(from_right, axis, left_pairs)]
    ppermute x12, waiting for transfers between devices: 40 us -> 96.3 us  [the longest x6 49 us: send(): lax.ppermute(self.pending, self.axis, [(j, (j + 1) % n) for j in range(n)])]
    dot_general x4 -> x10, matrix products: 57.7 us -> 89.1 us  [times_transpose(): lax.dot_general(left, right, (((1,), (1,)), ((), ())), preferred_element_...]
    ppermute x6, waiting for transfers between devices: 98.3 us -> 74.9 us  [line_reduce_scatter(): lax.ppermute(send_right.astype(send_dtype), axis, [(j, j + 1) for j in ra...]
    ppermute x12, starting transfers between devices: 29.5 us -> 8.01 us  [the longest x6 4.6 us: send(): lax.ppermute(self.pending, self.axis, [(j, (j + 1) % n) for j in range(n)])]
    reduce_scatter x4, waiting for transfers between devices: 127 us -> 108 us  [col_scatter(): lax.psum_scatter(low_part, COL, scatter_dimension=axis, tiled=True)]
    dot_general x4 -> x10, matrix products: 49.9 us -> 67.6 us  [product(): return jnp.dot(left, right, preferred_element_type=jnp.float32)]
    ppermute x9 -> x3, starting transfers between devices: 20.3 us -> 3.85 us  [line_all_gather(): from_right = lax.ppermute(from_right, axis, left_pairs)]
  transfers between devices with their start and end apart: 56 -> 44, of which waited for: 29 -> 28; matrix products, arithmetic and copies ran while one was open for 30% -> 38% of each run, Pallas kernels for 0% -> 0%
where the time goes in v6:
time: 919 us; the launch traced here: 912 us
  waiting for transfers between devices  415 us (45%)
  matrix products  260 us (28%)
  other arithmetic  92.6 us (10%)
  local copies, waits for them, and re-layouts  66 us (7%)
  starting transfers between devices  62.1 us (7%)
  between operations  15.5 us (2%)
    reduce_scatter x4, waiting for transfers between devices, col_scatter(): lax.psum_scatter(low_part, COL, scatter_dimension=axis, tiled=True)  108 us
    dot_general x10, matrix products, times_transpose(): lax.dot_general(left, right, (((1,), (1,)), ((), ())), preferred_element_...  89.1 us
    ppermute x6, waiting for transfers between devices, line_reduce_scatter(): lax.ppermute(send_right.astype(send_dtype), axis, [(j, j + 1) for j in ra...  74.9 us
    dot_general x10, matrix products, product(): return jnp.dot(left, right, preferred_element_type=jnp.float32)  67.6 us
    dot_general x4, matrix products, contract_rows(): lax.dot_general(left, right, (((0,), (0,)), ((), ())), preferred_element_...  56 us
    ppermute x6, waiting for transfers between devices, send(): lax.ppermute(self.pending, self.axis, [(j, (j + 1) % n) for j in range(n)])  49 us
    ppermute x6, waiting for transfers between devices, send(): lax.ppermute(value.astype(self.send_dtype), self.axis, [(j, (j + 1) % n)...  47.3 us
    ppermute x3, waiting for transfers between devices, send(): lax.ppermute(from_right, self.axis, [(j, j - 1) for j in range(1, n - ste...  36.8 us
  transfers between devices with their start and end apart: 44, of which 28 were waited for; matrix products, arithmetic and copies ran while one was open for 38% of the time, Pallas kernels for 0%

profile of v6, /device:TPU:0, one launch (start us, length us, event | category | flops | bytes accessed | tf_op | source)
XLA Modules:
  0.0 911.9 jit_solution(2458427749436537405)
XLA Ops:
  26.2 21.0 %collective-permute-done = bf16[256,2048]{1,0:T(8,128)(2,1)S(1)} collective-permute-done((bf16[256,2048]{1,0:T(8,128)(2,1)S(1)}, bf16[256,2048]{1,0:T(8,128)(2,1)S(1)}, u32[]{:S(2)}, u32[]{:S(2)}) %collective-permute-start) | collective-permute-done | bytes 1048608 | tf_op jit(solution)/shard_map/ppermute | solution.py:47
  60.1 18.3 %collective-permute-done.3 = bf16[256,2048]{1,0:T(8,128)(2,1)} collective-permute-done((bf16[256,2048]{1,0:T(8,128)(2,1)}, bf16[256,2048]{1,0:T(8,128)(2,1)}, u32[]{:S(2)}, u32[]{:S(2)}) %collective-permute-start.3) | collective-permute-done | bytes 1048608 | tf_op jit(solution)/shard_map/ppermute | solution.py:48
  91.3 12.5 %collective-permute-done.5 = bf16[256,2048]{1,0:T(8,128)(2,1)S(1)} collective-permute-done((bf16[256,2048]{1,0:T(8,128)(2,1)}, bf16[256,2048]{1,0:T(8,128)(2,1)S(1)}, u32[]{:S(2)}, u32[]{:S(2)}) %collective-permute-start.5) | collective-permute-done | bytes 1048608 | tf_op jit(solution)/shard_map/ppermute | solution.py:48
  165.3 19.5 %collective-permute-done.8 = bf16[256,2048]{1,0:T(8,128)(2,1)} collective-permute-done((bf16[256,2048]{1,0:T(8,128)(2,1)}, bf16[256,2048]{1,0:T(8,128)(2,1)}, u32[]{:S(2)}, u32[]{:S(2)}) %collective-permute-start.8) | collective-permute-done | bytes 1048608 | tf_op jit(solution)/shard_map/ppermute | solution.py:171
  189.3 16.7 %collective-permute-done.9 = bf16[256,2048]{1,0:T(8,128)(2,1)} collective-permute-done((bf16[256,2048]{1,0:T(8,128)(2,1)}, bf16[256,2048]{1,0:T(8,128)(2,1)}, u32[]{:S(2)}, u32[]{:S(2)}) %collective-permute-start.9) | collective-permute-done | bytes 1048608 | tf_op jit(solution)/shard_map/ppermute | solution.py:72
  214.5 17.0 %collective-permute-done.10 = bf16[256,2048]{1,0:T(8,128)(2,1)} collective-permute-done((bf16[256,2048]{1,0:T(8,128)(2,1)}, bf16[256,2048]{1,0:T(8,128)(2,1)}, u32[]{:S(2)}, u32[]{:S(2)}) %collective-permute-start.10) | collective-permute-done | bytes 1048608 | tf_op jit(solution)/shard_map/ppermute | solution.py:72
  265.9 14.4 %collective-permute-done.14 = bf16[256,2048]{1,0:T(8,128)(2,1)S(1)} collective-permute-done((bf16[256,2048]{1,0:T(8,128)(2,1)S(1)}, bf16[256,2048]{1,0:T(8,128)(2,1)S(1)}, u32[]{:S(2)}, u32[]{:S(2)}) %collective-permute-start.14) | collective-permute-done | bytes 1048608 | tf_op jit(solution)/shard_map/ppermute | solution.py:75
  385.2 12.2 %fusion.96 = bf16[256,2048]{1,0:T(8,128)(2,1)} fusion(bf16[2048,4096]{1,0:T(8,128)(2,1)} %all-gather.9.cloned.1.call-done, bf16[256,2048]{1,0:T(8,128)(2,1)} %copy-done.20, bf16[256,2048]{1,0:T(8,128)(2,1)} %copy-done.19), kind=kOutput, calls=%fused_computation.188 | convolution fusion | flops 4299161600 | bytes 19922944 | tf_op jit(solution)/shard_map/dot_general | solution.py:29
  402.0 11.9 %fusion.95 = f32[256,2048]{1,0:T(8,128)} fusion(bf16[2048,4096]{1,0:T(8,128)(2,1)} %all-gather.9.cloned.1.call-done, bf16[256,2048]{1,0:T(8,128)(2,1)} %copy-done.18, bf16[256,2048]{1,0:T(8,128)(2,1)S(1)} %get-tuple-element.239), kind=kOutput, calls=%fused_computation.187 | convolution fusion | flops 4299161600 | bytes 20971520 | tf_op jit(solution)/shard_map/dot_general | solution.py:29
  427.5 12.3 %fusion.94 = f32[256,2048]{1,0:T(8,128)} fusion(bf16[2048,4096]{1,0:T(8,128)(2,1)} %all-gather.9.cloned.1.call-done, bf16[256,2048]{1,0:T(8,128)(2,1)} %copy-done.43, bf16[256,2048]{1,0:T(8,128)(2,1)} %copy-done.42), kind=kOutput, calls=%fused_computation.186 | convolution fusion | flops 4299161600 | bytes 20971520 | tf_op jit(solution)/shard_map/dot_general | solution.py:29
  439.8 14.1 %collective-permute-done.20 = bf16[256,2048]{1,0:T(8,128)(2,1)} collective-permute-done((bf16[256,2048]{1,0:T(8,128)(2,1)}, bf16[256,2048]{1,0:T(8,128)(2,1)}, u32[]{:S(2)}, u32[]{:S(2)}) %collective-permute-start.20) | collective-permute-done | bytes 1048608 | tf_op jit(solution)/shard_map/ppermute | solution.py:194
  453.8 14.1 %fusion.17 = bf16[2048,2048]{1,0:T(8,128)(2,1)} fusion(bf16[256,2048]{1,0:T(8,128)(2,1)} %get-tuple-element.238, bf16[256,2048]{1,0:T(8,128)(2,1)} %copy-done.31, bf16[256,2048]{1,0:T(8,128)(2,1)} %copy-done.30, bf16[256,2048]{1,0:T(8,128)(2,1)S(1)} %copy-done.29, bf16[256,2048]{1,0:T(8,128)(2,1)} %collective-permute-done.8, ...), kind=kOutput, calls=%fused_computation.24 | convolution fusion | flops 8623489024 | bytes 16777216 | tf_op jit(solution)/shard_map/dot_general | solution.py:23
  482.2 26.0 %fusion.3 = bf16[2048,4096]{1,0:T(8,128)(2,1)} fusion(bf16[256,4096]{1,0:T(8,128)(2,1)S(1)} %copy-done.24, bf16[256,4096]{1,0:T(8,128)(2,1)} %pad_maximum_fusion.3, bf16[256,4096]{1,0:T(8,128)(2,1)} %pad_maximum_fusion.2, bf16[256,2048]{1,0:T(8,128)(2,1)} %get-tuple-element.237, bf16[256,2048]{1,0:T(8,128)(2,1)} %get-tuple-element.236, ...), kind=kOutput, calls=%fused_computation.9 | convolution fusion | flops 17238589440 | bytes 29360128 | tf_op jit(solution)/shard_map/dot_general | solution.py:23
  510.7 16.6 %collective-permute-done.23 = bf16[256,2048]{1,0:T(8,128)(2,1)S(1)} collective-permute-done((bf16[256,2048]{1,0:T(8,128)(2,1)S(1)}, bf16[256,2048]{1,0:T(8,128)(2,1)S(1)}, u32[]{:S(2)}, u32[]{:S(2)}) %collective-permute-start.23) | collective-permute-done | bytes 1048608 | tf_op jit(solution)/shard_map/ppermute | solution.py:194
  527.6 13.7 %fusion.57 = f32[256,2048]{1,0:T(8,128)} fusion(bf16[2048,4096]{1,0:T(8,128)(2,1)} %all-gather.9.cloned.1.call-done, bf16[256,2048]{1,0:T(8,128)(2,1)} %get-tuple-element.237, bf16[256,2048]{1,0:T(8,128)(2,1)} %get-tuple-element.236), kind=kOutput, calls=%fused_computation.72 | convolution fusion | flops 4299161600 | bytes 20971520 | tf_op jit(solution)/shard_map/dot_general | solution.py:29
  558.0 10.9 %collective-permute-done.24 = bf16[256,2048]{1,0:T(8,128)(2,1)S(1)} collective-permute-done((bf16[256,2048]{1,0:T(8,128)(2,1)S(1)}, bf16[256,2048]{1,0:T(8,128)(2,1)S(1)}, u32[]{:S(2)}, u32[]{:S(2)}) %collective-permute-start.24) | collective-permute-done | bytes 1048608 | tf_op jit(solution)/shard_map/ppermute | solution.py:98
  568.9 12.7 %collective-permute-done.25 = bf16[256,2048]{1,0:T(8,128)(2,1)S(1)} collective-permute-done((bf16[256,2048]{1,0:T(8,128)(2,1)S(1)}, bf16[256,2048]{1,0:T(8,128)(2,1)S(1)}, u32[]{:S(2)}, u32[]{:S(2)}) %collective-permute-start.25) | collective-permute-done | bytes 1048608 | tf_op jit(solution)/shard_map/ppermute | solution.py:99
  583.7 23.9 %collective-permute-done.27 = bf16[256,2048]{1,0:T(8,128)(2,1)S(1)} collective-permute-done((bf16[256,2048]{1,0:T(8,128)(2,1)S(1)}, bf16[256,2048]{1,0:T(8,128)(2,1)S(1)}, u32[]{:S(2)}, u32[]{:S(2)}) %collective-permute-start.27) | collective-permute-done | bytes 1048608 | tf_op jit(solution)/shard_map/ppermute | solution.py:99
  635.5 12.8 %multiply_reduce_fusion = (f32[4,1024]{1,0:T(4,128)S(1)}, f32[4,1024,1024]{1,2,0:T(8,128)}) fusion(f32[4,1024,1024]{1,2,0:T(8,128)} %fusion.73, f32[4,1024]{1,0:T(4,128)S(1)} %bitcast.102, pred[1024,1024]{0,1:T(8,128)(4,1)S(1)} %copy-done.3, bf16[1024,4,128]{0,2,1:T(8,128)(2,1)S(1)} %bitcast.96, bf16[1,1024,4,128]{3,2,1,0:T(4,128)(2,1)S(1)} %copy-done.12), kind=kOutput, calls=%fused_computation.1 | convolution fusion | flops 1094709248 | bytes 36732928 | tf_op jit(solution)/shard_map/while/body/eval_jaxpr/qhd,khd->hqk/dot_general | solution.py:314
  648.4 12.2 %multiply_convert_fusion = bf16[4,1024,1024]{1,2,0:T(8,128)(2,1)S(1)} fusion(f32[4,1024,1024]{1,2,0:T(8,128)} %get-tuple-element.275, f32[4,1024,1024]{1,2,0:T(8,128)} %fusion.73, f32[4,1024]{1,0:T(4,128)S(1)} %get-tuple-element.274, f32[4,1024]{1,0:T(4,128)S(1)} %bitcast.103, pred[1024,1024]{0,1:T(8,128)(4,1)S(1)} %copy-done.3), kind=kLoop, calls=%fused_computation | loop fusion | flops 25165824 | bytes 43024384 | tf_op jit(solution)/shard_map/while/body/eval_jaxpr/convert_element_type | solution.py:316
  715.0 15.8 %collective-permute-done.30 = bf16[256,2048]{1,0:T(8,128)(2,1)S(1)} collective-permute-done((bf16[256,2048]{1,0:T(8,128)(2,1)S(1)}, bf16[256,2048]{1,0:T(8,128)(2,1)S(1)}, u32[]{:S(2)}, u32[]{:S(2)}) %collective-permute-start.30) | collective-permute-done | bytes 1048608 | tf_op jit(solution)/shard_map/ppermute | solution.py:72
  735.5 13.8 %collective-permute-done.31 = bf16[256,2048]{1,0:T(8,128)(2,1)S(1)} collective-permute-done((bf16[256,2048]{1,0:T(8,128)(2,1)S(1)}, bf16[256,2048]{1,0:T(8,128)(2,1)S(1)}, u32[]{:S(2)}, u32[]{:S(2)}) %collective-permute-start.31) | collective-permute-done | bytes 1048608 | tf_op jit(solution)/shard_map/ppermute | solution.py:72
  768.4 17.2 %collective-permute-done.35 = bf16[256,2048]{1,0:T(8,128)(2,1)} collective-permute-done((bf16[256,2048]{1,0:T(8,128)(2,1)}, bf16[256,2048]{1,0:T(8,128)(2,1)}, u32[]{:S(2)}, u32[]{:S(2)}) %collective-permute-start.35) | collective-permute-done | bytes 1048608 | tf_op jit(solution)/shard_map/ppermute | solution.py:75
  792.8 108.0 %reduce-scatter.11.cloned.1.call-done = bf16[256,4096]{1,0:T(8,128)(2,1)} async-done(((bf16[2048,4096]{1,0:T(8,128)(2,1)}), bf16[256,4096]{1,0:T(8,128)(2,1)}) %reduce-scatter.11.cloned.1.call-update) | async-done | bytes 2097168 | tf_op jit(solution)/shard_map/reduce_scatter | solution.py:229
  (329 shorter events, 428.8 us)
Async XLA Ops:
  7.2 102.8 %all-gather.5.cloned.1.call-start = ((), (), s32[]{:S(2)}) async-start(), calls=%async_computation.4 | async-start | bytes 7077888 | tf_op jit(solution)/shard_map/all_gather | solution.py:224
  9.4 151.8 %all-gather.7.cloned.1.call-start = ((), (), s32[]{:S(2)}) async-start(), calls=%async_computation.5 | async-start | bytes 2359296 | tf_op jit(solution)/shard_map/all_gather | solution.py:224
  10.2 226.3 %all-gather.11.cloned.1.call-start = ((), (), s32[]{:S(2)}) async-start(), calls=%async_computation.7 | async-start | bytes 9437184 | tf_op jit(solution)/shard_map/all_gather | solution.py:224
  10.9 275.7 %all-gather.9.cloned.1.call-start = ((), (), s32[]{:S(2)}) async-start(), calls=%async_computation.6 | async-start | bytes 18874368 | tf_op jit(solution)/shard_map/all_gather | solution.py:224
  12.5 610.5 %reduce-scatter.5.cloned.1.call-start = ((), (), s32[]{:S(2)}) async-start(), calls=%async_computation.8 | async-start | bytes 9437184 | tf_op jit(solution)/shard_map/reduce_scatter | solution.py:229
  19.8 27.3 %collective-permute-start = (bf16[256,2048]{1,0:T(8,128)(2,1)S(1)}, bf16[256,2048]{1,0:T(8,128)(2,1)S(1)}, u32[]{:S(2)}, u32[]{:S(2)}) collective-permute-start(bf16[256,2048]{1,0:T(8,128)(2,1)S(1)} %get-tuple-element.223), channel_id=1, source_target_pairs={{0,8},{8,16},{16,24},{1,9},{9,17},{17,25},{2,10},{10,18},{18,26},{... | collective-permute-start | bytes 3145736 | tf_op jit(solution)/shard_map/ppermute | solution.py:47
  24.8 26.6 %collective-permute-start.1 = (bf16[256,2048]{1,0:T(8,128)(2,1)S(1)}, bf16[256,2048]{1,0:T(8,128)(2,1)}, u32[]{:S(2)}, u32[]{:S(2)}) collective-permute-start(bf16[256,2048]{1,0:T(8,128)(2,1)S(1)} %get-tuple-element.223), channel_id=1, source_target_pairs={{8,0},{16,8},{24,16},{9,1},{17,9},{25,17},{10,2},{18,10},{26,18},{... | collective-permute-start | bytes 3145736 | tf_op jit(solution)/shard_map/ppermute | solution.py:48
  51.5 27.0 %collective-permute-start.3 = (bf16[256,2048]{1,0:T(8,128)(2,1)}, bf16[256,2048]{1,0:T(8,128)(2,1)}, u32[]{:S(2)}, u32[]{:S(2)}) collective-permute-start(bf16[256,2048]{1,0:T(8,128)(2,1)} %collective-permute-done.1), channel_id=1, source_target_pairs={{8,0},{16,8},{9,1},{17,9},{10,2},{18,10},{11,3},{19,11},{12,4},{20... | collective-permute-start | bytes 3145736 | tf_op jit(solution)/shard_map/ppermute | solution.py:48
  54.8 34.3 %collective-permute-start.4 = (bf16[256,2048]{1,0:T(8,128)(2,1)}, bf16[256,2048]{1,0:T(8,128)(2,1)}, u32[]{:S(2)}, u32[]{:S(2)}) collective-permute-start(bf16[256,2048]{1,0:T(8,128)(2,1)} %collective-permute-done.2), channel_id=1, source_target_pairs={{16,24},{17,25},{18,26},{19,27},{20,28},{21,29},{22,30},{23,31}} | collective-permute-start | bytes 3145736 | tf_op jit(solution)/shard_map/ppermute | solution.py:47
  78.5 25.4 %collective-permute-start.5 = (bf16[256,2048]{1,0:T(8,128)(2,1)}, bf16[256,2048]{1,0:T(8,128)(2,1)S(1)}, u32[]{:S(2)}, u32[]{:S(2)}) collective-permute-start(bf16[256,2048]{1,0:T(8,128)(2,1)} %collective-permute-done.3), channel_id=1, source_target_pairs={{8,0},{9,1},{10,2},{11,3},{12,4},{13,5},{14,6},{15,7}} | collective-permute-start | bytes 3145736 | tf_op jit(solution)/shard_map/ppermute | solution.py:48
  109.8 24.7 %collective-permute-start.6 = (bf16[256,2048]{1,0:T(8,128)(2,1)}, bf16[256,2048]{1,0:T(8,128)(2,1)}, u32[]{:S(2)}, u32[]{:S(2)}) collective-permute-start(bf16[256,2048]{1,0:T(8,128)(2,1)} %param.19), channel_id=1, source_target_pairs={{0,8},{8,16},{16,24},{24,0},{1,9},{9,17},{17,25},{25,1},{2,10},{10... | collective-permute-start | bytes 3145736 | tf_op jit(solution)/shard_map/ppermute | solution.py:171
  136.9 24.4 %collective-permute-start.7 = (bf16[256,2048]{1,0:T(8,128)(2,1)}, bf16[256,2048]{1,0:T(8,128)(2,1)}, u32[]{:S(2)}, u32[]{:S(2)}) collective-permute-start(bf16[256,2048]{1,0:T(8,128)(2,1)} %collective-permute-done.6), channel_id=1, source_target_pairs={{0,8},{8,16},{16,24},{24,0},{1,9},{9,17},{17,25},{25,1},{2,10},{10... | collective-permute-start | bytes 3145736 | tf_op jit(solution)/shard_map/ppermute | solution.py:171
  188.3 26.2 %collective-permute-start.12 = (bf16[256,2048]{1,0:T(8,128)(2,1)S(1)}, bf16[256,2048]{1,0:T(8,128)(2,1)S(1)}, u32[]{:S(2)}, u32[]{:S(2)}) collective-permute-start(bf16[256,2048]{1,0:T(8,128)(2,1)S(1)} %get-tuple-element.231), channel_id=1, source_target_pairs={{24,16},{25,17},{26,18},{27,19},{28,20},{29,21},{30,22},{31,23}} | collective-permute-start | bytes 3145736 | tf_op jit(solution)/shard_map/ppermute | solution.py:75
  251.0 29.3 %collective-permute-start.14 = (bf16[256,2048]{1,0:T(8,128)(2,1)S(1)}, bf16[256,2048]{1,0:T(8,128)(2,1)S(1)}, u32[]{:S(2)}, u32[]{:S(2)}) collective-permute-start(bf16[256,2048]{1,0:T(8,128)(2,1)S(1)} %add_convert_fusion.9), channel_id=1, source_target_pairs={{8,0},{16,8},{24,16},{9,1},{17,9},{25,17},{10,2},{18,10},{26,18},{... | collective-permute-start | bytes 3145736 | tf_op jit(solution)/shard_map/ppermute | solution.py:75
  353.3 44.1 %collective-permute-start.18 = (bf16[256,2048]{1,0:T(8,128)(2,1)}, bf16[256,2048]{1,0:T(8,128)(2,1)}, u32[]{:S(2)}, u32[]{:S(2)}) collective-permute-start(bf16[256,2048]{1,0:T(8,128)(2,1)} %fusion.108), channel_id=1, source_target_pairs={{0,8},{8,16},{16,24},{24,0},{1,9},{9,17},{17,25},{25,1},{2,10},{10... | collective-permute-start | bytes 3145736 | tf_op jit(solution)/shard_map/ppermute | solution.py:194
  426.6 27.2 %collective-permute-start.20 = (bf16[256,2048]{1,0:T(8,128)(2,1)}, bf16[256,2048]{1,0:T(8,128)(2,1)}, u32[]{:S(2)}, u32[]{:S(2)}) collective-permute-start(bf16[256,2048]{1,0:T(8,128)(2,1)} %add_convert_fusion.7), channel_id=1, source_target_pairs={{0,8},{8,16},{16,24},{24,0},{1,9},{9,17},{17,25},{25,1},{2,10},{10... | collective-permute-start | bytes 3145736 | tf_op jit(solution)/shard_map/ppermute | solution.py:194
  453.8 25.9 %collective-permute-start.21 = (bf16[256,2048]{1,0:T(8,128)(2,1)}, bf16[256,2048]{1,0:T(8,128)(2,1)}, u32[]{:S(2)}, u32[]{:S(2)}) collective-permute-start(bf16[256,2048]{1,0:T(8,128)(2,1)} %fusion.96), channel_id=1, source_target_pairs={{0,8},{8,16},{16,24},{24,0},{1,9},{9,17},{17,25},{25,1},{2,10},{10... | collective-permute-start | bytes 3145736 | tf_op jit(solution)/shard_map/ppermute | solution.py:194
  482.2 26.3 %collective-permute-start.22 = (bf16[256,2048]{1,0:T(8,128)(2,1)}, bf16[256,2048]{1,0:T(8,128)(2,1)}, u32[]{:S(2)}, u32[]{:S(2)}) collective-permute-start(bf16[256,2048]{1,0:T(8,128)(2,1)} %add_convert_fusion.5), channel_id=1, source_target_pairs={{0,8},{8,16},{16,24},{24,0},{1,9},{9,17},{17,25},{25,1},{2,10},{10... | collective-permute-start | bytes 3145736 | tf_op jit(solution)/shard_map/ppermute | solution.py:194
  527.4 231.4 %reduce-scatter.9.cloned.1.call-start = ((), (), s32[]{:S(2)}) async-start(), calls=%async_computation.10 | async-start | bytes 2359296 | tf_op jit(solution)/shard_map/reduce_scatter | solution.py:229
  556.7 25.0 %collective-permute-start.25 = (bf16[256,2048]{1,0:T(8,128)(2,1)S(1)}, bf16[256,2048]{1,0:T(8,128)(2,1)S(1)}, u32[]{:S(2)}, u32[]{:S(2)}) collective-permute-start(bf16[256,2048]{1,0:T(8,128)(2,1)S(1)} %get-tuple-element.218), channel_id=1, source_target_pairs={{8,0},{16,8},{24,16},{9,1},{17,9},{25,17},{10,2},{18,10},{26,18},{... | collective-permute-start | bytes 3145736 | tf_op jit(solution)/shard_map/ppermute | solution.py:99
  582.4 25.2 %collective-permute-start.27 = (bf16[256,2048]{1,0:T(8,128)(2,1)S(1)}, bf16[256,2048]{1,0:T(8,128)(2,1)S(1)}, u32[]{:S(2)}, u32[]{:S(2)}) collective-permute-start(bf16[256,2048]{1,0:T(8,128)(2,1)S(1)} %collective-permute-done.25), channel_id=1, source_target_pairs={{8,0},{16,8},{9,1},{17,9},{10,2},{18,10},{11,3},{19,11},{12,4},{20... | collective-permute-start | bytes 3145736 | tf_op jit(solution)/shard_map/ppermute | solution.py:99
  673.4 117.0 %reduce-scatter.7.cloned.1.call-start = ((), (), s32[]{:S(2)}) async-start(), calls=%async_computation.9 | async-start | bytes 7077888 | tf_op jit(solution)/shard_map/reduce_scatter | solution.py:229
  697.4 203.3 %reduce-scatter.11.cloned.1.call-start = ((), (), s32[]{:S(2)}) async-start(), calls=%async_computation.11 | async-start | bytes 18874368 | tf_op jit(solution)/shard_map/reduce_scatter | solution.py:229
  757.4 28.2 %collective-permute-start.35 = (bf16[256,2048]{1,0:T(8,128)(2,1)}, bf16[256,2048]{1,0:T(8,128)(2,1)}, u32[]{:S(2)}, u32[]{:S(2)}) collective-permute-start(bf16[256,2048]{1,0:T(8,128)(2,1)} %add_convert_fusion), channel_id=1, source_target_pairs={{8,0},{16,8},{24,16},{9,1},{17,9},{25,17},{10,2},{18,10},{26,18},{... | collective-permute-start | bytes 3145736 | tf_op jit(solution)/shard_map/ppermute | solution.py:75
  (91 other events, 1301.4 us)
Sparse Core Ops, SparseCore 0:
  10.5 48.1 all-gather.4
  60.5 28.0 all-gather.6
  90.5 55.8 all-gather.10
  148.7 89.7 all-gather.8
  527.5 71.0 reduce-scatter.4
  673.5 42.2 reduce-scatter.8
  719.2 61.7 reduce-scatter.6
  784.6 116.1 reduce-scatter.10

commit v7 on v6

--- a/solution.py
+++ b/solution.py
@@ -29,53 +29,6 @@
     return lax.dot_general(
         left, right, (((1,), (1,)), ((), ())), preferred_element_type=jnp.float32
     )
-
-
-def line_all_gather(shard, axis):
-    n = lax.psum(1, axis)
-    if n == 1:
-        return shard
-    me = lax.axis_index(axis)
-    rows = shard.shape[0]
-    buf = jnp.zeros(((3 * n - 2) * rows,) + shard.shape[1:], shard.dtype)
-    buf = lax.dynamic_update_slice_in_dim(buf, shard, (me + n - 1) * rows, 0)
-    from_left = shard
-    from_right = shard
-    for step in range(1, n):
-        right_pairs = [(j, j + 1) for j in range(step - 1, n - 1)]
-        left_pairs = [(j, j - 1) for j in range(1, n - step + 1)]
-        from_left = lax.ppermute(from_left, axis, right_pairs)
-        from_right = lax.ppermute(from_right, axis, left_pairs)
-        buf = lax.dynamic_update_slice_in_dim(buf, from_left, (me - step + n - 1) * rows, 0)
-        buf = lax.dynamic_update_slice_in_dim(buf, from_right, (me + step + n - 1) * rows, 0)
-    return buf[(n - 1) * rows : (2 * n - 1) * rows]
-
-
-def line_reduce_scatter(partial, axis, send_dtype):
-    n = lax.psum(1, axis)
-    if n == 1:
-        return partial
-    me = lax.axis_index(axis)
-    rows = partial.shape[0] // n
-
-    def block(k):
-        return lax.dynamic_slice_in_dim(partial, jnp.clip(k, 0, n - 1) * rows, rows, 0)
-
-    recv_right = None
-    recv_left = None
-    for step in range(1, n):
-        send_right = block(n - step + me)
-        send_left = block(me + step - n)
-        if recv_right is not None:
-            send_right = send_right + recv_right
-            send_left = send_left + recv_left
-        recv_right = lax.ppermute(
-            send_right.astype(send_dtype), axis, [(j, j + 1) for j in range(0, step)]
-        ).astype(jnp.float32)
-        recv_left = lax.ppermute(
-            send_left.astype(send_dtype), axis, [(j, j - 1) for j in range(n - step, n)]
-        ).astype(jnp.float32)
-    return block(me) + recv_right + recv_left
 
 
 class GatherSteps:
@@ -157,11 +110,21 @@
 
 
 class RingGather:
-    def __init__(self, shard, axis):
+    def __init__(self, shard, axis, absolute=False):
         self.axis = axis
         self.n = lax.psum(1, axis)
+        self.me = lax.axis_index(axis)
+        self.rows = shard.shape[0]
         self.slots = [shard]
         self.pending = shard
+        self.buf = None
+        if absolute:
+            buf = jnp.zeros((self.n * self.rows,) + shard.shape[1:], shard.dtype)
+            self.buf = self.place(buf, shard, 0)
+
+    def place(self, buf, block, slot):
+        start = lax.rem(self.me - slot + self.n, self.n) * self.rows
+        return lax.dynamic_update_slice_in_dim(buf, block, start, 0)
 
     def steps(self):
         return self.n - 1
@@ -172,6 +135,11 @@
 
     def land(self):
         self.slots.append(self.pending)
+        if self.buf is not None:
+            self.buf = self.place(self.buf, self.pending, len(self.slots) - 1)
+
+    def result(self):
+        return self.buf
 
 
 class RingScatter:
@@ -203,18 +171,43 @@
         return self.slots[0] + self.pending.astype(jnp.float32)
 
 
+def ring_slots(partial, axis):
+    n = lax.psum(1, axis)
+    me = lax.axis_index(axis)
+    rows = partial.shape[0] // n
+    return [
+        lax.dynamic_slice_in_dim(partial, lax.rem(me - slot + n, n) * rows, rows, 0)
+        for slot in range(n)
+    ]
+
+
+def ring_all_gather(shard, axis):
+    chain = RingGather(shard, axis, absolute=True)
+    overlap(chain, [])
+    return chain.result()
+
+
+def ring_reduce_scatter(partial, axis, send_dtype):
+    chain = RingScatter(ring_slots(partial, axis), axis, send_dtype)
+    overlap(chain, [])
+    return chain.result()
+
+
 def overlap(chain, pieces):
-    value = ()
+    outputs = []
     count = chain.steps()
     for index in range(count):
         chain.send()
         if index < len(pieces):
-            value = pieces[index](value)
-        chain.pending, value = lax.optimization_barrier((chain.pending, value))
+            value = pieces[index](tuple(outputs))
+            chain.pending, value = lax.optimization_barrier((chain.pending, value))
+            outputs.append(value)
+        else:
+            chain.pending = lax.optimization_barrier(chain.pending)
         chain.land()
     for piece in pieces[count:]:
-        value = piece(value)
-    return value
+        outputs.append(piece(tuple(outputs)))
+    return tuple(outputs)
 
 
 COL = ("chip", "core")
@@ -339,7 +332,7 @@
     cosine, sine = rope_tables()
     inputs = layer_input.astype(jnp.float32)
     normed_first = layer_norm(inputs).astype(jnp.bfloat16)
-    first_rows = line_all_gather(normed_first, "row")
+    first_rows = ring_all_gather(normed_first, "row")
 
     def split_heads(matrix):
         return matrix.reshape(seq_count, LENGTH, heads_local, HD)
@@ -356,23 +349,25 @@
         values = split_heads(qkv_lin[:, 2 * width :]).astype(jnp.bfloat16)
         return dict(queries=queries, keys_rot=keys_rot, values=values)
 
-    def attend(state):
+    def attend(done):
+        state = done[0]
         mixed, log_total = lax.map(
             attend_forward, (state["queries"], state["keys_rot"], state["values"], piece_starts)
         )
-        return dict(state, mixed=mixed, log_total=log_total)
-
-    def out_project(state):
-        attended = merge_heads(state.pop("mixed").astype(jnp.bfloat16))
-        return dict(state, attended=attended, attn_partial=product(attended, full_output))
+        return dict(mixed=mixed, log_total=log_total)
+
+    def out_project(done):
+        attended = merge_heads(done[1]["mixed"].astype(jnp.bfloat16))
+        return dict(attended=attended, attn_partial=product(attended, full_output))
 
     cot_later, first_rows = lax.optimization_barrier((cotangent, first_rows))
     cot_ring = RingGather(cot_later, "row")
-    fwd = overlap(cot_ring, [project, attend, out_project])
+    projected, attention, mixed_out = overlap(cot_ring, [project, attend, out_project])
     cot_slots = cot_ring.slots
-    queries, keys_rot, values = fwd["queries"], fwd["keys_rot"], fwd["values"]
-    log_total, attended = fwd["log_total"], fwd["attended"]
-    attention_sum = line_reduce_scatter(fwd["attn_partial"], "row", jnp.bfloat16)
+    queries, keys_rot = projected["queries"], projected["keys_rot"]
+    values = projected["values"]
+    log_total, attended = attention["log_total"], mixed_out["attended"]
+    attention_sum = ring_reduce_scatter(mixed_out["attn_partial"], "row", jnp.bfloat16)
     middle = inputs + attention_sum
     normed_second = layer_norm(middle).astype(jnp.bfloat16)
     second_ring = RingGather(normed_second, "row")
@@ -385,7 +380,7 @@
             up_lin = gu_lin[:, hidden:]
             activation = (jax.nn.silu(gate_lin) * up_lin).astype(jnp.bfloat16)
             part = product(activation, full_down)
-            return done + ((gate_lin, up_lin, activation, part),)
+            return (gate_lin, up_lin, activation, part)
 
         return piece
 
@@ -404,7 +399,7 @@
             grad_gate = grad_activation * up_lin * sigma * (1.0 + gate_lin * (1.0 - sigma))
             grad_up = grad_activation * gate_lin * sigma
             grad_gu = jnp.concatenate([grad_gate, grad_up], axis=1).astype(jnp.bfloat16)
-            return done + ((grad_gu, times_transpose(grad_gu, full_gu)),)
+            return (grad_gu, times_transpose(grad_gu, full_gu))
 
         return piece
 
@@ -420,16 +415,17 @@
     def down_weight_grad(_):
         return contract_rows(jnp.concatenate(act_slots, axis=0), jnp.concatenate(cot_slots, axis=0))
 
-    def gate_up_weight_grad(grad_down_w):
-        return (grad_down_w, contract_rows(rows_second, grad_gu))
+    def gate_up_weight_grad(_):
+        return contract_rows(rows_second, grad_gu)
 
     grad_down_w, grad_gu_w = overlap(second_ring_back, [down_weight_grad, gate_up_weight_grad])
     grad_second = second_ring_back.result()
     down_sum = col_scatter(grad_down_w, 1)
     gu_sum = col_scatter(grad_gu_w, 0)
     grad_middle = cotangent.astype(jnp.float32) + norm_back(middle, grad_second)
-    branch_chain = GatherSteps(grad_middle.astype(jnp.bfloat16), "row")
-    down_sum = overlap(branch_chain, [lambda value: value] * (branch_chain.steps() - 1) + [lambda value: down_sum])
+    branch_chain = RingGather(grad_middle.astype(jnp.bfloat16), "row", absolute=True)
+    steps = branch_chain.steps()
+    down_sum = overlap(branch_chain, [lambda done: ()] * (steps - 1) + [lambda done: down_sum])[-1]
     grad_branch = branch_chain.result()
     output_sum = col_scatter(contract_rows(attended, grad_branch), 1)
     grad_mixed = split_heads(times_transpose(grad_branch, full_output).astype(jnp.bfloat16))
@@ -445,7 +441,7 @@
         axis=1,
     ).astype(jnp.bfloat16)
     qkv_sum = col_scatter(contract_rows(first_rows, grad_qkv), 0)
-    grad_first = line_reduce_scatter(times_transpose(grad_qkv, full_qkv), "row", jnp.bfloat16)
+    grad_first = ring_reduce_scatter(times_transpose(grad_qkv, full_qkv), "row", jnp.bfloat16)
     grad_input = grad_middle + norm_back(inputs, grad_first)
     return (
         output,

time: 919 us -> 822 us (0.89)
  starting transfers between devices: 62.1 us -> 7.35 us
  local copies, waits for them, and re-layouts: 66 us -> 46.8 us
  other arithmetic: 92.6 us -> 80.6 us
  matrix products: 260 us -> 250 us
    ppermute x24 -> x0, waiting for transfers between devices: 209 us -> none  [the longest x6 74.9 us: line_reduce_scatter(): lax.ppermute(send_right.astype(send_dtype), axis, [(j, j + 1) for j in ra...]
    ppermute x6 -> x12, waiting for transfers between devices: 49 us -> 174 us  [send(): lax.ppermute(self.pending, self.axis, [(j, (j + 1) % n) for j in range(n)])]
    ppermute x6 -> x12, waiting for transfers between devices: 47.3 us -> 135 us  [send(): lax.ppermute(value.astype(self.send_dtype), self.axis, [(j, (j + 1) % n)...]
    ppermute x24 -> x0, starting transfers between devices: 53.6 us -> none  [the longest x6 28.1 us: line_reduce_scatter(): lax.ppermute(send_right.astype(send_dtype), axis, [(j, j + 1) for j in ra...]
    convert_element_type x6 -> x0, other arithmetic: 11.5 us -> none  [the longest x4 8.36 us: line_reduce_scatter(): send_right.astype(send_dtype)]
    dynamic_update_slice x12 -> x6, local copies, waits for them, and re-layouts: 21.6 us -> 10.4 us  [place(): return lax.dynamic_update_slice_in_dim(buf, block, start, 0)]
  transfers between devices with their start and end apart: 44 -> 32, of which waited for: 28 -> 21; matrix products, arithmetic and copies ran while one was open for 38% -> 43% of each run, Pallas kernels for 0% -> 0%
where the time goes in v7:
time: 822 us; the launch traced here: 813 us
  waiting for transfers between devices  413 us (50%)
  matrix products  250 us (30%)
  other arithmetic  80.6 us (10%)
  local copies, waits for them, and re-layouts  46.8 us (6%)
  between operations  15.3 us (2%)
    ppermute x12, waiting for transfers between devices, send(): lax.ppermute(self.pending, self.axis, [(j, (j + 1) % n) for j in range(n)])  174 us
    ppermute x12, waiting for transfers between devices, send(): lax.ppermute(value.astype(self.send_dtype), self.axis, [(j, (j + 1) % n)...  135 us
    reduce_scatter x4, waiting for transfers between devices, col_scatter(): lax.psum_scatter(low_part, COL, scatter_dimension=axis, tiled=True)  102 us
    dot_general x10, matrix products, times_transpose(): lax.dot_general(left, right, (((1,), (1,)), ((), ())), preferred_element_...  83 us
    dot_general x10, matrix products, product(): return jnp.dot(left, right, preferred_element_type=jnp.float32)  68.9 us
    dot_general x4, matrix products, contract_rows(): lax.dot_general(left, right, (((0,), (0,)), ((), ())), preferred_element_...  56.1 us
  transfers between devices with their start and end apart: 32, of which 21 were waited for; matrix products, arithmetic and copies ran while one was open for 43% of the time, Pallas kernels for 0%

profile of v7, /device:TPU:0, one launch (start us, length us, event | category | flops | bytes accessed | tf_op | source)
XLA Modules:
  0.0 812.9 jit_solution(8883935733527847198)
XLA Ops:
  21.3 25.1 %collective-permute-done = bf16[256,2048]{1,0:T(8,128)(2,1)S(1)} collective-permute-done((bf16[256,2048]{1,0:T(8,128)(2,1)S(1)}, bf16[256,2048]{1,0:T(8,128)(2,1)S(1)}, u32[]{:S(2)}, u32[]{:S(2)}) %collective-permute-start) | collective-permute-done | bytes 1048608 | tf_op jit(solution)/shard_map/ppermute | solution.py:134
  47.9 24.7 %collective-permute-done.1 = bf16[256,2048]{1,0:T(8,128)(2,1)} collective-permute-done((bf16[256,2048]{1,0:T(8,128)(2,1)S(1)}, bf16[256,2048]{1,0:T(8,128)(2,1)}, u32[]{:S(2)}, u32[]{:S(2)}) %collective-permute-start.1) | collective-permute-done | bytes 1048608 | tf_op jit(solution)/shard_map/ppermute | solution.py:134
  81.6 16.6 %collective-permute-done.2 = bf16[256,2048]{1,0:T(8,128)(2,1)} collective-permute-done((bf16[256,2048]{1,0:T(8,128)(2,1)}, bf16[256,2048]{1,0:T(8,128)(2,1)}, u32[]{:S(2)}, u32[]{:S(2)}) %collective-permute-start.2) | collective-permute-done | bytes 1048608 | tf_op jit(solution)/shard_map/ppermute | solution.py:134
  156.1 19.7 %collective-permute-done.5 = bf16[256,2048]{1,0:T(8,128)(2,1)S(1)} collective-permute-done((bf16[256,2048]{1,0:T(8,128)(2,1)}, bf16[256,2048]{1,0:T(8,128)(2,1)S(1)}, u32[]{:S(2)}, u32[]{:S(2)}) %collective-permute-start.5) | collective-permute-done | bytes 1048608 | tf_op jit(solution)/shard_map/ppermute | solution.py:134
  176.9 22.7 %collective-permute-done.6 = bf16[256,2048]{1,0:T(8,128)(2,1)S(1)} collective-permute-done((bf16[256,2048]{1,0:T(8,128)(2,1)S(1)}, bf16[256,2048]{1,0:T(8,128)(2,1)S(1)}, u32[]{:S(2)}, u32[]{:S(2)}) %collective-permute-start.6) | collective-permute-done | bytes 1048608 | tf_op jit(solution)/shard_map/ppermute | solution.py:162
  207.4 16.6 %collective-permute-done.7 = bf16[256,2048]{1,0:T(8,128)(2,1)} collective-permute-done((bf16[256,2048]{1,0:T(8,128)(2,1)}, bf16[256,2048]{1,0:T(8,128)(2,1)}, u32[]{:S(2)}, u32[]{:S(2)}) %collective-permute-start.7) | collective-permute-done | bytes 1048608 | tf_op jit(solution)/shard_map/ppermute | solution.py:162
  235.6 12.2 %collective-permute-done.8 = bf16[256,2048]{1,0:T(8,128)(2,1)S(1)} collective-permute-done((bf16[256,2048]{1,0:T(8,128)(2,1)S(1)}, bf16[256,2048]{1,0:T(8,128)(2,1)S(1)}, u32[]{:S(2)}, u32[]{:S(2)}) %collective-permute-start.8) | collective-permute-done | bytes 1048608 | tf_op jit(solution)/shard_map/ppermute | solution.py:162
  312.6 11.6 %fusion.79 = bf16[256,2048]{1,0:T(8,128)(2,1)} fusion(bf16[2048,4096]{1,0:T(8,128)(2,1)} %all-gather.9.cloned.1.call-done, bf16[256,2048]{1,0:T(8,128)(2,1)} %copy-done.20, bf16[256,2048]{1,0:T(8,128)(2,1)S(1)} %get-tuple-element.164), kind=kOutput, calls=%fused_computation.165 | convolution fusion | flops 4299161600 | bytes 19922944 | tf_op jit(solution)/shard_map/dot_general | solution.py:29
  325.1 21.9 %collective-permute-done.11 = bf16[256,2048]{1,0:T(8,128)(2,1)} collective-permute-done((bf16[256,2048]{1,0:T(8,128)(2,1)}, bf16[256,2048]{1,0:T(8,128)(2,1)}, u32[]{:S(2)}, u32[]{:S(2)}) %collective-permute-start.11) | collective-permute-done | bytes 1048608 | tf_op jit(solution)/shard_map/ppermute | solution.py:134
  368.1 13.2 %fusion.16 = bf16[2048,2048]{1,0:T(8,128)(2,1)} fusion(bf16[256,2048]{1,0:T(8,128)(2,1)} %get-tuple-element.161, bf16[256,2048]{1,0:T(8,128)(2,1)S(1)} %copy-done.34, bf16[256,2048]{1,0:T(8,128)(2,1)S(1)} %copy-done.32, bf16[256,2048]{1,0:T(8,128)(2,1)S(1)} %copy-done.30, bf16[256,2048]{1,0:T(8,128)(2,1)} %copy-done.56, ...), kind=kOutput, calls=%fused_computation.23 | convolution fusion | flops 8623489024 | bytes 16777216 | tf_op jit(solution)/shard_map/dot_general | solution.py:23
  399.5 12.7 %fusion.77 = f32[256,2048]{1,0:T(8,128)} fusion(bf16[2048,4096]{1,0:T(8,128)(2,1)} %all-gather.9.cloned.1.call-done, bf16[256,2048]{1,0:T(8,128)(2,1)} %get-tuple-element.156, bf16[256,2048]{1,0:T(8,128)(2,1)S(1)} %copy-done.42), kind=kOutput, calls=%fused_computation.163 | convolution fusion | flops 4299161600 | bytes 20971520 | tf_op jit(solution)/shard_map/dot_general | solution.py:29
  419.3 15.6 %collective-permute-done.14 = bf16[256,2048]{1,0:T(8,128)(2,1)} collective-permute-done((bf16[256,2048]{1,0:T(8,128)(2,1)S(1)}, bf16[256,2048]{1,0:T(8,128)(2,1)}, u32[]{:S(2)}, u32[]{:S(2)}) %collective-permute-start.14) | collective-permute-done | bytes 1048608 | tf_op jit(solution)/shard_map/ppermute | solution.py:162
  434.9 26.0 %fusion.4 = bf16[2048,4096]{1,0:T(8,128)(2,1)} fusion(bf16[256,4096]{1,0:T(8,128)(2,1)} %pad_maximum_fusion.4, bf16[256,4096]{1,0:T(8,128)(2,1)} %pad_maximum_fusion.3, bf16[256,4096]{1,0:T(8,128)(2,1)S(1)} %copy-done.24, bf16[256,2048]{1,0:T(8,128)(2,1)} %get-tuple-element.160, bf16[256,2048]{1,0:T(8,128)(2,1)} %get-tuple-element.159, ...), kind=kOutput, calls=%fused_computation.9 | convolution fusion | flops 17238589440 | bytes 29360128 | tf_op jit(solution)/shard_map/dot_general | solution.py:23
  464.2 12.5 %fusion.49 = f32[256,2048]{1,0:T(8,128)} fusion(bf16[2048,4096]{1,0:T(8,128)(2,1)} %all-gather.9.cloned.1.call-done, bf16[256,2048]{1,0:T(8,128)(2,1)} %get-tuple-element.160, bf16[256,2048]{1,0:T(8,128)(2,1)} %get-tuple-element.159), kind=kOutput, calls=%fused_computation.67 | convolution fusion | flops 4299161600 | bytes 20971520 | tf_op jit(solution)/shard_map/dot_general | solution.py:29
  476.7 12.2 %collective-permute-done.17 = bf16[256,2048]{1,0:T(8,128)(2,1)S(1)} collective-permute-done((bf16[256,2048]{1,0:T(8,128)(2,1)}, bf16[256,2048]{1,0:T(8,128)(2,1)S(1)}, u32[]{:S(2)}, u32[]{:S(2)}) %collective-permute-start.17) | collective-permute-done | bytes 1048608 | tf_op jit(solution)/shard_map/ppermute | solution.py:162
  499.6 23.3 %collective-permute-done.18 = bf16[256,2048]{1,0:T(8,128)(2,1)S(1)} collective-permute-done((bf16[256,2048]{1,0:T(8,128)(2,1)S(1)}, bf16[256,2048]{1,0:T(8,128)(2,1)S(1)}, u32[]{:S(2)}, u32[]{:S(2)}) %collective-permute-start.18) | collective-permute-done | bytes 1048608 | tf_op jit(solution)/shard_map/ppermute | solution.py:134
  522.9 18.5 %collective-permute-done.19 = bf16[256,2048]{1,0:T(8,128)(2,1)S(1)} collective-permute-done((bf16[256,2048]{1,0:T(8,128)(2,1)S(1)}, bf16[256,2048]{1,0:T(8,128)(2,1)S(1)}, u32[]{:S(2)}, u32[]{:S(2)}) %collective-permute-start.19) | collective-permute-done | bytes 1048608 | tf_op jit(solution)/shard_map/ppermute | solution.py:134
  546.3 11.6 %collective-permute-done.20 = bf16[256,2048]{1,0:T(8,128)(2,1)S(1)} collective-permute-done((bf16[256,2048]{1,0:T(8,128)(2,1)S(1)}, bf16[256,2048]{1,0:T(8,128)(2,1)S(1)}, u32[]{:S(2)}, u32[]{:S(2)}) %collective-permute-start.20) | collective-permute-done | bytes 1048608 | tf_op jit(solution)/shard_map/ppermute | solution.py:134
  572.1 15.3 %multiply_reduce_fusion = (f32[4,1024]{1,0:T(4,128)}, f32[4,1024,1024]{1,2,0:T(8,128)}) fusion(f32[4,1024,1024]{1,2,0:T(8,128)} %get-tuple-element.196, f32[4,1024]{1,0:T(4,128)} %bitcast.103, bf16[1024,4,128]{0,2,1:T(8,128)(2,1)} %bitcast.95, bf16[1,1024,4,128]{3,2,1,0:T(4,128)(2,1)S(1)} %copy-done.14), kind=kOutput, calls=%fused_computation.1 | convolution fusion | flops 1086320640 | bytes 35684352 | tf_op jit(solution)/shard_map/while/body/eval_jaxpr/qhd,khd->hqk/dot_general | solution.py:307
  611.0 11.1 %convolution_convert_fusion = bf16[2048,1536]{1,0:T(8,128)(2,1)} fusion(bf16[1024,2048]{1,0:T(8,128)(2,1)} %constant_dynamic-update-slice_fusion.4, bf16[1024,512]{0,1:T(8,128)(2,1)} %bitcast.101, bf16[1024,512]{0,1:T(8,128)(2,1)} %bitcast.99, bf16[1024,512]{0,1:T(8,128)(2,1)} %bitcast.97), kind=kOutput, calls=%fused_computation.22 | convolution fusion | flops 6455033856 | bytes 13631488 | tf_op jit(solution)/shard_map/dot_general | solution.py:23
  633.6 23.8 %collective-permute-done.21 = bf16[256,2048]{1,0:T(8,128)(2,1)S(1)} collective-permute-done((bf16[256,2048]{1,0:T(8,128)(2,1)S(1)}, bf16[256,2048]{1,0:T(8,128)(2,1)S(1)}, u32[]{:S(2)}, u32[]{:S(2)}) %collective-permute-start.21) | collective-permute-done | bytes 1048608 | tf_op jit(solution)/shard_map/ppermute | solution.py:162
  657.8 16.6 %collective-permute-done.22 = bf16[256,2048]{1,0:T(8,128)(2,1)S(1)} collective-permute-done((bf16[256,2048]{1,0:T(8,128)(2,1)S(1)}, bf16[256,2048]{1,0:T(8,128)(2,1)S(1)}, u32[]{:S(2)}, u32[]{:S(2)}) %collective-permute-start.22) | collective-permute-done | bytes 1048608 | tf_op jit(solution)/shard_map/ppermute | solution.py:162
  676.5 14.8 %collective-permute-done.23 = bf16[256,2048]{1,0:T(8,128)(2,1)S(1)} collective-permute-done((bf16[256,2048]{1,0:T(8,128)(2,1)S(1)}, bf16[256,2048]{1,0:T(8,128)(2,1)S(1)}, u32[]{:S(2)}, u32[]{:S(2)}) %collective-permute-start.23) | collective-permute-done | bytes 1048608 | tf_op jit(solution)/shard_map/ppermute | solution.py:162
  700.2 101.6 %reduce-scatter.11.cloned.1.call-done = bf16[256,4096]{1,0:T(8,128)(2,1)} async-done(((bf16[2048,4096]{1,0:T(8,128)(2,1)}), bf16[256,4096]{1,0:T(8,128)(2,1)}) %reduce-scatter.11.cloned.1.call-update) | async-done | bytes 2097168 | tf_op jit(solution)/shard_map/reduce_scatter | solution.py:222
  (297 shorter events, 297.8 us)
Async XLA Ops:
  7.2 93.4 %all-gather.5.cloned.1.call-start = ((), (), s32[]{:S(2)}) async-start(), calls=%async_computation.4 | async-start | bytes 7077888 | tf_op jit(solution)/shard_map/all_gather | solution.py:217
  9.4 142.3 %all-gather.7.cloned.1.call-start = ((), (), s32[]{:S(2)}) async-start(), calls=%async_computation.5 | async-start | bytes 2359296 | tf_op jit(solution)/shard_map/all_gather | solution.py:217
  10.2 190.7 %all-gather.11.cloned.1.call-start = ((), (), s32[]{:S(2)}) async-start(), calls=%async_computation.7 | async-start | bytes 9437184 | tf_op jit(solution)/shard_map/all_gather | solution.py:217
  10.9 239.1 %all-gather.9.cloned.1.call-start = ((), (), s32[]{:S(2)}) async-start(), calls=%async_computation.6 | async-start | bytes 18874368 | tf_op jit(solution)/shard_map/all_gather | solution.py:217
  12.5 531.1 %reduce-scatter.5.cloned.1.call-start = ((), (), s32[]{:S(2)}) async-start(), calls=%async_computation.8 | async-start | bytes 9437184 | tf_op jit(solution)/shard_map/reduce_scatter | solution.py:222
  18.2 28.2 %collective-permute-start = (bf16[256,2048]{1,0:T(8,128)(2,1)S(1)}, bf16[256,2048]{1,0:T(8,128)(2,1)S(1)}, u32[]{:S(2)}, u32[]{:S(2)}) collective-permute-start(bf16[256,2048]{1,0:T(8,128)(2,1)S(1)} %get-tuple-element.154), channel_id=1, source_target_pairs={{0,8},{8,16},{16,24},{24,0},{1,9},{9,17},{17,25},{25,1},{2,10},{10... | collective-permute-start | bytes 3145736 | tf_op jit(solution)/shard_map/ppermute | solution.py:134
  46.4 26.2 %collective-permute-start.1 = (bf16[256,2048]{1,0:T(8,128)(2,1)S(1)}, bf16[256,2048]{1,0:T(8,128)(2,1)}, u32[]{:S(2)}, u32[]{:S(2)}) collective-permute-start(bf16[256,2048]{1,0:T(8,128)(2,1)S(1)} %collective-permute-done), channel_id=1, source_target_pairs={{0,8},{8,16},{16,24},{24,0},{1,9},{9,17},{17,25},{25,1},{2,10},{10... | collective-permute-start | bytes 3145736 | tf_op jit(solution)/shard_map/ppermute | solution.py:134
  72.6 25.6 %collective-permute-start.2 = (bf16[256,2048]{1,0:T(8,128)(2,1)}, bf16[256,2048]{1,0:T(8,128)(2,1)}, u32[]{:S(2)}, u32[]{:S(2)}) collective-permute-start(bf16[256,2048]{1,0:T(8,128)(2,1)} %collective-permute-done.1), channel_id=1, source_target_pairs={{0,8},{8,16},{16,24},{24,0},{1,9},{9,17},{17,25},{25,1},{2,10},{10... | collective-permute-start | bytes 3145736 | tf_op jit(solution)/shard_map/ppermute | solution.py:134
  100.6 24.6 %collective-permute-start.3 = (bf16[256,2048]{1,0:T(8,128)(2,1)}, bf16[256,2048]{1,0:T(8,128)(2,1)}, u32[]{:S(2)}, u32[]{:S(2)}) collective-permute-start(bf16[256,2048]{1,0:T(8,128)(2,1)} %param.19), channel_id=1, source_target_pairs={{0,8},{8,16},{16,24},{24,0},{1,9},{9,17},{17,25},{25,1},{2,10},{10... | collective-permute-start | bytes 3145736 | tf_op jit(solution)/shard_map/ppermute | solution.py:134
  125.3 25.6 %collective-permute-start.4 = (bf16[256,2048]{1,0:T(8,128)(2,1)}, bf16[256,2048]{1,0:T(8,128)(2,1)}, u32[]{:S(2)}, u32[]{:S(2)}) collective-permute-start(bf16[256,2048]{1,0:T(8,128)(2,1)} %collective-permute-done.3), channel_id=1, source_target_pairs={{0,8},{8,16},{16,24},{24,0},{1,9},{9,17},{17,25},{25,1},{2,10},{10... | collective-permute-start | bytes 3145736 | tf_op jit(solution)/shard_map/ppermute | solution.py:134
  150.8 24.9 %collective-permute-start.5 = (bf16[256,2048]{1,0:T(8,128)(2,1)}, bf16[256,2048]{1,0:T(8,128)(2,1)S(1)}, u32[]{:S(2)}, u32[]{:S(2)}) collective-permute-start(bf16[256,2048]{1,0:T(8,128)(2,1)} %collective-permute-done.4), channel_id=1, source_target_pairs={{0,8},{8,16},{16,24},{24,0},{1,9},{9,17},{17,25},{25,1},{2,10},{10... | collective-permute-start | bytes 3145736 | tf_op jit(solution)/shard_map/ppermute | solution.py:134
  175.9 23.7 %collective-permute-start.6 = (bf16[256,2048]{1,0:T(8,128)(2,1)S(1)}, bf16[256,2048]{1,0:T(8,128)(2,1)S(1)}, u32[]{:S(2)}, u32[]{:S(2)}) collective-permute-start(bf16[256,2048]{1,0:T(8,128)(2,1)S(1)} %dynamic-slice_convert_fusion.1), channel_id=1, source_target_pairs={{0,8},{8,16},{16,24},{24,0},{1,9},{9,17},{17,25},{25,1},{2,10},{10... | collective-permute-start | bytes 3145736 | tf_op jit(solution)/shard_map/ppermute | solution.py:162
  272.7 23.7 %collective-permute-start.10 = (bf16[256,2048]{1,0:T(8,128)(2,1)}, bf16[256,2048]{1,0:T(8,128)(2,1)}, u32[]{:S(2)}, u32[]{:S(2)}) collective-permute-start(bf16[256,2048]{1,0:T(8,128)(2,1)} %collective-permute-done.9), channel_id=1, source_target_pairs={{0,8},{8,16},{16,24},{24,0},{1,9},{9,17},{17,25},{25,1},{2,10},{10... | collective-permute-start | bytes 3145736 | tf_op jit(solution)/shard_map/ppermute | solution.py:134
  296.4 28.1 %collective-permute-start.12 = (bf16[256,2048]{1,0:T(8,128)(2,1)}, bf16[256,2048]{1,0:T(8,128)(2,1)}, u32[]{:S(2)}, u32[]{:S(2)}) collective-permute-start(bf16[256,2048]{1,0:T(8,128)(2,1)} %fusion.91), channel_id=1, source_target_pairs={{0,8},{8,16},{16,24},{24,0},{1,9},{9,17},{17,25},{25,1},{2,10},{10... | collective-permute-start | bytes 3145736 | tf_op jit(solution)/shard_map/ppermute | solution.py:162
  296.4 50.6 %collective-permute-start.11 = (bf16[256,2048]{1,0:T(8,128)(2,1)}, bf16[256,2048]{1,0:T(8,128)(2,1)}, u32[]{:S(2)}, u32[]{:S(2)}) collective-permute-start(bf16[256,2048]{1,0:T(8,128)(2,1)} %collective-permute-done.10), channel_id=1, source_target_pairs={{0,8},{8,16},{16,24},{24,0},{1,9},{9,17},{17,25},{25,1},{2,10},{10... | collective-permute-start | bytes 3145736 | tf_op jit(solution)/shard_map/ppermute | solution.py:134
  324.5 73.7 %collective-permute-start.15 = (bf16[256,2048]{1,0:T(8,128)(2,1)}, bf16[256,2048]{1,0:T(8,128)(2,1)}, u32[]{:S(2)}, u32[]{:S(2)}) collective-permute-start(bf16[256,2048]{1,0:T(8,128)(2,1)} %fusion.79), channel_id=1, source_target_pairs={{0,8},{8,16},{16,24},{24,0},{1,9},{9,17},{17,25},{25,1},{2,10},{10... | collective-permute-start | bytes 3145736 | tf_op jit(solution)/shard_map/ppermute | solution.py:162
  350.3 61.9 %collective-permute-start.13 = (bf16[256,2048]{1,0:T(8,128)(2,1)}, bf16[256,2048]{1,0:T(8,128)(2,1)}, u32[]{:S(2)}, u32[]{:S(2)}) collective-permute-start(bf16[256,2048]{1,0:T(8,128)(2,1)} %add_convert_fusion.6), channel_id=1, source_target_pairs={{0,8},{8,16},{16,24},{24,0},{1,9},{9,17},{17,25},{25,1},{2,10},{10... | collective-permute-start | bytes 3145736 | tf_op jit(solution)/shard_map/ppermute | solution.py:162
  398.3 276.5 %reduce-scatter.9.cloned.1.call-start = ((), (), s32[]{:S(2)}) async-start(), calls=%async_computation.10 | async-start | bytes 2359296 | tf_op jit(solution)/shard_map/reduce_scatter | solution.py:222
  419.3 41.6 %collective-permute-start.16 = (bf16[256,2048]{1,0:T(8,128)(2,1)}, bf16[256,2048]{1,0:T(8,128)(2,1)}, u32[]{:S(2)}, u32[]{:S(2)}) collective-permute-start(bf16[256,2048]{1,0:T(8,128)(2,1)} %add_convert_fusion.3), channel_id=1, source_target_pairs={{0,8},{8,16},{16,24},{24,0},{1,9},{9,17},{17,25},{25,1},{2,10},{10... | collective-permute-start | bytes 3145736 | tf_op jit(solution)/shard_map/ppermute | solution.py:162
  464.0 25.0 %collective-permute-start.17 = (bf16[256,2048]{1,0:T(8,128)(2,1)}, bf16[256,2048]{1,0:T(8,128)(2,1)S(1)}, u32[]{:S(2)}, u32[]{:S(2)}) collective-permute-start(bf16[256,2048]{1,0:T(8,128)(2,1)} %add_convert_fusion.2), channel_id=1, source_target_pairs={{0,8},{8,16},{16,24},{24,0},{1,9},{9,17},{17,25},{25,1},{2,10},{10... | collective-permute-start | bytes 3145736 | tf_op jit(solution)/shard_map/ppermute | solution.py:162
  499.6 23.3 %collective-permute-start.18 = (bf16[256,2048]{1,0:T(8,128)(2,1)S(1)}, bf16[256,2048]{1,0:T(8,128)(2,1)S(1)}, u32[]{:S(2)}, u32[]{:S(2)}) collective-permute-start(bf16[256,2048]{1,0:T(8,128)(2,1)S(1)} %get-tuple-element.149), channel_id=1, source_target_pairs={{0,8},{8,16},{16,24},{24,0},{1,9},{9,17},{17,25},{25,1},{2,10},{10... | collective-permute-start | bytes 3145736 | tf_op jit(solution)/shard_map/ppermute | solution.py:134
  564.9 132.8 %reduce-scatter.7.cloned.1.call-start = ((), (), s32[]{:S(2)}) async-start(), calls=%async_computation.9 | async-start | bytes 7077888 | tf_op jit(solution)/shard_map/reduce_scatter | solution.py:222
  622.2 179.6 %reduce-scatter.11.cloned.1.call-start = ((), (), s32[]{:S(2)}) async-start(), calls=%async_computation.11 | async-start | bytes 18874368 | tf_op jit(solution)/shard_map/reduce_scatter | solution.py:222
  633.5 23.8 %collective-permute-start.21 = (bf16[256,2048]{1,0:T(8,128)(2,1)S(1)}, bf16[256,2048]{1,0:T(8,128)(2,1)S(1)}, u32[]{:S(2)}, u32[]{:S(2)}) collective-permute-start(bf16[256,2048]{1,0:T(8,128)(2,1)S(1)} %dynamic-slice_convert_fusion), channel_id=1, source_target_pairs={{0,8},{8,16},{16,24},{24,0},{1,9},{9,17},{17,25},{25,1},{2,10},{10... | collective-permute-start | bytes 3145736 | tf_op jit(solution)/shard_map/ppermute | solution.py:162
  (80 other events, 997.8 us)
Sparse Core Ops, SparseCore 0:
  10.5 48.1 all-gather.4
  60.5 28.0 all-gather.6
  90.5 55.8 all-gather.10
  148.7 89.7 all-gather.8
  398.4 72.4 reduce-scatter.4
  565.0 39.1 reduce-scatter.8
  622.3 59.7 reduce-scatter.6
  685.6 116.1 reduce-scatter.10

commit v8 on v7

--- a/solution.py
+++ b/solution.py
@@ -404,7 +404,16 @@
         return piece
 
     order = list(range(1, slots)) + [0]
-    bwd = overlap(ffn_ring, [ffn_backward(slot) for slot in order])
+
+    def first_backward(done):
+        grad_down_w = contract_rows(
+            jnp.concatenate(act_slots, axis=0), jnp.concatenate(cot_slots, axis=0)
+        )
+        return (ffn_backward(order[0])(done), grad_down_w)
+
+    bwd = overlap(ffn_ring, [first_backward] + [ffn_backward(slot) for slot in order[1:]])
+    grad_down_w = bwd[0][1]
+    bwd = (bwd[0][0],) + bwd[1:]
     ffn_sum = ffn_ring.result()
     output = (middle + ffn_sum).astype(jnp.bfloat16)
     by_slot = dict(zip(order, bwd))
@@ -412,13 +421,10 @@
     second_ring_back = RingScatter([by_slot[slot][1] for slot in range(slots)], "row", jnp.bfloat16)
     rows_second = jnp.concatenate(second_slots, axis=0)
 
-    def down_weight_grad(_):
-        return contract_rows(jnp.concatenate(act_slots, axis=0), jnp.concatenate(cot_slots, axis=0))
-
     def gate_up_weight_grad(_):
         return contract_rows(rows_second, grad_gu)
 
-    grad_down_w, grad_gu_w = overlap(second_ring_back, [down_weight_grad, gate_up_weight_grad])
+    (grad_gu_w,) = overlap(second_ring_back, [gate_up_weight_grad])
     grad_second = second_ring_back.result()
     down_sum = col_scatter(grad_down_w, 1)
     gu_sum = col_scatter(grad_gu_w, 0)
@@ -427,7 +433,7 @@
     steps = branch_chain.steps()
     down_sum = overlap(branch_chain, [lambda done: ()] * (steps - 1) + [lambda done: down_sum])[-1]
     grad_branch = branch_chain.result()
-    output_sum = col_scatter(contract_rows(attended, grad_branch), 1)
+    grad_output_t = contract_rows(grad_branch, attended)
     grad_mixed = split_heads(times_transpose(grad_branch, full_output).astype(jnp.bfloat16))
     grad_q_rot, grad_k_rot, grad_values = lax.map(
         attend_backward, (queries, keys_rot, values, piece_starts, log_total, grad_mixed)
@@ -440,7 +446,11 @@
         ],
         axis=1,
     ).astype(jnp.bfloat16)
-    qkv_sum = col_scatter(contract_rows(first_rows, grad_qkv), 0)
+    attn_sum = col_scatter(
+        jnp.concatenate([contract_rows(first_rows, grad_qkv), grad_output_t], axis=1), 0
+    )
+    qkv_sum = attn_sum[:, : 3 * width]
+    output_sum = attn_sum[:, 3 * width :].T
     grad_first = ring_reduce_scatter(times_transpose(grad_qkv, full_qkv), "row", jnp.bfloat16)
     grad_input = grad_middle + norm_back(inputs, grad_first)
     return (

time: 822 us -> 858 us (1.044)
  waiting for transfers between devices: 413 us -> 446 us
    ppermute x12, waiting for transfers between devices: 135 us -> 171 us  [send(): lax.ppermute(value.astype(self.send_dtype), self.axis, [(j, (j + 1) % n)...]
    reduce_scatter x4 -> x3, waiting for transfers between devices: 102 us -> 98 us  [col_scatter(): lax.psum_scatter(low_part, COL, scatter_dimension=axis, tiled=True)]
  transfers between devices with their start and end apart: 32 -> 31, of which waited for: 21 -> 21; matrix products, arithmetic and copies ran while one was open for 43% -> 35% of each run, Pallas kernels for 0% -> 0%
where the time goes in v8:
time: 858 us; the launch traced here: 850 us
  waiting for transfers between devices  446 us (52%)
  matrix products  255 us (30%)
  other arithmetic  80.5 us (9%)
  local copies, waits for them, and re-layouts  46.5 us (5%)
  between operations  15.6 us (2%)
    ppermute x12, waiting for transfers between devices, send(): lax.ppermute(self.pending, self.axis, [(j, (j + 1) % n) for j in range(n)])  174 us
    ppermute x12, waiting for transfers between devices, send(): lax.ppermute(value.astype(self.send_dtype), self.axis, [(j, (j + 1) % n)...  171 us
    reduce_scatter x3, waiting for transfers between devices, col_scatter(): lax.psum_scatter(low_part, COL, scatter_dimension=axis, tiled=True)  98 us
    dot_general x10, matrix products, times_transpose(): lax.dot_general(left, right, (((1,), (1,)), ((), ())), preferred_element_...  86.2 us
    dot_general x10, matrix products, product(): return jnp.dot(left, right, preferred_element_type=jnp.float32)  69.9 us
    dot_general x4, matrix products, contract_rows(): lax.dot_general(left, right, (((0,), (0,)), ((), ())), preferred_element_...  57.3 us
  transfers between devices with their start and end apart: 31, of which 21 were waited for; matrix products, arithmetic and copies ran while one was open for 35% of the time, Pallas kernels for 0%

profile of v8, /device:TPU:0, one launch (start us, length us, event | category | flops | bytes accessed | tf_op | source)
XLA Modules:
  0.0 849.8 jit_solution(4815125137896074348)
XLA Ops:
  21.3 25.1 %collective-permute-done = bf16[256,2048]{1,0:T(8,128)(2,1)S(1)} collective-permute-done((bf16[256,2048]{1,0:T(8,128)(2,1)S(1)}, bf16[256,2048]{1,0:T(8,128)(2,1)S(1)}, u32[]{:S(2)}, u32[]{:S(2)}) %collective-permute-start) | collective-permute-done | bytes 1048608 | tf_op jit(solution)/shard_map/ppermute | solution.py:134
  47.9 24.7 %collective-permute-done.1 = bf16[256,2048]{1,0:T(8,128)(2,1)} collective-permute-done((bf16[256,2048]{1,0:T(8,128)(2,1)S(1)}, bf16[256,2048]{1,0:T(8,128)(2,1)}, u32[]{:S(2)}, u32[]{:S(2)}) %collective-permute-start.1) | collective-permute-done | bytes 1048608 | tf_op jit(solution)/shard_map/ppermute | solution.py:134
  81.6 16.6 %collective-permute-done.2 = bf16[256,2048]{1,0:T(8,128)(2,1)} collective-permute-done((bf16[256,2048]{1,0:T(8,128)(2,1)}, bf16[256,2048]{1,0:T(8,128)(2,1)}, u32[]{:S(2)}, u32[]{:S(2)}) %collective-permute-start.2) | collective-permute-done | bytes 1048608 | tf_op jit(solution)/shard_map/ppermute | solution.py:134
  156.3 19.8 %collective-permute-done.5 = bf16[256,2048]{1,0:T(8,128)(2,1)S(1)} collective-permute-done((bf16[256,2048]{1,0:T(8,128)(2,1)}, bf16[256,2048]{1,0:T(8,128)(2,1)S(1)}, u32[]{:S(2)}, u32[]{:S(2)}) %collective-permute-start.5) | collective-permute-done | bytes 1048608 | tf_op jit(solution)/shard_map/ppermute | solution.py:134
  177.0 23.0 %collective-permute-done.6 = bf16[256,2048]{1,0:T(8,128)(2,1)S(1)} collective-permute-done((bf16[256,2048]{1,0:T(8,128)(2,1)S(1)}, bf16[256,2048]{1,0:T(8,128)(2,1)S(1)}, u32[]{:S(2)}, u32[]{:S(2)}) %collective-permute-start.6) | collective-permute-done | bytes 1048608 | tf_op jit(solution)/shard_map/ppermute | solution.py:162
  207.7 16.6 %collective-permute-done.7 = bf16[256,2048]{1,0:T(8,128)(2,1)} collective-permute-done((bf16[256,2048]{1,0:T(8,128)(2,1)}, bf16[256,2048]{1,0:T(8,128)(2,1)}, u32[]{:S(2)}, u32[]{:S(2)}) %collective-permute-start.7) | collective-permute-done | bytes 1048608 | tf_op jit(solution)/shard_map/ppermute | solution.py:162
  236.1 12.1 %collective-permute-done.8 = bf16[256,2048]{1,0:T(8,128)(2,1)S(1)} collective-permute-done((bf16[256,2048]{1,0:T(8,128)(2,1)S(1)}, bf16[256,2048]{1,0:T(8,128)(2,1)S(1)}, u32[]{:S(2)}, u32[]{:S(2)}) %collective-permute-start.8) | collective-permute-done | bytes 1048608 | tf_op jit(solution)/shard_map/ppermute | solution.py:162
  313.2 11.6 %fusion.79 = bf16[256,2048]{1,0:T(8,128)(2,1)} fusion(bf16[2048,4096]{1,0:T(8,128)(2,1)} %all-gather.9.cloned.1.call-done, bf16[256,2048]{1,0:T(8,128)(2,1)} %copy-done.18, bf16[256,2048]{1,0:T(8,128)(2,1)S(1)} %get-tuple-element.180), kind=kOutput, calls=%fused_computation.167 | convolution fusion | flops 4299161600 | bytes 19922944 | tf_op jit(solution)/shard_map/dot_general | solution.py:29
  324.7 14.1 %collective-permute-done.11 = bf16[256,2048]{1,0:T(8,128)(2,1)} collective-permute-done((bf16[256,2048]{1,0:T(8,128)(2,1)}, bf16[256,2048]{1,0:T(8,128)(2,1)}, u32[]{:S(2)}, u32[]{:S(2)}) %collective-permute-start.11) | collective-permute-done | bytes 1048608 | tf_op jit(solution)/shard_map/ppermute | solution.py:134
  356.6 12.6 %fusion.16 = bf16[2048,2048]{1,0:T(8,128)(2,1)} fusion(bf16[256,2048]{1,0:T(8,128)(2,1)S(1)} %get-tuple-element.177, bf16[256,2048]{1,0:T(8,128)(2,1)S(1)} %copy-done.32, bf16[256,2048]{1,0:T(8,128)(2,1)S(1)} %copy-done.30, bf16[256,2048]{1,0:T(8,128)(2,1)S(1)} %copy-done.27, bf16[256,2048]{1,0:T(8,128)(2,1)S(1)} %copy-done.55, ...), kind=kOutput, calls=%fused_computation.24 | convolution fusion | flops 8623489024 | bytes 16777216 | tf_op jit(solution)/shard_map/dot_general | solution.py:23
  387.2 10.1 %fusion.78 = f32[256,2048]{1,0:T(8,128)} fusion(bf16[2048,4096]{1,0:T(8,128)(2,1)} %all-gather.9.cloned.1.call-done, bf16[256,2048]{1,0:T(8,128)(2,1)S(1)} %copy-done.17, bf16[256,2048]{1,0:T(8,128)(2,1)S(1)} %get-tuple-element.178), kind=kOutput, calls=%fused_computation.166 | convolution fusion | flops 4299161600 | bytes 20971520 | tf_op jit(solution)/shard_map/dot_general | solution.py:29
  404.5 12.9 %fusion.77 = f32[256,2048]{1,0:T(8,128)} fusion(bf16[2048,4096]{1,0:T(8,128)(2,1)} %all-gather.9.cloned.1.call-done, bf16[256,2048]{1,0:T(8,128)(2,1)} %get-tuple-element.172, bf16[256,2048]{1,0:T(8,128)(2,1)} %get-tuple-element.171), kind=kOutput, calls=%fused_computation.165 | convolution fusion | flops 4299161600 | bytes 20971520 | tf_op jit(solution)/shard_map/dot_general | solution.py:29
  417.4 18.8 %collective-permute-done.14 = bf16[256,2048]{1,0:T(8,128)(2,1)S(1)} collective-permute-done((bf16[256,2048]{1,0:T(8,128)(2,1)}, bf16[256,2048]{1,0:T(8,128)(2,1)S(1)}, u32[]{:S(2)}, u32[]{:S(2)}) %collective-permute-start.14) | collective-permute-done | bytes 1048608 | tf_op jit(solution)/shard_map/ppermute | solution.py:162
  436.2 26.5 %fusion.4 = bf16[2048,4096]{1,0:T(8,128)(2,1)} fusion(bf16[256,4096]{1,0:T(8,128)(2,1)} %pad_maximum_fusion.5, bf16[256,4096]{1,0:T(8,128)(2,1)} %pad_maximum_fusion.4, bf16[256,4096]{1,0:T(8,128)(2,1)S(1)} %copy-done.22, bf16[256,2048]{1,0:T(8,128)(2,1)} %get-tuple-element.176, bf16[256,2048]{1,0:T(8,128)(2,1)} %get-tuple-element.175, ...), kind=kOutput, calls=%fused_computation.9 | convolution fusion | flops 17238589440 | bytes 29360128 | tf_op jit(solution)/shard_map/dot_general | solution.py:23
  465.1 21.7 %collective-permute-done.16 = bf16[256,2048]{1,0:T(8,128)(2,1)S(1)} collective-permute-done((bf16[256,2048]{1,0:T(8,128)(2,1)S(1)}, bf16[256,2048]{1,0:T(8,128)(2,1)S(1)}, u32[]{:S(2)}, u32[]{:S(2)}) %collective-permute-start.16) | collective-permute-done | bytes 1048608 | tf_op jit(solution)/shard_map/ppermute | solution.py:162
  488.2 12.4 %fusion.49 = f32[256,2048]{1,0:T(8,128)} fusion(bf16[2048,4096]{1,0:T(8,128)(2,1)} %all-gather.9.cloned.1.call-done, bf16[256,2048]{1,0:T(8,128)(2,1)} %get-tuple-element.176, bf16[256,2048]{1,0:T(8,128)(2,1)} %get-tuple-element.175), kind=kOutput, calls=%fused_computation.68 | convolution fusion | flops 4299161600 | bytes 20971520 | tf_op jit(solution)/shard_map/dot_general | solution.py:29
  515.8 24.2 %collective-permute-done.18 = bf16[256,2048]{1,0:T(8,128)(2,1)S(1)} collective-permute-done((bf16[256,2048]{1,0:T(8,128)(2,1)S(1)}, bf16[256,2048]{1,0:T(8,128)(2,1)S(1)}, u32[]{:S(2)}, u32[]{:S(2)}) %collective-permute-start.18) | collective-permute-done | bytes 1048608 | tf_op jit(solution)/shard_map/ppermute | solution.py:134
  540.1 25.4 %collective-permute-done.19 = bf16[256,2048]{1,0:T(8,128)(2,1)S(1)} collective-permute-done((bf16[256,2048]{1,0:T(8,128)(2,1)S(1)}, bf16[256,2048]{1,0:T(8,128)(2,1)S(1)}, u32[]{:S(2)}, u32[]{:S(2)}) %collective-permute-start.19) | collective-permute-done | bytes 1048608 | tf_op jit(solution)/shard_map/ppermute | solution.py:134
  570.4 11.7 %collective-permute-done.20 = bf16[256,2048]{1,0:T(8,128)(2,1)S(1)} collective-permute-done((bf16[256,2048]{1,0:T(8,128)(2,1)S(1)}, bf16[256,2048]{1,0:T(8,128)(2,1)S(1)}, u32[]{:S(2)}, u32[]{:S(2)}) %collective-permute-start.20) | collective-permute-done | bytes 1048608 | tf_op jit(solution)/shard_map/ppermute | solution.py:134
  628.1 13.7 %convolution_convert_fusion = bf16[2048,1536]{0,1:T(8,128)(2,1)} fusion(bf16[1024,2048]{1,0:T(8,128)(2,1)} %constant_dynamic-update-slice_fusion.4, bf16[1024,512]{0,1:T(8,128)(2,1)S(1)} %bitcast.103, bf16[1024,512]{0,1:T(8,128)(2,1)S(1)} %bitcast.101, bf16[1024,512]{0,1:T(8,128)(2,1)S(1)} %bitcast.99), kind=kOutput, calls=%fused_computation.23 | convolution fusion | flops 6455033856 | bytes 13631488 | tf_op jit(solution)/shard_map/dot_general | solution.py:23
  660.4 27.5 %collective-permute-done.21 = bf16[256,2048]{1,0:T(8,128)(2,1)S(1)} collective-permute-done((bf16[256,2048]{1,0:T(8,128)(2,1)S(1)}, bf16[256,2048]{1,0:T(8,128)(2,1)S(1)}, u32[]{:S(2)}, u32[]{:S(2)}) %collective-permute-start.21) | collective-permute-done | bytes 1048608 | tf_op jit(solution)/shard_map/ppermute | solution.py:162
  688.3 27.0 %collective-permute-done.22 = bf16[256,2048]{1,0:T(8,128)(2,1)S(1)} collective-permute-done((bf16[256,2048]{1,0:T(8,128)(2,1)S(1)}, bf16[256,2048]{1,0:T(8,128)(2,1)S(1)}, u32[]{:S(2)}, u32[]{:S(2)}) %collective-permute-start.22) | collective-permute-done | bytes 1048608 | tf_op jit(solution)/shard_map/ppermute | solution.py:162
  715.7 16.6 %collective-permute-done.23 = bf16[256,2048]{1,0:T(8,128)(2,1)S(1)} collective-permute-done((bf16[256,2048]{1,0:T(8,128)(2,1)S(1)}, bf16[256,2048]{1,0:T(8,128)(2,1)S(1)}, u32[]{:S(2)}, u32[]{:S(2)}) %collective-permute-start.23) | collective-permute-done | bytes 1048608 | tf_op jit(solution)/shard_map/ppermute | solution.py:162
  740.5 98.0 %reduce-scatter.8.cloned.1.call-done = bf16[256,4096]{1,0:T(8,128)(2,1)} async-done(((bf16[2048,4096]{1,0:T(8,128)(2,1)}), bf16[256,4096]{1,0:T(8,128)(2,1)}) %reduce-scatter.8.cloned.1.call-update) | async-done | bytes 2097168 | tf_op jit(solution)/shard_map/reduce_scatter | solution.py:222
  (292 shorter events, 311.8 us)
Async XLA Ops:
  7.2 93.4 %all-gather.5.cloned.1.call-start = ((), (), s32[]{:S(2)}) async-start(), calls=%async_computation.3 | async-start | bytes 7077888 | tf_op jit(solution)/shard_map/all_gather | solution.py:217
  9.4 142.5 %all-gather.7.cloned.1.call-start = ((), (), s32[]{:S(2)}) async-start(), calls=%async_computation.4 | async-start | bytes 2359296 | tf_op jit(solution)/shard_map/all_gather | solution.py:217
  10.2 191.1 %all-gather.11.cloned.1.call-start = ((), (), s32[]{:S(2)}) async-start(), calls=%async_computation.6 | async-start | bytes 9437184 | tf_op jit(solution)/shard_map/all_gather | solution.py:217
  10.9 239.4 %all-gather.9.cloned.1.call-start = ((), (), s32[]{:S(2)}) async-start(), calls=%async_computation.5 | async-start | bytes 18874368 | tf_op jit(solution)/shard_map/all_gather | solution.py:217
  12.5 555.0 %reduce-scatter.4.cloned.1.call-start = ((), (), s32[]{:S(2)}) async-start(), calls=%async_computation.7 | async-start | bytes 9437184 | tf_op jit(solution)/shard_map/reduce_scatter | solution.py:222
  18.2 28.2 %collective-permute-start = (bf16[256,2048]{1,0:T(8,128)(2,1)S(1)}, bf16[256,2048]{1,0:T(8,128)(2,1)S(1)}, u32[]{:S(2)}, u32[]{:S(2)}) collective-permute-start(bf16[256,2048]{1,0:T(8,128)(2,1)S(1)} %get-tuple-element.170), channel_id=1, source_target_pairs={{0,8},{8,16},{16,24},{24,0},{1,9},{9,17},{17,25},{25,1},{2,10},{10... | collective-permute-start | bytes 3145736 | tf_op jit(solution)/shard_map/ppermute | solution.py:134
  46.4 26.2 %collective-permute-start.1 = (bf16[256,2048]{1,0:T(8,128)(2,1)S(1)}, bf16[256,2048]{1,0:T(8,128)(2,1)}, u32[]{:S(2)}, u32[]{:S(2)}) collective-permute-start(bf16[256,2048]{1,0:T(8,128)(2,1)S(1)} %collective-permute-done), channel_id=1, source_target_pairs={{0,8},{8,16},{16,24},{24,0},{1,9},{9,17},{17,25},{25,1},{2,10},{10... | collective-permute-start | bytes 3145736 | tf_op jit(solution)/shard_map/ppermute | solution.py:134
  72.6 25.6 %collective-permute-start.2 = (bf16[256,2048]{1,0:T(8,128)(2,1)}, bf16[256,2048]{1,0:T(8,128)(2,1)}, u32[]{:S(2)}, u32[]{:S(2)}) collective-permute-start(bf16[256,2048]{1,0:T(8,128)(2,1)} %collective-permute-done.1), channel_id=1, source_target_pairs={{0,8},{8,16},{16,24},{24,0},{1,9},{9,17},{17,25},{25,1},{2,10},{10... | collective-permute-start | bytes 3145736 | tf_op jit(solution)/shard_map/ppermute | solution.py:134
  100.6 24.6 %collective-permute-start.3 = (bf16[256,2048]{1,0:T(8,128)(2,1)}, bf16[256,2048]{1,0:T(8,128)(2,1)}, u32[]{:S(2)}, u32[]{:S(2)}) collective-permute-start(bf16[256,2048]{1,0:T(8,128)(2,1)} %param.19), channel_id=1, source_target_pairs={{0,8},{8,16},{16,24},{24,0},{1,9},{9,17},{17,25},{25,1},{2,10},{10... | collective-permute-start | bytes 3145736 | tf_op jit(solution)/shard_map/ppermute | solution.py:134
  125.3 26.0 %collective-permute-start.4 = (bf16[256,2048]{1,0:T(8,128)(2,1)}, bf16[256,2048]{1,0:T(8,128)(2,1)}, u32[]{:S(2)}, u32[]{:S(2)}) collective-permute-start(bf16[256,2048]{1,0:T(8,128)(2,1)} %collective-permute-done.3), channel_id=1, source_target_pairs={{0,8},{8,16},{16,24},{24,0},{1,9},{9,17},{17,25},{25,1},{2,10},{10... | collective-permute-start | bytes 3145736 | tf_op jit(solution)/shard_map/ppermute | solution.py:134
  151.3 24.8 %collective-permute-start.5 = (bf16[256,2048]{1,0:T(8,128)(2,1)}, bf16[256,2048]{1,0:T(8,128)(2,1)S(1)}, u32[]{:S(2)}, u32[]{:S(2)}) collective-permute-start(bf16[256,2048]{1,0:T(8,128)(2,1)} %collective-permute-done.4), channel_id=1, source_target_pairs={{0,8},{8,16},{16,24},{24,0},{1,9},{9,17},{17,25},{25,1},{2,10},{10... | collective-permute-start | bytes 3145736 | tf_op jit(solution)/shard_map/ppermute | solution.py:134
  176.2 23.7 %collective-permute-start.6 = (bf16[256,2048]{1,0:T(8,128)(2,1)S(1)}, bf16[256,2048]{1,0:T(8,128)(2,1)S(1)}, u32[]{:S(2)}, u32[]{:S(2)}) collective-permute-start(bf16[256,2048]{1,0:T(8,128)(2,1)S(1)} %dynamic-slice_convert_fusion.1), channel_id=1, source_target_pairs={{0,8},{8,16},{16,24},{24,0},{1,9},{9,17},{17,25},{25,1},{2,10},{10... | collective-permute-start | bytes 3145736 | tf_op jit(solution)/shard_map/ppermute | solution.py:162
  273.2 23.5 %collective-permute-start.10 = (bf16[256,2048]{1,0:T(8,128)(2,1)}, bf16[256,2048]{1,0:T(8,128)(2,1)}, u32[]{:S(2)}, u32[]{:S(2)}) collective-permute-start(bf16[256,2048]{1,0:T(8,128)(2,1)} %collective-permute-done.9), channel_id=1, source_target_pairs={{0,8},{8,16},{16,24},{24,0},{1,9},{9,17},{17,25},{25,1},{2,10},{10... | collective-permute-start | bytes 3145736 | tf_op jit(solution)/shard_map/ppermute | solution.py:134
  296.7 72.4 %collective-permute-start.12 = (bf16[256,2048]{1,0:T(8,128)(2,1)}, bf16[256,2048]{1,0:T(8,128)(2,1)}, u32[]{:S(2)}, u32[]{:S(2)}) collective-permute-start(bf16[256,2048]{1,0:T(8,128)(2,1)} %fusion.91), channel_id=1, source_target_pairs={{0,8},{8,16},{16,24},{24,0},{1,9},{9,17},{17,25},{25,1},{2,10},{10... | collective-permute-start | bytes 3145736 | tf_op jit(solution)/shard_map/ppermute | solution.py:162
  296.7 42.2 %collective-permute-start.11 = (bf16[256,2048]{1,0:T(8,128)(2,1)}, bf16[256,2048]{1,0:T(8,128)(2,1)}, u32[]{:S(2)}, u32[]{:S(2)}) collective-permute-start(bf16[256,2048]{1,0:T(8,128)(2,1)} %collective-permute-done.10), channel_id=1, source_target_pairs={{0,8},{8,16},{16,24},{24,0},{1,9},{9,17},{17,25},{25,1},{2,10},{10... | collective-permute-start | bytes 3145736 | tf_op jit(solution)/shard_map/ppermute | solution.py:134
  369.1 366.0 %reduce-scatter.6.cloned.1.call-start = ((), (), s32[]{:S(2)}) async-start(), calls=%async_computation.8 | async-start | bytes 9437184 | tf_op jit(solution)/shard_map/reduce_scatter | solution.py:222
  372.5 28.1 %collective-permute-start.13 = (bf16[256,2048]{1,0:T(8,128)(2,1)}, bf16[256,2048]{1,0:T(8,128)(2,1)}, u32[]{:S(2)}, u32[]{:S(2)}) collective-permute-start(bf16[256,2048]{1,0:T(8,128)(2,1)} %add_convert_fusion.6), channel_id=1, source_target_pairs={{0,8},{8,16},{16,24},{24,0},{1,9},{9,17},{17,25},{25,1},{2,10},{10... | collective-permute-start | bytes 3145736 | tf_op jit(solution)/shard_map/ppermute | solution.py:162
  372.5 90.2 %collective-permute-start.15 = (bf16[256,2048]{1,0:T(8,128)(2,1)}, bf16[256,2048]{1,0:T(8,128)(2,1)}, u32[]{:S(2)}, u32[]{:S(2)}) collective-permute-start(bf16[256,2048]{1,0:T(8,128)(2,1)} %fusion.79), channel_id=1, source_target_pairs={{0,8},{8,16},{16,24},{24,0},{1,9},{9,17},{17,25},{25,1},{2,10},{10... | collective-permute-start | bytes 3145736 | tf_op jit(solution)/shard_map/ppermute | solution.py:162
  404.1 32.1 %collective-permute-start.14 = (bf16[256,2048]{1,0:T(8,128)(2,1)}, bf16[256,2048]{1,0:T(8,128)(2,1)S(1)}, u32[]{:S(2)}, u32[]{:S(2)}) collective-permute-start(bf16[256,2048]{1,0:T(8,128)(2,1)} %add_convert_fusion.5), channel_id=1, source_target_pairs={{0,8},{8,16},{16,24},{24,0},{1,9},{9,17},{17,25},{25,1},{2,10},{10... | collective-permute-start | bytes 3145736 | tf_op jit(solution)/shard_map/ppermute | solution.py:162
  515.8 24.2 %collective-permute-start.18 = (bf16[256,2048]{1,0:T(8,128)(2,1)S(1)}, bf16[256,2048]{1,0:T(8,128)(2,1)S(1)}, u32[]{:S(2)}, u32[]{:S(2)}) collective-permute-start(bf16[256,2048]{1,0:T(8,128)(2,1)S(1)} %get-tuple-element.165), channel_id=1, source_target_pairs={{0,8},{8,16},{16,24},{24,0},{1,9},{9,17},{17,25},{25,1},{2,10},{10... | collective-permute-start | bytes 3145736 | tf_op jit(solution)/shard_map/ppermute | solution.py:134
  540.1 25.4 %collective-permute-start.19 = (bf16[256,2048]{1,0:T(8,128)(2,1)S(1)}, bf16[256,2048]{1,0:T(8,128)(2,1)S(1)}, u32[]{:S(2)}, u32[]{:S(2)}) collective-permute-start(bf16[256,2048]{1,0:T(8,128)(2,1)S(1)} %collective-permute-done.18), channel_id=1, source_target_pairs={{0,8},{8,16},{16,24},{24,0},{1,9},{9,17},{17,25},{25,1},{2,10},{10... | collective-permute-start | bytes 3145736 | tf_op jit(solution)/shard_map/ppermute | solution.py:134
  649.6 188.9 %reduce-scatter.8.cloned.1.call-start = ((), (), s32[]{:S(2)}) async-start(), calls=%async_computation.9 | async-start | bytes 18874368 | tf_op jit(solution)/shard_map/reduce_scatter | solution.py:222
  660.4 27.6 %collective-permute-start.21 = (bf16[256,2048]{1,0:T(8,128)(2,1)S(1)}, bf16[256,2048]{1,0:T(8,128)(2,1)S(1)}, u32[]{:S(2)}, u32[]{:S(2)}) collective-permute-start(bf16[256,2048]{1,0:T(8,128)(2,1)S(1)} %dynamic-slice_convert_fusion), channel_id=1, source_target_pairs={{0,8},{8,16},{16,24},{24,0},{1,9},{9,17},{17,25},{25,1},{2,10},{10... | collective-permute-start | bytes 3145736 | tf_op jit(solution)/shard_map/ppermute | solution.py:162
  688.3 27.1 %collective-permute-start.22 = (bf16[256,2048]{1,0:T(8,128)(2,1)S(1)}, bf16[256,2048]{1,0:T(8,128)(2,1)S(1)}, u32[]{:S(2)}, u32[]{:S(2)}) collective-permute-start(bf16[256,2048]{1,0:T(8,128)(2,1)S(1)} %add_convert_fusion.1), channel_id=1, source_target_pairs={{0,8},{8,16},{16,24},{24,0},{1,9},{9,17},{17,25},{25,1},{2,10},{10... | collective-permute-start | bytes 3145736 | tf_op jit(solution)/shard_map/ppermute | solution.py:162
  (76 other events, 961.5 us)
Sparse Core Ops, SparseCore 0:
  10.5 48.1 all-gather.4
  60.5 28.0 all-gather.6
  90.5 55.8 all-gather.10
  148.7 89.7 all-gather.8
  369.3 68.9 reduce-scatter.3
  649.7 68.9 reduce-scatter.5
  722.3 116.1 reduce-scatter.7

commit v9 on v7

--- a/solution.py
+++ b/solution.py
@@ -389,59 +389,97 @@
     gate_slots = [item[0] for item in ffn]
     up_slots = [item[1] for item in ffn]
     act_slots = [item[2] for item in ffn]
-    ffn_ring = RingScatter([item[3] for item in ffn], "row", jnp.bfloat16)
+    ffn_parts = [item[3] for item in ffn]
 
     def ffn_backward(slot):
-        def piece(done):
-            gate_lin, up_lin = gate_slots[slot], up_slots[slot]
-            grad_activation = times_transpose(cot_slots[slot], full_down)
-            sigma = jax.nn.sigmoid(gate_lin)
-            grad_gate = grad_activation * up_lin * sigma * (1.0 + gate_lin * (1.0 - sigma))
-            grad_up = grad_activation * gate_lin * sigma
-            grad_gu = jnp.concatenate([grad_gate, grad_up], axis=1).astype(jnp.bfloat16)
-            return (grad_gu, times_transpose(grad_gu, full_gu))
-
-        return piece
-
+        gate_lin, up_lin = gate_slots[slot], up_slots[slot]
+        grad_activation = times_transpose(cot_slots[slot], full_down)
+        sigma = jax.nn.sigmoid(gate_lin)
+        grad_gate = grad_activation * up_lin * sigma * (1.0 + gate_lin * (1.0 - sigma))
+        grad_up = grad_activation * gate_lin * sigma
+        grad_gu = jnp.concatenate([grad_gate, grad_up], axis=1).astype(jnp.bfloat16)
+        return (grad_gu, times_transpose(grad_gu, full_gu))
+
+    second_ring_back = RingScatter([None] * slots, "row", jnp.bfloat16)
+    grad_gu_slots = [None] * slots
     order = list(range(1, slots)) + [0]
-    bwd = overlap(ffn_ring, [ffn_backward(slot) for slot in order])
-    ffn_sum = ffn_ring.result()
-    output = (middle + ffn_sum).astype(jnp.bfloat16)
-    by_slot = dict(zip(order, bwd))
-    grad_gu = jnp.concatenate([by_slot[slot][0] for slot in range(slots)], axis=0)
-    second_ring_back = RingScatter([by_slot[slot][1] for slot in range(slots)], "row", jnp.bfloat16)
-    rows_second = jnp.concatenate(second_slots, axis=0)
-
-    def down_weight_grad(_):
-        return contract_rows(jnp.concatenate(act_slots, axis=0), jnp.concatenate(cot_slots, axis=0))
-
-    def gate_up_weight_grad(_):
-        return contract_rows(rows_second, grad_gu)
-
-    grad_down_w, grad_gu_w = overlap(second_ring_back, [down_weight_grad, gate_up_weight_grad])
+    grad_gu_slots[order[0]], second_ring_back.slots[order[0]] = ffn_backward(order[0])
+    grad_down_w = None
+    for index in range(second_ring_back.steps()):
+        second_ring_back.send()
+        slot = order[index + 1]
+        value = ffn_backward(slot)
+        if slot == 0:
+            grad_down_w = contract_rows(
+                jnp.concatenate(act_slots, axis=0), jnp.concatenate(cot_slots, axis=0)
+            )
+            value = value + (grad_down_w,)
+        second_ring_back.pending, value = lax.optimization_barrier(
+            (second_ring_back.pending, value)
+        )
+        grad_gu_slots[slot], second_ring_back.slots[slot] = value[0], value[1]
+        if slot == 0:
+            grad_down_w = value[2]
     grad_second = second_ring_back.result()
     down_sum = col_scatter(grad_down_w, 1)
-    gu_sum = col_scatter(grad_gu_w, 0)
+    grad_gu = jnp.concatenate(grad_gu_slots, axis=0)
+    rows_second = jnp.concatenate(second_slots, axis=0)
     grad_middle = cotangent.astype(jnp.float32) + norm_back(middle, grad_second)
     branch_chain = RingGather(grad_middle.astype(jnp.bfloat16), "row", absolute=True)
     steps = branch_chain.steps()
-    down_sum = overlap(branch_chain, [lambda done: ()] * (steps - 1) + [lambda done: down_sum])[-1]
+
+    def gate_up_weight_grad(_):
+        return contract_rows(rows_second, grad_gu)
+
+    tied = overlap(
+        branch_chain, [gate_up_weight_grad] + [lambda done: ()] * (steps - 2) + [lambda done: down_sum]
+    )
+    grad_gu_w, down_sum = tied[0], tied[-1]
+    gu_sum = col_scatter(grad_gu_w, 0)
     grad_branch = branch_chain.result()
+    ffn_parts, grad_branch = lax.optimization_barrier((ffn_parts, grad_branch))
+    ffn_ring = RingScatter(list(ffn_parts), "row", jnp.bfloat16)
     output_sum = col_scatter(contract_rows(attended, grad_branch), 1)
-    grad_mixed = split_heads(times_transpose(grad_branch, full_output).astype(jnp.bfloat16))
-    grad_q_rot, grad_k_rot, grad_values = lax.map(
-        attend_backward, (queries, keys_rot, values, piece_starts, log_total, grad_mixed)
-    )
-    grad_qkv = jnp.concatenate(
-        [
-            merge_heads(unrotate(grad_q_rot, cosine, sine)),
-            merge_heads(unrotate(grad_k_rot, cosine, sine)),
-            merge_heads(grad_values),
-        ],
-        axis=1,
-    ).astype(jnp.bfloat16)
+    half = heads_local // 2
+
+    def heads_backward(lo, hi):
+        def piece(done):
+            grad_mixed = times_transpose(grad_branch, full_output[lo * HD : hi * HD])
+            grad_mixed = grad_mixed.astype(jnp.bfloat16).reshape(seq_count, LENGTH, hi - lo, HD)
+            return lax.map(
+                attend_backward,
+                (
+                    queries[:, :, lo:hi],
+                    keys_rot[:, :, lo:hi],
+                    values[:, :, lo:hi],
+                    piece_starts,
+                    log_total[:, lo:hi],
+                    grad_mixed,
+                ),
+            )
+
+        return piece
+
+    def finish(done):
+        parts = [jnp.concatenate([a[k] for a in done], axis=2) for k in range(3)]
+        grad_q_rot, grad_k_rot, grad_values = parts
+        grad_qkv = jnp.concatenate(
+            [
+                merge_heads(unrotate(grad_q_rot, cosine, sine)),
+                merge_heads(unrotate(grad_k_rot, cosine, sine)),
+                merge_heads(grad_values),
+            ],
+            axis=1,
+        ).astype(jnp.bfloat16)
+        return (grad_qkv, times_transpose(grad_qkv, full_qkv))
+
+    pieces = [heads_backward(0, half), heads_backward(half, heads_local), finish]
+    grad_qkv, first_partial = overlap(ffn_ring, pieces)[-1]
+    ffn_sum = ffn_ring.result()
+    output = (middle + ffn_sum).astype(jnp.bfloat16)
     qkv_sum = col_scatter(contract_rows(first_rows, grad_qkv), 0)
-    grad_first = ring_reduce_scatter(times_transpose(grad_qkv, full_qkv), "row", jnp.bfloat16)
+    first_partial, gu_sum = lax.optimization_barrier((first_partial, gu_sum))
+    grad_first = ring_reduce_scatter(first_partial, "row", jnp.bfloat16)
     grad_input = grad_middle + norm_back(inputs, grad_first)
     return (
         output,

time: 822 us -> 732 us (0.89)
  waiting for transfers between devices: 413 us -> 258 us
  matrix products: 250 us -> 279 us
  other arithmetic: 80.6 us -> 99 us
  local copies, waits for them, and re-layouts: 46.8 us -> 63.2 us
    reduce_scatter x4, waiting for transfers between devices: 102 us -> 17.4 us  [col_scatter(): lax.psum_scatter(low_part, COL, scatter_dimension=axis, tiled=True)]
    ppermute x12, waiting for transfers between devices: 174 us -> 130 us  [send(): lax.ppermute(self.pending, self.axis, [(j, (j + 1) % n) for j in range(n)])]
    ppermute x12, waiting for transfers between devices: 135 us -> 108 us  [send(): lax.ppermute(value.astype(self.send_dtype), self.axis, [(j, (j + 1) % n)...]
    convert_element_type x1, other arithmetic: 8.07 us -> 18.3 us  [attend_backward(): grad_scores = (probs * (grad_probs - inner)).astype(jnp.bfloat16)]
    dot_general x1 -> x2, matrix products: 4.65 us -> 14.2 us  [attend_backward(): jnp.einsum('hqk,qhd->khd', probs_low, grad_mixed, preferred_element_type=...]
    dot_general x10 -> x11, matrix products: 83 us -> 89.1 us  [times_transpose(): lax.dot_general(left, right, (((1,), (1,)), ((), ())), preferred_element_...]
  transfers between devices with their start and end apart: 32 -> 32, of which waited for: 21 -> 16; matrix products, arithmetic and copies ran while one was open for 43% -> 57% of each run, Pallas kernels for 0% -> 0%
where the time goes in v9:
time: 732 us; the launch traced here: 726 us
  matrix products  279 us (38%)
  waiting for transfers between devices  258 us (35%)
  other arithmetic  99 us (14%)
  local copies, waits for them, and re-layouts  63.2 us (9%)
  between operations  15.6 us (2%)
  starting transfers between devices  11.6 us (2%)
    ppermute x12, waiting for transfers between devices, send(): lax.ppermute(self.pending, self.axis, [(j, (j + 1) % n) for j in range(n)])  130 us
    ppermute x12, waiting for transfers between devices, send(): lax.ppermute(value.astype(self.send_dtype), self.axis, [(j, (j + 1) % n)...  108 us
    dot_general x11, matrix products, times_transpose(): lax.dot_general(left, right, (((1,), (1,)), ((), ())), preferred_element_...  89.1 us
    dot_general x10, matrix products, product(): return jnp.dot(left, right, preferred_element_type=jnp.float32)  68.5 us
    dot_general x4, matrix products, contract_rows(): lax.dot_general(left, right, (((0,), (0,)), ((), ())), preferred_element_...  56.8 us
    convert_element_type x1, other arithmetic, attend_backward(): grad_scores = (probs * (grad_probs - inner)).astype(jnp.bfloat16)  18.3 us
    reduce_scatter x4, waiting for transfers between devices, col_scatter(): lax.psum_scatter(low_part, COL, scatter_dimension=axis, tiled=True)  17.4 us
    dot_general x2, matrix products, attend_backward(): jnp.einsum('qhd,khd->hqk', grad_mixed, values, preferred_element_type=jnp...  15.9 us
  transfers between devices with their start and end apart: 32, of which 16 were waited for; matrix products, arithmetic and copies ran while one was open for 57% of the time, Pallas kernels for 0%

profile of v9, /device:TPU:0, one launch (start us, length us, event | category | flops | bytes accessed | tf_op | source)
XLA Modules:
  0.0 725.7 jit_solution(10745077977959625612)
XLA Ops:
  21.2 25.2 %collective-permute-done = bf16[256,2048]{1,0:T(8,128)(2,1)S(1)} collective-permute-done((bf16[256,2048]{1,0:T(8,128)(2,1)S(1)}, bf16[256,2048]{1,0:T(8,128)(2,1)S(1)}, u32[]{:S(2)}, u32[]{:S(2)}) %collective-permute-start) | collective-permute-done | bytes 1048608 | tf_op jit(solution)/shard_map/ppermute | solution.py:134
  47.9 24.7 %collective-permute-done.1 = bf16[256,2048]{1,0:T(8,128)(2,1)} collective-permute-done((bf16[256,2048]{1,0:T(8,128)(2,1)S(1)}, bf16[256,2048]{1,0:T(8,128)(2,1)}, u32[]{:S(2)}, u32[]{:S(2)}) %collective-permute-start.1) | collective-permute-done | bytes 1048608 | tf_op jit(solution)/shard_map/ppermute | solution.py:134
  82.1 16.1 %collective-permute-done.2 = bf16[256,2048]{1,0:T(8,128)(2,1)} collective-permute-done((bf16[256,2048]{1,0:T(8,128)(2,1)}, bf16[256,2048]{1,0:T(8,128)(2,1)}, u32[]{:S(2)}, u32[]{:S(2)}) %collective-permute-start.2) | collective-permute-done | bytes 1048608 | tf_op jit(solution)/shard_map/ppermute | solution.py:134
  100.9 10.1 %fusion.119 = f32[1024,1536]{1,0:T(8,128)S(1)} fusion(bf16[1024,2048]{1,0:T(8,128)(2,1)} %constant_dynamic-update-slice_fusion.8, bf16[2048,1536]{1,0:T(8,128)(2,1)} %all-gather.5.cloned.1.call-done), kind=kOutput, calls=%fused_computation.217 | convolution fusion | flops 6442450944 | bytes 16777216 | tf_op jit(solution)/shard_map/dot_general | solution.py:19
  161.2 19.0 %collective-permute-done.5 = bf16[256,2048]{1,0:T(8,128)(2,1)S(1)} collective-permute-done((bf16[256,2048]{1,0:T(8,128)(2,1)}, bf16[256,2048]{1,0:T(8,128)(2,1)S(1)}, u32[]{:S(2)}, u32[]{:S(2)}) %collective-permute-start.5) | collective-permute-done | bytes 1048608 | tf_op jit(solution)/shard_map/ppermute | solution.py:134
  181.3 22.1 %collective-permute-done.6 = bf16[256,2048]{1,0:T(8,128)(2,1)S(1)} collective-permute-done((bf16[256,2048]{1,0:T(8,128)(2,1)S(1)}, bf16[256,2048]{1,0:T(8,128)(2,1)S(1)}, u32[]{:S(2)}, u32[]{:S(2)}) %collective-permute-start.6) | collective-permute-done | bytes 1048608 | tf_op jit(solution)/shard_map/ppermute | solution.py:162
  211.4 15.2 %collective-permute-done.7 = bf16[256,2048]{1,0:T(8,128)(2,1)S(1)} collective-permute-done((bf16[256,2048]{1,0:T(8,128)(2,1)S(1)}, bf16[256,2048]{1,0:T(8,128)(2,1)S(1)}, u32[]{:S(2)}, u32[]{:S(2)}) %collective-permute-start.7) | collective-permute-done | bytes 1048608 | tf_op jit(solution)/shard_map/ppermute | solution.py:162
  237.0 12.2 %collective-permute-done.8 = bf16[256,2048]{1,0:T(8,128)(2,1)S(1)} collective-permute-done((bf16[256,2048]{1,0:T(8,128)(2,1)S(1)}, bf16[256,2048]{1,0:T(8,128)(2,1)S(1)}, u32[]{:S(2)}, u32[]{:S(2)}) %collective-permute-start.8) | collective-permute-done | bytes 1048608 | tf_op jit(solution)/shard_map/ppermute | solution.py:162
  290.1 12.0 %fusion.108 = f32[256,2048]{1,0:T(8,128)} fusion(bf16[2048,4096]{1,0:T(8,128)(2,1)} %all-gather.9.cloned.1.call-done, bf16[256,2048]{1,0:T(8,128)(2,1)} %copy-done.28, bf16[256,2048]{1,0:T(8,128)(2,1)S(1)} %get-tuple-element.231), kind=kOutput, calls=%fused_computation.207 | convolution fusion | flops 4299161600 | bytes 20971520 | tf_op jit(solution)/shard_map/dot_general | solution.py:29
  307.3 12.0 %convolution_convert_fusion.2 = bf16[256,2048]{1,0:T(8,128)(2,1)} fusion(bf16[2048,4096]{1,0:T(8,128)(2,1)} %all-gather.9.cloned.1.call-done, bf16[256,2048]{1,0:T(8,128)(2,1)} %get-tuple-element.237, bf16[256,2048]{1,0:T(8,128)(2,1)S(1)} %get-tuple-element.236), kind=kOutput, calls=%fused_computation.59 | convolution fusion | flops 4299685888 | bytes 19922944 | tf_op jit(solution)/shard_map/dot_general | solution.py:29
  341.9 11.9 %fusion.110 = f32[256,2048]{1,0:T(8,128)} fusion(bf16[2048,4096]{1,0:T(8,128)(2,1)} %all-gather.9.cloned.1.call-done, bf16[256,2048]{1,0:T(8,128)(2,1)} %copy-done.29, bf16[256,2048]{1,0:T(8,128)(2,1)S(1)} %get-tuple-element.234), kind=kOutput, calls=%fused_computation.209 | convolution fusion | flops 4299161600 | bytes 20971520 | tf_op jit(solution)/shard_map/dot_general | solution.py:29
  375.0 12.3 %fusion.109 = f32[256,2048]{1,0:T(8,128)} fusion(bf16[2048,4096]{1,0:T(8,128)(2,1)} %all-gather.9.cloned.1.call-done, bf16[256,2048]{1,0:T(8,128)(2,1)} %copy-done.49, bf16[256,2048]{1,0:T(8,128)(2,1)} %copy-done.48), kind=kOutput, calls=%fused_computation.208 | convolution fusion | flops 4299161600 | bytes 20971520 | tf_op jit(solution)/shard_map/dot_general | solution.py:29
  390.9 13.0 %fusion.15 = bf16[2048,2048]{1,0:T(8,128)(2,1)} fusion(bf16[256,2048]{1,0:T(8,128)(2,1)} %get-tuple-element.233, bf16[256,2048]{1,0:T(8,128)(2,1)S(1)} %copy-done.40, bf16[256,2048]{1,0:T(8,128)(2,1)S(1)} %copy-done.38, bf16[256,2048]{1,0:T(8,128)(2,1)S(1)} %copy-done.36, bf16[256,2048]{1,0:T(8,128)(2,1)S(1)} %copy-done.64, ...), kind=kOutput, calls=%fused_computation.26 | convolution fusion | flops 8623489024 | bytes 16777216 | tf_op jit(solution)/shard_map/dot_general | solution.py:23
  417.4 26.8 %fusion.2 = bf16[2048,4096]{1,0:T(8,128)(2,1)} fusion(bf16[256,4096]{1,0:T(8,128)(2,1)} %pad_maximum_fusion.3, bf16[256,4096]{1,0:T(8,128)(2,1)} %pad_maximum_fusion.2, bf16[256,2048]{1,0:T(8,128)(2,1)} %get-tuple-element.237, bf16[256,2048]{1,0:T(8,128)(2,1)} %copy-done.50, bf16[256,4096]{1,0:T(8,128)(2,1)} %pad_maximum_fusion.4, ...), kind=kOutput, calls=%fused_computation.5 | convolution fusion | flops 17238589440 | bytes 29360128 | tf_op jit(solution)/shard_map/dot_general | solution.py:23
  456.9 18.2 %collective-permute-done.16 = bf16[256,2048]{1,0:T(8,128)(2,1)} collective-permute-done((bf16[256,2048]{1,0:T(8,128)(2,1)}, bf16[256,2048]{1,0:T(8,128)(2,1)}, u32[]{:S(2)}, u32[]{:S(2)}) %collective-permute-start.16) | collective-permute-done | bytes 1048608 | tf_op jit(solution)/shard_map/ppermute | solution.py:134
  485.1 14.2 %collective-permute-done.17 = bf16[256,2048]{1,0:T(8,128)(2,1)S(1)} collective-permute-done((bf16[256,2048]{1,0:T(8,128)(2,1)}, bf16[256,2048]{1,0:T(8,128)(2,1)S(1)}, u32[]{:S(2)}, u32[]{:S(2)}) %collective-permute-start.17) | collective-permute-done | bytes 1048608 | tf_op jit(solution)/shard_map/ppermute | solution.py:134
  513.7 11.4 %multiply_reduce_fusion = (f32[2,1024]{1,0:T(2,128)S(1)}, f32[2,1024]{1,0:T(2,128)S(1)}, f32[2,1024,1024]{1,2,0:T(8,128)}) fusion(f32[2,1024,1024]{1,2,0:T(8,128)S(1)} %bitcast.131, f32[2,1024]{1,0:T(2,128)S(1)} %get-tuple-element.265, pred[1024,1024]{0,1:T(8,128)(4,1)S(1)} %copy-done.1, f32[2,1024,1024]{1,2,0:T(8,128)} %fusion.78, ...), kind=kOutput, calls=%fused_computation.16 | convolution fusion | flops 557838336 | bytes 35684352 | tf_op jit(solution)/shard_map/while/body/eval_jaxpr/qhd,khd->hqk/dot_general | solution.py:307
  525.1 18.3 %multiply_convert_fusion = (bf16[2,1024,1024]{1,2,0:T(8,128)(2,1)}, bf16[2,1024,1024]{1,2,0:T(8,128)(2,1)}) fusion(f32[2,1024,1024]{1,2,0:T(8,128)} %get-tuple-element.270, f32[2,1024,1024]{1,2,0:T(8,128)} %fusion.80, f32[2,1024]{1,0:T(2,128)S(1)} %get-tuple-element.212, f32[2,1024]{1,0:T(2,128)S(1)} %get-tuple-element.265, ...), kind=kLoop, calls=%fused_computation.15 | loop fusion | flops 25165824 | bytes 43024384 | tf_op jit(solution)/shard_map/while/body/eval_jaxpr/convert_element_type | solution.py:309
  583.5 15.1 %collective-permute-done.19 = bf16[256,2048]{1,0:T(8,128)(2,1)} collective-permute-done((bf16[256,2048]{1,0:T(8,128)(2,1)}, bf16[256,2048]{1,0:T(8,128)(2,1)}, u32[]{:S(2)}, u32[]{:S(2)}) %collective-permute-start.19) | collective-permute-done | bytes 1048608 | tf_op jit(solution)/shard_map/ppermute | solution.py:162
  613.1 10.8 %fusion.111 = f32[1024,2048]{1,0:T(8,128)} fusion(bf16[2048,1536]{1,0:T(8,128)(2,1)} %all-gather.5.cloned.1.call-done, bf16[1024,512]{0,1:T(8,128)(2,1)S(1)} %bitcast.137, bf16[1024,512]{0,1:T(8,128)(2,1)S(1)} %bitcast.133, bf16[1024,512]{0,1:T(8,128)(2,1)S(1)} %bitcast.135), kind=kOutput, calls=%fused_computation.210 | convolution fusion | flops 6451888128 | bytes 17825792 | tf_op jit(solution)/shard_map/dot_general | solution.py:29
  624.0 11.0 %convolution_convert_fusion = bf16[2048,1536]{1,0:T(8,128)(2,1)} fusion(bf16[1024,2048]{1,0:T(8,128)(2,1)} %constant_dynamic-update-slice_fusion.8, bf16[1024,1536]{0,1:T(8,128)(2,1)S(1)} %pad_maximum_fusion), kind=kOutput, calls=%fused_computation.23 | convolution fusion | flops 6445596672 | bytes 13631488 | tf_op jit(solution)/shard_map/dot_general | solution.py:23
  641.4 21.6 %collective-permute-done.21 = bf16[256,2048]{1,0:T(8,128)(2,1)S(1)} collective-permute-done((bf16[256,2048]{1,0:T(8,128)(2,1)S(1)}, bf16[256,2048]{1,0:T(8,128)(2,1)S(1)}, u32[]{:S(2)}, u32[]{:S(2)}) %collective-permute-start.21) | collective-permute-done | bytes 1048608 | tf_op jit(solution)/shard_map/ppermute | solution.py:162
  663.4 18.5 %collective-permute-done.22 = bf16[256,2048]{1,0:T(8,128)(2,1)S(1)} collective-permute-done((bf16[256,2048]{1,0:T(8,128)(2,1)S(1)}, bf16[256,2048]{1,0:T(8,128)(2,1)S(1)}, u32[]{:S(2)}, u32[]{:S(2)}) %collective-permute-start.22) | collective-permute-done | bytes 1048608 | tf_op jit(solution)/shard_map/ppermute | solution.py:162
  688.0 17.4 %reduce-scatter.9.cloned.1.call-done = bf16[256,1536]{1,0:T(8,128)(2,1)} async-done(((bf16[2048,1536]{1,0:T(8,128)(2,1)}), bf16[256,1536]{1,0:T(8,128)(2,1)}) %reduce-scatter.9.cloned.1.call-update) | async-done | bytes 786448 | tf_op jit(solution)/shard_map/reduce_scatter | solution.py:222
  (334 shorter events, 321.3 us)
Async XLA Ops:
  7.2 93.7 %all-gather.5.cloned.1.call-start = ((), (), s32[]{:S(2)}) async-start(), calls=%async_computation.4 | async-start | bytes 7077888 | tf_op jit(solution)/shard_map/all_gather | solution.py:217
  9.4 147.0 %all-gather.7.cloned.1.call-start = ((), (), s32[]{:S(2)}) async-start(), calls=%async_computation.5 | async-start | bytes 2359296 | tf_op jit(solution)/shard_map/all_gather | solution.py:217
  10.2 193.6 %all-gather.11.cloned.1.call-start = ((), (), s32[]{:S(2)}) async-start(), calls=%async_computation.7 | async-start | bytes 9437184 | tf_op jit(solution)/shard_map/all_gather | solution.py:217
  10.9 239.5 %all-gather.9.cloned.1.call-start = ((), (), s32[]{:S(2)}) async-start(), calls=%async_computation.6 | async-start | bytes 18874368 | tf_op jit(solution)/shard_map/all_gather | solution.py:217
  12.5 469.7 %reduce-scatter.5.cloned.1.call-start = ((), (), s32[]{:S(2)}) async-start(), calls=%async_computation.8 | async-start | bytes 9437184 | tf_op jit(solution)/shard_map/reduce_scatter | solution.py:222
  18.1 28.2 %collective-permute-start = (bf16[256,2048]{1,0:T(8,128)(2,1)S(1)}, bf16[256,2048]{1,0:T(8,128)(2,1)S(1)}, u32[]{:S(2)}, u32[]{:S(2)}) collective-permute-start(bf16[256,2048]{1,0:T(8,128)(2,1)S(1)} %get-tuple-element.220), channel_id=1, source_target_pairs={{0,8},{8,16},{16,24},{24,0},{1,9},{9,17},{17,25},{25,1},{2,10},{10... | collective-permute-start | bytes 3145736 | tf_op jit(solution)/shard_map/ppermute | solution.py:134
  46.4 26.2 %collective-permute-start.1 = (bf16[256,2048]{1,0:T(8,128)(2,1)S(1)}, bf16[256,2048]{1,0:T(8,128)(2,1)}, u32[]{:S(2)}, u32[]{:S(2)}) collective-permute-start(bf16[256,2048]{1,0:T(8,128)(2,1)S(1)} %collective-permute-done), channel_id=1, source_target_pairs={{0,8},{8,16},{16,24},{24,0},{1,9},{9,17},{17,25},{25,1},{2,10},{10... | collective-permute-start | bytes 3145736 | tf_op jit(solution)/shard_map/ppermute | solution.py:134
  72.6 25.6 %collective-permute-start.2 = (bf16[256,2048]{1,0:T(8,128)(2,1)}, bf16[256,2048]{1,0:T(8,128)(2,1)}, u32[]{:S(2)}, u32[]{:S(2)}) collective-permute-start(bf16[256,2048]{1,0:T(8,128)(2,1)} %collective-permute-done.1), channel_id=1, source_target_pairs={{0,8},{8,16},{16,24},{24,0},{1,9},{9,17},{17,25},{25,1},{2,10},{10... | collective-permute-start | bytes 3145736 | tf_op jit(solution)/shard_map/ppermute | solution.py:134
  100.6 30.5 %collective-permute-start.3 = (bf16[256,2048]{1,0:T(8,128)(2,1)}, bf16[256,2048]{1,0:T(8,128)(2,1)}, u32[]{:S(2)}, u32[]{:S(2)}) collective-permute-start(bf16[256,2048]{1,0:T(8,128)(2,1)} %param.19), channel_id=1, source_target_pairs={{0,8},{8,16},{16,24},{24,0},{1,9},{9,17},{17,25},{25,1},{2,10},{10... | collective-permute-start | bytes 3145736 | tf_op jit(solution)/shard_map/ppermute | solution.py:134
  131.1 25.3 %collective-permute-start.4 = (bf16[256,2048]{1,0:T(8,128)(2,1)}, bf16[256,2048]{1,0:T(8,128)(2,1)}, u32[]{:S(2)}, u32[]{:S(2)}) collective-permute-start(bf16[256,2048]{1,0:T(8,128)(2,1)} %collective-permute-done.3), channel_id=1, source_target_pairs={{0,8},{8,16},{16,24},{24,0},{1,9},{9,17},{17,25},{25,1},{2,10},{10... | collective-permute-start | bytes 3145736 | tf_op jit(solution)/shard_map/ppermute | solution.py:134
  156.4 23.8 %collective-permute-start.5 = (bf16[256,2048]{1,0:T(8,128)(2,1)}, bf16[256,2048]{1,0:T(8,128)(2,1)S(1)}, u32[]{:S(2)}, u32[]{:S(2)}) collective-permute-start(bf16[256,2048]{1,0:T(8,128)(2,1)} %collective-permute-done.4), channel_id=1, source_target_pairs={{0,8},{8,16},{16,24},{24,0},{1,9},{9,17},{17,25},{25,1},{2,10},{10... | collective-permute-start | bytes 3145736 | tf_op jit(solution)/shard_map/ppermute | solution.py:134
  273.1 28.9 %collective-permute-start.10 = (bf16[256,2048]{1,0:T(8,128)(2,1)}, bf16[256,2048]{1,0:T(8,128)(2,1)}, u32[]{:S(2)}, u32[]{:S(2)}) collective-permute-start(bf16[256,2048]{1,0:T(8,128)(2,1)} %collective-permute-done.9), channel_id=1, source_target_pairs={{0,8},{8,16},{16,24},{24,0},{1,9},{9,17},{17,25},{25,1},{2,10},{10... | collective-permute-start | bytes 3145736 | tf_op jit(solution)/shard_map/ppermute | solution.py:134
  302.0 36.0 %collective-permute-start.11 = (bf16[256,2048]{1,0:T(8,128)(2,1)}, bf16[256,2048]{1,0:T(8,128)(2,1)}, u32[]{:S(2)}, u32[]{:S(2)}) collective-permute-start(bf16[256,2048]{1,0:T(8,128)(2,1)} %collective-permute-done.10), channel_id=1, source_target_pairs={{0,8},{8,16},{16,24},{24,0},{1,9},{9,17},{17,25},{25,1},{2,10},{10... | collective-permute-start | bytes 3145736 | tf_op jit(solution)/shard_map/ppermute | solution.py:134
  319.3 34.6 %collective-permute-start.12 = (bf16[256,2048]{1,0:T(8,128)(2,1)}, bf16[256,2048]{1,0:T(8,128)(2,1)}, u32[]{:S(2)}, u32[]{:S(2)}) collective-permute-start(bf16[256,2048]{1,0:T(8,128)(2,1)} %convolution_convert_fusion.2), channel_id=1, source_target_pairs={{0,8},{8,16},{16,24},{24,0},{1,9},{9,17},{17,25},{25,1},{2,10},{10... | collective-permute-start | bytes 3145736 | tf_op jit(solution)/shard_map/ppermute | solution.py:162
  356.2 31.1 %collective-permute-start.13 = (bf16[256,2048]{1,0:T(8,128)(2,1)S(1)}, bf16[256,2048]{1,0:T(8,128)(2,1)}, u32[]{:S(2)}, u32[]{:S(2)}) collective-permute-start(bf16[256,2048]{1,0:T(8,128)(2,1)S(1)} %add_convert_fusion.8), channel_id=1, source_target_pairs={{0,8},{8,16},{16,24},{24,0},{1,9},{9,17},{17,25},{25,1},{2,10},{10... | collective-permute-start | bytes 3145736 | tf_op jit(solution)/shard_map/ppermute | solution.py:162
  407.4 227.6 %reduce-scatter.7.cloned.1.call-start = ((), (), s32[]{:S(2)}) async-start(), calls=%async_computation.9 | async-start | bytes 18874368 | tf_op jit(solution)/shard_map/reduce_scatter | solution.py:222
  417.2 27.0 %collective-permute-start.15 = (bf16[256,2048]{1,0:T(8,128)(2,1)}, bf16[256,2048]{1,0:T(8,128)(2,1)S(1)}, u32[]{:S(2)}, u32[]{:S(2)}) collective-permute-start(bf16[256,2048]{1,0:T(8,128)(2,1)} %get-tuple-element.215), channel_id=1, source_target_pairs={{0,8},{8,16},{16,24},{24,0},{1,9},{9,17},{17,25},{25,1},{2,10},{10... | collective-permute-start | bytes 3145736 | tf_op jit(solution)/shard_map/ppermute | solution.py:134
  445.2 241.0 %reduce-scatter.11.cloned.1.call-start = ((), (), s32[]{:S(2)}) async-start(), calls=%async_computation.11 | async-start | bytes 2359296 | tf_op jit(solution)/shard_map/reduce_scatter | solution.py:222
  447.7 27.3 %collective-permute-start.16 = (bf16[256,2048]{1,0:T(8,128)(2,1)}, bf16[256,2048]{1,0:T(8,128)(2,1)}, u32[]{:S(2)}, u32[]{:S(2)}) collective-permute-start(bf16[256,2048]{1,0:T(8,128)(2,1)} %copy-done.42), channel_id=1, source_target_pairs={{0,8},{8,16},{16,24},{24,0},{1,9},{9,17},{17,25},{25,1},{2,10},{10... | collective-permute-start | bytes 3145736 | tf_op jit(solution)/shard_map/ppermute | solution.py:134
  475.1 24.2 %collective-permute-start.17 = (bf16[256,2048]{1,0:T(8,128)(2,1)}, bf16[256,2048]{1,0:T(8,128)(2,1)S(1)}, u32[]{:S(2)}, u32[]{:S(2)}) collective-permute-start(bf16[256,2048]{1,0:T(8,128)(2,1)} %collective-permute-done.16), channel_id=1, source_target_pairs={{0,8},{8,16},{16,24},{24,0},{1,9},{9,17},{17,25},{25,1},{2,10},{10... | collective-permute-start | bytes 3145736 | tf_op jit(solution)/shard_map/ppermute | solution.py:134
  500.3 68.2 %collective-permute-start.18 = (bf16[256,2048]{1,0:T(8,128)(2,1)}, bf16[256,2048]{1,0:T(8,128)(2,1)}, u32[]{:S(2)}, u32[]{:S(2)}) collective-permute-start(bf16[256,2048]{1,0:T(8,128)(2,1)} %fusion.124), channel_id=1, source_target_pairs={{0,8},{8,16},{16,24},{24,0},{1,9},{9,17},{17,25},{25,1},{2,10},{10... | collective-permute-start | bytes 3145736 | tf_op jit(solution)/shard_map/ppermute | solution.py:162
  571.3 27.2 %collective-permute-start.19 = (bf16[256,2048]{1,0:T(8,128)(2,1)}, bf16[256,2048]{1,0:T(8,128)(2,1)}, u32[]{:S(2)}, u32[]{:S(2)}) collective-permute-start(bf16[256,2048]{1,0:T(8,128)(2,1)} %add_convert_fusion.6), channel_id=1, source_target_pairs={{0,8},{8,16},{16,24},{24,0},{1,9},{9,17},{17,25},{25,1},{2,10},{10... | collective-permute-start | bytes 3145736 | tf_op jit(solution)/shard_map/ppermute | solution.py:162
  574.9 130.5 %reduce-scatter.9.cloned.1.call-start = ((), (), s32[]{:S(2)}) async-start(), calls=%async_computation.10 | async-start | bytes 7077888 | tf_op jit(solution)/shard_map/reduce_scatter | solution.py:222
  683.3 29.3 %collective-permute-start.23 = (bf16[256,2048]{1,0:T(8,128)(2,1)}, bf16[256,2048]{1,0:T(8,128)(2,1)S(1)}, u32[]{:S(2)}, u32[]{:S(2)}) collective-permute-start(bf16[256,2048]{1,0:T(8,128)(2,1)} %add_convert_fusion), channel_id=1, source_target_pairs={{0,8},{8,16},{16,24},{24,0},{1,9},{9,17},{17,25},{25,1},{2,10},{10... | collective-permute-start | bytes 3145736 | tf_op jit(solution)/shard_map/ppermute | solution.py:162
  (87 other events, 1010.1 us)
Sparse Core Ops, SparseCore 0:
  10.5 48.1 all-gather.4
  60.5 28.0 all-gather.6
  90.5 55.8 all-gather.10
  148.7 89.7 all-gather.8
  407.5 68.5 reduce-scatter.4
  479.6 116.1 reduce-scatter.6
  599.1 41.0 reduce-scatter.10
  643.6 61.7 reduce-scatter.8

commit v10 on v9

--- a/solution.py
+++ b/solution.py
@@ -367,7 +367,20 @@
     queries, keys_rot = projected["queries"], projected["keys_rot"]
     values = projected["values"]
     log_total, attended = attention["log_total"], mixed_out["attended"]
-    attention_sum = ring_reduce_scatter(mixed_out["attn_partial"], "row", jnp.bfloat16)
+    attn_ring = RingScatter(ring_slots(mixed_out["attn_partial"], "row"), "row", jnp.bfloat16)
+    cot_count = len(cot_slots)
+    per_step = -(-cot_count // attn_ring.steps())
+
+    def cot_grads(index):
+        def piece(done):
+            chosen = cot_slots[index * per_step : (index + 1) * per_step]
+            return tuple(times_transpose(block, full_down) for block in chosen)
+
+        return piece
+
+    grad_act_parts = overlap(attn_ring, [cot_grads(index) for index in range(attn_ring.steps())])
+    grad_act_slots = [block for part in grad_act_parts for block in part]
+    attention_sum = attn_ring.result()
     middle = inputs + attention_sum
     normed_second = layer_norm(middle).astype(jnp.bfloat16)
     second_ring = RingGather(normed_second, "row")
@@ -393,7 +406,7 @@
 
     def ffn_backward(slot):
         gate_lin, up_lin = gate_slots[slot], up_slots[slot]
-        grad_activation = times_transpose(cot_slots[slot], full_down)
+        grad_activation = grad_act_slots[slot]
         sigma = jax.nn.sigmoid(gate_lin)
         grad_gate = grad_activation * up_lin * sigma * (1.0 + gate_lin * (1.0 - sigma))
         grad_up = grad_activation * gate_lin * sigma

time: 732 us -> 731 us (level)
  transfers between devices with their start and end apart: 32 -> 32, of which waited for: 16 -> 16; matrix products, arithmetic and copies ran while one was open for 57% -> 58% of each run, Pallas kernels for 0% -> 0%
where the time goes in v10:
time: 731 us; the launch traced here: 725 us
  matrix products  278 us (38%)
  waiting for transfers between devices  254 us (35%)
  other arithmetic  102 us (14%)
  local copies, waits for them, and re-layouts  63.4 us (9%)
  between operations  15.5 us (2%)
  starting transfers between devices  11.5 us (2%)
    ppermute x12, waiting for transfers between devices, send(): lax.ppermute(self.pending, self.axis, [(j, (j + 1) % n) for j in range(n)])  130 us
    ppermute x12, waiting for transfers between devices, send(): lax.ppermute(value.astype(self.send_dtype), self.axis, [(j, (j + 1) % n)...  105 us
    dot_general x11, matrix products, times_transpose(): lax.dot_general(left, right, (((1,), (1,)), ((), ())), preferred_element_...  88.8 us
    dot_general x10, matrix products, product(): return jnp.dot(left, right, preferred_element_type=jnp.float32)  68.5 us
    dot_general x4, matrix products, contract_rows(): lax.dot_general(left, right, (((0,), (0,)), ((), ())), preferred_element_...  56.7 us
    convert_element_type x1, other arithmetic, attend_backward(): grad_scores = (probs * (grad_probs - inner)).astype(jnp.bfloat16)  18.3 us
    reduce_scatter x4, waiting for transfers between devices, col_scatter(): lax.psum_scatter(low_part, COL, scatter_dimension=axis, tiled=True)  17.5 us
    dot_general x2, matrix products, attend_backward(): jnp.einsum('qhd,khd->hqk', grad_mixed, values, preferred_element_type=jnp...  15.9 us
  transfers between devices with their start and end apart: 32, of which 16 were waited for; matrix products, arithmetic and copies ran while one was open for 58% of the time, Pallas kernels for 0%

profile of v10, /device:TPU:0, one launch (start us, length us, event | category | flops | bytes accessed | tf_op | source)
XLA Modules:
  0.0 725.0 jit_solution(7909534739923859278)
XLA Ops:
  21.2 25.2 %collective-permute-done = bf16[256,2048]{1,0:T(8,128)(2,1)S(1)} collective-permute-done((bf16[256,2048]{1,0:T(8,128)(2,1)S(1)}, bf16[256,2048]{1,0:T(8,128)(2,1)S(1)}, u32[]{:S(2)}, u32[]{:S(2)}) %collective-permute-start) | collective-permute-done | bytes 1048608 | tf_op jit(solution)/shard_map/ppermute | solution.py:134
  47.9 24.7 %collective-permute-done.1 = bf16[256,2048]{1,0:T(8,128)(2,1)} collective-permute-done((bf16[256,2048]{1,0:T(8,128)(2,1)S(1)}, bf16[256,2048]{1,0:T(8,128)(2,1)}, u32[]{:S(2)}, u32[]{:S(2)}) %collective-permute-start.1) | collective-permute-done | bytes 1048608 | tf_op jit(solution)/shard_map/ppermute | solution.py:134
  82.1 16.1 %collective-permute-done.2 = bf16[256,2048]{1,0:T(8,128)(2,1)} collective-permute-done((bf16[256,2048]{1,0:T(8,128)(2,1)}, bf16[256,2048]{1,0:T(8,128)(2,1)}, u32[]{:S(2)}, u32[]{:S(2)}) %collective-permute-start.2) | collective-permute-done | bytes 1048608 | tf_op jit(solution)/shard_map/ppermute | solution.py:134
  101.2 10.0 %fusion.119 = f32[1024,1536]{1,0:T(8,128)S(1)} fusion(bf16[1024,2048]{1,0:T(8,128)(2,1)} %constant_dynamic-update-slice_fusion.8, bf16[2048,1536]{1,0:T(8,128)(2,1)} %all-gather.5.cloned.1.call-done), kind=kOutput, calls=%fused_computation.217 | convolution fusion | flops 6442450944 | bytes 16777216 | tf_op jit(solution)/shard_map/dot_general | solution.py:19
  161.1 18.9 %collective-permute-done.5 = bf16[256,2048]{1,0:T(8,128)(2,1)S(1)} collective-permute-done((bf16[256,2048]{1,0:T(8,128)(2,1)}, bf16[256,2048]{1,0:T(8,128)(2,1)S(1)}, u32[]{:S(2)}, u32[]{:S(2)}) %collective-permute-start.5) | collective-permute-done | bytes 1048608 | tf_op jit(solution)/shard_map/ppermute | solution.py:134
  194.3 9.8 %collective-permute-done.6 = bf16[256,2048]{1,0:T(8,128)(2,1)S(1)} collective-permute-done((bf16[256,2048]{1,0:T(8,128)(2,1)S(1)}, bf16[256,2048]{1,0:T(8,128)(2,1)S(1)}, u32[]{:S(2)}, u32[]{:S(2)}) %collective-permute-start.6) | collective-permute-done | bytes 1048608 | tf_op jit(solution)/shard_map/ppermute | solution.py:162
  213.3 14.3 %collective-permute-done.7 = bf16[256,2048]{1,0:T(8,128)(2,1)S(1)} collective-permute-done((bf16[256,2048]{1,0:T(8,128)(2,1)S(1)}, bf16[256,2048]{1,0:T(8,128)(2,1)S(1)}, u32[]{:S(2)}, u32[]{:S(2)}) %collective-permute-start.7) | collective-permute-done | bytes 1048608 | tf_op jit(solution)/shard_map/ppermute | solution.py:162
  228.0 22.0 %collective-permute-done.8 = bf16[256,2048]{1,0:T(8,128)(2,1)S(1)} collective-permute-done((bf16[256,2048]{1,0:T(8,128)(2,1)S(1)}, bf16[256,2048]{1,0:T(8,128)(2,1)S(1)}, u32[]{:S(2)}, u32[]{:S(2)}) %collective-permute-start.8) | collective-permute-done | bytes 1048608 | tf_op jit(solution)/shard_map/ppermute | solution.py:162
  290.9 12.0 %fusion.108 = f32[256,2048]{1,0:T(8,128)} fusion(bf16[2048,4096]{1,0:T(8,128)(2,1)} %all-gather.11.cloned.1.call-done, bf16[256,2048]{1,0:T(8,128)(2,1)} %copy-done.28, bf16[256,2048]{1,0:T(8,128)(2,1)S(1)} %get-tuple-element.243), kind=kOutput, calls=%fused_computation.207 | convolution fusion | flops 4299161600 | bytes 20971520 | tf_op jit(solution)/shard_map/dot_general | solution.py:29
  308.2 12.0 %convolution_convert_fusion.2 = bf16[256,2048]{1,0:T(8,128)(2,1)} fusion(bf16[2048,4096]{1,0:T(8,128)(2,1)} %all-gather.11.cloned.1.call-done, bf16[256,2048]{1,0:T(8,128)(2,1)} %get-tuple-element.249, bf16[256,2048]{1,0:T(8,128)(2,1)S(1)} %get-tuple-element.248), kind=kOutput, calls=%fused_computation.59 | convolution fusion | flops 4299685888 | bytes 19922944 | tf_op jit(solution)/shard_map/dot_general | solution.py:29
  341.3 11.9 %fusion.110 = f32[256,2048]{1,0:T(8,128)} fusion(bf16[2048,4096]{1,0:T(8,128)(2,1)} %all-gather.11.cloned.1.call-done, bf16[256,2048]{1,0:T(8,128)(2,1)} %copy-done.29, bf16[256,2048]{1,0:T(8,128)(2,1)S(1)} %get-tuple-element.246), kind=kOutput, calls=%fused_computation.209 | convolution fusion | flops 4299161600 | bytes 20971520 | tf_op jit(solution)/shard_map/dot_general | solution.py:29
  374.5 11.9 %fusion.109 = f32[256,2048]{1,0:T(8,128)} fusion(bf16[2048,4096]{1,0:T(8,128)(2,1)} %all-gather.11.cloned.1.call-done, bf16[256,2048]{1,0:T(8,128)(2,1)} %copy-done.21, bf16[256,2048]{1,0:T(8,128)(2,1)S(1)} %get-tuple-element.233), kind=kOutput, calls=%fused_computation.208 | convolution fusion | flops 4299161600 | bytes 20971520 | tf_op jit(solution)/shard_map/dot_general | solution.py:29
  390.0 12.8 %fusion.15 = bf16[2048,2048]{1,0:T(8,128)(2,1)} fusion(bf16[256,2048]{1,0:T(8,128)(2,1)S(1)} %copy-done.36, bf16[256,2048]{1,0:T(8,128)(2,1)S(1)} %copy-done.43, bf16[256,2048]{1,0:T(8,128)(2,1)S(1)} %copy-done.41, bf16[256,2048]{1,0:T(8,128)(2,1)S(1)} %copy-done.39, bf16[256,2048]{1,0:T(8,128)(2,1)} %copy-done.63, ...), kind=kOutput, calls=%fused_computation.26 | convolution fusion | flops 8623489024 | bytes 16777216 | tf_op jit(solution)/shard_map/dot_general | solution.py:23
  416.6 26.8 %fusion.2 = bf16[2048,4096]{1,0:T(8,128)(2,1)} fusion(bf16[256,4096]{1,0:T(8,128)(2,1)} %pad_maximum_fusion.3, bf16[256,4096]{1,0:T(8,128)(2,1)} %pad_maximum_fusion.2, bf16[256,2048]{1,0:T(8,128)(2,1)} %get-tuple-element.249, bf16[256,2048]{1,0:T(8,128)(2,1)} %copy-done.51, bf16[256,4096]{1,0:T(8,128)(2,1)} %pad_maximum_fusion.4, ...), kind=kOutput, calls=%fused_computation.5 | convolution fusion | flops 17238589440 | bytes 29360128 | tf_op jit(solution)/shard_map/dot_general | solution.py:23
  456.1 18.2 %collective-permute-done.16 = bf16[256,2048]{1,0:T(8,128)(2,1)} collective-permute-done((bf16[256,2048]{1,0:T(8,128)(2,1)}, bf16[256,2048]{1,0:T(8,128)(2,1)}, u32[]{:S(2)}, u32[]{:S(2)}) %collective-permute-start.16) | collective-permute-done | bytes 1048608 | tf_op jit(solution)/shard_map/ppermute | solution.py:134
  484.3 14.1 %collective-permute-done.17 = bf16[256,2048]{1,0:T(8,128)(2,1)S(1)} collective-permute-done((bf16[256,2048]{1,0:T(8,128)(2,1)}, bf16[256,2048]{1,0:T(8,128)(2,1)S(1)}, u32[]{:S(2)}, u32[]{:S(2)}) %collective-permute-start.17) | collective-permute-done | bytes 1048608 | tf_op jit(solution)/shard_map/ppermute | solution.py:134
  512.8 11.4 %multiply_reduce_fusion = (f32[2,1024]{1,0:T(2,128)S(1)}, f32[2,1024]{1,0:T(2,128)S(1)}, f32[2,1024,1024]{1,2,0:T(8,128)}) fusion(f32[2,1024,1024]{1,2,0:T(8,128)S(1)} %bitcast.131, f32[2,1024]{1,0:T(2,128)S(1)} %get-tuple-element.277, pred[1024,1024]{0,1:T(8,128)(4,1)S(1)} %copy-done.1, f32[2,1024,1024]{1,2,0:T(8,128)} %fusion.78, ...), kind=kOutput, calls=%fused_computation.16 | convolution fusion | flops 557838336 | bytes 35684352 | tf_op jit(solution)/shard_map/while/body/eval_jaxpr/qhd,khd->hqk/dot_general | solution.py:307
  524.2 18.3 %multiply_convert_fusion = (bf16[2,1024,1024]{1,2,0:T(8,128)(2,1)}, bf16[2,1024,1024]{1,2,0:T(8,128)(2,1)}) fusion(f32[2,1024,1024]{1,2,0:T(8,128)} %get-tuple-element.282, f32[2,1024,1024]{1,2,0:T(8,128)} %fusion.80, f32[2,1024]{1,0:T(2,128)S(1)} %get-tuple-element.224, f32[2,1024]{1,0:T(2,128)S(1)} %get-tuple-element.277, ...), kind=kLoop, calls=%fused_computation.15 | loop fusion | flops 25165824 | bytes 43024384 | tf_op jit(solution)/shard_map/while/body/eval_jaxpr/convert_element_type | solution.py:309
  582.7 14.8 %collective-permute-done.19 = bf16[256,2048]{1,0:T(8,128)(2,1)} collective-permute-done((bf16[256,2048]{1,0:T(8,128)(2,1)}, bf16[256,2048]{1,0:T(8,128)(2,1)}, u32[]{:S(2)}, u32[]{:S(2)}) %collective-permute-start.19) | collective-permute-done | bytes 1048608 | tf_op jit(solution)/shard_map/ppermute | solution.py:162
  612.0 10.9 %fusion.111 = f32[1024,2048]{1,0:T(8,128)} fusion(bf16[2048,1536]{1,0:T(8,128)(2,1)} %all-gather.5.cloned.1.call-done, bf16[1024,512]{0,1:T(8,128)(2,1)S(1)} %bitcast.139, bf16[1024,512]{0,1:T(8,128)(2,1)S(1)} %bitcast.135, bf16[1024,512]{0,1:T(8,128)(2,1)S(1)} %bitcast.137), kind=kOutput, calls=%fused_computation.210 | convolution fusion | flops 6451888128 | bytes 17825792 | tf_op jit(solution)/shard_map/dot_general | solution.py:29
  623.0 11.1 %convolution_convert_fusion = bf16[2048,1536]{1,0:T(8,128)(2,1)} fusion(bf16[1024,2048]{1,0:T(8,128)(2,1)} %constant_dynamic-update-slice_fusion.8, bf16[1024,1536]{0,1:T(8,128)(2,1)S(1)} %pad_maximum_fusion), kind=kOutput, calls=%fused_computation.23 | convolution fusion | flops 6445596672 | bytes 13631488 | tf_op jit(solution)/shard_map/dot_general | solution.py:23
  640.5 21.6 %collective-permute-done.21 = bf16[256,2048]{1,0:T(8,128)(2,1)S(1)} collective-permute-done((bf16[256,2048]{1,0:T(8,128)(2,1)S(1)}, bf16[256,2048]{1,0:T(8,128)(2,1)S(1)}, u32[]{:S(2)}, u32[]{:S(2)}) %collective-permute-start.21) | collective-permute-done | bytes 1048608 | tf_op jit(solution)/shard_map/ppermute | solution.py:162
  662.6 18.6 %collective-permute-done.22 = bf16[256,2048]{1,0:T(8,128)(2,1)S(1)} collective-permute-done((bf16[256,2048]{1,0:T(8,128)(2,1)S(1)}, bf16[256,2048]{1,0:T(8,128)(2,1)S(1)}, u32[]{:S(2)}, u32[]{:S(2)}) %collective-permute-start.22) | collective-permute-done | bytes 1048608 | tf_op jit(solution)/shard_map/ppermute | solution.py:162
  687.2 17.5 %reduce-scatter.9.cloned.1.call-done = bf16[256,1536]{1,0:T(8,128)(2,1)} async-done(((bf16[2048,1536]{1,0:T(8,128)(2,1)}), bf16[256,1536]{1,0:T(8,128)(2,1)}) %reduce-scatter.9.cloned.1.call-update) | async-done | bytes 786448 | tf_op jit(solution)/shard_map/reduce_scatter | solution.py:222
  (333 shorter events, 324.5 us)
Async XLA Ops:
  7.2 94.0 %all-gather.5.cloned.1.call-start = ((), (), s32[]{:S(2)}) async-start(), calls=%async_computation.4 | async-start | bytes 7077888 | tf_op jit(solution)/shard_map/all_gather | solution.py:217
  9.4 146.8 %all-gather.7.cloned.1.call-start = ((), (), s32[]{:S(2)}) async-start(), calls=%async_computation.5 | async-start | bytes 2359296 | tf_op jit(solution)/shard_map/all_gather | solution.py:217
  10.2 171.1 %all-gather.9.cloned.1.call-start = ((), (), s32[]{:S(2)}) async-start(), calls=%async_computation.6 | async-start | bytes 9437184 | tf_op jit(solution)/shard_map/all_gather | solution.py:217
  10.9 240.4 %all-gather.11.cloned.1.call-start = ((), (), s32[]{:S(2)}) async-start(), calls=%async_computation.7 | async-start | bytes 18874368 | tf_op jit(solution)/shard_map/all_gather | solution.py:217
  12.5 468.9 %reduce-scatter.5.cloned.1.call-start = ((), (), s32[]{:S(2)}) async-start(), calls=%async_computation.8 | async-start | bytes 9437184 | tf_op jit(solution)/shard_map/reduce_scatter | solution.py:222
  18.1 28.2 %collective-permute-start = (bf16[256,2048]{1,0:T(8,128)(2,1)S(1)}, bf16[256,2048]{1,0:T(8,128)(2,1)S(1)}, u32[]{:S(2)}, u32[]{:S(2)}) collective-permute-start(bf16[256,2048]{1,0:T(8,128)(2,1)S(1)} %get-tuple-element.232), channel_id=1, source_target_pairs={{0,8},{8,16},{16,24},{24,0},{1,9},{9,17},{17,25},{25,1},{2,10},{10... | collective-permute-start | bytes 3145736 | tf_op jit(solution)/shard_map/ppermute | solution.py:134
  46.4 26.2 %collective-permute-start.1 = (bf16[256,2048]{1,0:T(8,128)(2,1)S(1)}, bf16[256,2048]{1,0:T(8,128)(2,1)}, u32[]{:S(2)}, u32[]{:S(2)}) collective-permute-start(bf16[256,2048]{1,0:T(8,128)(2,1)S(1)} %collective-permute-done), channel_id=1, source_target_pairs={{0,8},{8,16},{16,24},{24,0},{1,9},{9,17},{17,25},{25,1},{2,10},{10... | collective-permute-start | bytes 3145736 | tf_op jit(solution)/shard_map/ppermute | solution.py:134
  72.6 25.6 %collective-permute-start.2 = (bf16[256,2048]{1,0:T(8,128)(2,1)}, bf16[256,2048]{1,0:T(8,128)(2,1)}, u32[]{:S(2)}, u32[]{:S(2)}) collective-permute-start(bf16[256,2048]{1,0:T(8,128)(2,1)} %collective-permute-done.1), channel_id=1, source_target_pairs={{0,8},{8,16},{16,24},{24,0},{1,9},{9,17},{17,25},{25,1},{2,10},{10... | collective-permute-start | bytes 3145736 | tf_op jit(solution)/shard_map/ppermute | solution.py:134
  100.6 30.7 %collective-permute-start.3 = (bf16[256,2048]{1,0:T(8,128)(2,1)}, bf16[256,2048]{1,0:T(8,128)(2,1)}, u32[]{:S(2)}, u32[]{:S(2)}) collective-permute-start(bf16[256,2048]{1,0:T(8,128)(2,1)} %param.19), channel_id=1, source_target_pairs={{0,8},{8,16},{16,24},{24,0},{1,9},{9,17},{17,25},{25,1},{2,10},{10... | collective-permute-start | bytes 3145736 | tf_op jit(solution)/shard_map/ppermute | solution.py:134
  131.3 24.9 %collective-permute-start.4 = (bf16[256,2048]{1,0:T(8,128)(2,1)}, bf16[256,2048]{1,0:T(8,128)(2,1)}, u32[]{:S(2)}, u32[]{:S(2)}) collective-permute-start(bf16[256,2048]{1,0:T(8,128)(2,1)} %collective-permute-done.3), channel_id=1, source_target_pairs={{0,8},{8,16},{16,24},{24,0},{1,9},{9,17},{17,25},{25,1},{2,10},{10... | collective-permute-start | bytes 3145736 | tf_op jit(solution)/shard_map/ppermute | solution.py:134
  156.2 23.8 %collective-permute-start.5 = (bf16[256,2048]{1,0:T(8,128)(2,1)}, bf16[256,2048]{1,0:T(8,128)(2,1)S(1)}, u32[]{:S(2)}, u32[]{:S(2)}) collective-permute-start(bf16[256,2048]{1,0:T(8,128)(2,1)} %collective-permute-done.4), channel_id=1, source_target_pairs={{0,8},{8,16},{16,24},{24,0},{1,9},{9,17},{17,25},{25,1},{2,10},{10... | collective-permute-start | bytes 3145736 | tf_op jit(solution)/shard_map/ppermute | solution.py:134
  273.9 28.9 %collective-permute-start.10 = (bf16[256,2048]{1,0:T(8,128)(2,1)}, bf16[256,2048]{1,0:T(8,128)(2,1)}, u32[]{:S(2)}, u32[]{:S(2)}) collective-permute-start(bf16[256,2048]{1,0:T(8,128)(2,1)} %collective-permute-done.9), channel_id=1, source_target_pairs={{0,8},{8,16},{16,24},{24,0},{1,9},{9,17},{17,25},{25,1},{2,10},{10... | collective-permute-start | bytes 3145736 | tf_op jit(solution)/shard_map/ppermute | solution.py:134
  302.9 34.5 %collective-permute-start.11 = (bf16[256,2048]{1,0:T(8,128)(2,1)}, bf16[256,2048]{1,0:T(8,128)(2,1)}, u32[]{:S(2)}, u32[]{:S(2)}) collective-permute-start(bf16[256,2048]{1,0:T(8,128)(2,1)} %collective-permute-done.10), channel_id=1, source_target_pairs={{0,8},{8,16},{16,24},{24,0},{1,9},{9,17},{17,25},{25,1},{2,10},{10... | collective-permute-start | bytes 3145736 | tf_op jit(solution)/shard_map/ppermute | solution.py:134
  320.1 33.1 %collective-permute-start.12 = (bf16[256,2048]{1,0:T(8,128)(2,1)}, bf16[256,2048]{1,0:T(8,128)(2,1)}, u32[]{:S(2)}, u32[]{:S(2)}) collective-permute-start(bf16[256,2048]{1,0:T(8,128)(2,1)} %convolution_convert_fusion.2), channel_id=1, source_target_pairs={{0,8},{8,16},{16,24},{24,0},{1,9},{9,17},{17,25},{25,1},{2,10},{10... | collective-permute-start | bytes 3145736 | tf_op jit(solution)/shard_map/ppermute | solution.py:162
  356.4 30.1 %collective-permute-start.13 = (bf16[256,2048]{1,0:T(8,128)(2,1)}, bf16[256,2048]{1,0:T(8,128)(2,1)}, u32[]{:S(2)}, u32[]{:S(2)}) collective-permute-start(bf16[256,2048]{1,0:T(8,128)(2,1)} %add_convert_fusion.8), channel_id=1, source_target_pairs={{0,8},{8,16},{16,24},{24,0},{1,9},{9,17},{17,25},{25,1},{2,10},{10... | collective-permute-start | bytes 3145736 | tf_op jit(solution)/shard_map/ppermute | solution.py:162
  406.6 227.5 %reduce-scatter.7.cloned.1.call-start = ((), (), s32[]{:S(2)}) async-start(), calls=%async_computation.9 | async-start | bytes 18874368 | tf_op jit(solution)/shard_map/reduce_scatter | solution.py:222
  416.4 27.0 %collective-permute-start.15 = (bf16[256,2048]{1,0:T(8,128)(2,1)}, bf16[256,2048]{1,0:T(8,128)(2,1)S(1)}, u32[]{:S(2)}, u32[]{:S(2)}) collective-permute-start(bf16[256,2048]{1,0:T(8,128)(2,1)} %get-tuple-element.227), channel_id=1, source_target_pairs={{0,8},{8,16},{16,24},{24,0},{1,9},{9,17},{17,25},{25,1},{2,10},{10... | collective-permute-start | bytes 3145736 | tf_op jit(solution)/shard_map/ppermute | solution.py:134
  444.4 241.0 %reduce-scatter.11.cloned.1.call-start = ((), (), s32[]{:S(2)}) async-start(), calls=%async_computation.11 | async-start | bytes 2359296 | tf_op jit(solution)/shard_map/reduce_scatter | solution.py:222
  446.9 27.4 %collective-permute-start.16 = (bf16[256,2048]{1,0:T(8,128)(2,1)}, bf16[256,2048]{1,0:T(8,128)(2,1)}, u32[]{:S(2)}, u32[]{:S(2)}) collective-permute-start(bf16[256,2048]{1,0:T(8,128)(2,1)} %copy-done.45), channel_id=1, source_target_pairs={{0,8},{8,16},{16,24},{24,0},{1,9},{9,17},{17,25},{25,1},{2,10},{10... | collective-permute-start | bytes 3145736 | tf_op jit(solution)/shard_map/ppermute | solution.py:134
  474.3 24.0 %collective-permute-start.17 = (bf16[256,2048]{1,0:T(8,128)(2,1)}, bf16[256,2048]{1,0:T(8,128)(2,1)S(1)}, u32[]{:S(2)}, u32[]{:S(2)}) collective-permute-start(bf16[256,2048]{1,0:T(8,128)(2,1)} %collective-permute-done.16), channel_id=1, source_target_pairs={{0,8},{8,16},{16,24},{24,0},{1,9},{9,17},{17,25},{25,1},{2,10},{10... | collective-permute-start | bytes 3145736 | tf_op jit(solution)/shard_map/ppermute | solution.py:134
  499.4 68.3 %collective-permute-start.18 = (bf16[256,2048]{1,0:T(8,128)(2,1)}, bf16[256,2048]{1,0:T(8,128)(2,1)}, u32[]{:S(2)}, u32[]{:S(2)}) collective-permute-start(bf16[256,2048]{1,0:T(8,128)(2,1)} %fusion.128), channel_id=1, source_target_pairs={{0,8},{8,16},{16,24},{24,0},{1,9},{9,17},{17,25},{25,1},{2,10},{10... | collective-permute-start | bytes 3145736 | tf_op jit(solution)/shard_map/ppermute | solution.py:162
  570.4 27.0 %collective-permute-start.19 = (bf16[256,2048]{1,0:T(8,128)(2,1)}, bf16[256,2048]{1,0:T(8,128)(2,1)}, u32[]{:S(2)}, u32[]{:S(2)}) collective-permute-start(bf16[256,2048]{1,0:T(8,128)(2,1)} %add_convert_fusion.6), channel_id=1, source_target_pairs={{0,8},{8,16},{16,24},{24,0},{1,9},{9,17},{17,25},{25,1},{2,10},{10... | collective-permute-start | bytes 3145736 | tf_op jit(solution)/shard_map/ppermute | solution.py:162
  574.0 130.6 %reduce-scatter.9.cloned.1.call-start = ((), (), s32[]{:S(2)}) async-start(), calls=%async_computation.10 | async-start | bytes 7077888 | tf_op jit(solution)/shard_map/reduce_scatter | solution.py:222
  682.4 29.4 %collective-permute-start.23 = (bf16[256,2048]{1,0:T(8,128)(2,1)}, bf16[256,2048]{1,0:T(8,128)(2,1)S(1)}, u32[]{:S(2)}, u32[]{:S(2)}) collective-permute-start(bf16[256,2048]{1,0:T(8,128)(2,1)} %add_convert_fusion), channel_id=1, source_target_pairs={{0,8},{8,16},{16,24},{24,0},{1,9},{9,17},{17,25},{25,1},{2,10},{10... | collective-permute-start | bytes 3145736 | tf_op jit(solution)/shard_map/ppermute | solution.py:162
  (86 other events, 966.0 us)
Sparse Core Ops, SparseCore 0:
  10.5 48.1 all-gather.4
  60.5 28.0 all-gather.6
  90.5 55.8 all-gather.8
  148.7 89.7 all-gather.10
  406.7 68.7 reduce-scatter.4
  478.9 116.1 reduce-scatter.6
  598.4 41.1 reduce-scatter.10
  642.9 61.6 reduce-scatter.8

commit v11 on v10

--- a/solution.py
+++ b/solution.py
@@ -422,7 +422,7 @@
         second_ring_back.send()
         slot = order[index + 1]
         value = ffn_backward(slot)
-        if slot == 0:
+        if index == 0:
             grad_down_w = contract_rows(
                 jnp.concatenate(act_slots, axis=0), jnp.concatenate(cot_slots, axis=0)
             )
@@ -431,7 +431,7 @@
             (second_ring_back.pending, value)
         )
         grad_gu_slots[slot], second_ring_back.slots[slot] = value[0], value[1]
-        if slot == 0:
+        if index == 0:
             grad_down_w = value[2]
     grad_second = second_ring_back.result()
     down_sum = col_scatter(grad_down_w, 1)
@@ -486,7 +486,10 @@
         ).astype(jnp.bfloat16)
         return (grad_qkv, times_transpose(grad_qkv, full_qkv))
 
-    pieces = [heads_backward(0, half), heads_backward(half, heads_local), finish]
+    def second_group_and_finish(done):
+        return finish(done + (heads_backward(half, heads_local)(done),))
+
+    pieces = [heads_backward(0, half), second_group_and_finish]
     grad_qkv, first_partial = overlap(ffn_ring, pieces)[-1]
     ffn_sum = ffn_ring.result()
     output = (middle + ffn_sum).astype(jnp.bfloat16)

time: 731 us -> 734 us (level)
  waiting for transfers between devices: 254 us -> 242 us
  starting transfers between devices: 11.5 us -> 20.1 us
    reduce_scatter x4, waiting for transfers between devices: 17.5 us -> 0.03 us  [col_scatter(): lax.psum_scatter(low_part, COL, scatter_dimension=axis, tiled=True)]
  transfers between devices with their start and end apart: 32 -> 32, of which waited for: 16 -> 18; matrix products, arithmetic and copies ran while one was open for 58% -> 60% of each run, Pallas kernels for 0% -> 0%
where the time goes in v11:
time: 734 us; the launch traced here: 728 us
  matrix products  285 us (39%)
  waiting for transfers between devices  242 us (33%)
  other arithmetic  103 us (14%)
  local copies, waits for them, and re-layouts  62 us (8%)
  starting transfers between devices  20.1 us (3%)
  between operations  15.8 us (2%)
    ppermute x12, waiting for transfers between devices, send(): lax.ppermute(self.pending, self.axis, [(j, (j + 1) % n) for j in range(n)])  134 us
    ppermute x12, waiting for transfers between devices, send(): lax.ppermute(value.astype(self.send_dtype), self.axis, [(j, (j + 1) % n)...  107 us
    dot_general x11, matrix products, times_transpose(): lax.dot_general(left, right, (((1,), (1,)), ((), ())), preferred_element_...  90.8 us
    dot_general x10, matrix products, product(): return jnp.dot(left, right, preferred_element_type=jnp.float32)  72.3 us
    dot_general x4, matrix products, contract_rows(): lax.dot_general(left, right, (((0,), (0,)), ((), ())), preferred_element_...  55.8 us
    convert_element_type x1, other arithmetic, attend_backward(): grad_scores = (probs * (grad_probs - inner)).astype(jnp.bfloat16)  17.2 us
    dot_general x2, matrix products, attend_backward(): jnp.einsum('qhd,khd->hqk', grad_mixed, values, preferred_element_type=jnp...  16 us
    dot_general x3, matrix products, masked_scores(): jnp.einsum('qhd,khd->hqk', queries, keys_rot, preferred_element_type=jnp....  15.9 us
  transfers between devices with their start and end apart: 32, of which 18 were waited for; matrix products, arithmetic and copies ran while one was open for 60% of the time, Pallas kernels for 0%

profile of v11, /device:TPU:0, one launch (start us, length us, event | category | flops | bytes accessed | tf_op | source)
XLA Modules:
  0.0 727.6 jit_solution(12114710536162264187)
XLA Ops:
  21.2 25.2 %collective-permute-done = bf16[256,2048]{1,0:T(8,128)(2,1)S(1)} collective-permute-done((bf16[256,2048]{1,0:T(8,128)(2,1)S(1)}, bf16[256,2048]{1,0:T(8,128)(2,1)S(1)}, u32[]{:S(2)}, u32[]{:S(2)}) %collective-permute-start) | collective-permute-done | bytes 1048608 | tf_op jit(solution)/shard_map/ppermute | solution.py:134
  47.9 24.7 %collective-permute-done.1 = bf16[256,2048]{1,0:T(8,128)(2,1)} collective-permute-done((bf16[256,2048]{1,0:T(8,128)(2,1)S(1)}, bf16[256,2048]{1,0:T(8,128)(2,1)}, u32[]{:S(2)}, u32[]{:S(2)}) %collective-permute-start.1) | collective-permute-done | bytes 1048608 | tf_op jit(solution)/shard_map/ppermute | solution.py:134
  82.1 16.1 %collective-permute-done.2 = bf16[256,2048]{1,0:T(8,128)(2,1)} collective-permute-done((bf16[256,2048]{1,0:T(8,128)(2,1)}, bf16[256,2048]{1,0:T(8,128)(2,1)}, u32[]{:S(2)}, u32[]{:S(2)}) %collective-permute-start.2) | collective-permute-done | bytes 1048608 | tf_op jit(solution)/shard_map/ppermute | solution.py:134
  100.8 10.1 %fusion.122 = f32[1024,1536]{1,0:T(8,128)S(1)} fusion(bf16[1024,2048]{1,0:T(8,128)(2,1)} %constant_dynamic-update-slice_fusion.4, bf16[2048,1536]{1,0:T(8,128)(2,1)} %all-gather.5.cloned.1.call-done), kind=kOutput, calls=%fused_computation.218 | convolution fusion | flops 6442450944 | bytes 16777216 | tf_op jit(solution)/shard_map/dot_general | solution.py:19
  161.1 19.1 %collective-permute-done.5 = bf16[256,2048]{1,0:T(8,128)(2,1)S(1)} collective-permute-done((bf16[256,2048]{1,0:T(8,128)(2,1)}, bf16[256,2048]{1,0:T(8,128)(2,1)S(1)}, u32[]{:S(2)}, u32[]{:S(2)}) %collective-permute-start.5) | collective-permute-done | bytes 1048608 | tf_op jit(solution)/shard_map/ppermute | solution.py:134
  194.4 9.8 %collective-permute-done.6 = bf16[256,2048]{1,0:T(8,128)(2,1)S(1)} collective-permute-done((bf16[256,2048]{1,0:T(8,128)(2,1)S(1)}, bf16[256,2048]{1,0:T(8,128)(2,1)S(1)}, u32[]{:S(2)}, u32[]{:S(2)}) %collective-permute-start.6) | collective-permute-done | bytes 1048608 | tf_op jit(solution)/shard_map/ppermute | solution.py:162
  213.4 14.4 %collective-permute-done.7 = bf16[256,2048]{1,0:T(8,128)(2,1)S(1)} collective-permute-done((bf16[256,2048]{1,0:T(8,128)(2,1)S(1)}, bf16[256,2048]{1,0:T(8,128)(2,1)S(1)}, u32[]{:S(2)}, u32[]{:S(2)}) %collective-permute-start.7) | collective-permute-done | bytes 1048608 | tf_op jit(solution)/shard_map/ppermute | solution.py:162
  228.1 22.0 %collective-permute-done.8 = bf16[256,2048]{1,0:T(8,128)(2,1)S(1)} collective-permute-done((bf16[256,2048]{1,0:T(8,128)(2,1)S(1)}, bf16[256,2048]{1,0:T(8,128)(2,1)S(1)}, u32[]{:S(2)}, u32[]{:S(2)}) %collective-permute-start.8) | collective-permute-done | bytes 1048608 | tf_op jit(solution)/shard_map/ppermute | solution.py:162
  288.5 9.4 %collective-permute-done.10 = bf16[256,2048]{1,0:T(8,128)(2,1)} collective-permute-done((bf16[256,2048]{1,0:T(8,128)(2,1)}, bf16[256,2048]{1,0:T(8,128)(2,1)}, u32[]{:S(2)}, u32[]{:S(2)}) %collective-permute-start.10) | collective-permute-done | bytes 1048608 | tf_op jit(solution)/shard_map/ppermute | solution.py:134
  300.1 12.0 %convolution_convert_fusion.2 = bf16[256,2048]{1,0:T(8,128)(2,1)} fusion(bf16[2048,4096]{1,0:T(8,128)(2,1)} %all-gather.11.cloned.1.call-done, bf16[256,2048]{1,0:T(8,128)(2,1)} %get-tuple-element.241, bf16[256,2048]{1,0:T(8,128)(2,1)S(1)} %get-tuple-element.240), kind=kOutput, calls=%fused_computation.59 | convolution fusion | flops 4299685888 | bytes 19922944 | tf_op jit(solution)/shard_map/dot_general | solution.py:29
  345.0 12.8 %fusion.15 = bf16[2048,2048]{1,0:T(8,128)(2,1)} fusion(bf16[256,2048]{1,0:T(8,128)(2,1)S(1)} %get-tuple-element.237, bf16[256,2048]{1,0:T(8,128)(2,1)S(1)} %get-tuple-element.177, bf16[256,2048]{1,0:T(8,128)(2,1)S(1)} %copy-done.42, bf16[256,2048]{1,0:T(8,128)(2,1)S(1)} %copy-done.40, bf16[256,2048]{1,0:T(8,128)(2,1)S(1)} %copy-done.64, ...), kind=kOutput, calls=%fused_computation.26 | convolution fusion | flops 8623489024 | bytes 16777216 | tf_op jit(solution)/shard_map/dot_general | solution.py:23
  357.7 12.3 %fusion.113 = f32[256,2048]{1,0:T(8,128)} fusion(bf16[2048,4096]{1,0:T(8,128)(2,1)} %all-gather.11.cloned.1.call-done, bf16[256,2048]{1,0:T(8,128)(2,1)} %copy-done.29, bf16[256,2048]{1,0:T(8,128)(2,1)} %copy-done.28), kind=kOutput, calls=%fused_computation.210 | convolution fusion | flops 4299161600 | bytes 20971520 | tf_op jit(solution)/shard_map/dot_general | solution.py:29
  382.3 13.6 %fusion.112 = f32[256,2048]{1,0:T(8,128)} fusion(bf16[2048,4096]{1,0:T(8,128)(2,1)} %all-gather.11.cloned.1.call-done, bf16[256,2048]{1,0:T(8,128)(2,1)} %get-tuple-element.226, bf16[256,2048]{1,0:T(8,128)(2,1)S(1)} %get-tuple-element.225), kind=kOutput, calls=%fused_computation.209 | convolution fusion | flops 4299161600 | bytes 20971520 | tf_op jit(solution)/shard_map/dot_general | solution.py:29
  408.3 12.7 %fusion.111 = f32[256,2048]{1,0:T(8,128)} fusion(bf16[2048,4096]{1,0:T(8,128)(2,1)} %all-gather.11.cloned.1.call-done, bf16[256,2048]{1,0:T(8,128)(2,1)} %copy-done.27, bf16[256,2048]{1,0:T(8,128)(2,1)} %copy-done.26), kind=kOutput, calls=%fused_computation.208 | convolution fusion | flops 4299161600 | bytes 20971520 | tf_op jit(solution)/shard_map/dot_general | solution.py:29
  435.2 25.9 %fusion.2 = bf16[2048,4096]{1,0:T(8,128)(2,1)} fusion(bf16[256,4096]{1,0:T(8,128)(2,1)} %pad_maximum_fusion.5, bf16[256,4096]{1,0:T(8,128)(2,1)} %pad_maximum_fusion.4, bf16[256,2048]{1,0:T(8,128)(2,1)} %get-tuple-element.241, bf16[256,2048]{1,0:T(8,128)(2,1)} %copy-done.50, bf16[256,4096]{1,0:T(8,128)(2,1)} %pad_maximum_fusion.6, ...), kind=kOutput, calls=%fused_computation.5 | convolution fusion | flops 17238589440 | bytes 29360128 | tf_op jit(solution)/shard_map/dot_general | solution.py:23
  478.9 11.9 %collective-permute-done.16 = bf16[256,2048]{1,0:T(8,128)(2,1)} collective-permute-done((bf16[256,2048]{1,0:T(8,128)(2,1)}, bf16[256,2048]{1,0:T(8,128)(2,1)}, u32[]{:S(2)}, u32[]{:S(2)}) %collective-permute-start.16) | collective-permute-done | bytes 1048608 | tf_op jit(solution)/shard_map/ppermute | solution.py:134
  501.2 16.1 %collective-permute-done.17 = bf16[256,2048]{1,0:T(8,128)(2,1)S(1)} collective-permute-done((bf16[256,2048]{1,0:T(8,128)(2,1)}, bf16[256,2048]{1,0:T(8,128)(2,1)S(1)}, u32[]{:S(2)}, u32[]{:S(2)}) %collective-permute-start.17) | collective-permute-done | bytes 1048608 | tf_op jit(solution)/shard_map/ppermute | solution.py:134
  531.4 11.0 %multiply_reduce_fusion = (f32[2,1024]{1,0:T(2,128)S(1)}, f32[2,1024]{1,0:T(2,128)S(1)}, f32[2,1024,1024]{1,2,0:T(8,128)}) fusion(f32[2,1024,1024]{1,2,0:T(8,128)S(1)} %bitcast.131, f32[2,1024]{1,0:T(2,128)S(1)} %get-tuple-element.269, pred[1024,1024]{0,1:T(8,128)(4,1)S(1)} %copy-done.1, f32[2,1024,1024]{1,2,0:T(8,128)} %fusion.81, ...), kind=kOutput, calls=%fused_computation.16 | convolution fusion | flops 557838336 | bytes 35684352 | tf_op jit(solution)/shard_map/while/body/eval_jaxpr/qhd,khd->hqk/dot_general | solution.py:307
  542.4 17.2 %multiply_convert_fusion = (bf16[2,1024,1024]{1,2,0:T(8,128)(2,1)}, bf16[2,1024,1024]{1,2,0:T(8,128)(2,1)}) fusion(f32[2,1024,1024]{1,2,0:T(8,128)} %get-tuple-element.274, f32[2,1024,1024]{1,2,0:T(8,128)} %fusion.83, f32[2,1024]{1,0:T(2,128)S(1)} %get-tuple-element.216, f32[2,1024]{1,0:T(2,128)S(1)} %get-tuple-element.269, ...), kind=kLoop, calls=%fused_computation.15 | loop fusion | flops 25165824 | bytes 43024384 | tf_op jit(solution)/shard_map/while/body/eval_jaxpr/convert_element_type | solution.py:309
  610.3 11.0 %fusion.114 = f32[1024,2048]{1,0:T(8,128)} fusion(bf16[2048,1536]{1,0:T(8,128)(2,1)} %all-gather.5.cloned.1.call-done, bf16[1024,512]{0,1:T(8,128)(2,1)S(1)} %bitcast.139, bf16[1024,512]{0,1:T(8,128)(2,1)S(1)} %bitcast.135, bf16[1024,512]{0,1:T(8,128)(2,1)S(1)} %bitcast.137), kind=kOutput, calls=%fused_computation.211 | convolution fusion | flops 6451888128 | bytes 17825792 | tf_op jit(solution)/shard_map/dot_general | solution.py:29
  621.2 11.2 %convolution_convert_fusion = bf16[2048,1536]{1,0:T(8,128)(2,1)} fusion(bf16[1024,2048]{1,0:T(8,128)(2,1)} %constant_dynamic-update-slice_fusion.4, bf16[1024,1536]{0,1:T(8,128)(2,1)S(1)} %pad_maximum_fusion), kind=kOutput, calls=%fused_computation.23 | convolution fusion | flops 6445596672 | bytes 13631488 | tf_op jit(solution)/shard_map/dot_general | solution.py:23
  645.3 15.3 %collective-permute-done.21 = bf16[256,2048]{1,0:T(8,128)(2,1)S(1)} collective-permute-done((bf16[256,2048]{1,0:T(8,128)(2,1)S(1)}, bf16[256,2048]{1,0:T(8,128)(2,1)S(1)}, u32[]{:S(2)}, u32[]{:S(2)}) %collective-permute-start.21) | collective-permute-done | bytes 1048608 | tf_op jit(solution)/shard_map/ppermute | solution.py:162
  662.9 18.3 %collective-permute-done.20 = bf16[256,2048]{1,0:T(8,128)(2,1)S(1)} collective-permute-done((bf16[256,2048]{1,0:T(8,128)(2,1)S(1)}, bf16[256,2048]{1,0:T(8,128)(2,1)S(1)}, u32[]{:S(2)}, u32[]{:S(2)}) %collective-permute-start.20) | collective-permute-done | bytes 1048608 | tf_op jit(solution)/shard_map/ppermute | solution.py:162
  681.2 13.1 %collective-permute-done.22 = bf16[256,2048]{1,0:T(8,128)(2,1)S(1)} collective-permute-done((bf16[256,2048]{1,0:T(8,128)(2,1)S(1)}, bf16[256,2048]{1,0:T(8,128)(2,1)S(1)}, u32[]{:S(2)}, u32[]{:S(2)}) %collective-permute-start.22) | collective-permute-done | bytes 1048608 | tf_op jit(solution)/shard_map/ppermute | solution.py:162
  (324 shorter events, 346.7 us)
Async XLA Ops:
  7.2 93.6 %all-gather.5.cloned.1.call-start = ((), (), s32[]{:S(2)}) async-start(), calls=%async_computation.4 | async-start | bytes 7077888 | tf_op jit(solution)/shard_map/all_gather | solution.py:217
  9.4 146.8 %all-gather.7.cloned.1.call-start = ((), (), s32[]{:S(2)}) async-start(), calls=%async_computation.5 | async-start | bytes 2359296 | tf_op jit(solution)/shard_map/all_gather | solution.py:217
  10.2 171.2 %all-gather.9.cloned.1.call-start = ((), (), s32[]{:S(2)}) async-start(), calls=%async_computation.6 | async-start | bytes 9437184 | tf_op jit(solution)/shard_map/all_gather | solution.py:217
  10.9 240.5 %all-gather.11.cloned.1.call-start = ((), (), s32[]{:S(2)}) async-start(), calls=%async_computation.7 | async-start | bytes 18874368 | tf_op jit(solution)/shard_map/all_gather | solution.py:217
  12.5 485.5 %reduce-scatter.5.cloned.1.call-start = ((), (), s32[]{:S(2)}) async-start(), calls=%async_computation.8 | async-start | bytes 9437184 | tf_op jit(solution)/shard_map/reduce_scatter | solution.py:222
  18.1 28.2 %collective-permute-start = (bf16[256,2048]{1,0:T(8,128)(2,1)S(1)}, bf16[256,2048]{1,0:T(8,128)(2,1)S(1)}, u32[]{:S(2)}, u32[]{:S(2)}) collective-permute-start(bf16[256,2048]{1,0:T(8,128)(2,1)S(1)} %get-tuple-element.224), channel_id=1, source_target_pairs={{0,8},{8,16},{16,24},{24,0},{1,9},{9,17},{17,25},{25,1},{2,10},{10... | collective-permute-start | bytes 3145736 | tf_op jit(solution)/shard_map/ppermute | solution.py:134
  46.4 26.2 %collective-permute-start.1 = (bf16[256,2048]{1,0:T(8,128)(2,1)S(1)}, bf16[256,2048]{1,0:T(8,128)(2,1)}, u32[]{:S(2)}, u32[]{:S(2)}) collective-permute-start(bf16[256,2048]{1,0:T(8,128)(2,1)S(1)} %collective-permute-done), channel_id=1, source_target_pairs={{0,8},{8,16},{16,24},{24,0},{1,9},{9,17},{17,25},{25,1},{2,10},{10... | collective-permute-start | bytes 3145736 | tf_op jit(solution)/shard_map/ppermute | solution.py:134
  72.6 25.6 %collective-permute-start.2 = (bf16[256,2048]{1,0:T(8,128)(2,1)}, bf16[256,2048]{1,0:T(8,128)(2,1)}, u32[]{:S(2)}, u32[]{:S(2)}) collective-permute-start(bf16[256,2048]{1,0:T(8,128)(2,1)} %collective-permute-done.1), channel_id=1, source_target_pairs={{0,8},{8,16},{16,24},{24,0},{1,9},{9,17},{17,25},{25,1},{2,10},{10... | collective-permute-start | bytes 3145736 | tf_op jit(solution)/shard_map/ppermute | solution.py:134
  100.6 30.4 %collective-permute-start.3 = (bf16[256,2048]{1,0:T(8,128)(2,1)}, bf16[256,2048]{1,0:T(8,128)(2,1)}, u32[]{:S(2)}, u32[]{:S(2)}) collective-permute-start(bf16[256,2048]{1,0:T(8,128)(2,1)} %param.19), channel_id=1, source_target_pairs={{0,8},{8,16},{16,24},{24,0},{1,9},{9,17},{17,25},{25,1},{2,10},{10... | collective-permute-start | bytes 3145736 | tf_op jit(solution)/shard_map/ppermute | solution.py:134
  131.0 25.3 %collective-permute-start.4 = (bf16[256,2048]{1,0:T(8,128)(2,1)}, bf16[256,2048]{1,0:T(8,128)(2,1)}, u32[]{:S(2)}, u32[]{:S(2)}) collective-permute-start(bf16[256,2048]{1,0:T(8,128)(2,1)} %collective-permute-done.3), channel_id=1, source_target_pairs={{0,8},{8,16},{16,24},{24,0},{1,9},{9,17},{17,25},{25,1},{2,10},{10... | collective-permute-start | bytes 3145736 | tf_op jit(solution)/shard_map/ppermute | solution.py:134
  156.2 23.9 %collective-permute-start.5 = (bf16[256,2048]{1,0:T(8,128)(2,1)}, bf16[256,2048]{1,0:T(8,128)(2,1)S(1)}, u32[]{:S(2)}, u32[]{:S(2)}) collective-permute-start(bf16[256,2048]{1,0:T(8,128)(2,1)} %collective-permute-done.4), channel_id=1, source_target_pairs={{0,8},{8,16},{16,24},{24,0},{1,9},{9,17},{17,25},{25,1},{2,10},{10... | collective-permute-start | bytes 3145736 | tf_op jit(solution)/shard_map/ppermute | solution.py:134
  274.4 23.5 %collective-permute-start.10 = (bf16[256,2048]{1,0:T(8,128)(2,1)}, bf16[256,2048]{1,0:T(8,128)(2,1)}, u32[]{:S(2)}, u32[]{:S(2)}) collective-permute-start(bf16[256,2048]{1,0:T(8,128)(2,1)} %collective-permute-done.9), channel_id=1, source_target_pairs={{0,8},{8,16},{16,24},{24,0},{1,9},{9,17},{17,25},{25,1},{2,10},{10... | collective-permute-start | bytes 3145736 | tf_op jit(solution)/shard_map/ppermute | solution.py:134
  297.9 31.2 %collective-permute-start.11 = (bf16[256,2048]{1,0:T(8,128)(2,1)}, bf16[256,2048]{1,0:T(8,128)(2,1)}, u32[]{:S(2)}, u32[]{:S(2)}) collective-permute-start(bf16[256,2048]{1,0:T(8,128)(2,1)} %collective-permute-done.10), channel_id=1, source_target_pairs={{0,8},{8,16},{16,24},{24,0},{1,9},{9,17},{17,25},{25,1},{2,10},{10... | collective-permute-start | bytes 3145736 | tf_op jit(solution)/shard_map/ppermute | solution.py:134
  312.1 57.9 %collective-permute-start.12 = (bf16[256,2048]{1,0:T(8,128)(2,1)}, bf16[256,2048]{1,0:T(8,128)(2,1)}, u32[]{:S(2)}, u32[]{:S(2)}) collective-permute-start(bf16[256,2048]{1,0:T(8,128)(2,1)} %convolution_convert_fusion.2), channel_id=1, source_target_pairs={{0,8},{8,16},{16,24},{24,0},{1,9},{9,17},{17,25},{25,1},{2,10},{10... | collective-permute-start | bytes 3145736 | tf_op jit(solution)/shard_map/ppermute | solution.py:162
  370.0 262.5 %reduce-scatter.7.cloned.1.call-start = ((), (), s32[]{:S(2)}) async-start(), calls=%async_computation.9 | async-start | bytes 18874368 | tf_op jit(solution)/shard_map/reduce_scatter | solution.py:222
  431.8 29.3 %collective-permute-start.15 = (bf16[256,2048]{1,0:T(8,128)(2,1)}, bf16[256,2048]{1,0:T(8,128)(2,1)S(1)}, u32[]{:S(2)}, u32[]{:S(2)}) collective-permute-start(bf16[256,2048]{1,0:T(8,128)(2,1)} %get-tuple-element.219), channel_id=1, source_target_pairs={{0,8},{8,16},{16,24},{24,0},{1,9},{9,17},{17,25},{25,1},{2,10},{10... | collective-permute-start | bytes 3145736 | tf_op jit(solution)/shard_map/ppermute | solution.py:134
  462.1 236.9 %reduce-scatter.11.cloned.1.call-start = ((), (), s32[]{:S(2)}) async-start(), calls=%async_computation.11 | async-start | bytes 2359296 | tf_op jit(solution)/shard_map/reduce_scatter | solution.py:222
  464.7 26.2 %collective-permute-start.16 = (bf16[256,2048]{1,0:T(8,128)(2,1)}, bf16[256,2048]{1,0:T(8,128)(2,1)}, u32[]{:S(2)}, u32[]{:S(2)}) collective-permute-start(bf16[256,2048]{1,0:T(8,128)(2,1)} %copy-done.44), channel_id=1, source_target_pairs={{0,8},{8,16},{16,24},{24,0},{1,9},{9,17},{17,25},{25,1},{2,10},{10... | collective-permute-start | bytes 3145736 | tf_op jit(solution)/shard_map/ppermute | solution.py:134
  490.9 26.5 %collective-permute-start.17 = (bf16[256,2048]{1,0:T(8,128)(2,1)}, bf16[256,2048]{1,0:T(8,128)(2,1)S(1)}, u32[]{:S(2)}, u32[]{:S(2)}) collective-permute-start(bf16[256,2048]{1,0:T(8,128)(2,1)} %collective-permute-done.16), channel_id=1, source_target_pairs={{0,8},{8,16},{16,24},{24,0},{1,9},{9,17},{17,25},{25,1},{2,10},{10... | collective-permute-start | bytes 3145736 | tf_op jit(solution)/shard_map/ppermute | solution.py:134
  518.4 75.4 %collective-permute-start.18 = (bf16[256,2048]{1,0:T(8,128)(2,1)}, bf16[256,2048]{1,0:T(8,128)(2,1)}, u32[]{:S(2)}, u32[]{:S(2)}) collective-permute-start(bf16[256,2048]{1,0:T(8,128)(2,1)} %fusion.131), channel_id=1, source_target_pairs={{0,8},{8,16},{16,24},{24,0},{1,9},{9,17},{17,25},{25,1},{2,10},{10... | collective-permute-start | bytes 3145736 | tf_op jit(solution)/shard_map/ppermute | solution.py:162
  582.2 118.5 %reduce-scatter.9.cloned.1.call-start = ((), (), s32[]{:S(2)}) async-start(), calls=%async_computation.10 | async-start | bytes 7077888 | tf_op jit(solution)/shard_map/reduce_scatter | solution.py:222
  596.5 24.8 %collective-permute-start.19 = (bf16[256,2048]{1,0:T(8,128)(2,1)}, bf16[256,2048]{1,0:T(8,128)(2,1)}, u32[]{:S(2)}, u32[]{:S(2)}) collective-permute-start(bf16[256,2048]{1,0:T(8,128)(2,1)} %add_convert_fusion.6), channel_id=1, source_target_pairs={{0,8},{8,16},{16,24},{24,0},{1,9},{9,17},{17,25},{25,1},{2,10},{10... | collective-permute-start | bytes 3145736 | tf_op jit(solution)/shard_map/ppermute | solution.py:162
  641.1 40.2 %collective-permute-start.20 = (bf16[256,2048]{1,0:T(8,128)(2,1)S(1)}, bf16[256,2048]{1,0:T(8,128)(2,1)S(1)}, u32[]{:S(2)}, u32[]{:S(2)}) collective-permute-start(bf16[256,2048]{1,0:T(8,128)(2,1)S(1)} %add_convert_fusion.3), channel_id=1, source_target_pairs={{0,8},{8,16},{16,24},{24,0},{1,9},{9,17},{17,25},{25,1},{2,10},{10... | collective-permute-start | bytes 3145736 | tf_op jit(solution)/shard_map/ppermute | solution.py:162
  662.5 31.8 %collective-permute-start.22 = (bf16[256,2048]{1,0:T(8,128)(2,1)S(1)}, bf16[256,2048]{1,0:T(8,128)(2,1)S(1)}, u32[]{:S(2)}, u32[]{:S(2)}) collective-permute-start(bf16[256,2048]{1,0:T(8,128)(2,1)S(1)} %add_convert_fusion.1), channel_id=1, source_target_pairs={{0,8},{8,16},{16,24},{24,0},{1,9},{9,17},{17,25},{25,1},{2,10},{10... | collective-permute-start | bytes 3145736 | tf_op jit(solution)/shard_map/ppermute | solution.py:162
  (84 other events, 925.9 us)
Sparse Core Ops, SparseCore 0:
  10.5 48.1 all-gather.4
  60.5 28.0 all-gather.6
  90.5 55.8 all-gather.8
  148.7 89.7 all-gather.10
  370.2 72.1 reduce-scatter.4
  462.2 116.2 reduce-scatter.6
  582.4 40.8 reduce-scatter.10
  632.6 61.8 reduce-scatter.8

commit v12 on v9

--- a/solution.py
+++ b/solution.py
@@ -391,35 +391,48 @@
     act_slots = [item[2] for item in ffn]
     ffn_parts = [item[3] for item in ffn]
 
-    def ffn_backward(slot):
-        gate_lin, up_lin = gate_slots[slot], up_slots[slot]
-        grad_activation = times_transpose(cot_slots[slot], full_down)
+    def ffn_backward(group):
+        def rows(blocks):
+            return jnp.concatenate([blocks[slot] for slot in group], axis=0)
+
+        gate_lin, up_lin = rows(gate_slots), rows(up_slots)
+        grad_activation = times_transpose(rows(cot_slots), full_down)
         sigma = jax.nn.sigmoid(gate_lin)
         grad_gate = grad_activation * up_lin * sigma * (1.0 + gate_lin * (1.0 - sigma))
         grad_up = grad_activation * gate_lin * sigma
         grad_gu = jnp.concatenate([grad_gate, grad_up], axis=1).astype(jnp.bfloat16)
-        return (grad_gu, times_transpose(grad_gu, full_gu))
+        partial = times_transpose(grad_gu, full_gu)
+        size = partial.shape[0] // len(group)
+        return tuple(
+            (grad_gu[k * size : (k + 1) * size], partial[k * size : (k + 1) * size])
+            for k in range(len(group))
+        )
 
     second_ring_back = RingScatter([None] * slots, "row", jnp.bfloat16)
     grad_gu_slots = [None] * slots
     order = list(range(1, slots)) + [0]
-    grad_gu_slots[order[0]], second_ring_back.slots[order[0]] = ffn_backward(order[0])
+    groups = [order[k : k + 2] for k in range(0, slots, 2)]
+    for slot, item in zip(groups[0], ffn_backward(groups[0])):
+        grad_gu_slots[slot], second_ring_back.slots[slot] = item
     grad_down_w = None
     for index in range(second_ring_back.steps()):
         second_ring_back.send()
-        slot = order[index + 1]
-        value = ffn_backward(slot)
-        if slot == 0:
-            grad_down_w = contract_rows(
+        value = ()
+        if index + 1 < len(groups):
+            value = ffn_backward(groups[index + 1])
+        fresh = None
+        if index == 1 or (index == 0 and len(groups) == 1):
+            fresh = contract_rows(
                 jnp.concatenate(act_slots, axis=0), jnp.concatenate(cot_slots, axis=0)
             )
-            value = value + (grad_down_w,)
-        second_ring_back.pending, value = lax.optimization_barrier(
-            (second_ring_back.pending, value)
-        )
-        grad_gu_slots[slot], second_ring_back.slots[slot] = value[0], value[1]
-        if slot == 0:
-            grad_down_w = value[2]
+        second_ring_back.pending, value, fresh = lax.optimization_barrier(
+            (second_ring_back.pending, value, fresh)
+        )
+        if fresh is not None:
+            grad_down_w = fresh
+        if index + 1 < len(groups):
+            for slot, item in zip(groups[index + 1], value):
+                grad_gu_slots[slot], second_ring_back.slots[slot] = item
     grad_second = second_ring_back.result()
     down_sum = col_scatter(grad_down_w, 1)
     grad_gu = jnp.concatenate(grad_gu_slots, axis=0)
@@ -473,7 +486,10 @@
         ).astype(jnp.bfloat16)
         return (grad_qkv, times_transpose(grad_qkv, full_qkv))
 
-    pieces = [heads_backward(0, half), heads_backward(half, heads_local), finish]
+    def second_group_and_finish(done):
+        return finish(done + (heads_backward(half, heads_local)(done),))
+
+    pieces = [heads_backward(0, half), second_group_and_finish]
     grad_qkv, first_partial = overlap(ffn_ring, pieces)[-1]
     ffn_sum = ffn_ring.result()
     output = (middle + ffn_sum).astype(jnp.bfloat16)

time: 732 us -> 752 us (1.027)
  matrix products: 279 us -> 255 us
  waiting for transfers between devices: 258 us -> 282 us
  local copies, waits for them, and re-layouts: 63.2 us -> 73.5 us
  starting transfers between devices: 11.6 us -> 20.8 us
    ppermute x12, waiting for transfers between devices: 108 us -> 144 us  [send(): lax.ppermute(value.astype(self.send_dtype), self.axis, [(j, (j + 1) % n)...]
    dot_general x11 -> x7, matrix products: 89.1 us -> 66 us  [times_transpose(): lax.dot_general(left, right, (((1,), (1,)), ((), ())), preferred_element_...]
    reduce_scatter x4, waiting for transfers between devices: 17.4 us -> 1.05 us  [col_scatter(): lax.psum_scatter(low_part, COL, scatter_dimension=axis, tiled=True)]
  transfers between devices with their start and end apart: 32 -> 32, of which waited for: 16 -> 20; matrix products, arithmetic and copies ran while one was open for 57% -> 50% of each run, Pallas kernels for 0% -> 0%
where the time goes in v12:
time: 752 us; the launch traced here: 745 us
  waiting for transfers between devices  282 us (38%)
  matrix products  255 us (34%)
  other arithmetic  97.7 us (13%)
  local copies, waits for them, and re-layouts  73.5 us (10%)
  starting transfers between devices  20.8 us (3%)
  between operations  15.4 us (2%)
    ppermute x12, waiting for transfers between devices, send(): lax.ppermute(value.astype(self.send_dtype), self.axis, [(j, (j + 1) % n)...  144 us
    ppermute x12, waiting for transfers between devices, send(): lax.ppermute(self.pending, self.axis, [(j, (j + 1) % n) for j in range(n)])  136 us
    dot_general x10, matrix products, product(): return jnp.dot(left, right, preferred_element_type=jnp.float32)  70.3 us
    dot_general x7, matrix products, times_transpose(): lax.dot_general(left, right, (((1,), (1,)), ((), ())), preferred_element_...  66 us
    dot_general x4, matrix products, contract_rows(): lax.dot_general(left, right, (((0,), (0,)), ((), ())), preferred_element_...  55.2 us
    convert_element_type x1, other arithmetic, attend_backward(): grad_scores = (probs * (grad_probs - inner)).astype(jnp.bfloat16)  18.1 us
    dot_general x2, matrix products, attend_backward(): jnp.einsum('qhd,khd->hqk', grad_mixed, values, preferred_element_type=jnp...  15.9 us
  transfers between devices with their start and end apart: 32, of which 20 were waited for; matrix products, arithmetic and copies ran while one was open for 50% of the time, Pallas kernels for 0%

profile of v12, /device:TPU:0, one launch (start us, length us, event | category | flops | bytes accessed | tf_op | source)
XLA Modules:
  0.0 745.3 jit_solution(14037868048402120952)
XLA Ops:
  20.9 25.1 %collective-permute-done = bf16[256,2048]{1,0:T(8,128)(2,1)S(1)} collective-permute-done((bf16[256,2048]{1,0:T(8,128)(2,1)S(1)}, bf16[256,2048]{1,0:T(8,128)(2,1)S(1)}, u32[]{:S(2)}, u32[]{:S(2)}) %collective-permute-start) | collective-permute-done | bytes 1048608 | tf_op jit(solution)/shard_map/ppermute | solution.py:134
  47.6 24.6 %collective-permute-done.1 = bf16[256,2048]{1,0:T(8,128)(2,1)} collective-permute-done((bf16[256,2048]{1,0:T(8,128)(2,1)S(1)}, bf16[256,2048]{1,0:T(8,128)(2,1)}, u32[]{:S(2)}, u32[]{:S(2)}) %collective-permute-start.1) | collective-permute-done | bytes 1048608 | tf_op jit(solution)/shard_map/ppermute | solution.py:134
  81.8 16.1 %collective-permute-done.2 = bf16[256,2048]{1,0:T(8,128)(2,1)} collective-permute-done((bf16[256,2048]{1,0:T(8,128)(2,1)}, bf16[256,2048]{1,0:T(8,128)(2,1)}, u32[]{:S(2)}, u32[]{:S(2)}) %collective-permute-start.2) | collective-permute-done | bytes 1048608 | tf_op jit(solution)/shard_map/ppermute | solution.py:134
  100.8 10.5 %fusion.141 = f32[1024,1536]{1,0:T(8,128)S(1)} fusion(bf16[1024,2048]{1,0:T(8,128)(2,1)} %constant_dynamic-update-slice_fusion.6, bf16[2048,1536]{1,0:T(8,128)(2,1)} %all-gather.5.cloned.1.call-done), kind=kOutput, calls=%fused_computation.236 | convolution fusion | flops 6442450944 | bytes 16777216 | tf_op jit(solution)/shard_map/dot_general | solution.py:19
  173.2 19.3 %collective-permute-done.5 = bf16[256,2048]{1,0:T(8,128)(2,1)S(1)} collective-permute-done((bf16[256,2048]{1,0:T(8,128)(2,1)}, bf16[256,2048]{1,0:T(8,128)(2,1)S(1)}, u32[]{:S(2)}, u32[]{:S(2)}) %collective-permute-start.5) | collective-permute-done | bytes 1048608 | tf_op jit(solution)/shard_map/ppermute | solution.py:134
  192.8 22.9 %collective-permute-done.6 = bf16[256,2048]{1,0:T(8,128)(2,1)S(1)} collective-permute-done((bf16[256,2048]{1,0:T(8,128)(2,1)S(1)}, bf16[256,2048]{1,0:T(8,128)(2,1)S(1)}, u32[]{:S(2)}, u32[]{:S(2)}) %collective-permute-start.6) | collective-permute-done | bytes 1048608 | tf_op jit(solution)/shard_map/ppermute | solution.py:162
  216.1 22.9 %collective-permute-done.7 = bf16[256,2048]{1,0:T(8,128)(2,1)S(1)} collective-permute-done((bf16[256,2048]{1,0:T(8,128)(2,1)S(1)}, bf16[256,2048]{1,0:T(8,128)(2,1)S(1)}, u32[]{:S(2)}, u32[]{:S(2)}) %collective-permute-start.7) | collective-permute-done | bytes 1048608 | tf_op jit(solution)/shard_map/ppermute | solution.py:162
  239.4 20.1 %collective-permute-done.8 = bf16[256,2048]{1,0:T(8,128)(2,1)S(1)} collective-permute-done((bf16[256,2048]{1,0:T(8,128)(2,1)S(1)}, bf16[256,2048]{1,0:T(8,128)(2,1)S(1)}, u32[]{:S(2)}, u32[]{:S(2)}) %collective-permute-start.8) | collective-permute-done | bytes 1048608 | tf_op jit(solution)/shard_map/ppermute | solution.py:162
  299.0 10.4 %collective-permute-done.10 = bf16[256,2048]{1,0:T(8,128)(2,1)S(1)} collective-permute-done((bf16[256,2048]{1,0:T(8,128)(2,1)}, bf16[256,2048]{1,0:T(8,128)(2,1)S(1)}, u32[]{:S(2)}, u32[]{:S(2)}) %collective-permute-start.10) | collective-permute-done | bytes 1048608 | tf_op jit(solution)/shard_map/ppermute | solution.py:134
  349.0 13.0 %fusion.17 = f32[512,2048]{1,0:T(8,128)S(1)} fusion(bf16[2048,4096]{1,0:T(8,128)(2,1)} %all-gather.9.cloned.1.call-done, bf16[512,2048]{1,0:T(8,128)(2,1)} %get-tuple-element.210, bf16[512,2048]{1,0:T(8,128)(2,1)} %get-tuple-element.209), kind=kOutput, calls=%fused_computation.34 | convolution fusion | flops 8598323200 | bytes 25165824 | tf_op jit(solution)/shard_map/dot_general | solution.py:29
  363.7 10.9 %multiply_convert_fusion.2 = (bf16[512,2048]{1,0:T(8,128)(2,1)}, bf16[512,2048]{1,0:T(8,128)(2,1)}) fusion(f32[256,2048]{1,0:T(8,128)} %get-tuple-element.163, f32[256,2048]{1,0:T(8,128)} %get-tuple-element.223, f32[256,2048]{1,0:T(8,128)S(1)} %get-tuple-element.162, f32[256,2048]{1,0:T(8,128)} %get-tuple-element.225, ...), kind=kOutput, calls=%fused_computation.65 | convolution fusion | flops 4314890240 | bytes 23068672 | tf_op jit(solution)/shard_map/dot_general | solution.py:29
  374.7 13.1 %fusion.13 = f32[512,2048]{1,0:T(8,128)S(1)} fusion(bf16[2048,4096]{1,0:T(8,128)(2,1)} %all-gather.9.cloned.1.call-done, bf16[512,2048]{1,0:T(8,128)(2,1)} %get-tuple-element.207, bf16[512,2048]{1,0:T(8,128)(2,1)} %get-tuple-element.208), kind=kOutput, calls=%fused_computation.29 | convolution fusion | flops 8598323200 | bytes 25165824 | tf_op jit(solution)/shard_map/dot_general | solution.py:29
  397.7 12.6 %fusion.24 = bf16[2048,2048]{1,0:T(8,128)(2,1)} fusion(bf16[256,2048]{1,0:T(8,128)(2,1)S(1)} %get-tuple-element.224, bf16[256,2048]{1,0:T(8,128)(2,1)S(1)} %copy-done.39, bf16[256,2048]{1,0:T(8,128)(2,1)S(1)} %copy-done.37, bf16[256,2048]{1,0:T(8,128)(2,1)S(1)} %copy-done.35, bf16[256,2048]{1,0:T(8,128)(2,1)S(1)} %copy-done.58, ...), kind=kOutput, calls=%fused_computation.43 | convolution fusion | flops 8623489024 | bytes 16777216 | tf_op jit(solution)/shard_map/dot_general | solution.py:23
  422.2 15.1 %collective-permute-done.14 = bf16[256,2048]{1,0:T(8,128)(2,1)S(1)} collective-permute-done((bf16[256,2048]{1,0:T(8,128)(2,1)S(1)}, bf16[256,2048]{1,0:T(8,128)(2,1)S(1)}, u32[]{:S(2)}, u32[]{:S(2)}) %collective-permute-start.14) | collective-permute-done | bytes 1048608 | tf_op jit(solution)/shard_map/ppermute | solution.py:162
  446.7 25.6 %fusion.2 = bf16[2048,4096]{1,0:T(8,128)(2,1)} fusion(bf16[256,4096]{1,0:T(8,128)(2,1)} %get-tuple-element.172, bf16[512,2048]{1,0:T(8,128)(2,1)} %get-tuple-element.210, bf16[512,2048]{1,0:T(8,128)(2,1)} %get-tuple-element.209, bf16[256,4096]{1,0:T(8,128)(2,1)} %get-tuple-element.171, bf16[256,2048]{1,0:T(8,128)(2,1)} %copy-done.61, ...), kind=kOutput, calls=%fused_computation.5 | convolution fusion | flops 17230200832 | bytes 29360128 | tf_op jit(solution)/shard_map/dot_general | solution.py:23
  487.5 13.8 %collective-permute-done.16 = bf16[256,2048]{1,0:T(8,128)(2,1)} collective-permute-done((bf16[256,2048]{1,0:T(8,128)(2,1)}, bf16[256,2048]{1,0:T(8,128)(2,1)}, u32[]{:S(2)}, u32[]{:S(2)}) %collective-permute-start.16) | collective-permute-done | bytes 1048608 | tf_op jit(solution)/shard_map/ppermute | solution.py:134
  514.9 13.4 %collective-permute-done.17 = bf16[256,2048]{1,0:T(8,128)(2,1)S(1)} collective-permute-done((bf16[256,2048]{1,0:T(8,128)(2,1)}, bf16[256,2048]{1,0:T(8,128)(2,1)S(1)}, u32[]{:S(2)}, u32[]{:S(2)}) %collective-permute-start.17) | collective-permute-done | bytes 1048608 | tf_op jit(solution)/shard_map/ppermute | solution.py:134
  542.8 11.0 %multiply_reduce_fusion = (f32[2,1024]{1,0:T(2,128)S(1)}, f32[2,1024]{1,0:T(2,128)S(1)}, f32[2,1024,1024]{1,2,0:T(8,128)}) fusion(f32[2,1024,1024]{1,2,0:T(8,128)S(1)} %bitcast.123, f32[2,1024]{1,0:T(2,128)S(1)} %get-tuple-element.253, pred[1024,1024]{0,1:T(8,128)(4,1)S(1)} %copy-done.3, f32[2,1024,1024]{1,2,0:T(8,128)} %fusion.98, ...), kind=kOutput, calls=%fused_computation.14 | convolution fusion | flops 557838336 | bytes 35684352 | tf_op jit(solution)/shard_map/while/body/eval_jaxpr/qhd,khd->hqk/dot_general | solution.py:307
  553.8 18.1 %multiply_convert_fusion = (bf16[2,1024,1024]{1,2,0:T(8,128)(2,1)}, bf16[2,1024,1024]{1,2,0:T(8,128)(2,1)}) fusion(f32[2,1024,1024]{1,2,0:T(8,128)} %get-tuple-element.258, f32[2,1024,1024]{1,2,0:T(8,128)} %fusion.100, f32[2,1024]{1,0:T(2,128)S(1)} %get-tuple-element.198, f32[2,1024]{1,0:T(2,128)S(1)} %get-tuple-element.253, ...), kind=kLoop, calls=%fused_computation.13 | loop fusion | flops 25165824 | bytes 43024384 | tf_op jit(solution)/shard_map/while/body/eval_jaxpr/convert_element_type | solution.py:309
  623.9 11.0 %fusion.131 = f32[1024,2048]{1,0:T(8,128)} fusion(bf16[2048,1536]{1,0:T(8,128)(2,1)} %all-gather.5.cloned.1.call-done, bf16[1024,512]{0,1:T(8,128)(2,1)S(1)} %bitcast.129, bf16[1024,512]{0,1:T(8,128)(2,1)S(1)} %bitcast.125, bf16[1024,512]{0,1:T(8,128)(2,1)S(1)} %bitcast.127), kind=kOutput, calls=%fused_computation.227 | convolution fusion | flops 6451888128 | bytes 17825792 | tf_op jit(solution)/shard_map/dot_general | solution.py:29
  634.9 11.1 %convolution_convert_fusion = bf16[2048,1536]{1,0:T(8,128)(2,1)} fusion(bf16[1024,2048]{1,0:T(8,128)(2,1)} %constant_dynamic-update-slice_fusion.6, bf16[1024,1536]{0,1:T(8,128)(2,1)S(1)} %pad_maximum_fusion.3), kind=kOutput, calls=%fused_computation.21 | convolution fusion | flops 6445596672 | bytes 13631488 | tf_op jit(solution)/shard_map/dot_general | solution.py:23
  658.5 20.1 %collective-permute-done.21 = bf16[256,2048]{1,0:T(8,128)(2,1)S(1)} collective-permute-done((bf16[256,2048]{1,0:T(8,128)(2,1)S(1)}, bf16[256,2048]{1,0:T(8,128)(2,1)S(1)}, u32[]{:S(2)}, u32[]{:S(2)}) %collective-permute-start.21) | collective-permute-done | bytes 1048608 | tf_op jit(solution)/shard_map/ppermute | solution.py:162
  680.6 14.1 %collective-permute-done.20 = bf16[256,2048]{1,0:T(8,128)(2,1)S(1)} collective-permute-done((bf16[256,2048]{1,0:T(8,128)(2,1)S(1)}, bf16[256,2048]{1,0:T(8,128)(2,1)S(1)}, u32[]{:S(2)}, u32[]{:S(2)}) %collective-permute-start.20) | collective-permute-done | bytes 1048608 | tf_op jit(solution)/shard_map/ppermute | solution.py:162
  694.7 17.6 %collective-permute-done.22 = bf16[256,2048]{1,0:T(8,128)(2,1)S(1)} collective-permute-done((bf16[256,2048]{1,0:T(8,128)(2,1)S(1)}, bf16[256,2048]{1,0:T(8,128)(2,1)S(1)}, u32[]{:S(2)}, u32[]{:S(2)}) %collective-permute-start.22) | collective-permute-done | bytes 1048608 | tf_op jit(solution)/shard_map/ppermute | solution.py:162
  (306 shorter events, 337.2 us)
Async XLA Ops:
  7.2 93.6 %all-gather.5.cloned.1.call-start = ((), (), s32[]{:S(2)}) async-start(), calls=%async_computation.4 | async-start | bytes 7077888 | tf_op jit(solution)/shard_map/all_gather | solution.py:217
  9.4 159.8 %all-gather.7.cloned.1.call-start = ((), (), s32[]{:S(2)}) async-start(), calls=%async_computation.5 | async-start | bytes 2359296 | tf_op jit(solution)/shard_map/all_gather | solution.py:217
  10.1 252.7 %all-gather.9.cloned.1.call-start = ((), (), s32[]{:S(2)}) async-start(), calls=%async_computation.6 | async-start | bytes 18874368 | tf_op jit(solution)/shard_map/all_gather | solution.py:217
  13.2 260.1 %all-gather.11.cloned.1.call-start = ((), (), s32[]{:S(2)}) async-start(), calls=%async_computation.7 | async-start | bytes 9437184 | tf_op jit(solution)/shard_map/all_gather | solution.py:217
  17.8 28.2 %collective-permute-start = (bf16[256,2048]{1,0:T(8,128)(2,1)S(1)}, bf16[256,2048]{1,0:T(8,128)(2,1)S(1)}, u32[]{:S(2)}, u32[]{:S(2)}) collective-permute-start(bf16[256,2048]{1,0:T(8,128)(2,1)S(1)} %get-tuple-element.206), channel_id=1, source_target_pairs={{0,8},{8,16},{16,24},{24,0},{1,9},{9,17},{17,25},{25,1},{2,10},{10... | collective-permute-start | bytes 3145736 | tf_op jit(solution)/shard_map/ppermute | solution.py:134
  46.0 26.2 %collective-permute-start.1 = (bf16[256,2048]{1,0:T(8,128)(2,1)S(1)}, bf16[256,2048]{1,0:T(8,128)(2,1)}, u32[]{:S(2)}, u32[]{:S(2)}) collective-permute-start(bf16[256,2048]{1,0:T(8,128)(2,1)S(1)} %collective-permute-done), channel_id=1, source_target_pairs={{0,8},{8,16},{16,24},{24,0},{1,9},{9,17},{17,25},{25,1},{2,10},{10... | collective-permute-start | bytes 3145736 | tf_op jit(solution)/shard_map/ppermute | solution.py:134
  46.1 465.9 %reduce-scatter.5.cloned.1.call-start = ((), (), s32[]{:S(2)}) async-start(), calls=%async_computation.8 | async-start | bytes 9437184 | tf_op jit(solution)/shard_map/reduce_scatter | solution.py:222
  72.3 25.6 %collective-permute-start.2 = (bf16[256,2048]{1,0:T(8,128)(2,1)}, bf16[256,2048]{1,0:T(8,128)(2,1)}, u32[]{:S(2)}, u32[]{:S(2)}) collective-permute-start(bf16[256,2048]{1,0:T(8,128)(2,1)} %collective-permute-done.1), channel_id=1, source_target_pairs={{0,8},{8,16},{16,24},{24,0},{1,9},{9,17},{17,25},{25,1},{2,10},{10... | collective-permute-start | bytes 3145736 | tf_op jit(solution)/shard_map/ppermute | solution.py:134
  100.4 44.5 %collective-permute-start.3 = (bf16[256,2048]{1,0:T(8,128)(2,1)}, bf16[256,2048]{1,0:T(8,128)(2,1)}, u32[]{:S(2)}, u32[]{:S(2)}) collective-permute-start(bf16[256,2048]{1,0:T(8,128)(2,1)} %param.19), channel_id=1, source_target_pairs={{0,8},{8,16},{16,24},{24,0},{1,9},{9,17},{17,25},{25,1},{2,10},{10... | collective-permute-start | bytes 3145736 | tf_op jit(solution)/shard_map/ppermute | solution.py:134
  144.9 24.3 %collective-permute-start.4 = (bf16[256,2048]{1,0:T(8,128)(2,1)}, bf16[256,2048]{1,0:T(8,128)(2,1)}, u32[]{:S(2)}, u32[]{:S(2)}) collective-permute-start(bf16[256,2048]{1,0:T(8,128)(2,1)} %collective-permute-done.3), channel_id=1, source_target_pairs={{0,8},{8,16},{16,24},{24,0},{1,9},{9,17},{17,25},{25,1},{2,10},{10... | collective-permute-start | bytes 3145736 | tf_op jit(solution)/shard_map/ppermute | solution.py:134
  262.6 23.5 %collective-permute-start.9 = (bf16[256,2048]{1,0:T(8,128)(2,1)}, bf16[256,2048]{1,0:T(8,128)(2,1)}, u32[]{:S(2)}, u32[]{:S(2)}) collective-permute-start(bf16[256,2048]{1,0:T(8,128)(2,1)} %fusion.75), channel_id=1, source_target_pairs={{0,8},{8,16},{16,24},{24,0},{1,9},{9,17},{17,25},{25,1},{2,10},{10... | collective-permute-start | bytes 3145736 | tf_op jit(solution)/shard_map/ppermute | solution.py:134
  286.1 23.3 %collective-permute-start.10 = (bf16[256,2048]{1,0:T(8,128)(2,1)}, bf16[256,2048]{1,0:T(8,128)(2,1)S(1)}, u32[]{:S(2)}, u32[]{:S(2)}) collective-permute-start(bf16[256,2048]{1,0:T(8,128)(2,1)} %collective-permute-done.9), channel_id=1, source_target_pairs={{0,8},{8,16},{16,24},{24,0},{1,9},{9,17},{17,25},{25,1},{2,10},{10... | collective-permute-start | bytes 3145736 | tf_op jit(solution)/shard_map/ppermute | solution.py:134
  363.3 30.4 %collective-permute-start.12 = (bf16[256,2048]{1,0:T(8,128)(2,1)}, bf16[256,2048]{1,0:T(8,128)(2,1)}, u32[]{:S(2)}, u32[]{:S(2)}) collective-permute-start(bf16[256,2048]{1,0:T(8,128)(2,1)} %slice.286), channel_id=1, source_target_pairs={{0,8},{8,16},{16,24},{24,0},{1,9},{9,17},{17,25},{25,1},{2,10},{10... | collective-permute-start | bytes 3145736 | tf_op jit(solution)/shard_map/ppermute | solution.py:162
  417.6 228.5 %reduce-scatter.7.cloned.1.call-start = ((), (), s32[]{:S(2)}) async-start(), calls=%async_computation.9 | async-start | bytes 18874368 | tf_op jit(solution)/shard_map/reduce_scatter | solution.py:222
  444.9 27.4 %collective-permute-start.15 = (bf16[256,2048]{1,0:T(8,128)(2,1)}, bf16[256,2048]{1,0:T(8,128)(2,1)}, u32[]{:S(2)}, u32[]{:S(2)}) collective-permute-start(bf16[256,2048]{1,0:T(8,128)(2,1)} %get-tuple-element.201), channel_id=1, source_target_pairs={{0,8},{8,16},{16,24},{24,0},{1,9},{9,17},{17,25},{25,1},{2,10},{10... | collective-permute-start | bytes 3145736 | tf_op jit(solution)/shard_map/ppermute | solution.py:134
  472.3 244.6 %reduce-scatter.11.cloned.1.call-start = ((), (), s32[]{:S(2)}) async-start(), calls=%async_computation.11 | async-start | bytes 2359296 | tf_op jit(solution)/shard_map/reduce_scatter | solution.py:222
  474.8 26.6 %collective-permute-start.16 = (bf16[256,2048]{1,0:T(8,128)(2,1)}, bf16[256,2048]{1,0:T(8,128)(2,1)}, u32[]{:S(2)}, u32[]{:S(2)}) collective-permute-start(bf16[256,2048]{1,0:T(8,128)(2,1)} %collective-permute-done.15), channel_id=1, source_target_pairs={{0,8},{8,16},{16,24},{24,0},{1,9},{9,17},{17,25},{25,1},{2,10},{10... | collective-permute-start | bytes 3145736 | tf_op jit(solution)/shard_map/ppermute | solution.py:134
  501.3 27.0 %collective-permute-start.17 = (bf16[256,2048]{1,0:T(8,128)(2,1)}, bf16[256,2048]{1,0:T(8,128)(2,1)S(1)}, u32[]{:S(2)}, u32[]{:S(2)}) collective-permute-start(bf16[256,2048]{1,0:T(8,128)(2,1)} %collective-permute-done.16), channel_id=1, source_target_pairs={{0,8},{8,16},{16,24},{24,0},{1,9},{9,17},{17,25},{25,1},{2,10},{10... | collective-permute-start | bytes 3145736 | tf_op jit(solution)/shard_map/ppermute | solution.py:134
  529.4 76.9 %collective-permute-start.18 = (bf16[256,2048]{1,0:T(8,128)(2,1)}, bf16[256,2048]{1,0:T(8,128)(2,1)}, u32[]{:S(2)}, u32[]{:S(2)}) collective-permute-start(bf16[256,2048]{1,0:T(8,128)(2,1)} %fusion.146), channel_id=1, source_target_pairs={{0,8},{8,16},{16,24},{24,0},{1,9},{9,17},{17,25},{25,1},{2,10},{10... | collective-permute-start | bytes 3145736 | tf_op jit(solution)/shard_map/ppermute | solution.py:162
  594.8 125.0 %reduce-scatter.9.cloned.1.call-start = ((), (), s32[]{:S(2)}) async-start(), calls=%async_computation.10 | async-start | bytes 7077888 | tf_op jit(solution)/shard_map/reduce_scatter | solution.py:222
  609.0 26.0 %collective-permute-start.19 = (bf16[256,2048]{1,0:T(8,128)(2,1)}, bf16[256,2048]{1,0:T(8,128)(2,1)}, u32[]{:S(2)}, u32[]{:S(2)}) collective-permute-start(bf16[256,2048]{1,0:T(8,128)(2,1)} %add_convert_fusion.6), channel_id=1, source_target_pairs={{0,8},{8,16},{16,24},{24,0},{1,9},{9,17},{17,25},{25,1},{2,10},{10... | collective-permute-start | bytes 3145736 | tf_op jit(solution)/shard_map/ppermute | solution.py:162
  652.1 26.5 %collective-permute-start.21 = (bf16[256,2048]{1,0:T(8,128)(2,1)S(1)}, bf16[256,2048]{1,0:T(8,128)(2,1)S(1)}, u32[]{:S(2)}, u32[]{:S(2)}) collective-permute-start(bf16[256,2048]{1,0:T(8,128)(2,1)S(1)} %dynamic-slice_convert_fusion), channel_id=1, source_target_pairs={{0,8},{8,16},{16,24},{24,0},{1,9},{9,17},{17,25},{25,1},{2,10},{10... | collective-permute-start | bytes 3145736 | tf_op jit(solution)/shard_map/ppermute | solution.py:162
  654.7 40.0 %collective-permute-start.20 = (bf16[256,2048]{1,0:T(8,128)(2,1)S(1)}, bf16[256,2048]{1,0:T(8,128)(2,1)S(1)}, u32[]{:S(2)}, u32[]{:S(2)}) collective-permute-start(bf16[256,2048]{1,0:T(8,128)(2,1)S(1)} %add_convert_fusion.3), channel_id=1, source_target_pairs={{0,8},{8,16},{16,24},{24,0},{1,9},{9,17},{17,25},{25,1},{2,10},{10... | collective-permute-start | bytes 3145736 | tf_op jit(solution)/shard_map/ppermute | solution.py:162
  680.5 31.8 %collective-permute-start.22 = (bf16[256,2048]{1,0:T(8,128)(2,1)S(1)}, bf16[256,2048]{1,0:T(8,128)(2,1)S(1)}, u32[]{:S(2)}, u32[]{:S(2)}) collective-permute-start(bf16[256,2048]{1,0:T(8,128)(2,1)S(1)} %add_convert_fusion.1), channel_id=1, source_target_pairs={{0,8},{8,16},{16,24},{24,0},{1,9},{9,17},{17,25},{25,1},{2,10},{10... | collective-permute-start | bytes 3145736 | tf_op jit(solution)/shard_map/ppermute | solution.py:162
  (78 other events, 1117.8 us)
Sparse Core Ops, SparseCore 0:
  10.5 48.1 all-gather.4
  60.5 28.0 all-gather.6
  90.5 89.7 all-gather.8
  182.0 55.8 all-gather.10
  417.7 72.7 reduce-scatter.4
  493.9 116.1 reduce-scatter.6
  613.4 41.1 reduce-scatter.10
  658.0 61.7 reduce-scatter.8

commit v13 on v11

--- a/solution.py
+++ b/solution.py
@@ -325,8 +325,9 @@
     width = w_query.shape[1]
     hidden = w_gate.shape[1]
     heads_local = width // HD
-    full_qkv = col_gather(jnp.concatenate([w_query, w_key, w_value], axis=1), 0)
-    full_output = col_gather(w_output, 1)
+    full_qkvo = col_gather(jnp.concatenate([w_query, w_key, w_value, w_output.T], axis=1), 0)
+    full_qkv = full_qkvo[:, : 3 * width]
+    output_t = full_qkvo[:, 3 * width :]
     full_gu = col_gather(jnp.concatenate([w_gate, w_up], axis=1), 0)
     full_down = col_gather(w_down, 1)
     cosine, sine = rope_tables()
@@ -358,7 +359,7 @@
 
     def out_project(done):
         attended = merge_heads(done[1]["mixed"].astype(jnp.bfloat16))
-        return dict(attended=attended, attn_partial=product(attended, full_output))
+        return dict(attended=attended, attn_partial=times_transpose(attended, output_t))
 
     cot_later, first_rows = lax.optimization_barrier((cotangent, first_rows))
     cot_ring = RingGather(cot_later, "row")
@@ -367,7 +368,8 @@
     queries, keys_rot = projected["queries"], projected["keys_rot"]
     values = projected["values"]
     log_total, attended = attention["log_total"], mixed_out["attended"]
-    attn_ring = RingScatter(ring_slots(mixed_out["attn_partial"], "row"), "row", jnp.bfloat16)
+    full_down, attn_partial = lax.optimization_barrier((full_down, mixed_out["attn_partial"]))
+    attn_ring = RingScatter(ring_slots(attn_partial, "row"), "row", jnp.bfloat16)
     cot_count = len(cot_slots)
     per_step = -(-cot_count // attn_ring.steps())
 
@@ -383,6 +385,7 @@
     attention_sum = attn_ring.result()
     middle = inputs + attention_sum
     normed_second = layer_norm(middle).astype(jnp.bfloat16)
+    full_gu, normed_second = lax.optimization_barrier((full_gu, normed_second))
     second_ring = RingGather(normed_second, "row")
     slots = second_ring.n
 
@@ -457,7 +460,7 @@
 
     def heads_backward(lo, hi):
         def piece(done):
-            grad_mixed = times_transpose(grad_branch, full_output[lo * HD : hi * HD])
+            grad_mixed = product(grad_branch, output_t[:, lo * HD : hi * HD])
             grad_mixed = grad_mixed.astype(jnp.bfloat16).reshape(seq_count, LENGTH, hi - lo, HD)
             return lax.map(
                 attend_backward,

time: 734 us -> 738 us (level)
    dot_general x10 -> x11, matrix products: 72.3 us -> 73.7 us  [product(): return jnp.dot(left, right, preferred_element_type=jnp.float32)]
    dot_general x11 -> x10, matrix products: 90.8 us -> 90.5 us  [times_transpose(): lax.dot_general(left, right, (((1,), (1,)), ((), ())), preferred_element_...]
  transfers between devices with their start and end apart: 32 -> 31, of which waited for: 18 -> 18; matrix products, arithmetic and copies ran while one was open for 60% -> 60% of each run, Pallas kernels for 0% -> 0%
where the time goes in v13:
time: 738 us; the launch traced here: 730 us
  matrix products  285 us (39%)
  waiting for transfers between devices  237 us (32%)
  other arithmetic  105 us (14%)
  local copies, waits for them, and re-layouts  66.9 us (9%)
  starting transfers between devices  21.1 us (3%)
  between operations  15.8 us (2%)
    ppermute x12, waiting for transfers between devices, send(): lax.ppermute(self.pending, self.axis, [(j, (j + 1) % n) for j in range(n)])  129 us
    ppermute x12, waiting for transfers between devices, send(): lax.ppermute(value.astype(self.send_dtype), self.axis, [(j, (j + 1) % n)...  107 us
    dot_general x10, matrix products, times_transpose(): lax.dot_general(left, right, (((1,), (1,)), ((), ())), preferred_element_...  90.5 us
    dot_general x11, matrix products, product(): return jnp.dot(left, right, preferred_element_type=jnp.float32)  73.7 us
    dot_general x4, matrix products, contract_rows(): lax.dot_general(left, right, (((0,), (0,)), ((), ())), preferred_element_...  55.6 us
    convert_element_type x1, other arithmetic, attend_backward(): grad_scores = (probs * (grad_probs - inner)).astype(jnp.bfloat16)  17.6 us
    dot_general x3, matrix products, masked_scores(): jnp.einsum('qhd,khd->hqk', queries, keys_rot, preferred_element_type=jnp....  16.1 us
    dot_general x2, matrix products, attend_backward(): jnp.einsum('qhd,khd->hqk', grad_mixed, values, preferred_element_type=jnp...  15.7 us
  transfers between devices with their start and end apart: 31, of which 18 were waited for; matrix products, arithmetic and copies ran while one was open for 60% of the time, Pallas kernels for 0%

profile of v13, /device:TPU:0, one launch (start us, length us, event | category | flops | bytes accessed | tf_op | source)
XLA Modules:
  0.0 730.3 jit_solution(2870879090627813916)
XLA Ops:
  23.7 25.2 %collective-permute-done = bf16[256,2048]{1,0:T(8,128)(2,1)S(1)} collective-permute-done((bf16[256,2048]{1,0:T(8,128)(2,1)S(1)}, bf16[256,2048]{1,0:T(8,128)(2,1)S(1)}, u32[]{:S(2)}, u32[]{:S(2)}) %collective-permute-start) | collective-permute-done | bytes 1048608 | tf_op jit(solution)/shard_map/ppermute | solution.py:134
  50.4 24.7 %collective-permute-done.1 = bf16[256,2048]{1,0:T(8,128)(2,1)} collective-permute-done((bf16[256,2048]{1,0:T(8,128)(2,1)S(1)}, bf16[256,2048]{1,0:T(8,128)(2,1)}, u32[]{:S(2)}, u32[]{:S(2)}) %collective-permute-start.1) | collective-permute-done | bytes 1048608 | tf_op jit(solution)/shard_map/ppermute | solution.py:134
  84.8 15.9 %collective-permute-done.2 = bf16[256,2048]{1,0:T(8,128)(2,1)} collective-permute-done((bf16[256,2048]{1,0:T(8,128)(2,1)}, bf16[256,2048]{1,0:T(8,128)(2,1)}, u32[]{:S(2)}, u32[]{:S(2)}) %collective-permute-start.2) | collective-permute-done | bytes 1048608 | tf_op jit(solution)/shard_map/ppermute | solution.py:134
  103.6 10.3 %fusion.15 = f32[1024,1536]{1,0:T(8,128)S(1)} fusion(bf16[1024,2048]{1,0:T(8,128)(2,1)} %constant_dynamic-update-slice_fusion.4, bf16[2048,2048]{0,1:T(8,128)(2,1)} %all-gather.6.cloned.1.call-done), kind=kOutput, calls=%fused_computation.26 | convolution fusion | flops 6442450944 | bytes 16777216 | tf_op jit(solution)/shard_map/dot_general | solution.py:19
  166.0 16.2 %collective-permute-done.5 = bf16[256,2048]{1,0:T(8,128)(2,1)S(1)} collective-permute-done((bf16[256,2048]{1,0:T(8,128)(2,1)}, bf16[256,2048]{1,0:T(8,128)(2,1)S(1)}, u32[]{:S(2)}, u32[]{:S(2)}) %collective-permute-start.5) | collective-permute-done | bytes 1048608 | tf_op jit(solution)/shard_map/ppermute | solution.py:134
  197.3 9.9 %collective-permute-done.6 = bf16[256,2048]{1,0:T(8,128)(2,1)S(1)} collective-permute-done((bf16[256,2048]{1,0:T(8,128)(2,1)S(1)}, bf16[256,2048]{1,0:T(8,128)(2,1)S(1)}, u32[]{:S(2)}, u32[]{:S(2)}) %collective-permute-start.6) | collective-permute-done | bytes 1048608 | tf_op jit(solution)/shard_map/ppermute | solution.py:162
  216.3 14.4 %collective-permute-done.7 = bf16[256,2048]{1,0:T(8,128)(2,1)S(1)} collective-permute-done((bf16[256,2048]{1,0:T(8,128)(2,1)S(1)}, bf16[256,2048]{1,0:T(8,128)(2,1)S(1)}, u32[]{:S(2)}, u32[]{:S(2)}) %collective-permute-start.7) | collective-permute-done | bytes 1048608 | tf_op jit(solution)/shard_map/ppermute | solution.py:162
  231.1 22.0 %collective-permute-done.8 = bf16[256,2048]{1,0:T(8,128)(2,1)S(1)} collective-permute-done((bf16[256,2048]{1,0:T(8,128)(2,1)S(1)}, bf16[256,2048]{1,0:T(8,128)(2,1)S(1)}, u32[]{:S(2)}, u32[]{:S(2)}) %collective-permute-start.8) | collective-permute-done | bytes 1048608 | tf_op jit(solution)/shard_map/ppermute | solution.py:162
  290.6 10.2 %collective-permute-done.10 = bf16[256,2048]{1,0:T(8,128)(2,1)} collective-permute-done((bf16[256,2048]{1,0:T(8,128)(2,1)S(1)}, bf16[256,2048]{1,0:T(8,128)(2,1)}, u32[]{:S(2)}, u32[]{:S(2)}) %collective-permute-start.10) | collective-permute-done | bytes 1048608 | tf_op jit(solution)/shard_map/ppermute | solution.py:134
  310.7 12.0 %convolution_convert_fusion.2 = bf16[256,2048]{1,0:T(8,128)(2,1)} fusion(bf16[2048,4096]{1,0:T(8,128)(2,1)} %all-gather.8.cloned.1.call-done, bf16[256,2048]{1,0:T(8,128)(2,1)} %get-tuple-element.249, bf16[256,2048]{1,0:T(8,128)(2,1)S(1)} %get-tuple-element.248), kind=kOutput, calls=%fused_computation.63 | convolution fusion | flops 4299685888 | bytes 19922944 | tf_op jit(solution)/shard_map/dot_general | solution.py:29
  349.2 12.7 %fusion.19 = bf16[2048,2048]{1,0:T(8,128)(2,1)} fusion(bf16[256,2048]{1,0:T(8,128)(2,1)S(1)} %get-tuple-element.245, bf16[256,2048]{1,0:T(8,128)(2,1)S(1)} %get-tuple-element.185, bf16[256,2048]{1,0:T(8,128)(2,1)S(1)} %copy-done.41, bf16[256,2048]{1,0:T(8,128)(2,1)S(1)} %copy-done.39, bf16[256,2048]{1,0:T(8,128)(2,1)S(1)} %copy-done.61, ...), kind=kOutput, calls=%fused_computation.30 | convolution fusion | flops 8623489024 | bytes 16777216 | tf_op jit(solution)/shard_map/dot_general | solution.py:23
  362.0 12.2 %fusion.119 = f32[256,2048]{1,0:T(8,128)} fusion(bf16[2048,4096]{1,0:T(8,128)(2,1)} %all-gather.8.cloned.1.call-done, bf16[256,2048]{1,0:T(8,128)(2,1)} %copy-done.28, bf16[256,2048]{1,0:T(8,128)(2,1)} %copy-done.27), kind=kOutput, calls=%fused_computation.216 | convolution fusion | flops 4299161600 | bytes 20971520 | tf_op jit(solution)/shard_map/dot_general | solution.py:29
  386.8 13.8 %fusion.118 = f32[256,2048]{1,0:T(8,128)} fusion(bf16[2048,4096]{1,0:T(8,128)(2,1)} %all-gather.8.cloned.1.call-done, bf16[256,2048]{1,0:T(8,128)(2,1)} %get-tuple-element.234, bf16[256,2048]{1,0:T(8,128)(2,1)S(1)} %get-tuple-element.233), kind=kOutput, calls=%fused_computation.215 | convolution fusion | flops 4299161600 | bytes 20971520 | tf_op jit(solution)/shard_map/dot_general | solution.py:29
  413.1 12.7 %fusion.117 = f32[256,2048]{1,0:T(8,128)} fusion(bf16[2048,4096]{1,0:T(8,128)(2,1)} %all-gather.8.cloned.1.call-done, bf16[256,2048]{1,0:T(8,128)(2,1)} %copy-done.26, bf16[256,2048]{1,0:T(8,128)(2,1)} %copy-done.25), kind=kOutput, calls=%fused_computation.214 | convolution fusion | flops 4299161600 | bytes 20971520 | tf_op jit(solution)/shard_map/dot_general | solution.py:29
  440.8 25.9 %fusion.2 = bf16[2048,4096]{1,0:T(8,128)(2,1)} fusion(bf16[256,4096]{1,0:T(8,128)(2,1)} %pad_maximum_fusion.5, bf16[256,4096]{1,0:T(8,128)(2,1)} %pad_maximum_fusion.4, bf16[256,2048]{1,0:T(8,128)(2,1)} %get-tuple-element.249, bf16[256,2048]{1,0:T(8,128)(2,1)} %copy-done.49, bf16[256,4096]{1,0:T(8,128)(2,1)} %pad_maximum_fusion.6, ...), kind=kOutput, calls=%fused_computation.5 | convolution fusion | flops 17238589440 | bytes 29360128 | tf_op jit(solution)/shard_map/dot_general | solution.py:23
  484.5 10.4 %collective-permute-done.16 = bf16[256,2048]{1,0:T(8,128)(2,1)} collective-permute-done((bf16[256,2048]{1,0:T(8,128)(2,1)}, bf16[256,2048]{1,0:T(8,128)(2,1)}, u32[]{:S(2)}, u32[]{:S(2)}) %collective-permute-start.16) | collective-permute-done | bytes 1048608 | tf_op jit(solution)/shard_map/ppermute | solution.py:134
  504.8 14.9 %collective-permute-done.17 = bf16[256,2048]{1,0:T(8,128)(2,1)S(1)} collective-permute-done((bf16[256,2048]{1,0:T(8,128)(2,1)}, bf16[256,2048]{1,0:T(8,128)(2,1)S(1)}, u32[]{:S(2)}, u32[]{:S(2)}) %collective-permute-start.17) | collective-permute-done | bytes 1048608 | tf_op jit(solution)/shard_map/ppermute | solution.py:134
  533.9 11.0 %multiply_reduce_fusion = (f32[2,1024]{1,0:T(2,128)S(1)}, f32[2,1024]{1,0:T(2,128)S(1)}, f32[2,1024,1024]{1,2,0:T(8,128)}) fusion(f32[2,1024,1024]{1,2,0:T(8,128)S(1)} %bitcast.129, f32[2,1024]{1,0:T(2,128)S(1)} %get-tuple-element.277, pred[1024,1024]{0,1:T(8,128)(4,1)S(1)} %copy-done.1, f32[2,1024,1024]{1,2,0:T(8,128)} %fusion.87, ...), kind=kOutput, calls=%fused_computation.16 | convolution fusion | flops 557838336 | bytes 35684352 | tf_op jit(solution)/shard_map/while/body/eval_jaxpr/qhd,khd->hqk/dot_general | solution.py:307
  544.9 17.6 %multiply_convert_fusion = (bf16[2,1024,1024]{1,2,0:T(8,128)(2,1)}, bf16[2,1024,1024]{1,2,0:T(8,128)(2,1)}) fusion(f32[2,1024,1024]{1,2,0:T(8,128)} %get-tuple-element.282, f32[2,1024,1024]{1,2,0:T(8,128)} %fusion.89, f32[2,1024]{1,0:T(2,128)S(1)} %get-tuple-element.224, f32[2,1024]{1,0:T(2,128)S(1)} %get-tuple-element.277, ...), kind=kLoop, calls=%fused_computation.15 | loop fusion | flops 25165824 | bytes 43024384 | tf_op jit(solution)/shard_map/while/body/eval_jaxpr/convert_element_type | solution.py:309
  613.5 11.0 %fusion.13 = f32[1024,2048]{1,0:T(8,128)} fusion(bf16[2048,2048]{0,1:T(8,128)(2,1)} %all-gather.6.cloned.1.call-done, bf16[1024,512]{0,1:T(8,128)(2,1)S(1)} %bitcast.137, bf16[1024,512]{0,1:T(8,128)(2,1)S(1)} %bitcast.133, bf16[1024,512]{0,1:T(8,128)(2,1)S(1)} %bitcast.135), kind=kOutput, calls=%fused_computation.24 | convolution fusion | flops 6451888128 | bytes 17825792 | tf_op jit(solution)/shard_map/dot_general | solution.py:29
  624.5 11.1 %convolution_convert_fusion = bf16[2048,1536]{1,0:T(8,128)(2,1)} fusion(bf16[1024,2048]{1,0:T(8,128)(2,1)} %constant_dynamic-update-slice_fusion.4, bf16[1024,1536]{0,1:T(8,128)(2,1)S(1)} %pad_maximum_fusion), kind=kOutput, calls=%fused_computation.23 | convolution fusion | flops 6445596672 | bytes 13631488 | tf_op jit(solution)/shard_map/dot_general | solution.py:23
  648.0 15.3 %collective-permute-done.21 = bf16[256,2048]{1,0:T(8,128)(2,1)S(1)} collective-permute-done((bf16[256,2048]{1,0:T(8,128)(2,1)S(1)}, bf16[256,2048]{1,0:T(8,128)(2,1)S(1)}, u32[]{:S(2)}, u32[]{:S(2)}) %collective-permute-start.21) | collective-permute-done | bytes 1048608 | tf_op jit(solution)/shard_map/ppermute | solution.py:162
  666.1 17.9 %collective-permute-done.20 = bf16[256,2048]{1,0:T(8,128)(2,1)S(1)} collective-permute-done((bf16[256,2048]{1,0:T(8,128)(2,1)S(1)}, bf16[256,2048]{1,0:T(8,128)(2,1)S(1)}, u32[]{:S(2)}, u32[]{:S(2)}) %collective-permute-start.20) | collective-permute-done | bytes 1048608 | tf_op jit(solution)/shard_map/ppermute | solution.py:162
  684.1 12.9 %collective-permute-done.22 = bf16[256,2048]{1,0:T(8,128)(2,1)S(1)} collective-permute-done((bf16[256,2048]{1,0:T(8,128)(2,1)S(1)}, bf16[256,2048]{1,0:T(8,128)(2,1)S(1)}, u32[]{:S(2)}, u32[]{:S(2)}) %collective-permute-start.22) | collective-permute-done | bytes 1048608 | tf_op jit(solution)/shard_map/ppermute | solution.py:162
  (325 shorter events, 354.1 us)
Async XLA Ops:
  7.2 96.4 %all-gather.6.cloned.1.call-start = ((), (), s32[]{:S(2)}) async-start(), calls=%async_computation.5 | async-start | bytes 9437184 | tf_op jit(solution)/shard_map/all_gather | solution.py:217
  12.7 169.5 %all-gather.4.cloned.1.call-start = ((), (), s32[]{:S(2)}) async-start(), calls=%async_computation.4 | async-start | bytes 9437184 | tf_op jit(solution)/shard_map/all_gather | solution.py:217
  13.4 240.9 %all-gather.8.cloned.1.call-start = ((), (), s32[]{:S(2)}) async-start(), calls=%async_computation.6 | async-start | bytes 18874368 | tf_op jit(solution)/shard_map/all_gather | solution.py:217
  15.0 487.1 %reduce-scatter.5.cloned.1.call-start = ((), (), s32[]{:S(2)}) async-start(), calls=%async_computation.7 | async-start | bytes 9437184 | tf_op jit(solution)/shard_map/reduce_scatter | solution.py:222
  20.7 28.2 %collective-permute-start = (bf16[256,2048]{1,0:T(8,128)(2,1)S(1)}, bf16[256,2048]{1,0:T(8,128)(2,1)S(1)}, u32[]{:S(2)}, u32[]{:S(2)}) collective-permute-start(bf16[256,2048]{1,0:T(8,128)(2,1)S(1)} %get-tuple-element.232), channel_id=1, source_target_pairs={{0,8},{8,16},{16,24},{24,0},{1,9},{9,17},{17,25},{25,1},{2,10},{10... | collective-permute-start | bytes 3145736 | tf_op jit(solution)/shard_map/ppermute | solution.py:134
  48.9 26.2 %collective-permute-start.1 = (bf16[256,2048]{1,0:T(8,128)(2,1)S(1)}, bf16[256,2048]{1,0:T(8,128)(2,1)}, u32[]{:S(2)}, u32[]{:S(2)}) collective-permute-start(bf16[256,2048]{1,0:T(8,128)(2,1)S(1)} %collective-permute-done), channel_id=1, source_target_pairs={{0,8},{8,16},{16,24},{24,0},{1,9},{9,17},{17,25},{25,1},{2,10},{10... | collective-permute-start | bytes 3145736 | tf_op jit(solution)/shard_map/ppermute | solution.py:134
  75.1 25.6 %collective-permute-start.2 = (bf16[256,2048]{1,0:T(8,128)(2,1)}, bf16[256,2048]{1,0:T(8,128)(2,1)}, u32[]{:S(2)}, u32[]{:S(2)}) collective-permute-start(bf16[256,2048]{1,0:T(8,128)(2,1)} %collective-permute-done.1), channel_id=1, source_target_pairs={{0,8},{8,16},{16,24},{24,0},{1,9},{9,17},{17,25},{25,1},{2,10},{10... | collective-permute-start | bytes 3145736 | tf_op jit(solution)/shard_map/ppermute | solution.py:134
  103.4 30.6 %collective-permute-start.3 = (bf16[256,2048]{1,0:T(8,128)(2,1)}, bf16[256,2048]{1,0:T(8,128)(2,1)}, u32[]{:S(2)}, u32[]{:S(2)}) collective-permute-start(bf16[256,2048]{1,0:T(8,128)(2,1)} %param.19), channel_id=1, source_target_pairs={{0,8},{8,16},{16,24},{24,0},{1,9},{9,17},{17,25},{25,1},{2,10},{10... | collective-permute-start | bytes 3145736 | tf_op jit(solution)/shard_map/ppermute | solution.py:134
  133.9 24.8 %collective-permute-start.4 = (bf16[256,2048]{1,0:T(8,128)(2,1)}, bf16[256,2048]{1,0:T(8,128)(2,1)}, u32[]{:S(2)}, u32[]{:S(2)}) collective-permute-start(bf16[256,2048]{1,0:T(8,128)(2,1)} %collective-permute-done.3), channel_id=1, source_target_pairs={{0,8},{8,16},{16,24},{24,0},{1,9},{9,17},{17,25},{25,1},{2,10},{10... | collective-permute-start | bytes 3145736 | tf_op jit(solution)/shard_map/ppermute | solution.py:134
  158.7 23.5 %collective-permute-start.5 = (bf16[256,2048]{1,0:T(8,128)(2,1)}, bf16[256,2048]{1,0:T(8,128)(2,1)S(1)}, u32[]{:S(2)}, u32[]{:S(2)}) collective-permute-start(bf16[256,2048]{1,0:T(8,128)(2,1)} %collective-permute-done.4), channel_id=1, source_target_pairs={{0,8},{8,16},{16,24},{24,0},{1,9},{9,17},{17,25},{25,1},{2,10},{10... | collective-permute-start | bytes 3145736 | tf_op jit(solution)/shard_map/ppermute | solution.py:134
  207.5 23.2 %collective-permute-start.7 = (bf16[256,2048]{1,0:T(8,128)(2,1)S(1)}, bf16[256,2048]{1,0:T(8,128)(2,1)S(1)}, u32[]{:S(2)}, u32[]{:S(2)}) collective-permute-start(bf16[256,2048]{1,0:T(8,128)(2,1)S(1)} %add_convert_fusion.10), channel_id=1, source_target_pairs={{0,8},{8,16},{16,24},{24,0},{1,9},{9,17},{17,25},{25,1},{2,10},{10... | collective-permute-start | bytes 3145736 | tf_op jit(solution)/shard_map/ppermute | solution.py:162
  277.5 23.3 %collective-permute-start.10 = (bf16[256,2048]{1,0:T(8,128)(2,1)S(1)}, bf16[256,2048]{1,0:T(8,128)(2,1)}, u32[]{:S(2)}, u32[]{:S(2)}) collective-permute-start(bf16[256,2048]{1,0:T(8,128)(2,1)S(1)} %collective-permute-done.9), channel_id=1, source_target_pairs={{0,8},{8,16},{16,24},{24,0},{1,9},{9,17},{17,25},{25,1},{2,10},{10... | collective-permute-start | bytes 3145736 | tf_op jit(solution)/shard_map/ppermute | solution.py:134
  300.9 32.4 %collective-permute-start.11 = (bf16[256,2048]{1,0:T(8,128)(2,1)}, bf16[256,2048]{1,0:T(8,128)(2,1)}, u32[]{:S(2)}, u32[]{:S(2)}) collective-permute-start(bf16[256,2048]{1,0:T(8,128)(2,1)} %collective-permute-done.10), channel_id=1, source_target_pairs={{0,8},{8,16},{16,24},{24,0},{1,9},{9,17},{17,25},{25,1},{2,10},{10... | collective-permute-start | bytes 3145736 | tf_op jit(solution)/shard_map/ppermute | solution.py:134
  322.7 51.5 %collective-permute-start.12 = (bf16[256,2048]{1,0:T(8,128)(2,1)}, bf16[256,2048]{1,0:T(8,128)(2,1)}, u32[]{:S(2)}, u32[]{:S(2)}) collective-permute-start(bf16[256,2048]{1,0:T(8,128)(2,1)} %convolution_convert_fusion.2), channel_id=1, source_target_pairs={{0,8},{8,16},{16,24},{24,0},{1,9},{9,17},{17,25},{25,1},{2,10},{10... | collective-permute-start | bytes 3145736 | tf_op jit(solution)/shard_map/ppermute | solution.py:162
  374.2 261.4 %reduce-scatter.7.cloned.1.call-start = ((), (), s32[]{:S(2)}) async-start(), calls=%async_computation.8 | async-start | bytes 18874368 | tf_op jit(solution)/shard_map/reduce_scatter | solution.py:222
  437.5 29.3 %collective-permute-start.15 = (bf16[256,2048]{1,0:T(8,128)(2,1)}, bf16[256,2048]{1,0:T(8,128)(2,1)S(1)}, u32[]{:S(2)}, u32[]{:S(2)}) collective-permute-start(bf16[256,2048]{1,0:T(8,128)(2,1)} %get-tuple-element.227), channel_id=1, source_target_pairs={{0,8},{8,16},{16,24},{24,0},{1,9},{9,17},{17,25},{25,1},{2,10},{10... | collective-permute-start | bytes 3145736 | tf_op jit(solution)/shard_map/ppermute | solution.py:134
  467.8 234.0 %reduce-scatter.11.cloned.1.call-start = ((), (), s32[]{:S(2)}) async-start(), calls=%async_computation.10 | async-start | bytes 2359296 | tf_op jit(solution)/shard_map/reduce_scatter | solution.py:222
  470.3 24.6 %collective-permute-start.16 = (bf16[256,2048]{1,0:T(8,128)(2,1)}, bf16[256,2048]{1,0:T(8,128)(2,1)}, u32[]{:S(2)}, u32[]{:S(2)}) collective-permute-start(bf16[256,2048]{1,0:T(8,128)(2,1)} %copy-done.43), channel_id=1, source_target_pairs={{0,8},{8,16},{16,24},{24,0},{1,9},{9,17},{17,25},{25,1},{2,10},{10... | collective-permute-start | bytes 3145736 | tf_op jit(solution)/shard_map/ppermute | solution.py:134
  494.9 24.8 %collective-permute-start.17 = (bf16[256,2048]{1,0:T(8,128)(2,1)}, bf16[256,2048]{1,0:T(8,128)(2,1)S(1)}, u32[]{:S(2)}, u32[]{:S(2)}) collective-permute-start(bf16[256,2048]{1,0:T(8,128)(2,1)} %collective-permute-done.16), channel_id=1, source_target_pairs={{0,8},{8,16},{16,24},{24,0},{1,9},{9,17},{17,25},{25,1},{2,10},{10... | collective-permute-start | bytes 3145736 | tf_op jit(solution)/shard_map/ppermute | solution.py:134
  520.8 76.2 %collective-permute-start.18 = (bf16[256,2048]{1,0:T(8,128)(2,1)}, bf16[256,2048]{1,0:T(8,128)(2,1)}, u32[]{:S(2)}, u32[]{:S(2)}) collective-permute-start(bf16[256,2048]{1,0:T(8,128)(2,1)} %fusion.134), channel_id=1, source_target_pairs={{0,8},{8,16},{16,24},{24,0},{1,9},{9,17},{17,25},{25,1},{2,10},{10... | collective-permute-start | bytes 3145736 | tf_op jit(solution)/shard_map/ppermute | solution.py:162
  585.7 117.8 %reduce-scatter.9.cloned.1.call-start = ((), (), s32[]{:S(2)}) async-start(), calls=%async_computation.9 | async-start | bytes 7077888 | tf_op jit(solution)/shard_map/reduce_scatter | solution.py:222
  599.6 24.8 %collective-permute-start.19 = (bf16[256,2048]{1,0:T(8,128)(2,1)}, bf16[256,2048]{1,0:T(8,128)(2,1)}, u32[]{:S(2)}, u32[]{:S(2)}) collective-permute-start(bf16[256,2048]{1,0:T(8,128)(2,1)} %add_convert_fusion.6), channel_id=1, source_target_pairs={{0,8},{8,16},{16,24},{24,0},{1,9},{9,17},{17,25},{25,1},{2,10},{10... | collective-permute-start | bytes 3145736 | tf_op jit(solution)/shard_map/ppermute | solution.py:162
  643.5 40.6 %collective-permute-start.20 = (bf16[256,2048]{1,0:T(8,128)(2,1)S(1)}, bf16[256,2048]{1,0:T(8,128)(2,1)S(1)}, u32[]{:S(2)}, u32[]{:S(2)}) collective-permute-start(bf16[256,2048]{1,0:T(8,128)(2,1)S(1)} %add_convert_fusion.3), channel_id=1, source_target_pairs={{0,8},{8,16},{16,24},{24,0},{1,9},{9,17},{17,25},{25,1},{2,10},{10... | collective-permute-start | bytes 3145736 | tf_op jit(solution)/shard_map/ppermute | solution.py:162
  665.2 31.7 %collective-permute-start.22 = (bf16[256,2048]{1,0:T(8,128)(2,1)S(1)}, bf16[256,2048]{1,0:T(8,128)(2,1)S(1)}, u32[]{:S(2)}, u32[]{:S(2)}) collective-permute-start(bf16[256,2048]{1,0:T(8,128)(2,1)S(1)} %add_convert_fusion.1), channel_id=1, source_target_pairs={{0,8},{8,16},{16,24},{24,0},{1,9},{9,17},{17,25},{25,1},{2,10},{10... | collective-permute-start | bytes 3145736 | tf_op jit(solution)/shard_map/ppermute | solution.py:162
  (83 other events, 906.6 us)
Sparse Core Ops, SparseCore 0:
  12.8 58.5 all-gather.5
  73.3 55.8 all-gather.3
  131.7 89.7 all-gather.7
  374.4 72.9 reduce-scatter.4
  467.9 115.0 reduce-scatter.6
  586.1 42.9 reduce-scatter.10
  635.7 64.6 reduce-scatter.8

commit v14 on v13

--- a/solution.py
+++ b/solution.py
@@ -357,31 +357,33 @@
         )
         return dict(mixed=mixed, log_total=log_total)
 
-    def out_project(done):
-        attended = merge_heads(done[1]["mixed"].astype(jnp.bfloat16))
-        return dict(attended=attended, attn_partial=times_transpose(attended, output_t))
-
     cot_later, first_rows = lax.optimization_barrier((cotangent, first_rows))
     cot_ring = RingGather(cot_later, "row")
-    projected, attention, mixed_out = overlap(cot_ring, [project, attend, out_project])
+
+    def attend_and_project(done):
+        attention = attend(done)
+        attended = merge_heads(attention["mixed"].astype(jnp.bfloat16))
+        return dict(
+            log_total=attention["log_total"],
+            attended=attended,
+            attn_partial=times_transpose(attended, output_t),
+        )
+
+    def early_cot_grads(done):
+        return tuple(times_transpose(block, full_down) for block in cot_ring.slots)
+
+    projected, mixed_out, early = overlap(cot_ring, [project, attend_and_project, early_cot_grads])
     cot_slots = cot_ring.slots
     queries, keys_rot = projected["queries"], projected["keys_rot"]
     values = projected["values"]
-    log_total, attended = attention["log_total"], mixed_out["attended"]
-    full_down, attn_partial = lax.optimization_barrier((full_down, mixed_out["attn_partial"]))
-    attn_ring = RingScatter(ring_slots(attn_partial, "row"), "row", jnp.bfloat16)
-    cot_count = len(cot_slots)
-    per_step = -(-cot_count // attn_ring.steps())
-
-    def cot_grads(index):
-        def piece(done):
-            chosen = cot_slots[index * per_step : (index + 1) * per_step]
-            return tuple(times_transpose(block, full_down) for block in chosen)
-
-        return piece
-
-    grad_act_parts = overlap(attn_ring, [cot_grads(index) for index in range(attn_ring.steps())])
-    grad_act_slots = [block for part in grad_act_parts for block in part]
+    log_total, attended = mixed_out["log_total"], mixed_out["attended"]
+    attn_ring = RingScatter(ring_slots(mixed_out["attn_partial"], "row"), "row", jnp.bfloat16)
+
+    def late_cot_grads(done):
+        return tuple(times_transpose(block, full_down) for block in cot_slots[len(early) :])
+
+    (late,) = overlap(attn_ring, [late_cot_grads])
+    grad_act_slots = list(early) + list(late)
     attention_sum = attn_ring.result()
     middle = inputs + attention_sum
     normed_second = layer_norm(middle).astype(jnp.bfloat16)

time: 738 us -> 749 us (1.015)
  waiting for transfers between devices: 237 us -> 252 us
    ppermute x12, waiting for transfers between devices: 107 us -> 125 us  [send(): lax.ppermute(value.astype(self.send_dtype), self.axis, [(j, (j + 1) % n)...]
  transfers between devices with their start and end apart: 31 -> 31, of which waited for: 18 -> 17; matrix products, arithmetic and copies ran while one was open for 60% -> 59% of each run, Pallas kernels for 0% -> 0%
where the time goes in v14:
time: 749 us; the launch traced here: 743 us
  matrix products  283 us (38%)
  waiting for transfers between devices  252 us (34%)
  other arithmetic  105 us (14%)
  local copies, waits for them, and re-layouts  65.2 us (9%)
  starting transfers between devices  21.3 us (3%)
  between operations  15.7 us (2%)
    ppermute x12, waiting for transfers between devices, send(): lax.ppermute(self.pending, self.axis, [(j, (j + 1) % n) for j in range(n)])  126 us
    ppermute x12, waiting for transfers between devices, send(): lax.ppermute(value.astype(self.send_dtype), self.axis, [(j, (j + 1) % n)...  125 us
    dot_general x10, matrix products, times_transpose(): lax.dot_general(left, right, (((1,), (1,)), ((), ())), preferred_element_...  90 us
    dot_general x11, matrix products, product(): return jnp.dot(left, right, preferred_element_type=jnp.float32)  73.4 us
    dot_general x4, matrix products, contract_rows(): lax.dot_general(left, right, (((0,), (0,)), ((), ())), preferred_element_...  55.6 us
    convert_element_type x1, other arithmetic, attend_backward(): grad_scores = (probs * (grad_probs - inner)).astype(jnp.bfloat16)  17.8 us
    convert_element_type x8, other arithmetic, send(): value.astype(self.send_dtype)  16 us
    dot_general x2, matrix products, attend_backward(): jnp.einsum('qhd,khd->hqk', grad_mixed, values, preferred_element_type=jnp...  15.6 us
  transfers between devices with their start and end apart: 31, of which 17 were waited for; matrix products, arithmetic and copies ran while one was open for 59% of the time, Pallas kernels for 0%

profile of v14, /device:TPU:0, one launch (start us, length us, event | category | flops | bytes accessed | tf_op | source)
XLA Modules:
  0.0 742.6 jit_solution(9609556285729892306)
XLA Ops:
  23.7 25.2 %collective-permute-done = bf16[256,2048]{1,0:T(8,128)(2,1)S(1)} collective-permute-done((bf16[256,2048]{1,0:T(8,128)(2,1)S(1)}, bf16[256,2048]{1,0:T(8,128)(2,1)S(1)}, u32[]{:S(2)}, u32[]{:S(2)}) %collective-permute-start) | collective-permute-done | bytes 1048608 | tf_op jit(solution)/shard_map/ppermute | solution.py:134
  50.4 24.7 %collective-permute-done.1 = bf16[256,2048]{1,0:T(8,128)(2,1)} collective-permute-done((bf16[256,2048]{1,0:T(8,128)(2,1)S(1)}, bf16[256,2048]{1,0:T(8,128)(2,1)}, u32[]{:S(2)}, u32[]{:S(2)}) %collective-permute-start.1) | collective-permute-done | bytes 1048608 | tf_op jit(solution)/shard_map/ppermute | solution.py:134
  84.8 15.9 %collective-permute-done.2 = bf16[256,2048]{1,0:T(8,128)(2,1)} collective-permute-done((bf16[256,2048]{1,0:T(8,128)(2,1)}, bf16[256,2048]{1,0:T(8,128)(2,1)}, u32[]{:S(2)}, u32[]{:S(2)}) %collective-permute-start.2) | collective-permute-done | bytes 1048608 | tf_op jit(solution)/shard_map/ppermute | solution.py:134
  103.6 10.3 %fusion.15 = f32[1024,1536]{1,0:T(8,128)S(1)} fusion(bf16[1024,2048]{1,0:T(8,128)(2,1)} %constant_dynamic-update-slice_fusion.4, bf16[2048,2048]{0,1:T(8,128)(2,1)} %all-gather.4.cloned.1.call-done), kind=kOutput, calls=%fused_computation.26 | convolution fusion | flops 6442450944 | bytes 16777216 | tf_op jit(solution)/shard_map/dot_general | solution.py:19
  181.1 12.9 %collective-permute-done.6 = bf16[256,2048]{1,0:T(8,128)(2,1)S(1)} collective-permute-done((bf16[256,2048]{1,0:T(8,128)(2,1)}, bf16[256,2048]{1,0:T(8,128)(2,1)S(1)}, u32[]{:S(2)}, u32[]{:S(2)}) %collective-permute-start.6) | collective-permute-done | bytes 1048608 | tf_op jit(solution)/shard_map/ppermute | solution.py:134
  197.6 15.1 %collective-permute-done.5 = bf16[256,2048]{1,0:T(8,128)(2,1)S(1)} collective-permute-done((bf16[256,2048]{1,0:T(8,128)(2,1)S(1)}, bf16[256,2048]{1,0:T(8,128)(2,1)S(1)}, u32[]{:S(2)}, u32[]{:S(2)}) %collective-permute-start.5) | collective-permute-done | bytes 1048608 | tf_op jit(solution)/shard_map/ppermute | solution.py:162
  214.2 22.1 %collective-permute-done.7 = bf16[256,2048]{1,0:T(8,128)(2,1)S(1)} collective-permute-done((bf16[256,2048]{1,0:T(8,128)(2,1)S(1)}, bf16[256,2048]{1,0:T(8,128)(2,1)S(1)}, u32[]{:S(2)}, u32[]{:S(2)}) %collective-permute-start.7) | collective-permute-done | bytes 1048608 | tf_op jit(solution)/shard_map/ppermute | solution.py:162
  237.6 21.5 %collective-permute-done.8 = bf16[256,2048]{1,0:T(8,128)(2,1)S(1)} collective-permute-done((bf16[256,2048]{1,0:T(8,128)(2,1)S(1)}, bf16[256,2048]{1,0:T(8,128)(2,1)S(1)}, u32[]{:S(2)}, u32[]{:S(2)}) %collective-permute-start.8) | collective-permute-done | bytes 1048608 | tf_op jit(solution)/shard_map/ppermute | solution.py:162
  297.1 9.8 %collective-permute-done.10 = bf16[256,2048]{1,0:T(8,128)(2,1)} collective-permute-done((bf16[256,2048]{1,0:T(8,128)(2,1)S(1)}, bf16[256,2048]{1,0:T(8,128)(2,1)}, u32[]{:S(2)}, u32[]{:S(2)}) %collective-permute-start.10) | collective-permute-done | bytes 1048608 | tf_op jit(solution)/shard_map/ppermute | solution.py:134
  317.1 12.0 %convolution_convert_fusion.2 = bf16[256,2048]{1,0:T(8,128)(2,1)} fusion(bf16[2048,4096]{1,0:T(8,128)(2,1)} %all-gather.8.cloned.1.call-done, bf16[256,2048]{1,0:T(8,128)(2,1)} %get-tuple-element.241, bf16[256,2048]{1,0:T(8,128)(2,1)S(1)} %get-tuple-element.240), kind=kOutput, calls=%fused_computation.63 | convolution fusion | flops 4299685888 | bytes 19922944 | tf_op jit(solution)/shard_map/dot_general | solution.py:29
  358.0 12.7 %fusion.19 = bf16[2048,2048]{1,0:T(8,128)(2,1)} fusion(bf16[256,2048]{1,0:T(8,128)(2,1)S(1)} %get-tuple-element.237, bf16[256,2048]{1,0:T(8,128)(2,1)S(1)} %get-tuple-element.177, bf16[256,2048]{1,0:T(8,128)(2,1)S(1)} %copy-done.41, bf16[256,2048]{1,0:T(8,128)(2,1)S(1)} %copy-done.39, bf16[256,2048]{1,0:T(8,128)(2,1)S(1)} %copy-done.62, ...), kind=kOutput, calls=%fused_computation.30 | convolution fusion | flops 8623489024 | bytes 16777216 | tf_op jit(solution)/shard_map/dot_general | solution.py:23
  370.8 12.2 %fusion.119 = f32[256,2048]{1,0:T(8,128)} fusion(bf16[2048,4096]{1,0:T(8,128)(2,1)} %all-gather.8.cloned.1.call-done, bf16[256,2048]{1,0:T(8,128)(2,1)} %copy-done.28, bf16[256,2048]{1,0:T(8,128)(2,1)} %copy-done.27), kind=kOutput, calls=%fused_computation.216 | convolution fusion | flops 4299161600 | bytes 20971520 | tf_op jit(solution)/shard_map/dot_general | solution.py:29
  394.8 13.1 %fusion.118 = f32[256,2048]{1,0:T(8,128)} fusion(bf16[2048,4096]{1,0:T(8,128)(2,1)} %all-gather.8.cloned.1.call-done, bf16[256,2048]{1,0:T(8,128)(2,1)} %get-tuple-element.226, bf16[256,2048]{1,0:T(8,128)(2,1)S(1)} %get-tuple-element.225), kind=kOutput, calls=%fused_computation.215 | convolution fusion | flops 4299161600 | bytes 20971520 | tf_op jit(solution)/shard_map/dot_general | solution.py:29
  418.9 12.8 %fusion.117 = f32[256,2048]{1,0:T(8,128)} fusion(bf16[2048,4096]{1,0:T(8,128)(2,1)} %all-gather.8.cloned.1.call-done, bf16[256,2048]{1,0:T(8,128)(2,1)} %copy-done.26, bf16[256,2048]{1,0:T(8,128)(2,1)} %copy-done.25), kind=kOutput, calls=%fused_computation.214 | convolution fusion | flops 4299161600 | bytes 20971520 | tf_op jit(solution)/shard_map/dot_general | solution.py:29
  445.6 26.0 %fusion.2 = bf16[2048,4096]{1,0:T(8,128)(2,1)} fusion(bf16[256,4096]{1,0:T(8,128)(2,1)} %pad_maximum_fusion.5, bf16[256,4096]{1,0:T(8,128)(2,1)} %pad_maximum_fusion.4, bf16[256,2048]{1,0:T(8,128)(2,1)} %get-tuple-element.241, bf16[256,2048]{1,0:T(8,128)(2,1)} %copy-done.49, bf16[256,4096]{1,0:T(8,128)(2,1)} %pad_maximum_fusion.6, ...), kind=kOutput, calls=%fused_computation.5 | convolution fusion | flops 17238589440 | bytes 29360128 | tf_op jit(solution)/shard_map/dot_general | solution.py:23
  486.4 16.8 %collective-permute-done.16 = bf16[256,2048]{1,0:T(8,128)(2,1)} collective-permute-done((bf16[256,2048]{1,0:T(8,128)(2,1)}, bf16[256,2048]{1,0:T(8,128)(2,1)}, u32[]{:S(2)}, u32[]{:S(2)}) %collective-permute-start.16) | collective-permute-done | bytes 1048608 | tf_op jit(solution)/shard_map/ppermute | solution.py:134
  513.4 17.6 %collective-permute-done.17 = bf16[256,2048]{1,0:T(8,128)(2,1)S(1)} collective-permute-done((bf16[256,2048]{1,0:T(8,128)(2,1)}, bf16[256,2048]{1,0:T(8,128)(2,1)S(1)}, u32[]{:S(2)}, u32[]{:S(2)}) %collective-permute-start.17) | collective-permute-done | bytes 1048608 | tf_op jit(solution)/shard_map/ppermute | solution.py:134
  545.1 10.9 %multiply_reduce_fusion = (f32[2,1024]{1,0:T(2,128)S(1)}, f32[2,1024]{1,0:T(2,128)S(1)}, f32[2,1024,1024]{1,2,0:T(8,128)}) fusion(f32[2,1024,1024]{1,2,0:T(8,128)S(1)} %bitcast.127, f32[2,1024]{1,0:T(2,128)S(1)} %get-tuple-element.269, pred[1024,1024]{0,1:T(8,128)(4,1)S(1)} %copy-done.1, f32[2,1024,1024]{1,2,0:T(8,128)} %fusion.87, ...), kind=kOutput, calls=%fused_computation.16 | convolution fusion | flops 557838336 | bytes 35684352 | tf_op jit(solution)/shard_map/while/body/eval_jaxpr/qhd,khd->hqk/dot_general | solution.py:307
  556.0 17.8 %multiply_convert_fusion = (bf16[2,1024,1024]{1,2,0:T(8,128)(2,1)}, bf16[2,1024,1024]{1,2,0:T(8,128)(2,1)}) fusion(f32[2,1024,1024]{1,2,0:T(8,128)} %get-tuple-element.274, f32[2,1024,1024]{1,2,0:T(8,128)} %fusion.89, f32[2,1024]{1,0:T(2,128)S(1)} %get-tuple-element.216, f32[2,1024]{1,0:T(2,128)S(1)} %get-tuple-element.269, ...), kind=kLoop, calls=%fused_computation.15 | loop fusion | flops 25165824 | bytes 43024384 | tf_op jit(solution)/shard_map/while/body/eval_jaxpr/convert_element_type | solution.py:309
  624.8 11.2 %fusion.13 = f32[1024,2048]{1,0:T(8,128)} fusion(bf16[2048,2048]{0,1:T(8,128)(2,1)} %all-gather.4.cloned.1.call-done, bf16[1024,512]{0,1:T(8,128)(2,1)S(1)} %bitcast.135, bf16[1024,512]{0,1:T(8,128)(2,1)S(1)} %bitcast.131, bf16[1024,512]{0,1:T(8,128)(2,1)S(1)} %bitcast.133), kind=kOutput, calls=%fused_computation.24 | convolution fusion | flops 6451888128 | bytes 17825792 | tf_op jit(solution)/shard_map/dot_general | solution.py:29
  635.9 11.1 %convolution_convert_fusion = bf16[2048,1536]{1,0:T(8,128)(2,1)} fusion(bf16[1024,2048]{1,0:T(8,128)(2,1)} %constant_dynamic-update-slice_fusion.4, bf16[1024,1536]{0,1:T(8,128)(2,1)S(1)} %pad_maximum_fusion), kind=kOutput, calls=%fused_computation.23 | convolution fusion | flops 6445596672 | bytes 13631488 | tf_op jit(solution)/shard_map/dot_general | solution.py:23
  659.6 15.9 %collective-permute-done.21 = bf16[256,2048]{1,0:T(8,128)(2,1)S(1)} collective-permute-done((bf16[256,2048]{1,0:T(8,128)(2,1)S(1)}, bf16[256,2048]{1,0:T(8,128)(2,1)S(1)}, u32[]{:S(2)}, u32[]{:S(2)}) %collective-permute-start.21) | collective-permute-done | bytes 1048608 | tf_op jit(solution)/shard_map/ppermute | solution.py:162
  677.6 18.3 %collective-permute-done.20 = bf16[256,2048]{1,0:T(8,128)(2,1)S(1)} collective-permute-done((bf16[256,2048]{1,0:T(8,128)(2,1)S(1)}, bf16[256,2048]{1,0:T(8,128)(2,1)S(1)}, u32[]{:S(2)}, u32[]{:S(2)}) %collective-permute-start.20) | collective-permute-done | bytes 1048608 | tf_op jit(solution)/shard_map/ppermute | solution.py:162
  695.8 13.4 %collective-permute-done.22 = bf16[256,2048]{1,0:T(8,128)(2,1)S(1)} collective-permute-done((bf16[256,2048]{1,0:T(8,128)(2,1)S(1)}, bf16[256,2048]{1,0:T(8,128)(2,1)S(1)}, u32[]{:S(2)}, u32[]{:S(2)}) %collective-permute-start.22) | collective-permute-done | bytes 1048608 | tf_op jit(solution)/shard_map/ppermute | solution.py:162
  (322 shorter events, 347.5 us)
Async XLA Ops:
  7.2 96.4 %all-gather.4.cloned.1.call-start = ((), (), s32[]{:S(2)}) async-start(), calls=%async_computation.4 | async-start | bytes 9437184 | tf_op jit(solution)/shard_map/all_gather | solution.py:217
  12.7 145.6 %all-gather.6.cloned.1.call-start = ((), (), s32[]{:S(2)}) async-start(), calls=%async_computation.5 | async-start | bytes 9437184 | tf_op jit(solution)/shard_map/all_gather | solution.py:217
  13.4 246.9 %all-gather.8.cloned.1.call-start = ((), (), s32[]{:S(2)}) async-start(), calls=%async_computation.6 | async-start | bytes 18874368 | tf_op jit(solution)/shard_map/all_gather | solution.py:217
  15.0 495.7 %reduce-scatter.5.cloned.1.call-start = ((), (), s32[]{:S(2)}) async-start(), calls=%async_computation.7 | async-start | bytes 9437184 | tf_op jit(solution)/shard_map/reduce_scatter | solution.py:222
  20.7 28.2 %collective-permute-start = (bf16[256,2048]{1,0:T(8,128)(2,1)S(1)}, bf16[256,2048]{1,0:T(8,128)(2,1)S(1)}, u32[]{:S(2)}, u32[]{:S(2)}) collective-permute-start(bf16[256,2048]{1,0:T(8,128)(2,1)S(1)} %get-tuple-element.224), channel_id=1, source_target_pairs={{0,8},{8,16},{16,24},{24,0},{1,9},{9,17},{17,25},{25,1},{2,10},{10... | collective-permute-start | bytes 3145736 | tf_op jit(solution)/shard_map/ppermute | solution.py:134
  48.9 26.2 %collective-permute-start.1 = (bf16[256,2048]{1,0:T(8,128)(2,1)S(1)}, bf16[256,2048]{1,0:T(8,128)(2,1)}, u32[]{:S(2)}, u32[]{:S(2)}) collective-permute-start(bf16[256,2048]{1,0:T(8,128)(2,1)S(1)} %collective-permute-done), channel_id=1, source_target_pairs={{0,8},{8,16},{16,24},{24,0},{1,9},{9,17},{17,25},{25,1},{2,10},{10... | collective-permute-start | bytes 3145736 | tf_op jit(solution)/shard_map/ppermute | solution.py:134
  75.1 25.6 %collective-permute-start.2 = (bf16[256,2048]{1,0:T(8,128)(2,1)}, bf16[256,2048]{1,0:T(8,128)(2,1)}, u32[]{:S(2)}, u32[]{:S(2)}) collective-permute-start(bf16[256,2048]{1,0:T(8,128)(2,1)} %collective-permute-done.1), channel_id=1, source_target_pairs={{0,8},{8,16},{16,24},{24,0},{1,9},{9,17},{17,25},{25,1},{2,10},{10... | collective-permute-start | bytes 3145736 | tf_op jit(solution)/shard_map/ppermute | solution.py:134
  103.3 30.6 %collective-permute-start.3 = (bf16[256,2048]{1,0:T(8,128)(2,1)}, bf16[256,2048]{1,0:T(8,128)(2,1)}, u32[]{:S(2)}, u32[]{:S(2)}) collective-permute-start(bf16[256,2048]{1,0:T(8,128)(2,1)} %param.19), channel_id=1, source_target_pairs={{0,8},{8,16},{16,24},{24,0},{1,9},{9,17},{17,25},{25,1},{2,10},{10... | collective-permute-start | bytes 3145736 | tf_op jit(solution)/shard_map/ppermute | solution.py:134
  133.9 32.0 %collective-permute-start.4 = (bf16[256,2048]{1,0:T(8,128)(2,1)}, bf16[256,2048]{1,0:T(8,128)(2,1)}, u32[]{:S(2)}, u32[]{:S(2)}) collective-permute-start(bf16[256,2048]{1,0:T(8,128)(2,1)} %collective-permute-done.3), channel_id=1, source_target_pairs={{0,8},{8,16},{16,24},{24,0},{1,9},{9,17},{17,25},{25,1},{2,10},{10... | collective-permute-start | bytes 3145736 | tf_op jit(solution)/shard_map/ppermute | solution.py:134
  165.9 28.0 %collective-permute-start.6 = (bf16[256,2048]{1,0:T(8,128)(2,1)}, bf16[256,2048]{1,0:T(8,128)(2,1)S(1)}, u32[]{:S(2)}, u32[]{:S(2)}) collective-permute-start(bf16[256,2048]{1,0:T(8,128)(2,1)} %collective-permute-done.4), channel_id=1, source_target_pairs={{0,8},{8,16},{16,24},{24,0},{1,9},{9,17},{17,25},{25,1},{2,10},{10... | collective-permute-start | bytes 3145736 | tf_op jit(solution)/shard_map/ppermute | solution.py:134
  171.4 41.3 %collective-permute-start.5 = (bf16[256,2048]{1,0:T(8,128)(2,1)S(1)}, bf16[256,2048]{1,0:T(8,128)(2,1)S(1)}, u32[]{:S(2)}, u32[]{:S(2)}) collective-permute-start(bf16[256,2048]{1,0:T(8,128)(2,1)S(1)} %dynamic-slice_convert_fusion.1), channel_id=1, source_target_pairs={{0,8},{8,16},{16,24},{24,0},{1,9},{9,17},{17,25},{25,1},{2,10},{10... | collective-permute-start | bytes 3145736 | tf_op jit(solution)/shard_map/ppermute | solution.py:162
  213.0 23.3 %collective-permute-start.7 = (bf16[256,2048]{1,0:T(8,128)(2,1)S(1)}, bf16[256,2048]{1,0:T(8,128)(2,1)S(1)}, u32[]{:S(2)}, u32[]{:S(2)}) collective-permute-start(bf16[256,2048]{1,0:T(8,128)(2,1)S(1)} %add_convert_fusion.10), channel_id=1, source_target_pairs={{0,8},{8,16},{16,24},{24,0},{1,9},{9,17},{17,25},{25,1},{2,10},{10... | collective-permute-start | bytes 3145736 | tf_op jit(solution)/shard_map/ppermute | solution.py:162
  306.8 35.2 %collective-permute-start.11 = (bf16[256,2048]{1,0:T(8,128)(2,1)}, bf16[256,2048]{1,0:T(8,128)(2,1)}, u32[]{:S(2)}, u32[]{:S(2)}) collective-permute-start(bf16[256,2048]{1,0:T(8,128)(2,1)} %collective-permute-done.10), channel_id=1, source_target_pairs={{0,8},{8,16},{16,24},{24,0},{1,9},{9,17},{17,25},{25,1},{2,10},{10... | collective-permute-start | bytes 3145736 | tf_op jit(solution)/shard_map/ppermute | solution.py:134
  329.1 53.9 %collective-permute-start.12 = (bf16[256,2048]{1,0:T(8,128)(2,1)}, bf16[256,2048]{1,0:T(8,128)(2,1)}, u32[]{:S(2)}, u32[]{:S(2)}) collective-permute-start(bf16[256,2048]{1,0:T(8,128)(2,1)} %convolution_convert_fusion.2), channel_id=1, source_target_pairs={{0,8},{8,16},{16,24},{24,0},{1,9},{9,17},{17,25},{25,1},{2,10},{10... | collective-permute-start | bytes 3145736 | tf_op jit(solution)/shard_map/ppermute | solution.py:162
  383.0 264.0 %reduce-scatter.7.cloned.1.call-start = ((), (), s32[]{:S(2)}) async-start(), calls=%async_computation.8 | async-start | bytes 18874368 | tf_op jit(solution)/shard_map/reduce_scatter | solution.py:222
  445.3 26.4 %collective-permute-start.15 = (bf16[256,2048]{1,0:T(8,128)(2,1)}, bf16[256,2048]{1,0:T(8,128)(2,1)S(1)}, u32[]{:S(2)}, u32[]{:S(2)}) collective-permute-start(bf16[256,2048]{1,0:T(8,128)(2,1)} %get-tuple-element.219), channel_id=1, source_target_pairs={{0,8},{8,16},{16,24},{24,0},{1,9},{9,17},{17,25},{25,1},{2,10},{10... | collective-permute-start | bytes 3145736 | tf_op jit(solution)/shard_map/ppermute | solution.py:134
  472.6 241.3 %reduce-scatter.11.cloned.1.call-start = ((), (), s32[]{:S(2)}) async-start(), calls=%async_computation.10 | async-start | bytes 2359296 | tf_op jit(solution)/shard_map/reduce_scatter | solution.py:222
  475.2 28.1 %collective-permute-start.16 = (bf16[256,2048]{1,0:T(8,128)(2,1)}, bf16[256,2048]{1,0:T(8,128)(2,1)}, u32[]{:S(2)}, u32[]{:S(2)}) collective-permute-start(bf16[256,2048]{1,0:T(8,128)(2,1)} %copy-done.43), channel_id=1, source_target_pairs={{0,8},{8,16},{16,24},{24,0},{1,9},{9,17},{17,25},{25,1},{2,10},{10... | collective-permute-start | bytes 3145736 | tf_op jit(solution)/shard_map/ppermute | solution.py:134
  503.2 27.8 %collective-permute-start.17 = (bf16[256,2048]{1,0:T(8,128)(2,1)}, bf16[256,2048]{1,0:T(8,128)(2,1)S(1)}, u32[]{:S(2)}, u32[]{:S(2)}) collective-permute-start(bf16[256,2048]{1,0:T(8,128)(2,1)} %collective-permute-done.16), channel_id=1, source_target_pairs={{0,8},{8,16},{16,24},{24,0},{1,9},{9,17},{17,25},{25,1},{2,10},{10... | collective-permute-start | bytes 3145736 | tf_op jit(solution)/shard_map/ppermute | solution.py:134
  532.1 76.1 %collective-permute-start.18 = (bf16[256,2048]{1,0:T(8,128)(2,1)}, bf16[256,2048]{1,0:T(8,128)(2,1)}, u32[]{:S(2)}, u32[]{:S(2)}) collective-permute-start(bf16[256,2048]{1,0:T(8,128)(2,1)} %fusion.134), channel_id=1, source_target_pairs={{0,8},{8,16},{16,24},{24,0},{1,9},{9,17},{17,25},{25,1},{2,10},{10... | collective-permute-start | bytes 3145736 | tf_op jit(solution)/shard_map/ppermute | solution.py:162
  596.7 119.0 %reduce-scatter.9.cloned.1.call-start = ((), (), s32[]{:S(2)}) async-start(), calls=%async_computation.9 | async-start | bytes 7077888 | tf_op jit(solution)/shard_map/reduce_scatter | solution.py:222
  610.9 25.0 %collective-permute-start.19 = (bf16[256,2048]{1,0:T(8,128)(2,1)}, bf16[256,2048]{1,0:T(8,128)(2,1)}, u32[]{:S(2)}, u32[]{:S(2)}) collective-permute-start(bf16[256,2048]{1,0:T(8,128)(2,1)} %add_convert_fusion.6), channel_id=1, source_target_pairs={{0,8},{8,16},{16,24},{24,0},{1,9},{9,17},{17,25},{25,1},{2,10},{10... | collective-permute-start | bytes 3145736 | tf_op jit(solution)/shard_map/ppermute | solution.py:162
  655.8 40.0 %collective-permute-start.20 = (bf16[256,2048]{1,0:T(8,128)(2,1)S(1)}, bf16[256,2048]{1,0:T(8,128)(2,1)S(1)}, u32[]{:S(2)}, u32[]{:S(2)}) collective-permute-start(bf16[256,2048]{1,0:T(8,128)(2,1)S(1)} %add_convert_fusion.3), channel_id=1, source_target_pairs={{0,8},{8,16},{16,24},{24,0},{1,9},{9,17},{17,25},{25,1},{2,10},{10... | collective-permute-start | bytes 3145736 | tf_op jit(solution)/shard_map/ppermute | solution.py:162
  677.5 31.8 %collective-permute-start.22 = (bf16[256,2048]{1,0:T(8,128)(2,1)S(1)}, bf16[256,2048]{1,0:T(8,128)(2,1)S(1)}, u32[]{:S(2)}, u32[]{:S(2)}) collective-permute-start(bf16[256,2048]{1,0:T(8,128)(2,1)S(1)} %add_convert_fusion.1), channel_id=1, source_target_pairs={{0,8},{8,16},{16,24},{24,0},{1,9},{9,17},{17,25},{25,1},{2,10},{10... | collective-permute-start | bytes 3145736 | tf_op jit(solution)/shard_map/ppermute | solution.py:162
  (82 other events, 864.8 us)
Sparse Core Ops, SparseCore 0:
  12.8 58.5 all-gather.3
  73.3 55.8 all-gather.5
  131.7 89.7 all-gather.7
  383.1 70.2 reduce-scatter.4
  472.7 115.7 reduce-scatter.6
  596.9 40.5 reduce-scatter.10
  647.2 61.6 reduce-scatter.8

commit v15 on v11

--- a/solution.py
+++ b/solution.py
@@ -453,7 +453,6 @@
     ffn_parts, grad_branch = lax.optimization_barrier((ffn_parts, grad_branch))
     ffn_ring = RingScatter(list(ffn_parts), "row", jnp.bfloat16)
     output_sum = col_scatter(contract_rows(attended, grad_branch), 1)
-    half = heads_local // 2
 
     def heads_backward(lo, hi):
         def piece(done):
@@ -486,10 +485,7 @@
         ).astype(jnp.bfloat16)
         return (grad_qkv, times_transpose(grad_qkv, full_qkv))
 
-    def second_group_and_finish(done):
-        return finish(done + (heads_backward(half, heads_local)(done),))
-
-    pieces = [heads_backward(0, half), second_group_and_finish]
+    pieces = [heads_backward(0, heads_local), finish]
     grad_qkv, first_partial = overlap(ffn_ring, pieces)[-1]
     ffn_sum = ffn_ring.result()
     output = (middle + ffn_sum).astype(jnp.bfloat16)

time: 734 us -> 732 us (level)
  waiting for transfers between devices: 242 us -> 288 us
  matrix products: 285 us -> 268 us
  other arithmetic: 103 us -> 87.1 us
  local copies, waits for them, and re-layouts: 62 us -> 51.6 us
    ppermute x12, waiting for transfers between devices: 134 us -> 156 us  [send(): lax.ppermute(self.pending, self.axis, [(j, (j + 1) % n) for j in range(n)])]
    reduce_scatter x4, waiting for transfers between devices: 0.03 us -> 15.3 us  [col_scatter(): lax.psum_scatter(low_part, COL, scatter_dimension=axis, tiled=True)]
    convert_element_type x1, other arithmetic: 17.2 us -> 8.21 us  [attend_backward(): grad_scores = (probs * (grad_probs - inner)).astype(jnp.bfloat16)]
    ppermute x12, waiting for transfers between devices: 107 us -> 115 us  [send(): lax.ppermute(value.astype(self.send_dtype), self.axis, [(j, (j + 1) % n)...]
    dot_general x3 -> x1, matrix products: 15.9 us -> 7.72 us  [masked_scores(): jnp.einsum('qhd,khd->hqk', queries, keys_rot, preferred_element_type=jnp....]
    dot_general x11 -> x10, matrix products: 90.8 us -> 85.7 us  [times_transpose(): lax.dot_general(left, right, (((1,), (1,)), ((), ())), preferred_element_...]
    dot_general x2 -> x1, matrix products: 16 us -> 14.8 us  [attend_backward(): jnp.einsum('qhd,khd->hqk', grad_mixed, values, preferred_element_type=jnp...]
  transfers between devices with their start and end apart: 32 -> 32, of which waited for: 18 -> 20; matrix products, arithmetic and copies ran while one was open for 60% -> 51% of each run, Pallas kernels for 0% -> 0%
where the time goes in v15:
time: 732 us; the launch traced here: 723 us
  waiting for transfers between devices  288 us (39%)
  matrix products  268 us (37%)
  other arithmetic  87.1 us (12%)
  local copies, waits for them, and re-layouts  51.6 us (7%)
  between operations  15.4 us (2%)
  starting transfers between devices  13.2 us (2%)
    ppermute x12, waiting for transfers between devices, send(): lax.ppermute(self.pending, self.axis, [(j, (j + 1) % n) for j in range(n)])  156 us
    ppermute x12, waiting for transfers between devices, send(): lax.ppermute(value.astype(self.send_dtype), self.axis, [(j, (j + 1) % n)...  115 us
    dot_general x10, matrix products, times_transpose(): lax.dot_general(left, right, (((1,), (1,)), ((), ())), preferred_element_...  85.7 us
    dot_general x10, matrix products, product(): return jnp.dot(left, right, preferred_element_type=jnp.float32)  75.9 us
    dot_general x4, matrix products, contract_rows(): lax.dot_general(left, right, (((0,), (0,)), ((), ())), preferred_element_...  56 us
    reduce_scatter x4, waiting for transfers between devices, col_scatter(): lax.psum_scatter(low_part, COL, scatter_dimension=axis, tiled=True)  15.3 us
    dot_general x1, matrix products, attend_backward(): jnp.einsum('qhd,khd->hqk', grad_mixed, values, preferred_element_type=jnp...  14.8 us
  transfers between devices with their start and end apart: 32, of which 20 were waited for; matrix products, arithmetic and copies ran while one was open for 51% of the time, Pallas kernels for 0%

profile of v15, /device:TPU:0, one launch (start us, length us, event | category | flops | bytes accessed | tf_op | source)
XLA Modules:
  0.0 723.1 jit_solution(9201778459829182630)
XLA Ops:
  21.2 25.1 %collective-permute-done = bf16[256,2048]{1,0:T(8,128)(2,1)S(1)} collective-permute-done((bf16[256,2048]{1,0:T(8,128)(2,1)S(1)}, bf16[256,2048]{1,0:T(8,128)(2,1)S(1)}, u32[]{:S(2)}, u32[]{:S(2)}) %collective-permute-start) | collective-permute-done | bytes 1048608 | tf_op jit(solution)/shard_map/ppermute | solution.py:134
  47.9 24.7 %collective-permute-done.1 = bf16[256,2048]{1,0:T(8,128)(2,1)} collective-permute-done((bf16[256,2048]{1,0:T(8,128)(2,1)S(1)}, bf16[256,2048]{1,0:T(8,128)(2,1)}, u32[]{:S(2)}, u32[]{:S(2)}) %collective-permute-start.1) | collective-permute-done | bytes 1048608 | tf_op jit(solution)/shard_map/ppermute | solution.py:134
  81.6 16.6 %collective-permute-done.2 = bf16[256,2048]{1,0:T(8,128)(2,1)} collective-permute-done((bf16[256,2048]{1,0:T(8,128)(2,1)}, bf16[256,2048]{1,0:T(8,128)(2,1)}, u32[]{:S(2)}, u32[]{:S(2)}) %collective-permute-start.2) | collective-permute-done | bytes 1048608 | tf_op jit(solution)/shard_map/ppermute | solution.py:134
  100.6 10.1 %fusion.83 = f32[1024,1536]{1,0:T(8,128)S(1)} fusion(bf16[1024,2048]{1,0:T(8,128)(2,1)} %constant_dynamic-update-slice_fusion.4, bf16[2048,1536]{1,0:T(8,128)(2,1)} %all-gather.5.cloned.1.call-done), kind=kOutput, calls=%fused_computation.169 | convolution fusion | flops 6442450944 | bytes 16777216 | tf_op jit(solution)/shard_map/dot_general | solution.py:19
  156.3 19.8 %collective-permute-done.5 = bf16[256,2048]{1,0:T(8,128)(2,1)S(1)} collective-permute-done((bf16[256,2048]{1,0:T(8,128)(2,1)}, bf16[256,2048]{1,0:T(8,128)(2,1)S(1)}, u32[]{:S(2)}, u32[]{:S(2)}) %collective-permute-start.5) | collective-permute-done | bytes 1048608 | tf_op jit(solution)/shard_map/ppermute | solution.py:134
  190.3 10.9 %collective-permute-done.6 = bf16[256,2048]{1,0:T(8,128)(2,1)S(1)} collective-permute-done((bf16[256,2048]{1,0:T(8,128)(2,1)S(1)}, bf16[256,2048]{1,0:T(8,128)(2,1)S(1)}, u32[]{:S(2)}, u32[]{:S(2)}) %collective-permute-start.6) | collective-permute-done | bytes 1048608 | tf_op jit(solution)/shard_map/ppermute | solution.py:162
  210.2 14.3 %collective-permute-done.7 = bf16[256,2048]{1,0:T(8,128)(2,1)S(1)} collective-permute-done((bf16[256,2048]{1,0:T(8,128)(2,1)S(1)}, bf16[256,2048]{1,0:T(8,128)(2,1)S(1)}, u32[]{:S(2)}, u32[]{:S(2)}) %collective-permute-start.7) | collective-permute-done | bytes 1048608 | tf_op jit(solution)/shard_map/ppermute | solution.py:162
  224.8 22.0 %collective-permute-done.8 = bf16[256,2048]{1,0:T(8,128)(2,1)S(1)} collective-permute-done((bf16[256,2048]{1,0:T(8,128)(2,1)S(1)}, bf16[256,2048]{1,0:T(8,128)(2,1)S(1)}, u32[]{:S(2)}, u32[]{:S(2)}) %collective-permute-start.8) | collective-permute-done | bytes 1048608 | tf_op jit(solution)/shard_map/ppermute | solution.py:162
  294.0 12.0 %convolution_convert_fusion.2 = bf16[256,2048]{1,0:T(8,128)(2,1)} fusion(bf16[2048,4096]{1,0:T(8,128)(2,1)} %all-gather.11.cloned.1.call-done, bf16[256,2048]{1,0:T(8,128)(2,1)} %get-tuple-element.205, bf16[256,2048]{1,0:T(8,128)(2,1)S(1)} %get-tuple-element.204), kind=kOutput, calls=%fused_computation.52 | convolution fusion | flops 4299685888 | bytes 19922944 | tf_op jit(solution)/shard_map/dot_general | solution.py:29
  322.9 25.2 %collective-permute-done.11 = bf16[256,2048]{1,0:T(8,128)(2,1)S(1)} collective-permute-done((bf16[256,2048]{1,0:T(8,128)(2,1)}, bf16[256,2048]{1,0:T(8,128)(2,1)S(1)}, u32[]{:S(2)}, u32[]{:S(2)}) %collective-permute-start.11) | collective-permute-done | bytes 1048608 | tf_op jit(solution)/shard_map/ppermute | solution.py:134
  364.2 12.7 %fusion.16 = bf16[2048,2048]{1,0:T(8,128)(2,1)} fusion(bf16[256,2048]{1,0:T(8,128)(2,1)S(1)} %get-tuple-element.201, bf16[256,2048]{1,0:T(8,128)(2,1)S(1)} %get-tuple-element.147, bf16[256,2048]{1,0:T(8,128)(2,1)S(1)} %copy-done.36, bf16[256,2048]{1,0:T(8,128)(2,1)S(1)} %copy-done.34, bf16[256,2048]{1,0:T(8,128)(2,1)S(1)} %copy-done.53, ...), kind=kOutput, calls=%fused_computation.23 | convolution fusion | flops 8623489024 | bytes 16777216 | tf_op jit(solution)/shard_map/dot_general | solution.py:23
  376.9 12.3 %fusion.75 = f32[256,2048]{1,0:T(8,128)} fusion(bf16[2048,4096]{1,0:T(8,128)(2,1)} %all-gather.11.cloned.1.call-done, bf16[256,2048]{1,0:T(8,128)(2,1)} %copy-done.20, bf16[256,2048]{1,0:T(8,128)(2,1)} %copy-done.19), kind=kOutput, calls=%fused_computation.162 | convolution fusion | flops 4299161600 | bytes 20971520 | tf_op jit(solution)/shard_map/dot_general | solution.py:29
  401.4 12.4 %fusion.74 = f32[256,2048]{1,0:T(8,128)} fusion(bf16[2048,4096]{1,0:T(8,128)(2,1)} %all-gather.11.cloned.1.call-done, bf16[256,2048]{1,0:T(8,128)(2,1)} %get-tuple-element.194, bf16[256,2048]{1,0:T(8,128)(2,1)S(1)} %get-tuple-element.193), kind=kOutput, calls=%fused_computation.161 | convolution fusion | flops 4299161600 | bytes 20971520 | tf_op jit(solution)/shard_map/dot_general | solution.py:29
  423.4 12.8 %fusion.73 = f32[256,2048]{1,0:T(8,128)} fusion(bf16[2048,4096]{1,0:T(8,128)(2,1)} %all-gather.11.cloned.1.call-done, bf16[256,2048]{1,0:T(8,128)(2,1)} %copy-done.18, bf16[256,2048]{1,0:T(8,128)(2,1)} %copy-done.17), kind=kOutput, calls=%fused_computation.160 | convolution fusion | flops 4299161600 | bytes 20971520 | tf_op jit(solution)/shard_map/dot_general | solution.py:29
  450.3 26.0 %fusion.4 = bf16[2048,4096]{1,0:T(8,128)(2,1)} fusion(bf16[256,4096]{1,0:T(8,128)(2,1)} %pad_maximum_fusion.3, bf16[256,4096]{1,0:T(8,128)(2,1)} %pad_maximum_fusion.2, bf16[256,2048]{1,0:T(8,128)(2,1)} %get-tuple-element.205, bf16[256,2048]{1,0:T(8,128)(2,1)} %copy-done.41, bf16[256,4096]{1,0:T(8,128)(2,1)} %pad_maximum_fusion.4, ...), kind=kOutput, calls=%fused_computation.9 | convolution fusion | flops 17238589440 | bytes 29360128 | tf_op jit(solution)/shard_map/dot_general | solution.py:23
  476.4 24.5 %collective-permute-done.16 = bf16[256,2048]{1,0:T(8,128)(2,1)S(1)} collective-permute-done((bf16[256,2048]{1,0:T(8,128)(2,1)S(1)}, bf16[256,2048]{1,0:T(8,128)(2,1)S(1)}, u32[]{:S(2)}, u32[]{:S(2)}) %collective-permute-start.16) | collective-permute-done | bytes 1048608 | tf_op jit(solution)/shard_map/ppermute | solution.py:134
  513.8 10.5 %collective-permute-done.17 = bf16[256,2048]{1,0:T(8,128)(2,1)} collective-permute-done((bf16[256,2048]{1,0:T(8,128)(2,1)S(1)}, bf16[256,2048]{1,0:T(8,128)(2,1)}, u32[]{:S(2)}, u32[]{:S(2)}) %collective-permute-start.17) | collective-permute-done | bytes 1048608 | tf_op jit(solution)/shard_map/ppermute | solution.py:134
  532.7 14.8 %multiply_reduce_fusion = (f32[4,1024]{1,0:T(4,128)}, f32[4,1024,1024]{1,2,0:T(8,128)}) fusion(f32[4,1024,1024]{1,2,0:T(8,128)} %get-tuple-element.233, f32[4,1024]{1,0:T(4,128)} %bitcast.108, bf16[1024,4,128]{0,2,1:T(8,128)(2,1)} %bitcast.98, bf16[1,1024,4,128]{3,2,1,0:T(4,128)(2,1)S(1)} %copy-done.13), kind=kOutput, calls=%fused_computation.1 | convolution fusion | flops 1086320640 | bytes 35684352 | tf_op jit(solution)/shard_map/while/body/eval_jaxpr/qhd,khd->hqk/dot_general | solution.py:307
  575.3 9.4 %fusion.53 = bf16[1,1024,4,128]{1,3,2,0:T(8,128)(2,1)S(1)} fusion(bf16[1024,4,128]{0,2,1:T(8,128)(2,1)S(1)} %bitcast.99, f32[4,1024,1024]{1,2,0:T(8,128)} %get-tuple-element.233, f32[4,1024]{1,0:T(4,128)S(1)} %bitcast.110), kind=kOutput, calls=%fused_computation.107 | convolution fusion | flops 1082130432 | bytes 18890752 | tf_op jit(solution)/shard_map/while/body/eval_jaxpr/hqk,qhd->khd/dot_general | solution.py:304
  603.1 11.3 %convolution_convert_fusion = bf16[2048,1536]{1,0:T(8,128)(2,1)} fusion(bf16[1024,2048]{1,0:T(8,128)(2,1)} %constant_dynamic-update-slice_fusion.4, bf16[1024,1536]{0,1:T(8,128)(2,1)S(1)} %pad_maximum_fusion), kind=kOutput, calls=%fused_computation.22 | convolution fusion | flops 6445596672 | bytes 13631488 | tf_op jit(solution)/shard_map/dot_general | solution.py:23
  624.9 23.4 %collective-permute-done.21 = bf16[256,2048]{1,0:T(8,128)(2,1)S(1)} collective-permute-done((bf16[256,2048]{1,0:T(8,128)(2,1)S(1)}, bf16[256,2048]{1,0:T(8,128)(2,1)S(1)}, u32[]{:S(2)}, u32[]{:S(2)}) %collective-permute-start.21) | collective-permute-done | bytes 1048608 | tf_op jit(solution)/shard_map/ppermute | solution.py:162
  650.9 13.1 %collective-permute-done.20 = bf16[256,2048]{1,0:T(8,128)(2,1)S(1)} collective-permute-done((bf16[256,2048]{1,0:T(8,128)(2,1)S(1)}, bf16[256,2048]{1,0:T(8,128)(2,1)S(1)}, u32[]{:S(2)}, u32[]{:S(2)}) %collective-permute-start.20) | collective-permute-done | bytes 1048608 | tf_op jit(solution)/shard_map/ppermute | solution.py:162
  663.9 18.2 %collective-permute-done.22 = bf16[256,2048]{1,0:T(8,128)(2,1)S(1)} collective-permute-done((bf16[256,2048]{1,0:T(8,128)(2,1)S(1)}, bf16[256,2048]{1,0:T(8,128)(2,1)S(1)}, u32[]{:S(2)}, u32[]{:S(2)}) %collective-permute-start.22) | collective-permute-done | bytes 1048608 | tf_op jit(solution)/shard_map/ppermute | solution.py:162
  687.4 15.3 %reduce-scatter.9.cloned.1.call-done = bf16[256,1536]{1,0:T(8,128)(2,1)} async-done(((bf16[2048,1536]{1,0:T(8,128)(2,1)}), bf16[256,1536]{1,0:T(8,128)(2,1)}) %reduce-scatter.9.cloned.1.call-update) | async-done | bytes 786448 | tf_op jit(solution)/shard_map/reduce_scatter | solution.py:222
  (293 shorter events, 310.4 us)
Async XLA Ops:
  7.2 93.4 %all-gather.5.cloned.1.call-start = ((), (), s32[]{:S(2)}) async-start(), calls=%async_computation.4 | async-start | bytes 7077888 | tf_op jit(solution)/shard_map/all_gather | solution.py:217
  9.4 142.5 %all-gather.7.cloned.1.call-start = ((), (), s32[]{:S(2)}) async-start(), calls=%async_computation.5 | async-start | bytes 2359296 | tf_op jit(solution)/shard_map/all_gather | solution.py:217
  10.2 167.4 %all-gather.9.cloned.1.call-start = ((), (), s32[]{:S(2)}) async-start(), calls=%async_computation.6 | async-start | bytes 9437184 | tf_op jit(solution)/shard_map/all_gather | solution.py:217
  10.9 237.3 %all-gather.11.cloned.1.call-start = ((), (), s32[]{:S(2)}) async-start(), calls=%async_computation.7 | async-start | bytes 18874368 | tf_op jit(solution)/shard_map/all_gather | solution.py:217
  12.5 498.5 %reduce-scatter.5.cloned.1.call-start = ((), (), s32[]{:S(2)}) async-start(), calls=%async_computation.8 | async-start | bytes 9437184 | tf_op jit(solution)/shard_map/reduce_scatter | solution.py:222
  18.2 28.2 %collective-permute-start = (bf16[256,2048]{1,0:T(8,128)(2,1)S(1)}, bf16[256,2048]{1,0:T(8,128)(2,1)S(1)}, u32[]{:S(2)}, u32[]{:S(2)}) collective-permute-start(bf16[256,2048]{1,0:T(8,128)(2,1)S(1)} %get-tuple-element.192), channel_id=1, source_target_pairs={{0,8},{8,16},{16,24},{24,0},{1,9},{9,17},{17,25},{25,1},{2,10},{10... | collective-permute-start | bytes 3145736 | tf_op jit(solution)/shard_map/ppermute | solution.py:134
  46.4 26.2 %collective-permute-start.1 = (bf16[256,2048]{1,0:T(8,128)(2,1)S(1)}, bf16[256,2048]{1,0:T(8,128)(2,1)}, u32[]{:S(2)}, u32[]{:S(2)}) collective-permute-start(bf16[256,2048]{1,0:T(8,128)(2,1)S(1)} %collective-permute-done), channel_id=1, source_target_pairs={{0,8},{8,16},{16,24},{24,0},{1,9},{9,17},{17,25},{25,1},{2,10},{10... | collective-permute-start | bytes 3145736 | tf_op jit(solution)/shard_map/ppermute | solution.py:134
  72.6 25.6 %collective-permute-start.2 = (bf16[256,2048]{1,0:T(8,128)(2,1)}, bf16[256,2048]{1,0:T(8,128)(2,1)}, u32[]{:S(2)}, u32[]{:S(2)}) collective-permute-start(bf16[256,2048]{1,0:T(8,128)(2,1)} %collective-permute-done.1), channel_id=1, source_target_pairs={{0,8},{8,16},{16,24},{24,0},{1,9},{9,17},{17,25},{25,1},{2,10},{10... | collective-permute-start | bytes 3145736 | tf_op jit(solution)/shard_map/ppermute | solution.py:134
  100.6 24.6 %collective-permute-start.3 = (bf16[256,2048]{1,0:T(8,128)(2,1)}, bf16[256,2048]{1,0:T(8,128)(2,1)}, u32[]{:S(2)}, u32[]{:S(2)}) collective-permute-start(bf16[256,2048]{1,0:T(8,128)(2,1)} %param.19), channel_id=1, source_target_pairs={{0,8},{8,16},{16,24},{24,0},{1,9},{9,17},{17,25},{25,1},{2,10},{10... | collective-permute-start | bytes 3145736 | tf_op jit(solution)/shard_map/ppermute | solution.py:134
  125.3 26.0 %collective-permute-start.4 = (bf16[256,2048]{1,0:T(8,128)(2,1)}, bf16[256,2048]{1,0:T(8,128)(2,1)}, u32[]{:S(2)}, u32[]{:S(2)}) collective-permute-start(bf16[256,2048]{1,0:T(8,128)(2,1)} %collective-permute-done.3), channel_id=1, source_target_pairs={{0,8},{8,16},{16,24},{24,0},{1,9},{9,17},{17,25},{25,1},{2,10},{10... | collective-permute-start | bytes 3145736 | tf_op jit(solution)/shard_map/ppermute | solution.py:134
  151.3 24.9 %collective-permute-start.5 = (bf16[256,2048]{1,0:T(8,128)(2,1)}, bf16[256,2048]{1,0:T(8,128)(2,1)S(1)}, u32[]{:S(2)}, u32[]{:S(2)}) collective-permute-start(bf16[256,2048]{1,0:T(8,128)(2,1)} %collective-permute-done.4), channel_id=1, source_target_pairs={{0,8},{8,16},{16,24},{24,0},{1,9},{9,17},{17,25},{25,1},{2,10},{10... | collective-permute-start | bytes 3145736 | tf_op jit(solution)/shard_map/ppermute | solution.py:134
  177.2 23.9 %collective-permute-start.6 = (bf16[256,2048]{1,0:T(8,128)(2,1)S(1)}, bf16[256,2048]{1,0:T(8,128)(2,1)S(1)}, u32[]{:S(2)}, u32[]{:S(2)}) collective-permute-start(bf16[256,2048]{1,0:T(8,128)(2,1)S(1)} %dynamic-slice_convert_fusion.1), channel_id=1, source_target_pairs={{0,8},{8,16},{16,24},{24,0},{1,9},{9,17},{17,25},{25,1},{2,10},{10... | collective-permute-start | bytes 3145736 | tf_op jit(solution)/shard_map/ppermute | solution.py:162
  306.0 83.2 %collective-permute-start.12 = (bf16[256,2048]{1,0:T(8,128)(2,1)}, bf16[256,2048]{1,0:T(8,128)(2,1)}, u32[]{:S(2)}, u32[]{:S(2)}) collective-permute-start(bf16[256,2048]{1,0:T(8,128)(2,1)} %convolution_convert_fusion.2), channel_id=1, source_target_pairs={{0,8},{8,16},{16,24},{24,0},{1,9},{9,17},{17,25},{25,1},{2,10},{10... | collective-permute-start | bytes 3145736 | tf_op jit(solution)/shard_map/ppermute | solution.py:162
  306.0 42.1 %collective-permute-start.11 = (bf16[256,2048]{1,0:T(8,128)(2,1)}, bf16[256,2048]{1,0:T(8,128)(2,1)S(1)}, u32[]{:S(2)}, u32[]{:S(2)}) collective-permute-start(bf16[256,2048]{1,0:T(8,128)(2,1)} %copy-done.50), channel_id=1, source_target_pairs={{0,8},{8,16},{16,24},{24,0},{1,9},{9,17},{17,25},{25,1},{2,10},{10... | collective-permute-start | bytes 3145736 | tf_op jit(solution)/shard_map/ppermute | solution.py:134
  389.2 225.2 %reduce-scatter.7.cloned.1.call-start = ((), (), s32[]{:S(2)}) async-start(), calls=%async_computation.9 | async-start | bytes 18874368 | tf_op jit(solution)/shard_map/reduce_scatter | solution.py:222
  449.9 26.4 %collective-permute-start.15 = (bf16[256,2048]{1,0:T(8,128)(2,1)}, bf16[256,2048]{1,0:T(8,128)(2,1)S(1)}, u32[]{:S(2)}, u32[]{:S(2)}) collective-permute-start(bf16[256,2048]{1,0:T(8,128)(2,1)} %get-tuple-element.187), channel_id=1, source_target_pairs={{0,8},{8,16},{16,24},{24,0},{1,9},{9,17},{17,25},{25,1},{2,10},{10... | collective-permute-start | bytes 3145736 | tf_op jit(solution)/shard_map/ppermute | solution.py:134
  476.3 209.3 %reduce-scatter.11.cloned.1.call-start = ((), (), s32[]{:S(2)}) async-start(), calls=%async_computation.11 | async-start | bytes 2359296 | tf_op jit(solution)/shard_map/reduce_scatter | solution.py:222
  476.3 24.5 %collective-permute-start.16 = (bf16[256,2048]{1,0:T(8,128)(2,1)S(1)}, bf16[256,2048]{1,0:T(8,128)(2,1)S(1)}, u32[]{:S(2)}, u32[]{:S(2)}) collective-permute-start(bf16[256,2048]{1,0:T(8,128)(2,1)S(1)} %collective-permute-done.15), channel_id=1, source_target_pairs={{0,8},{8,16},{16,24},{24,0},{1,9},{9,17},{17,25},{25,1},{2,10},{10... | collective-permute-start | bytes 3145736 | tf_op jit(solution)/shard_map/ppermute | solution.py:134
  526.6 58.1 %collective-permute-start.18 = (bf16[256,2048]{1,0:T(8,128)(2,1)}, bf16[256,2048]{1,0:T(8,128)(2,1)}, u32[]{:S(2)}, u32[]{:S(2)}) collective-permute-start(bf16[256,2048]{1,0:T(8,128)(2,1)} %fusion.92), channel_id=1, source_target_pairs={{0,8},{8,16},{16,24},{24,0},{1,9},{9,17},{17,25},{25,1},{2,10},{10... | collective-permute-start | bytes 3145736 | tf_op jit(solution)/shard_map/ppermute | solution.py:162
  574.1 128.6 %reduce-scatter.9.cloned.1.call-start = ((), (), s32[]{:S(2)}) async-start(), calls=%async_computation.10 | async-start | bytes 7077888 | tf_op jit(solution)/shard_map/reduce_scatter | solution.py:222
  620.3 27.9 %collective-permute-start.21 = (bf16[256,2048]{1,0:T(8,128)(2,1)S(1)}, bf16[256,2048]{1,0:T(8,128)(2,1)S(1)}, u32[]{:S(2)}, u32[]{:S(2)}) collective-permute-start(bf16[256,2048]{1,0:T(8,128)(2,1)S(1)} %dynamic-slice_convert_fusion), channel_id=1, source_target_pairs={{0,8},{8,16},{16,24},{24,0},{1,9},{9,17},{17,25},{25,1},{2,10},{10... | collective-permute-start | bytes 3145736 | tf_op jit(solution)/shard_map/ppermute | solution.py:162
  622.3 41.6 %collective-permute-start.20 = (bf16[256,2048]{1,0:T(8,128)(2,1)S(1)}, bf16[256,2048]{1,0:T(8,128)(2,1)S(1)}, u32[]{:S(2)}, u32[]{:S(2)}) collective-permute-start(bf16[256,2048]{1,0:T(8,128)(2,1)S(1)} %add_convert_fusion.3), channel_id=1, source_target_pairs={{0,8},{8,16},{16,24},{24,0},{1,9},{9,17},{17,25},{25,1},{2,10},{10... | collective-permute-start | bytes 3145736 | tf_op jit(solution)/shard_map/ppermute | solution.py:162
  650.5 31.6 %collective-permute-start.22 = (bf16[256,2048]{1,0:T(8,128)(2,1)S(1)}, bf16[256,2048]{1,0:T(8,128)(2,1)S(1)}, u32[]{:S(2)}, u32[]{:S(2)}) collective-permute-start(bf16[256,2048]{1,0:T(8,128)(2,1)S(1)} %add_convert_fusion.1), channel_id=1, source_target_pairs={{0,8},{8,16},{16,24},{24,0},{1,9},{9,17},{17,25},{25,1},{2,10},{10... | collective-permute-start | bytes 3145736 | tf_op jit(solution)/shard_map/ppermute | solution.py:162
  684.0 25.8 %collective-permute-start.23 = (bf16[256,2048]{1,0:T(8,128)(2,1)S(1)}, bf16[256,2048]{1,0:T(8,128)(2,1)S(1)}, u32[]{:S(2)}, u32[]{:S(2)}) collective-permute-start(bf16[256,2048]{1,0:T(8,128)(2,1)S(1)} %add_convert_fusion), channel_id=1, source_target_pairs={{0,8},{8,16},{16,24},{24,0},{1,9},{9,17},{17,25},{25,1},{2,10},{10... | collective-permute-start | bytes 3145736 | tf_op jit(solution)/shard_map/ppermute | solution.py:162
  (76 other events, 1015.0 us)
Sparse Core Ops, SparseCore 0:
  10.5 48.1 all-gather.4
  60.5 28.0 all-gather.6
  90.5 55.8 all-gather.8
  148.7 89.7 all-gather.10
  389.3 68.7 reduce-scatter.4
  476.4 116.6 reduce-scatter.6
  596.4 41.0 reduce-scatter.10
  640.9 61.6 reduce-scatter.8

commit v16 on v11

--- a/solution.py
+++ b/solution.py
@@ -117,10 +117,8 @@
         self.rows = shard.shape[0]
         self.slots = [shard]
         self.pending = shard
+        self.absolute = absolute
         self.buf = None
-        if absolute:
-            buf = jnp.zeros((self.n * self.rows,) + shard.shape[1:], shard.dtype)
-            self.buf = self.place(buf, shard, 0)
 
     def place(self, buf, block, slot):
         start = lax.rem(self.me - slot + self.n, self.n) * self.rows
@@ -135,7 +133,11 @@
 
     def land(self):
         self.slots.append(self.pending)
-        if self.buf is not None:
+        if self.absolute:
+            if self.buf is None:
+                shard = self.slots[0]
+                buf = jnp.zeros((self.n * self.rows,) + shard.shape[1:], shard.dtype)
+                self.buf = self.place(buf, shard, 0)
             self.buf = self.place(self.buf, self.pending, len(self.slots) - 1)
 
     def result(self):

time: 734 us -> 734 us (level)
  no operation moved by 1% of the time
where the time goes in v16:
time: 734 us; the launch traced here: 728 us
  matrix products  285 us (39%)
  waiting for transfers between devices  242 us (33%)
  other arithmetic  103 us (14%)
  local copies, waits for them, and re-layouts  62 us (8%)
  starting transfers between devices  20.1 us (3%)
  between operations  15.8 us (2%)
    ppermute x12, waiting for transfers between devices, send(): lax.ppermute(self.pending, self.axis, [(j, (j + 1) % n) for j in range(n)])  134 us
    ppermute x12, waiting for transfers between devices, send(): lax.ppermute(value.astype(self.send_dtype), self.axis, [(j, (j + 1) % n)...  107 us
    dot_general x11, matrix products, times_transpose(): lax.dot_general(left, right, (((1,), (1,)), ((), ())), preferred_element_...  90.8 us
    dot_general x10, matrix products, product(): return jnp.dot(left, right, preferred_element_type=jnp.float32)  72.3 us
    dot_general x4, matrix products, contract_rows(): lax.dot_general(left, right, (((0,), (0,)), ((), ())), preferred_element_...  55.8 us
    convert_element_type x1, other arithmetic, attend_backward(): grad_scores = (probs * (grad_probs - inner)).astype(jnp.bfloat16)  17.2 us
    dot_general x2, matrix products, attend_backward(): jnp.einsum('qhd,khd->hqk', grad_mixed, values, preferred_element_type=jnp...  16 us
    dot_general x3, matrix products, masked_scores(): jnp.einsum('qhd,khd->hqk', queries, keys_rot, preferred_element_type=jnp....  15.9 us
  transfers between devices with their start and end apart: 32, of which 18 were waited for; matrix products, arithmetic and copies ran while one was open for 60% of the time, Pallas kernels for 0%

profile of v16, /device:TPU:0, one launch (start us, length us, event | category | flops | bytes accessed | tf_op | source)
XLA Modules:
  0.0 727.6 jit_solution(12114710536162264187)
XLA Ops:
  21.2 25.2 %collective-permute-done = bf16[256,2048]{1,0:T(8,128)(2,1)S(1)} collective-permute-done((bf16[256,2048]{1,0:T(8,128)(2,1)S(1)}, bf16[256,2048]{1,0:T(8,128)(2,1)S(1)}, u32[]{:S(2)}, u32[]{:S(2)}) %collective-permute-start) | collective-permute-done | bytes 1048608 | tf_op jit(solution)/shard_map/ppermute | solution.py:132
  47.9 24.7 %collective-permute-done.1 = bf16[256,2048]{1,0:T(8,128)(2,1)} collective-permute-done((bf16[256,2048]{1,0:T(8,128)(2,1)S(1)}, bf16[256,2048]{1,0:T(8,128)(2,1)}, u32[]{:S(2)}, u32[]{:S(2)}) %collective-permute-start.1) | collective-permute-done | bytes 1048608 | tf_op jit(solution)/shard_map/ppermute | solution.py:132
  82.1 16.1 %collective-permute-done.2 = bf16[256,2048]{1,0:T(8,128)(2,1)} collective-permute-done((bf16[256,2048]{1,0:T(8,128)(2,1)}, bf16[256,2048]{1,0:T(8,128)(2,1)}, u32[]{:S(2)}, u32[]{:S(2)}) %collective-permute-start.2) | collective-permute-done | bytes 1048608 | tf_op jit(solution)/shard_map/ppermute | solution.py:132
  100.8 10.1 %fusion.122 = f32[1024,1536]{1,0:T(8,128)S(1)} fusion(bf16[1024,2048]{1,0:T(8,128)(2,1)} %constant_dynamic-update-slice_fusion.4, bf16[2048,1536]{1,0:T(8,128)(2,1)} %all-gather.5.cloned.1.call-done), kind=kOutput, calls=%fused_computation.218 | convolution fusion | flops 6442450944 | bytes 16777216 | tf_op jit(solution)/shard_map/dot_general | solution.py:19
  161.1 19.1 %collective-permute-done.5 = bf16[256,2048]{1,0:T(8,128)(2,1)S(1)} collective-permute-done((bf16[256,2048]{1,0:T(8,128)(2,1)}, bf16[256,2048]{1,0:T(8,128)(2,1)S(1)}, u32[]{:S(2)}, u32[]{:S(2)}) %collective-permute-start.5) | collective-permute-done | bytes 1048608 | tf_op jit(solution)/shard_map/ppermute | solution.py:132
  194.4 9.8 %collective-permute-done.6 = bf16[256,2048]{1,0:T(8,128)(2,1)S(1)} collective-permute-done((bf16[256,2048]{1,0:T(8,128)(2,1)S(1)}, bf16[256,2048]{1,0:T(8,128)(2,1)S(1)}, u32[]{:S(2)}, u32[]{:S(2)}) %collective-permute-start.6) | collective-permute-done | bytes 1048608 | tf_op jit(solution)/shard_map/ppermute | solution.py:164
  213.4 14.4 %collective-permute-done.7 = bf16[256,2048]{1,0:T(8,128)(2,1)S(1)} collective-permute-done((bf16[256,2048]{1,0:T(8,128)(2,1)S(1)}, bf16[256,2048]{1,0:T(8,128)(2,1)S(1)}, u32[]{:S(2)}, u32[]{:S(2)}) %collective-permute-start.7) | collective-permute-done | bytes 1048608 | tf_op jit(solution)/shard_map/ppermute | solution.py:164
  228.1 22.0 %collective-permute-done.8 = bf16[256,2048]{1,0:T(8,128)(2,1)S(1)} collective-permute-done((bf16[256,2048]{1,0:T(8,128)(2,1)S(1)}, bf16[256,2048]{1,0:T(8,128)(2,1)S(1)}, u32[]{:S(2)}, u32[]{:S(2)}) %collective-permute-start.8) | collective-permute-done | bytes 1048608 | tf_op jit(solution)/shard_map/ppermute | solution.py:164
  288.5 9.4 %collective-permute-done.10 = bf16[256,2048]{1,0:T(8,128)(2,1)} collective-permute-done((bf16[256,2048]{1,0:T(8,128)(2,1)}, bf16[256,2048]{1,0:T(8,128)(2,1)}, u32[]{:S(2)}, u32[]{:S(2)}) %collective-permute-start.10) | collective-permute-done | bytes 1048608 | tf_op jit(solution)/shard_map/ppermute | solution.py:132
  300.1 12.0 %convolution_convert_fusion.2 = bf16[256,2048]{1,0:T(8,128)(2,1)} fusion(bf16[2048,4096]{1,0:T(8,128)(2,1)} %all-gather.11.cloned.1.call-done, bf16[256,2048]{1,0:T(8,128)(2,1)} %get-tuple-element.241, bf16[256,2048]{1,0:T(8,128)(2,1)S(1)} %get-tuple-element.240), kind=kOutput, calls=%fused_computation.59 | convolution fusion | flops 4299685888 | bytes 19922944 | tf_op jit(solution)/shard_map/dot_general | solution.py:29
  345.0 12.8 %fusion.15 = bf16[2048,2048]{1,0:T(8,128)(2,1)} fusion(bf16[256,2048]{1,0:T(8,128)(2,1)S(1)} %get-tuple-element.237, bf16[256,2048]{1,0:T(8,128)(2,1)S(1)} %get-tuple-element.177, bf16[256,2048]{1,0:T(8,128)(2,1)S(1)} %copy-done.42, bf16[256,2048]{1,0:T(8,128)(2,1)S(1)} %copy-done.40, bf16[256,2048]{1,0:T(8,128)(2,1)S(1)} %copy-done.64, ...), kind=kOutput, calls=%fused_computation.26 | convolution fusion | flops 8623489024 | bytes 16777216 | tf_op jit(solution)/shard_map/dot_general | solution.py:23
  357.7 12.3 %fusion.113 = f32[256,2048]{1,0:T(8,128)} fusion(bf16[2048,4096]{1,0:T(8,128)(2,1)} %all-gather.11.cloned.1.call-done, bf16[256,2048]{1,0:T(8,128)(2,1)} %copy-done.29, bf16[256,2048]{1,0:T(8,128)(2,1)} %copy-done.28), kind=kOutput, calls=%fused_computation.210 | convolution fusion | flops 4299161600 | bytes 20971520 | tf_op jit(solution)/shard_map/dot_general | solution.py:29
  382.3 13.6 %fusion.112 = f32[256,2048]{1,0:T(8,128)} fusion(bf16[2048,4096]{1,0:T(8,128)(2,1)} %all-gather.11.cloned.1.call-done, bf16[256,2048]{1,0:T(8,128)(2,1)} %get-tuple-element.226, bf16[256,2048]{1,0:T(8,128)(2,1)S(1)} %get-tuple-element.225), kind=kOutput, calls=%fused_computation.209 | convolution fusion | flops 4299161600 | bytes 20971520 | tf_op jit(solution)/shard_map/dot_general | solution.py:29
  408.3 12.7 %fusion.111 = f32[256,2048]{1,0:T(8,128)} fusion(bf16[2048,4096]{1,0:T(8,128)(2,1)} %all-gather.11.cloned.1.call-done, bf16[256,2048]{1,0:T(8,128)(2,1)} %copy-done.27, bf16[256,2048]{1,0:T(8,128)(2,1)} %copy-done.26), kind=kOutput, calls=%fused_computation.208 | convolution fusion | flops 4299161600 | bytes 20971520 | tf_op jit(solution)/shard_map/dot_general | solution.py:29
  435.2 25.9 %fusion.2 = bf16[2048,4096]{1,0:T(8,128)(2,1)} fusion(bf16[256,4096]{1,0:T(8,128)(2,1)} %pad_maximum_fusion.5, bf16[256,4096]{1,0:T(8,128)(2,1)} %pad_maximum_fusion.4, bf16[256,2048]{1,0:T(8,128)(2,1)} %get-tuple-element.241, bf16[256,2048]{1,0:T(8,128)(2,1)} %copy-done.50, bf16[256,4096]{1,0:T(8,128)(2,1)} %pad_maximum_fusion.6, ...), kind=kOutput, calls=%fused_computation.5 | convolution fusion | flops 17238589440 | bytes 29360128 | tf_op jit(solution)/shard_map/dot_general | solution.py:23
  478.9 11.9 %collective-permute-done.16 = bf16[256,2048]{1,0:T(8,128)(2,1)} collective-permute-done((bf16[256,2048]{1,0:T(8,128)(2,1)}, bf16[256,2048]{1,0:T(8,128)(2,1)}, u32[]{:S(2)}, u32[]{:S(2)}) %collective-permute-start.16) | collective-permute-done | bytes 1048608 | tf_op jit(solution)/shard_map/ppermute | solution.py:132
  501.2 16.1 %collective-permute-done.17 = bf16[256,2048]{1,0:T(8,128)(2,1)S(1)} collective-permute-done((bf16[256,2048]{1,0:T(8,128)(2,1)}, bf16[256,2048]{1,0:T(8,128)(2,1)S(1)}, u32[]{:S(2)}, u32[]{:S(2)}) %collective-permute-start.17) | collective-permute-done | bytes 1048608 | tf_op jit(solution)/shard_map/ppermute | solution.py:132
  531.4 11.0 %multiply_reduce_fusion = (f32[2,1024]{1,0:T(2,128)S(1)}, f32[2,1024]{1,0:T(2,128)S(1)}, f32[2,1024,1024]{1,2,0:T(8,128)}) fusion(f32[2,1024,1024]{1,2,0:T(8,128)S(1)} %bitcast.131, f32[2,1024]{1,0:T(2,128)S(1)} %get-tuple-element.269, pred[1024,1024]{0,1:T(8,128)(4,1)S(1)} %copy-done.1, f32[2,1024,1024]{1,2,0:T(8,128)} %fusion.81, ...), kind=kOutput, calls=%fused_computation.16 | convolution fusion | flops 557838336 | bytes 35684352 | tf_op jit(solution)/shard_map/while/body/eval_jaxpr/qhd,khd->hqk/dot_general | solution.py:309
  542.4 17.2 %multiply_convert_fusion = (bf16[2,1024,1024]{1,2,0:T(8,128)(2,1)}, bf16[2,1024,1024]{1,2,0:T(8,128)(2,1)}) fusion(f32[2,1024,1024]{1,2,0:T(8,128)} %get-tuple-element.274, f32[2,1024,1024]{1,2,0:T(8,128)} %fusion.83, f32[2,1024]{1,0:T(2,128)S(1)} %get-tuple-element.216, f32[2,1024]{1,0:T(2,128)S(1)} %get-tuple-element.269, ...), kind=kLoop, calls=%fused_computation.15 | loop fusion | flops 25165824 | bytes 43024384 | tf_op jit(solution)/shard_map/while/body/eval_jaxpr/convert_element_type | solution.py:311
  610.3 11.0 %fusion.114 = f32[1024,2048]{1,0:T(8,128)} fusion(bf16[2048,1536]{1,0:T(8,128)(2,1)} %all-gather.5.cloned.1.call-done, bf16[1024,512]{0,1:T(8,128)(2,1)S(1)} %bitcast.139, bf16[1024,512]{0,1:T(8,128)(2,1)S(1)} %bitcast.135, bf16[1024,512]{0,1:T(8,128)(2,1)S(1)} %bitcast.137), kind=kOutput, calls=%fused_computation.211 | convolution fusion | flops 6451888128 | bytes 17825792 | tf_op jit(solution)/shard_map/dot_general | solution.py:29
  621.2 11.2 %convolution_convert_fusion = bf16[2048,1536]{1,0:T(8,128)(2,1)} fusion(bf16[1024,2048]{1,0:T(8,128)(2,1)} %constant_dynamic-update-slice_fusion.4, bf16[1024,1536]{0,1:T(8,128)(2,1)S(1)} %pad_maximum_fusion), kind=kOutput, calls=%fused_computation.23 | convolution fusion | flops 6445596672 | bytes 13631488 | tf_op jit(solution)/shard_map/dot_general | solution.py:23
  645.3 15.3 %collective-permute-done.21 = bf16[256,2048]{1,0:T(8,128)(2,1)S(1)} collective-permute-done((bf16[256,2048]{1,0:T(8,128)(2,1)S(1)}, bf16[256,2048]{1,0:T(8,128)(2,1)S(1)}, u32[]{:S(2)}, u32[]{:S(2)}) %collective-permute-start.21) | collective-permute-done | bytes 1048608 | tf_op jit(solution)/shard_map/ppermute | solution.py:164
  662.9 18.3 %collective-permute-done.20 = bf16[256,2048]{1,0:T(8,128)(2,1)S(1)} collective-permute-done((bf16[256,2048]{1,0:T(8,128)(2,1)S(1)}, bf16[256,2048]{1,0:T(8,128)(2,1)S(1)}, u32[]{:S(2)}, u32[]{:S(2)}) %collective-permute-start.20) | collective-permute-done | bytes 1048608 | tf_op jit(solution)/shard_map/ppermute | solution.py:164
  681.2 13.1 %collective-permute-done.22 = bf16[256,2048]{1,0:T(8,128)(2,1)S(1)} collective-permute-done((bf16[256,2048]{1,0:T(8,128)(2,1)S(1)}, bf16[256,2048]{1,0:T(8,128)(2,1)S(1)}, u32[]{:S(2)}, u32[]{:S(2)}) %collective-permute-start.22) | collective-permute-done | bytes 1048608 | tf_op jit(solution)/shard_map/ppermute | solution.py:164
  (324 shorter events, 346.7 us)
Async XLA Ops:
  7.2 93.6 %all-gather.5.cloned.1.call-start = ((), (), s32[]{:S(2)}) async-start(), calls=%async_computation.4 | async-start | bytes 7077888 | tf_op jit(solution)/shard_map/all_gather | solution.py:219
  9.4 146.8 %all-gather.7.cloned.1.call-start = ((), (), s32[]{:S(2)}) async-start(), calls=%async_computation.5 | async-start | bytes 2359296 | tf_op jit(solution)/shard_map/all_gather | solution.py:219
  10.2 171.2 %all-gather.9.cloned.1.call-start = ((), (), s32[]{:S(2)}) async-start(), calls=%async_computation.6 | async-start | bytes 9437184 | tf_op jit(solution)/shard_map/all_gather | solution.py:219
  10.9 240.5 %all-gather.11.cloned.1.call-start = ((), (), s32[]{:S(2)}) async-start(), calls=%async_computation.7 | async-start | bytes 18874368 | tf_op jit(solution)/shard_map/all_gather | solution.py:219
  12.5 485.5 %reduce-scatter.5.cloned.1.call-start = ((), (), s32[]{:S(2)}) async-start(), calls=%async_computation.8 | async-start | bytes 9437184 | tf_op jit(solution)/shard_map/reduce_scatter | solution.py:224
  18.1 28.2 %collective-permute-start = (bf16[256,2048]{1,0:T(8,128)(2,1)S(1)}, bf16[256,2048]{1,0:T(8,128)(2,1)S(1)}, u32[]{:S(2)}, u32[]{:S(2)}) collective-permute-start(bf16[256,2048]{1,0:T(8,128)(2,1)S(1)} %get-tuple-element.224), channel_id=1, source_target_pairs={{0,8},{8,16},{16,24},{24,0},{1,9},{9,17},{17,25},{25,1},{2,10},{10... | collective-permute-start | bytes 3145736 | tf_op jit(solution)/shard_map/ppermute | solution.py:132
  46.4 26.2 %collective-permute-start.1 = (bf16[256,2048]{1,0:T(8,128)(2,1)S(1)}, bf16[256,2048]{1,0:T(8,128)(2,1)}, u32[]{:S(2)}, u32[]{:S(2)}) collective-permute-start(bf16[256,2048]{1,0:T(8,128)(2,1)S(1)} %collective-permute-done), channel_id=1, source_target_pairs={{0,8},{8,16},{16,24},{24,0},{1,9},{9,17},{17,25},{25,1},{2,10},{10... | collective-permute-start | bytes 3145736 | tf_op jit(solution)/shard_map/ppermute | solution.py:132
  72.6 25.6 %collective-permute-start.2 = (bf16[256,2048]{1,0:T(8,128)(2,1)}, bf16[256,2048]{1,0:T(8,128)(2,1)}, u32[]{:S(2)}, u32[]{:S(2)}) collective-permute-start(bf16[256,2048]{1,0:T(8,128)(2,1)} %collective-permute-done.1), channel_id=1, source_target_pairs={{0,8},{8,16},{16,24},{24,0},{1,9},{9,17},{17,25},{25,1},{2,10},{10... | collective-permute-start | bytes 3145736 | tf_op jit(solution)/shard_map/ppermute | solution.py:132
  100.6 30.4 %collective-permute-start.3 = (bf16[256,2048]{1,0:T(8,128)(2,1)}, bf16[256,2048]{1,0:T(8,128)(2,1)}, u32[]{:S(2)}, u32[]{:S(2)}) collective-permute-start(bf16[256,2048]{1,0:T(8,128)(2,1)} %param.19), channel_id=1, source_target_pairs={{0,8},{8,16},{16,24},{24,0},{1,9},{9,17},{17,25},{25,1},{2,10},{10... | collective-permute-start | bytes 3145736 | tf_op jit(solution)/shard_map/ppermute | solution.py:132
  131.0 25.3 %collective-permute-start.4 = (bf16[256,2048]{1,0:T(8,128)(2,1)}, bf16[256,2048]{1,0:T(8,128)(2,1)}, u32[]{:S(2)}, u32[]{:S(2)}) collective-permute-start(bf16[256,2048]{1,0:T(8,128)(2,1)} %collective-permute-done.3), channel_id=1, source_target_pairs={{0,8},{8,16},{16,24},{24,0},{1,9},{9,17},{17,25},{25,1},{2,10},{10... | collective-permute-start | bytes 3145736 | tf_op jit(solution)/shard_map/ppermute | solution.py:132
  156.2 23.9 %collective-permute-start.5 = (bf16[256,2048]{1,0:T(8,128)(2,1)}, bf16[256,2048]{1,0:T(8,128)(2,1)S(1)}, u32[]{:S(2)}, u32[]{:S(2)}) collective-permute-start(bf16[256,2048]{1,0:T(8,128)(2,1)} %collective-permute-done.4), channel_id=1, source_target_pairs={{0,8},{8,16},{16,24},{24,0},{1,9},{9,17},{17,25},{25,1},{2,10},{10... | collective-permute-start | bytes 3145736 | tf_op jit(solution)/shard_map/ppermute | solution.py:132
  274.4 23.5 %collective-permute-start.10 = (bf16[256,2048]{1,0:T(8,128)(2,1)}, bf16[256,2048]{1,0:T(8,128)(2,1)}, u32[]{:S(2)}, u32[]{:S(2)}) collective-permute-start(bf16[256,2048]{1,0:T(8,128)(2,1)} %collective-permute-done.9), channel_id=1, source_target_pairs={{0,8},{8,16},{16,24},{24,0},{1,9},{9,17},{17,25},{25,1},{2,10},{10... | collective-permute-start | bytes 3145736 | tf_op jit(solution)/shard_map/ppermute | solution.py:132
  297.9 31.2 %collective-permute-start.11 = (bf16[256,2048]{1,0:T(8,128)(2,1)}, bf16[256,2048]{1,0:T(8,128)(2,1)}, u32[]{:S(2)}, u32[]{:S(2)}) collective-permute-start(bf16[256,2048]{1,0:T(8,128)(2,1)} %collective-permute-done.10), channel_id=1, source_target_pairs={{0,8},{8,16},{16,24},{24,0},{1,9},{9,17},{17,25},{25,1},{2,10},{10... | collective-permute-start | bytes 3145736 | tf_op jit(solution)/shard_map/ppermute | solution.py:132
  312.1 57.9 %collective-permute-start.12 = (bf16[256,2048]{1,0:T(8,128)(2,1)}, bf16[256,2048]{1,0:T(8,128)(2,1)}, u32[]{:S(2)}, u32[]{:S(2)}) collective-permute-start(bf16[256,2048]{1,0:T(8,128)(2,1)} %convolution_convert_fusion.2), channel_id=1, source_target_pairs={{0,8},{8,16},{16,24},{24,0},{1,9},{9,17},{17,25},{25,1},{2,10},{10... | collective-permute-start | bytes 3145736 | tf_op jit(solution)/shard_map/ppermute | solution.py:164
  370.0 262.5 %reduce-scatter.7.cloned.1.call-start = ((), (), s32[]{:S(2)}) async-start(), calls=%async_computation.9 | async-start | bytes 18874368 | tf_op jit(solution)/shard_map/reduce_scatter | solution.py:224
  431.8 29.3 %collective-permute-start.15 = (bf16[256,2048]{1,0:T(8,128)(2,1)}, bf16[256,2048]{1,0:T(8,128)(2,1)S(1)}, u32[]{:S(2)}, u32[]{:S(2)}) collective-permute-start(bf16[256,2048]{1,0:T(8,128)(2,1)} %get-tuple-element.219), channel_id=1, source_target_pairs={{0,8},{8,16},{16,24},{24,0},{1,9},{9,17},{17,25},{25,1},{2,10},{10... | collective-permute-start | bytes 3145736 | tf_op jit(solution)/shard_map/ppermute | solution.py:132
  462.1 236.9 %reduce-scatter.11.cloned.1.call-start = ((), (), s32[]{:S(2)}) async-start(), calls=%async_computation.11 | async-start | bytes 2359296 | tf_op jit(solution)/shard_map/reduce_scatter | solution.py:224
  464.7 26.2 %collective-permute-start.16 = (bf16[256,2048]{1,0:T(8,128)(2,1)}, bf16[256,2048]{1,0:T(8,128)(2,1)}, u32[]{:S(2)}, u32[]{:S(2)}) collective-permute-start(bf16[256,2048]{1,0:T(8,128)(2,1)} %copy-done.44), channel_id=1, source_target_pairs={{0,8},{8,16},{16,24},{24,0},{1,9},{9,17},{17,25},{25,1},{2,10},{10... | collective-permute-start | bytes 3145736 | tf_op jit(solution)/shard_map/ppermute | solution.py:132
  490.9 26.5 %collective-permute-start.17 = (bf16[256,2048]{1,0:T(8,128)(2,1)}, bf16[256,2048]{1,0:T(8,128)(2,1)S(1)}, u32[]{:S(2)}, u32[]{:S(2)}) collective-permute-start(bf16[256,2048]{1,0:T(8,128)(2,1)} %collective-permute-done.16), channel_id=1, source_target_pairs={{0,8},{8,16},{16,24},{24,0},{1,9},{9,17},{17,25},{25,1},{2,10},{10... | collective-permute-start | bytes 3145736 | tf_op jit(solution)/shard_map/ppermute | solution.py:132
  518.4 75.4 %collective-permute-start.18 = (bf16[256,2048]{1,0:T(8,128)(2,1)}, bf16[256,2048]{1,0:T(8,128)(2,1)}, u32[]{:S(2)}, u32[]{:S(2)}) collective-permute-start(bf16[256,2048]{1,0:T(8,128)(2,1)} %fusion.131), channel_id=1, source_target_pairs={{0,8},{8,16},{16,24},{24,0},{1,9},{9,17},{17,25},{25,1},{2,10},{10... | collective-permute-start | bytes 3145736 | tf_op jit(solution)/shard_map/ppermute | solution.py:164
  582.2 118.5 %reduce-scatter.9.cloned.1.call-start = ((), (), s32[]{:S(2)}) async-start(), calls=%async_computation.10 | async-start | bytes 7077888 | tf_op jit(solution)/shard_map/reduce_scatter | solution.py:224
  596.5 24.8 %collective-permute-start.19 = (bf16[256,2048]{1,0:T(8,128)(2,1)}, bf16[256,2048]{1,0:T(8,128)(2,1)}, u32[]{:S(2)}, u32[]{:S(2)}) collective-permute-start(bf16[256,2048]{1,0:T(8,128)(2,1)} %add_convert_fusion.6), channel_id=1, source_target_pairs={{0,8},{8,16},{16,24},{24,0},{1,9},{9,17},{17,25},{25,1},{2,10},{10... | collective-permute-start | bytes 3145736 | tf_op jit(solution)/shard_map/ppermute | solution.py:164
  641.1 40.2 %collective-permute-start.20 = (bf16[256,2048]{1,0:T(8,128)(2,1)S(1)}, bf16[256,2048]{1,0:T(8,128)(2,1)S(1)}, u32[]{:S(2)}, u32[]{:S(2)}) collective-permute-start(bf16[256,2048]{1,0:T(8,128)(2,1)S(1)} %add_convert_fusion.3), channel_id=1, source_target_pairs={{0,8},{8,16},{16,24},{24,0},{1,9},{9,17},{17,25},{25,1},{2,10},{10... | collective-permute-start | bytes 3145736 | tf_op jit(solution)/shard_map/ppermute | solution.py:164
  662.5 31.8 %collective-permute-start.22 = (bf16[256,2048]{1,0:T(8,128)(2,1)S(1)}, bf16[256,2048]{1,0:T(8,128)(2,1)S(1)}, u32[]{:S(2)}, u32[]{:S(2)}) collective-permute-start(bf16[256,2048]{1,0:T(8,128)(2,1)S(1)} %add_convert_fusion.1), channel_id=1, source_target_pairs={{0,8},{8,16},{16,24},{24,0},{1,9},{9,17},{17,25},{25,1},{2,10},{10... | collective-permute-start | bytes 3145736 | tf_op jit(solution)/shard_map/ppermute | solution.py:164
  (84 other events, 925.9 us)
Sparse Core Ops, SparseCore 0:
  10.5 48.1 all-gather.4
  60.5 28.0 all-gather.6
  90.5 55.8 all-gather.8
  148.7 89.7 all-gather.10
  370.2 72.1 reduce-scatter.4
  462.2 116.2 reduce-scatter.6
  582.4 40.8 reduce-scatter.10
  632.6 61.8 reduce-scatter.8

commit v17 on v11

--- a/solution.py
+++ b/solution.py
@@ -156,7 +156,7 @@
 
     def send(self):
         n, step = self.n, self.step + 1
-        value = self.slots[step]
+        value = self.slots[step].astype(jnp.float32)
         if self.pending is not None:
             value = value + self.pending.astype(jnp.float32)
         self.pending = lax.ppermute(
@@ -168,7 +168,7 @@
         pass
 
     def result(self):
-        return self.slots[0] + self.pending.astype(jnp.float32)
+        return self.slots[0].astype(jnp.float32) + self.pending.astype(jnp.float32)
 
 
 def ring_slots(partial, axis):
@@ -358,7 +358,9 @@
 
     def out_project(done):
         attended = merge_heads(done[1]["mixed"].astype(jnp.bfloat16))
-        return dict(attended=attended, attn_partial=product(attended, full_output))
+        return dict(
+            attended=attended, attn_partial=product(attended, full_output).astype(jnp.bfloat16)
+        )
 
     cot_later, first_rows = lax.optimization_barrier((cotangent, first_rows))
     cot_ring = RingGather(cot_later, "row")
@@ -392,7 +394,7 @@
             gate_lin = gu_lin[:, :hidden]
             up_lin = gu_lin[:, hidden:]
             activation = (jax.nn.silu(gate_lin) * up_lin).astype(jnp.bfloat16)
-            part = product(activation, full_down)
+            part = product(activation, full_down).astype(jnp.bfloat16)
             return (gate_lin, up_lin, activation, part)
 
         return piece
@@ -411,7 +413,7 @@
         grad_gate = grad_activation * up_lin * sigma * (1.0 + gate_lin * (1.0 - sigma))
         grad_up = grad_activation * gate_lin * sigma
         grad_gu = jnp.concatenate([grad_gate, grad_up], axis=1).astype(jnp.bfloat16)
-        return (grad_gu, times_transpose(grad_gu, full_gu))
+        return (grad_gu, times_transpose(grad_gu, full_gu).astype(jnp.bfloat16))
 
     second_ring_back = RingScatter([None] * slots, "row", jnp.bfloat16)
     grad_gu_slots = [None] * slots
@@ -484,7 +486,7 @@
             ],
             axis=1,
         ).astype(jnp.bfloat16)
-        return (grad_qkv, times_transpose(grad_qkv, full_qkv))
+        return (grad_qkv, times_transpose(grad_qkv, full_qkv).astype(jnp.bfloat16))
 
     def second_group_and_finish(done):
         return finish(done + (heads_backward(half, heads_local)(done),))

time: 734 us -> 728 us (level)
  waiting for transfers between devices: 242 us -> 262 us
  other arithmetic: 103 us -> 86.5 us
    ppermute x12, waiting for transfers between devices: 107 us -> 124 us  [send(): lax.ppermute(value.astype(self.send_dtype), self.axis, [(j, (j + 1) % n)...]
  transfers between devices with their start and end apart: 32 -> 32, of which waited for: 18 -> 19; matrix products, arithmetic and copies ran while one was open for 60% -> 58% of each run, Pallas kernels for 0% -> 0%
where the time goes in v17:
time: 728 us; the launch traced here: 721 us
  matrix products  286 us (39%)
  waiting for transfers between devices  262 us (36%)
  other arithmetic  86.5 us (12%)
  local copies, waits for them, and re-layouts  55.3 us (8%)
  between operations  15.9 us (2%)
  starting transfers between devices  15.6 us (2%)
    ppermute x12, waiting for transfers between devices, send(): lax.ppermute(self.pending, self.axis, [(j, (j + 1) % n) for j in range(n)])  136 us
    ppermute x12, waiting for transfers between devices, send(): lax.ppermute(value.astype(self.send_dtype), self.axis, [(j, (j + 1) % n)...  124 us
    dot_general x11, matrix products, times_transpose(): lax.dot_general(left, right, (((1,), (1,)), ((), ())), preferred_element_...  92.1 us
    dot_general x10, matrix products, product(): return jnp.dot(left, right, preferred_element_type=jnp.float32)  71.3 us
    dot_general x4, matrix products, contract_rows(): lax.dot_general(left, right, (((0,), (0,)), ((), ())), preferred_element_...  55.9 us
    dot_general x3, matrix products, masked_scores(): jnp.einsum('qhd,khd->hqk', queries, keys_rot, preferred_element_type=jnp....  16 us
    convert_element_type x1, other arithmetic, attend_backward(): grad_scores = (probs * (grad_probs - inner)).astype(jnp.bfloat16)  15.5 us
    dot_general x2, matrix products, attend_backward(): jnp.einsum('qhd,khd->hqk', grad_mixed, values, preferred_element_type=jnp...  15.1 us
  transfers between devices with their start and end apart: 32, of which 19 were waited for; matrix products, arithmetic and copies ran while one was open for 58% of the time, Pallas kernels for 0%

profile of v17, /device:TPU:0, one launch (start us, length us, event | category | flops | bytes accessed | tf_op | source)
XLA Modules:
  0.0 721.2 jit_solution(17606465061163977801)
XLA Ops:
  21.2 25.2 %collective-permute-done = bf16[256,2048]{1,0:T(8,128)(2,1)S(1)} collective-permute-done((bf16[256,2048]{1,0:T(8,128)(2,1)S(1)}, bf16[256,2048]{1,0:T(8,128)(2,1)S(1)}, u32[]{:S(2)}, u32[]{:S(2)}) %collective-permute-start) | collective-permute-done | bytes 1048608 | tf_op jit(solution)/shard_map/ppermute | solution.py:134
  47.9 24.7 %collective-permute-done.1 = bf16[256,2048]{1,0:T(8,128)(2,1)} collective-permute-done((bf16[256,2048]{1,0:T(8,128)(2,1)S(1)}, bf16[256,2048]{1,0:T(8,128)(2,1)}, u32[]{:S(2)}, u32[]{:S(2)}) %collective-permute-start.1) | collective-permute-done | bytes 1048608 | tf_op jit(solution)/shard_map/ppermute | solution.py:134
  82.1 16.1 %collective-permute-done.2 = bf16[256,2048]{1,0:T(8,128)(2,1)} collective-permute-done((bf16[256,2048]{1,0:T(8,128)(2,1)}, bf16[256,2048]{1,0:T(8,128)(2,1)}, u32[]{:S(2)}, u32[]{:S(2)}) %collective-permute-start.2) | collective-permute-done | bytes 1048608 | tf_op jit(solution)/shard_map/ppermute | solution.py:134
  100.8 10.1 %fusion.118 = f32[1024,1536]{1,0:T(8,128)S(1)} fusion(bf16[1024,2048]{1,0:T(8,128)(2,1)} %constant_dynamic-update-slice_fusion.4, bf16[2048,1536]{1,0:T(8,128)(2,1)} %all-gather.5.cloned.1.call-done), kind=kOutput, calls=%fused_computation.223 | convolution fusion | flops 6442450944 | bytes 16777216 | tf_op jit(solution)/shard_map/dot_general | solution.py:19
  148.8 10.2 %collective-permute-done.4 = bf16[256,2048]{1,0:T(8,128)(2,1)} collective-permute-done((bf16[256,2048]{1,0:T(8,128)(2,1)}, bf16[256,2048]{1,0:T(8,128)(2,1)}, u32[]{:S(2)}, u32[]{:S(2)}) %collective-permute-start.4) | collective-permute-done | bytes 1048608 | tf_op jit(solution)/shard_map/ppermute | solution.py:134
  163.8 19.2 %collective-permute-done.5 = bf16[256,2048]{1,0:T(8,128)(2,1)} collective-permute-done((bf16[256,2048]{1,0:T(8,128)(2,1)}, bf16[256,2048]{1,0:T(8,128)(2,1)}, u32[]{:S(2)}, u32[]{:S(2)}) %collective-permute-start.5) | collective-permute-done | bytes 1048608 | tf_op jit(solution)/shard_map/ppermute | solution.py:134
  216.4 13.1 %collective-permute-done.7 = bf16[256,2048]{1,0:T(8,128)(2,1)S(1)} collective-permute-done((bf16[256,2048]{1,0:T(8,128)(2,1)S(1)}, bf16[256,2048]{1,0:T(8,128)(2,1)S(1)}, u32[]{:S(2)}, u32[]{:S(2)}) %collective-permute-start.7) | collective-permute-done | bytes 1048608 | tf_op jit(solution)/shard_map/ppermute | solution.py:162
  230.0 22.0 %collective-permute-done.8 = bf16[256,2048]{1,0:T(8,128)(2,1)S(1)} collective-permute-done((bf16[256,2048]{1,0:T(8,128)(2,1)S(1)}, bf16[256,2048]{1,0:T(8,128)(2,1)S(1)}, u32[]{:S(2)}, u32[]{:S(2)}) %collective-permute-start.8) | collective-permute-done | bytes 1048608 | tf_op jit(solution)/shard_map/ppermute | solution.py:162
  302.0 11.9 %convolution_convert_fusion.7 = bf16[256,2048]{1,0:T(8,128)(2,1)} fusion(bf16[2048,4096]{1,0:T(8,128)(2,1)} %all-gather.11.cloned.1.call-done, bf16[256,2048]{1,0:T(8,128)(2,1)} %get-tuple-element.241, bf16[256,2048]{1,0:T(8,128)(2,1)S(1)} %get-tuple-element.240), kind=kOutput, calls=%fused_computation.64 | convolution fusion | flops 4299685888 | bytes 19922944 | tf_op jit(solution)/shard_map/dot_general | solution.py:29
  346.2 12.9 %fusion.15 = bf16[2048,2048]{1,0:T(8,128)(2,1)} fusion(bf16[256,2048]{1,0:T(8,128)(2,1)S(1)} %get-tuple-element.237, bf16[256,2048]{1,0:T(8,128)(2,1)S(1)} %get-tuple-element.177, bf16[256,2048]{1,0:T(8,128)(2,1)S(1)} %copy-done.46, bf16[256,2048]{1,0:T(8,128)(2,1)S(1)} %copy-done.44, bf16[256,2048]{1,0:T(8,128)(2,1)} %collective-permute-done.5, ...), kind=kOutput, calls=%fused_computation.26 | convolution fusion | flops 8623489024 | bytes 16777216 | tf_op jit(solution)/shard_map/dot_general | solution.py:23
  359.1 11.9 %convolution_convert_fusion.6 = bf16[256,2048]{1,0:T(8,128)(2,1)} fusion(bf16[2048,4096]{1,0:T(8,128)(2,1)} %all-gather.11.cloned.1.call-done, bf16[256,2048]{1,0:T(8,128)(2,1)} %copy-done.34, bf16[256,2048]{1,0:T(8,128)(2,1)} %copy-done.33), kind=kOutput, calls=%fused_computation.63 | convolution fusion | flops 4299685888 | bytes 19922944 | tf_op jit(solution)/shard_map/dot_general | solution.py:29
  382.8 13.5 %convolution_convert_fusion.5 = bf16[256,2048]{1,0:T(8,128)(2,1)} fusion(bf16[2048,4096]{1,0:T(8,128)(2,1)} %all-gather.11.cloned.1.call-done, bf16[256,2048]{1,0:T(8,128)(2,1)} %get-tuple-element.226, bf16[256,2048]{1,0:T(8,128)(2,1)S(1)} %get-tuple-element.225), kind=kOutput, calls=%fused_computation.62 | convolution fusion | flops 4299685888 | bytes 19922944 | tf_op jit(solution)/shard_map/dot_general | solution.py:29
  408.6 12.5 %convolution_convert_fusion.4 = bf16[256,2048]{1,0:T(8,128)(2,1)} fusion(bf16[2048,4096]{1,0:T(8,128)(2,1)} %all-gather.11.cloned.1.call-done, bf16[256,2048]{1,0:T(8,128)(2,1)} %copy-done.32, bf16[256,2048]{1,0:T(8,128)(2,1)} %copy-done.31), kind=kOutput, calls=%fused_computation.61 | convolution fusion | flops 4299685888 | bytes 19922944 | tf_op jit(solution)/shard_map/dot_general | solution.py:29
  435.4 25.9 %fusion.2 = bf16[2048,4096]{1,0:T(8,128)(2,1)} fusion(bf16[256,4096]{1,0:T(8,128)(2,1)} %pad_maximum_fusion.5, bf16[256,4096]{1,0:T(8,128)(2,1)} %pad_maximum_fusion.4, bf16[256,2048]{1,0:T(8,128)(2,1)} %get-tuple-element.241, bf16[256,2048]{1,0:T(8,128)(2,1)} %copy-done.55, bf16[256,4096]{1,0:T(8,128)(2,1)} %pad_maximum_fusion.6, ...), kind=kOutput, calls=%fused_computation.5 | convolution fusion | flops 17238589440 | bytes 29360128 | tf_op jit(solution)/shard_map/dot_general | solution.py:23
  478.7 10.7 %collective-permute-done.16 = bf16[256,2048]{1,0:T(8,128)(2,1)S(1)} collective-permute-done((bf16[256,2048]{1,0:T(8,128)(2,1)}, bf16[256,2048]{1,0:T(8,128)(2,1)S(1)}, u32[]{:S(2)}, u32[]{:S(2)}) %collective-permute-start.16) | collective-permute-done | bytes 1048608 | tf_op jit(solution)/shard_map/ppermute | solution.py:134
  497.9 17.3 %collective-permute-done.17 = bf16[256,2048]{1,0:T(8,128)(2,1)S(1)} collective-permute-done((bf16[256,2048]{1,0:T(8,128)(2,1)S(1)}, bf16[256,2048]{1,0:T(8,128)(2,1)S(1)}, u32[]{:S(2)}, u32[]{:S(2)}) %collective-permute-start.17) | collective-permute-done | bytes 1048608 | tf_op jit(solution)/shard_map/ppermute | solution.py:134
  529.5 10.5 %multiply_reduce_fusion = (f32[2,1024]{1,0:T(2,128)}, f32[2,1024]{1,0:T(2,128)}, f32[2,1024,1024]{1,2,0:T(8,128)}) fusion(f32[2,1024,1024]{1,2,0:T(8,128)S(1)} %bitcast.131, f32[2,1024]{1,0:T(2,128)S(1)} %get-tuple-element.269, pred[1024,1024]{0,1:T(8,128)(4,1)S(1)} %copy-done.3, f32[2,1024,1024]{1,2,0:T(8,128)} %fusion.81, ...), kind=kOutput, calls=%fused_computation.16 | convolution fusion | flops 557838336 | bytes 35684352 | tf_op jit(solution)/shard_map/while/body/eval_jaxpr/qhd,khd->hqk/dot_general | solution.py:307
  540.1 15.5 %multiply_convert_fusion = (bf16[2,1024,1024]{1,2,0:T(8,128)(2,1)}, bf16[2,1024,1024]{1,2,0:T(8,128)(2,1)S(1)}) fusion(f32[2,1024,1024]{1,2,0:T(8,128)} %get-tuple-element.274, f32[2,1024,1024]{1,2,0:T(8,128)} %fusion.83, f32[2,1024]{1,0:T(2,128)} %get-tuple-element.216, f32[2,1024]{1,0:T(2,128)S(1)} %get-tuple-element.269, ...), kind=kLoop, calls=%fused_computation.15 | loop fusion | flops 25165824 | bytes 43024384 | tf_op jit(solution)/shard_map/while/body/eval_jaxpr/convert_element_type | solution.py:309
  599.2 11.1 %convolution_convert_fusion.1 = bf16[1024,2048]{1,0:T(8,128)(2,1)} fusion(bf16[2048,1536]{1,0:T(8,128)(2,1)} %all-gather.5.cloned.1.call-done, bf16[1024,512]{0,1:T(8,128)(2,1)S(1)} %bitcast.139, bf16[1024,512]{0,1:T(8,128)(2,1)S(1)} %bitcast.137, bf16[1024,512]{0,1:T(8,128)(2,1)S(1)} %bitcast.135), kind=kOutput, calls=%fused_computation.54 | convolution fusion | flops 6453985280 | bytes 13631488 | tf_op jit(solution)/shard_map/dot_general | solution.py:29
  610.2 13.2 %collective-permute-done.19 = bf16[256,2048]{1,0:T(8,128)(2,1)S(1)} collective-permute-done((bf16[256,2048]{1,0:T(8,128)(2,1)S(1)}, bf16[256,2048]{1,0:T(8,128)(2,1)S(1)}, u32[]{:S(2)}, u32[]{:S(2)}) %collective-permute-start.19) | collective-permute-done | bytes 1048608 | tf_op jit(solution)/shard_map/ppermute | solution.py:162
  623.5 11.1 %convolution_convert_fusion = bf16[2048,1536]{1,0:T(8,128)(2,1)} fusion(bf16[1024,2048]{1,0:T(8,128)(2,1)} %constant_dynamic-update-slice_fusion.4, bf16[1024,1536]{0,1:T(8,128)(2,1)S(1)} %pad_maximum_fusion), kind=kOutput, calls=%fused_computation.23 | convolution fusion | flops 6445596672 | bytes 13631488 | tf_op jit(solution)/shard_map/dot_general | solution.py:23
  642.1 19.9 %collective-permute-done.21 = bf16[256,2048]{1,0:T(8,128)(2,1)S(1)} collective-permute-done((bf16[256,2048]{1,0:T(8,128)(2,1)S(1)}, bf16[256,2048]{1,0:T(8,128)(2,1)S(1)}, u32[]{:S(2)}, u32[]{:S(2)}) %collective-permute-start.21) | collective-permute-done | bytes 1048608 | tf_op jit(solution)/shard_map/ppermute | solution.py:162
  662.8 19.8 %collective-permute-done.20 = bf16[256,2048]{1,0:T(8,128)(2,1)S(1)} collective-permute-done((bf16[256,2048]{1,0:T(8,128)(2,1)S(1)}, bf16[256,2048]{1,0:T(8,128)(2,1)S(1)}, u32[]{:S(2)}, u32[]{:S(2)}) %collective-permute-start.20) | collective-permute-done | bytes 1048608 | tf_op jit(solution)/shard_map/ppermute | solution.py:162
  682.6 11.2 %collective-permute-done.22 = bf16[256,2048]{1,0:T(8,128)(2,1)S(1)} collective-permute-done((bf16[256,2048]{1,0:T(8,128)(2,1)S(1)}, bf16[256,2048]{1,0:T(8,128)(2,1)S(1)}, u32[]{:S(2)}, u32[]{:S(2)}) %collective-permute-start.22) | collective-permute-done | bytes 1048608 | tf_op jit(solution)/shard_map/ppermute | solution.py:162
  (332 shorter events, 335.6 us)
Async XLA Ops:
  7.2 93.6 %all-gather.5.cloned.1.call-start = ((), (), s32[]{:S(2)}) async-start(), calls=%async_computation.4 | async-start | bytes 7077888 | tf_op jit(solution)/shard_map/all_gather | solution.py:217
  9.4 149.5 %all-gather.7.cloned.1.call-start = ((), (), s32[]{:S(2)}) async-start(), calls=%async_computation.5 | async-start | bytes 2359296 | tf_op jit(solution)/shard_map/all_gather | solution.py:217
  10.2 173.0 %all-gather.9.cloned.1.call-start = ((), (), s32[]{:S(2)}) async-start(), calls=%async_computation.6 | async-start | bytes 9437184 | tf_op jit(solution)/shard_map/all_gather | solution.py:217
  10.9 242.4 %all-gather.11.cloned.1.call-start = ((), (), s32[]{:S(2)}) async-start(), calls=%async_computation.7 | async-start | bytes 18874368 | tf_op jit(solution)/shard_map/all_gather | solution.py:217
  12.5 482.5 %reduce-scatter.5.cloned.1.call-start = ((), (), s32[]{:S(2)}) async-start(), calls=%async_computation.8 | async-start | bytes 9437184 | tf_op jit(solution)/shard_map/reduce_scatter | solution.py:222
  18.1 28.2 %collective-permute-start = (bf16[256,2048]{1,0:T(8,128)(2,1)S(1)}, bf16[256,2048]{1,0:T(8,128)(2,1)S(1)}, u32[]{:S(2)}, u32[]{:S(2)}) collective-permute-start(bf16[256,2048]{1,0:T(8,128)(2,1)S(1)} %get-tuple-element.224), channel_id=1, source_target_pairs={{0,8},{8,16},{16,24},{24,0},{1,9},{9,17},{17,25},{25,1},{2,10},{10... | collective-permute-start | bytes 3145736 | tf_op jit(solution)/shard_map/ppermute | solution.py:134
  46.4 26.2 %collective-permute-start.1 = (bf16[256,2048]{1,0:T(8,128)(2,1)S(1)}, bf16[256,2048]{1,0:T(8,128)(2,1)}, u32[]{:S(2)}, u32[]{:S(2)}) collective-permute-start(bf16[256,2048]{1,0:T(8,128)(2,1)S(1)} %collective-permute-done), channel_id=1, source_target_pairs={{0,8},{8,16},{16,24},{24,0},{1,9},{9,17},{17,25},{25,1},{2,10},{10... | collective-permute-start | bytes 3145736 | tf_op jit(solution)/shard_map/ppermute | solution.py:134
  72.6 25.6 %collective-permute-start.2 = (bf16[256,2048]{1,0:T(8,128)(2,1)}, bf16[256,2048]{1,0:T(8,128)(2,1)}, u32[]{:S(2)}, u32[]{:S(2)}) collective-permute-start(bf16[256,2048]{1,0:T(8,128)(2,1)} %collective-permute-done.1), channel_id=1, source_target_pairs={{0,8},{8,16},{16,24},{24,0},{1,9},{9,17},{17,25},{25,1},{2,10},{10... | collective-permute-start | bytes 3145736 | tf_op jit(solution)/shard_map/ppermute | solution.py:134
  100.6 30.4 %collective-permute-start.3 = (bf16[256,2048]{1,0:T(8,128)(2,1)}, bf16[256,2048]{1,0:T(8,128)(2,1)}, u32[]{:S(2)}, u32[]{:S(2)}) collective-permute-start(bf16[256,2048]{1,0:T(8,128)(2,1)} %param.19), channel_id=1, source_target_pairs={{0,8},{8,16},{16,24},{24,0},{1,9},{9,17},{17,25},{25,1},{2,10},{10... | collective-permute-start | bytes 3145736 | tf_op jit(solution)/shard_map/ppermute | solution.py:134
  133.7 25.3 %collective-permute-start.4 = (bf16[256,2048]{1,0:T(8,128)(2,1)}, bf16[256,2048]{1,0:T(8,128)(2,1)}, u32[]{:S(2)}, u32[]{:S(2)}) collective-permute-start(bf16[256,2048]{1,0:T(8,128)(2,1)} %collective-permute-done.3), channel_id=1, source_target_pairs={{0,8},{8,16},{16,24},{24,0},{1,9},{9,17},{17,25},{25,1},{2,10},{10... | collective-permute-start | bytes 3145736 | tf_op jit(solution)/shard_map/ppermute | solution.py:134
  159.0 24.0 %collective-permute-start.5 = (bf16[256,2048]{1,0:T(8,128)(2,1)}, bf16[256,2048]{1,0:T(8,128)(2,1)}, u32[]{:S(2)}, u32[]{:S(2)}) collective-permute-start(bf16[256,2048]{1,0:T(8,128)(2,1)} %collective-permute-done.4), channel_id=1, source_target_pairs={{0,8},{8,16},{16,24},{24,0},{1,9},{9,17},{17,25},{25,1},{2,10},{10... | collective-permute-start | bytes 3145736 | tf_op jit(solution)/shard_map/ppermute | solution.py:134
  276.2 23.5 %collective-permute-start.10 = (bf16[256,2048]{1,0:T(8,128)(2,1)}, bf16[256,2048]{1,0:T(8,128)(2,1)}, u32[]{:S(2)}, u32[]{:S(2)}) collective-permute-start(bf16[256,2048]{1,0:T(8,128)(2,1)} %collective-permute-done.9), channel_id=1, source_target_pairs={{0,8},{8,16},{16,24},{24,0},{1,9},{9,17},{17,25},{25,1},{2,10},{10... | collective-permute-start | bytes 3145736 | tf_op jit(solution)/shard_map/ppermute | solution.py:134
  299.7 30.8 %collective-permute-start.11 = (bf16[256,2048]{1,0:T(8,128)(2,1)}, bf16[256,2048]{1,0:T(8,128)(2,1)}, u32[]{:S(2)}, u32[]{:S(2)}) collective-permute-start(bf16[256,2048]{1,0:T(8,128)(2,1)} %collective-permute-done.10), channel_id=1, source_target_pairs={{0,8},{8,16},{16,24},{24,0},{1,9},{9,17},{17,25},{25,1},{2,10},{10... | collective-permute-start | bytes 3145736 | tf_op jit(solution)/shard_map/ppermute | solution.py:134
  313.9 57.1 %collective-permute-start.12 = (bf16[256,2048]{1,0:T(8,128)(2,1)}, bf16[256,2048]{1,0:T(8,128)(2,1)}, u32[]{:S(2)}, u32[]{:S(2)}) collective-permute-start(bf16[256,2048]{1,0:T(8,128)(2,1)} %convolution_convert_fusion.7), channel_id=1, source_target_pairs={{0,8},{8,16},{16,24},{24,0},{1,9},{9,17},{17,25},{25,1},{2,10},{10... | collective-permute-start | bytes 3145736 | tf_op jit(solution)/shard_map/ppermute | solution.py:162
  371.0 263.6 %reduce-scatter.7.cloned.1.call-start = ((), (), s32[]{:S(2)}) async-start(), calls=%async_computation.9 | async-start | bytes 18874368 | tf_op jit(solution)/shard_map/reduce_scatter | solution.py:222
  432.6 28.7 %collective-permute-start.15 = (bf16[256,2048]{1,0:T(8,128)(2,1)}, bf16[256,2048]{1,0:T(8,128)(2,1)S(1)}, u32[]{:S(2)}, u32[]{:S(2)}) collective-permute-start(bf16[256,2048]{1,0:T(8,128)(2,1)} %get-tuple-element.219), channel_id=1, source_target_pairs={{0,8},{8,16},{16,24},{24,0},{1,9},{9,17},{17,25},{25,1},{2,10},{10... | collective-permute-start | bytes 3145736 | tf_op jit(solution)/shard_map/ppermute | solution.py:134
  462.3 233.5 %reduce-scatter.11.cloned.1.call-start = ((), (), s32[]{:S(2)}) async-start(), calls=%async_computation.11 | async-start | bytes 2359296 | tf_op jit(solution)/shard_map/reduce_scatter | solution.py:222
  464.0 25.4 %collective-permute-start.16 = (bf16[256,2048]{1,0:T(8,128)(2,1)}, bf16[256,2048]{1,0:T(8,128)(2,1)S(1)}, u32[]{:S(2)}, u32[]{:S(2)}) collective-permute-start(bf16[256,2048]{1,0:T(8,128)(2,1)} %copy-done.49), channel_id=1, source_target_pairs={{0,8},{8,16},{16,24},{24,0},{1,9},{9,17},{17,25},{25,1},{2,10},{10... | collective-permute-start | bytes 3145736 | tf_op jit(solution)/shard_map/ppermute | solution.py:134
  489.4 25.8 %collective-permute-start.17 = (bf16[256,2048]{1,0:T(8,128)(2,1)S(1)}, bf16[256,2048]{1,0:T(8,128)(2,1)S(1)}, u32[]{:S(2)}, u32[]{:S(2)}) collective-permute-start(bf16[256,2048]{1,0:T(8,128)(2,1)S(1)} %collective-permute-done.16), channel_id=1, source_target_pairs={{0,8},{8,16},{16,24},{24,0},{1,9},{9,17},{17,25},{25,1},{2,10},{10... | collective-permute-start | bytes 3145736 | tf_op jit(solution)/shard_map/ppermute | solution.py:134
  516.3 74.7 %collective-permute-start.18 = (bf16[256,2048]{1,0:T(8,128)(2,1)}, bf16[256,2048]{1,0:T(8,128)(2,1)}, u32[]{:S(2)}, u32[]{:S(2)}) collective-permute-start(bf16[256,2048]{1,0:T(8,128)(2,1)} %convolution_convert_fusion.10), channel_id=1, source_target_pairs={{0,8},{8,16},{16,24},{24,0},{1,9},{9,17},{17,25},{25,1},{2,10},{10... | collective-permute-start | bytes 3145736 | tf_op jit(solution)/shard_map/ppermute | solution.py:162
  579.9 117.7 %reduce-scatter.9.cloned.1.call-start = ((), (), s32[]{:S(2)}) async-start(), calls=%async_computation.10 | async-start | bytes 7077888 | tf_op jit(solution)/shard_map/reduce_scatter | solution.py:222
  598.6 24.9 %collective-permute-start.19 = (bf16[256,2048]{1,0:T(8,128)(2,1)S(1)}, bf16[256,2048]{1,0:T(8,128)(2,1)S(1)}, u32[]{:S(2)}, u32[]{:S(2)}) collective-permute-start(bf16[256,2048]{1,0:T(8,128)(2,1)S(1)} %add_convert_fusion.6), channel_id=1, source_target_pairs={{0,8},{8,16},{16,24},{24,0},{1,9},{9,17},{17,25},{25,1},{2,10},{10... | collective-permute-start | bytes 3145736 | tf_op jit(solution)/shard_map/ppermute | solution.py:162
  640.8 41.8 %collective-permute-start.20 = (bf16[256,2048]{1,0:T(8,128)(2,1)S(1)}, bf16[256,2048]{1,0:T(8,128)(2,1)S(1)}, u32[]{:S(2)}, u32[]{:S(2)}) collective-permute-start(bf16[256,2048]{1,0:T(8,128)(2,1)S(1)} %add_convert_fusion.3), channel_id=1, source_target_pairs={{0,8},{8,16},{16,24},{24,0},{1,9},{9,17},{17,25},{25,1},{2,10},{10... | collective-permute-start | bytes 3145736 | tf_op jit(solution)/shard_map/ppermute | solution.py:162
  662.4 31.4 %collective-permute-start.22 = (bf16[256,2048]{1,0:T(8,128)(2,1)S(1)}, bf16[256,2048]{1,0:T(8,128)(2,1)S(1)}, u32[]{:S(2)}, u32[]{:S(2)}) collective-permute-start(bf16[256,2048]{1,0:T(8,128)(2,1)S(1)} %add_convert_fusion.1), channel_id=1, source_target_pairs={{0,8},{8,16},{16,24},{24,0},{1,9},{9,17},{17,25},{25,1},{2,10},{10... | collective-permute-start | bytes 3145736 | tf_op jit(solution)/shard_map/ppermute | solution.py:162
  (88 other events, 1161.1 us)
Sparse Core Ops, SparseCore 0:
  10.5 48.1 all-gather.4
  60.5 28.0 all-gather.6
  90.5 55.8 all-gather.8
  148.7 89.7 all-gather.10
  371.2 72.0 reduce-scatter.4
  462.4 115.8 reduce-scatter.6
  582.1 41.0 reduce-scatter.10
  634.7 61.3 reduce-scatter.8

commit v18 on v17

--- a/solution.py
+++ b/solution.py
@@ -117,10 +117,8 @@
         self.rows = shard.shape[0]
         self.slots = [shard]
         self.pending = shard
+        self.absolute = absolute
         self.buf = None
-        if absolute:
-            buf = jnp.zeros((self.n * self.rows,) + shard.shape[1:], shard.dtype)
-            self.buf = self.place(buf, shard, 0)
 
     def place(self, buf, block, slot):
         start = lax.rem(self.me - slot + self.n, self.n) * self.rows
@@ -135,7 +133,11 @@
 
     def land(self):
         self.slots.append(self.pending)
-        if self.buf is not None:
+        if self.absolute:
+            if self.buf is None:
+                shard = self.slots[0]
+                buf = jnp.zeros((self.n * self.rows,) + shard.shape[1:], shard.dtype)
+                self.buf = self.place(buf, shard, 0)
             self.buf = self.place(self.buf, self.pending, len(self.slots) - 1)
 
     def result(self):

time: 728 us -> 728 us (level)
  no operation moved by 1% of the time
where the time goes in v18:
time: 728 us; the launch traced here: 721 us
  matrix products  286 us (39%)
  waiting for transfers between devices  262 us (36%)
  other arithmetic  86.5 us (12%)
  local copies, waits for them, and re-layouts  55.3 us (8%)
  between operations  15.9 us (2%)
  starting transfers between devices  15.6 us (2%)
    ppermute x12, waiting for transfers between devices, send(): lax.ppermute(self.pending, self.axis, [(j, (j + 1) % n) for j in range(n)])  136 us
    ppermute x12, waiting for transfers between devices, send(): lax.ppermute(value.astype(self.send_dtype), self.axis, [(j, (j + 1) % n)...  124 us
    dot_general x11, matrix products, times_transpose(): lax.dot_general(left, right, (((1,), (1,)), ((), ())), preferred_element_...  92.1 us
    dot_general x10, matrix products, product(): return jnp.dot(left, right, preferred_element_type=jnp.float32)  71.3 us
    dot_general x4, matrix products, contract_rows(): lax.dot_general(left, right, (((0,), (0,)), ((), ())), preferred_element_...  55.9 us
    dot_general x3, matrix products, masked_scores(): jnp.einsum('qhd,khd->hqk', queries, keys_rot, preferred_element_type=jnp....  16 us
    convert_element_type x1, other arithmetic, attend_backward(): grad_scores = (probs * (grad_probs - inner)).astype(jnp.bfloat16)  15.5 us
    dot_general x2, matrix products, attend_backward(): jnp.einsum('qhd,khd->hqk', grad_mixed, values, preferred_element_type=jnp...  15.1 us
  transfers between devices with their start and end apart: 32, of which 19 were waited for; matrix products, arithmetic and copies ran while one was open for 58% of the time, Pallas kernels for 0%

profile of v18, /device:TPU:0, one launch (start us, length us, event | category | flops | bytes accessed | tf_op | source)
XLA Modules:
  0.0 721.2 jit_solution(17606465061163977801)
XLA Ops:
  21.2 25.2 %collective-permute-done = bf16[256,2048]{1,0:T(8,128)(2,1)S(1)} collective-permute-done((bf16[256,2048]{1,0:T(8,128)(2,1)S(1)}, bf16[256,2048]{1,0:T(8,128)(2,1)S(1)}, u32[]{:S(2)}, u32[]{:S(2)}) %collective-permute-start) | collective-permute-done | bytes 1048608 | tf_op jit(solution)/shard_map/ppermute | solution.py:132
  47.9 24.7 %collective-permute-done.1 = bf16[256,2048]{1,0:T(8,128)(2,1)} collective-permute-done((bf16[256,2048]{1,0:T(8,128)(2,1)S(1)}, bf16[256,2048]{1,0:T(8,128)(2,1)}, u32[]{:S(2)}, u32[]{:S(2)}) %collective-permute-start.1) | collective-permute-done | bytes 1048608 | tf_op jit(solution)/shard_map/ppermute | solution.py:132
  82.1 16.1 %collective-permute-done.2 = bf16[256,2048]{1,0:T(8,128)(2,1)} collective-permute-done((bf16[256,2048]{1,0:T(8,128)(2,1)}, bf16[256,2048]{1,0:T(8,128)(2,1)}, u32[]{:S(2)}, u32[]{:S(2)}) %collective-permute-start.2) | collective-permute-done | bytes 1048608 | tf_op jit(solution)/shard_map/ppermute | solution.py:132
  100.8 10.1 %fusion.118 = f32[1024,1536]{1,0:T(8,128)S(1)} fusion(bf16[1024,2048]{1,0:T(8,128)(2,1)} %constant_dynamic-update-slice_fusion.4, bf16[2048,1536]{1,0:T(8,128)(2,1)} %all-gather.5.cloned.1.call-done), kind=kOutput, calls=%fused_computation.223 | convolution fusion | flops 6442450944 | bytes 16777216 | tf_op jit(solution)/shard_map/dot_general | solution.py:19
  148.8 10.2 %collective-permute-done.4 = bf16[256,2048]{1,0:T(8,128)(2,1)} collective-permute-done((bf16[256,2048]{1,0:T(8,128)(2,1)}, bf16[256,2048]{1,0:T(8,128)(2,1)}, u32[]{:S(2)}, u32[]{:S(2)}) %collective-permute-start.4) | collective-permute-done | bytes 1048608 | tf_op jit(solution)/shard_map/ppermute | solution.py:132
  163.8 19.2 %collective-permute-done.5 = bf16[256,2048]{1,0:T(8,128)(2,1)} collective-permute-done((bf16[256,2048]{1,0:T(8,128)(2,1)}, bf16[256,2048]{1,0:T(8,128)(2,1)}, u32[]{:S(2)}, u32[]{:S(2)}) %collective-permute-start.5) | collective-permute-done | bytes 1048608 | tf_op jit(solution)/shard_map/ppermute | solution.py:132
  216.4 13.1 %collective-permute-done.7 = bf16[256,2048]{1,0:T(8,128)(2,1)S(1)} collective-permute-done((bf16[256,2048]{1,0:T(8,128)(2,1)S(1)}, bf16[256,2048]{1,0:T(8,128)(2,1)S(1)}, u32[]{:S(2)}, u32[]{:S(2)}) %collective-permute-start.7) | collective-permute-done | bytes 1048608 | tf_op jit(solution)/shard_map/ppermute | solution.py:164
  230.0 22.0 %collective-permute-done.8 = bf16[256,2048]{1,0:T(8,128)(2,1)S(1)} collective-permute-done((bf16[256,2048]{1,0:T(8,128)(2,1)S(1)}, bf16[256,2048]{1,0:T(8,128)(2,1)S(1)}, u32[]{:S(2)}, u32[]{:S(2)}) %collective-permute-start.8) | collective-permute-done | bytes 1048608 | tf_op jit(solution)/shard_map/ppermute | solution.py:164
  302.0 11.9 %convolution_convert_fusion.7 = bf16[256,2048]{1,0:T(8,128)(2,1)} fusion(bf16[2048,4096]{1,0:T(8,128)(2,1)} %all-gather.11.cloned.1.call-done, bf16[256,2048]{1,0:T(8,128)(2,1)} %get-tuple-element.241, bf16[256,2048]{1,0:T(8,128)(2,1)S(1)} %get-tuple-element.240), kind=kOutput, calls=%fused_computation.64 | convolution fusion | flops 4299685888 | bytes 19922944 | tf_op jit(solution)/shard_map/dot_general | solution.py:29
  346.2 12.9 %fusion.15 = bf16[2048,2048]{1,0:T(8,128)(2,1)} fusion(bf16[256,2048]{1,0:T(8,128)(2,1)S(1)} %get-tuple-element.237, bf16[256,2048]{1,0:T(8,128)(2,1)S(1)} %get-tuple-element.177, bf16[256,2048]{1,0:T(8,128)(2,1)S(1)} %copy-done.46, bf16[256,2048]{1,0:T(8,128)(2,1)S(1)} %copy-done.44, bf16[256,2048]{1,0:T(8,128)(2,1)} %collective-permute-done.5, ...), kind=kOutput, calls=%fused_computation.26 | convolution fusion | flops 8623489024 | bytes 16777216 | tf_op jit(solution)/shard_map/dot_general | solution.py:23
  359.1 11.9 %convolution_convert_fusion.6 = bf16[256,2048]{1,0:T(8,128)(2,1)} fusion(bf16[2048,4096]{1,0:T(8,128)(2,1)} %all-gather.11.cloned.1.call-done, bf16[256,2048]{1,0:T(8,128)(2,1)} %copy-done.34, bf16[256,2048]{1,0:T(8,128)(2,1)} %copy-done.33), kind=kOutput, calls=%fused_computation.63 | convolution fusion | flops 4299685888 | bytes 19922944 | tf_op jit(solution)/shard_map/dot_general | solution.py:29
  382.8 13.5 %convolution_convert_fusion.5 = bf16[256,2048]{1,0:T(8,128)(2,1)} fusion(bf16[2048,4096]{1,0:T(8,128)(2,1)} %all-gather.11.cloned.1.call-done, bf16[256,2048]{1,0:T(8,128)(2,1)} %get-tuple-element.226, bf16[256,2048]{1,0:T(8,128)(2,1)S(1)} %get-tuple-element.225), kind=kOutput, calls=%fused_computation.62 | convolution fusion | flops 4299685888 | bytes 19922944 | tf_op jit(solution)/shard_map/dot_general | solution.py:29
  408.6 12.5 %convolution_convert_fusion.4 = bf16[256,2048]{1,0:T(8,128)(2,1)} fusion(bf16[2048,4096]{1,0:T(8,128)(2,1)} %all-gather.11.cloned.1.call-done, bf16[256,2048]{1,0:T(8,128)(2,1)} %copy-done.32, bf16[256,2048]{1,0:T(8,128)(2,1)} %copy-done.31), kind=kOutput, calls=%fused_computation.61 | convolution fusion | flops 4299685888 | bytes 19922944 | tf_op jit(solution)/shard_map/dot_general | solution.py:29
  435.4 25.9 %fusion.2 = bf16[2048,4096]{1,0:T(8,128)(2,1)} fusion(bf16[256,4096]{1,0:T(8,128)(2,1)} %pad_maximum_fusion.5, bf16[256,4096]{1,0:T(8,128)(2,1)} %pad_maximum_fusion.4, bf16[256,2048]{1,0:T(8,128)(2,1)} %get-tuple-element.241, bf16[256,2048]{1,0:T(8,128)(2,1)} %copy-done.55, bf16[256,4096]{1,0:T(8,128)(2,1)} %pad_maximum_fusion.6, ...), kind=kOutput, calls=%fused_computation.5 | convolution fusion | flops 17238589440 | bytes 29360128 | tf_op jit(solution)/shard_map/dot_general | solution.py:23
  478.7 10.7 %collective-permute-done.16 = bf16[256,2048]{1,0:T(8,128)(2,1)S(1)} collective-permute-done((bf16[256,2048]{1,0:T(8,128)(2,1)}, bf16[256,2048]{1,0:T(8,128)(2,1)S(1)}, u32[]{:S(2)}, u32[]{:S(2)}) %collective-permute-start.16) | collective-permute-done | bytes 1048608 | tf_op jit(solution)/shard_map/ppermute | solution.py:132
  497.9 17.3 %collective-permute-done.17 = bf16[256,2048]{1,0:T(8,128)(2,1)S(1)} collective-permute-done((bf16[256,2048]{1,0:T(8,128)(2,1)S(1)}, bf16[256,2048]{1,0:T(8,128)(2,1)S(1)}, u32[]{:S(2)}, u32[]{:S(2)}) %collective-permute-start.17) | collective-permute-done | bytes 1048608 | tf_op jit(solution)/shard_map/ppermute | solution.py:132
  529.5 10.5 %multiply_reduce_fusion = (f32[2,1024]{1,0:T(2,128)}, f32[2,1024]{1,0:T(2,128)}, f32[2,1024,1024]{1,2,0:T(8,128)}) fusion(f32[2,1024,1024]{1,2,0:T(8,128)S(1)} %bitcast.131, f32[2,1024]{1,0:T(2,128)S(1)} %get-tuple-element.269, pred[1024,1024]{0,1:T(8,128)(4,1)S(1)} %copy-done.3, f32[2,1024,1024]{1,2,0:T(8,128)} %fusion.81, ...), kind=kOutput, calls=%fused_computation.16 | convolution fusion | flops 557838336 | bytes 35684352 | tf_op jit(solution)/shard_map/while/body/eval_jaxpr/qhd,khd->hqk/dot_general | solution.py:309
  540.1 15.5 %multiply_convert_fusion = (bf16[2,1024,1024]{1,2,0:T(8,128)(2,1)}, bf16[2,1024,1024]{1,2,0:T(8,128)(2,1)S(1)}) fusion(f32[2,1024,1024]{1,2,0:T(8,128)} %get-tuple-element.274, f32[2,1024,1024]{1,2,0:T(8,128)} %fusion.83, f32[2,1024]{1,0:T(2,128)} %get-tuple-element.216, f32[2,1024]{1,0:T(2,128)S(1)} %get-tuple-element.269, ...), kind=kLoop, calls=%fused_computation.15 | loop fusion | flops 25165824 | bytes 43024384 | tf_op jit(solution)/shard_map/while/body/eval_jaxpr/convert_element_type | solution.py:311
  599.2 11.1 %convolution_convert_fusion.1 = bf16[1024,2048]{1,0:T(8,128)(2,1)} fusion(bf16[2048,1536]{1,0:T(8,128)(2,1)} %all-gather.5.cloned.1.call-done, bf16[1024,512]{0,1:T(8,128)(2,1)S(1)} %bitcast.139, bf16[1024,512]{0,1:T(8,128)(2,1)S(1)} %bitcast.137, bf16[1024,512]{0,1:T(8,128)(2,1)S(1)} %bitcast.135), kind=kOutput, calls=%fused_computation.54 | convolution fusion | flops 6453985280 | bytes 13631488 | tf_op jit(solution)/shard_map/dot_general | solution.py:29
  610.2 13.2 %collective-permute-done.19 = bf16[256,2048]{1,0:T(8,128)(2,1)S(1)} collective-permute-done((bf16[256,2048]{1,0:T(8,128)(2,1)S(1)}, bf16[256,2048]{1,0:T(8,128)(2,1)S(1)}, u32[]{:S(2)}, u32[]{:S(2)}) %collective-permute-start.19) | collective-permute-done | bytes 1048608 | tf_op jit(solution)/shard_map/ppermute | solution.py:164
  623.5 11.1 %convolution_convert_fusion = bf16[2048,1536]{1,0:T(8,128)(2,1)} fusion(bf16[1024,2048]{1,0:T(8,128)(2,1)} %constant_dynamic-update-slice_fusion.4, bf16[1024,1536]{0,1:T(8,128)(2,1)S(1)} %pad_maximum_fusion), kind=kOutput, calls=%fused_computation.23 | convolution fusion | flops 6445596672 | bytes 13631488 | tf_op jit(solution)/shard_map/dot_general | solution.py:23
  642.1 19.9 %collective-permute-done.21 = bf16[256,2048]{1,0:T(8,128)(2,1)S(1)} collective-permute-done((bf16[256,2048]{1,0:T(8,128)(2,1)S(1)}, bf16[256,2048]{1,0:T(8,128)(2,1)S(1)}, u32[]{:S(2)}, u32[]{:S(2)}) %collective-permute-start.21) | collective-permute-done | bytes 1048608 | tf_op jit(solution)/shard_map/ppermute | solution.py:164
  662.8 19.8 %collective-permute-done.20 = bf16[256,2048]{1,0:T(8,128)(2,1)S(1)} collective-permute-done((bf16[256,2048]{1,0:T(8,128)(2,1)S(1)}, bf16[256,2048]{1,0:T(8,128)(2,1)S(1)}, u32[]{:S(2)}, u32[]{:S(2)}) %collective-permute-start.20) | collective-permute-done | bytes 1048608 | tf_op jit(solution)/shard_map/ppermute | solution.py:164
  682.6 11.2 %collective-permute-done.22 = bf16[256,2048]{1,0:T(8,128)(2,1)S(1)} collective-permute-done((bf16[256,2048]{1,0:T(8,128)(2,1)S(1)}, bf16[256,2048]{1,0:T(8,128)(2,1)S(1)}, u32[]{:S(2)}, u32[]{:S(2)}) %collective-permute-start.22) | collective-permute-done | bytes 1048608 | tf_op jit(solution)/shard_map/ppermute | solution.py:164
  (332 shorter events, 335.6 us)
Async XLA Ops:
  7.2 93.6 %all-gather.5.cloned.1.call-start = ((), (), s32[]{:S(2)}) async-start(), calls=%async_computation.4 | async-start | bytes 7077888 | tf_op jit(solution)/shard_map/all_gather | solution.py:219
  9.4 149.5 %all-gather.7.cloned.1.call-start = ((), (), s32[]{:S(2)}) async-start(), calls=%async_computation.5 | async-start | bytes 2359296 | tf_op jit(solution)/shard_map/all_gather | solution.py:219
  10.2 173.0 %all-gather.9.cloned.1.call-start = ((), (), s32[]{:S(2)}) async-start(), calls=%async_computation.6 | async-start | bytes 9437184 | tf_op jit(solution)/shard_map/all_gather | solution.py:219
  10.9 242.4 %all-gather.11.cloned.1.call-start = ((), (), s32[]{:S(2)}) async-start(), calls=%async_computation.7 | async-start | bytes 18874368 | tf_op jit(solution)/shard_map/all_gather | solution.py:219
  12.5 482.5 %reduce-scatter.5.cloned.1.call-start = ((), (), s32[]{:S(2)}) async-start(), calls=%async_computation.8 | async-start | bytes 9437184 | tf_op jit(solution)/shard_map/reduce_scatter | solution.py:224
  18.1 28.2 %collective-permute-start = (bf16[256,2048]{1,0:T(8,128)(2,1)S(1)}, bf16[256,2048]{1,0:T(8,128)(2,1)S(1)}, u32[]{:S(2)}, u32[]{:S(2)}) collective-permute-start(bf16[256,2048]{1,0:T(8,128)(2,1)S(1)} %get-tuple-element.224), channel_id=1, source_target_pairs={{0,8},{8,16},{16,24},{24,0},{1,9},{9,17},{17,25},{25,1},{2,10},{10... | collective-permute-start | bytes 3145736 | tf_op jit(solution)/shard_map/ppermute | solution.py:132
  46.4 26.2 %collective-permute-start.1 = (bf16[256,2048]{1,0:T(8,128)(2,1)S(1)}, bf16[256,2048]{1,0:T(8,128)(2,1)}, u32[]{:S(2)}, u32[]{:S(2)}) collective-permute-start(bf16[256,2048]{1,0:T(8,128)(2,1)S(1)} %collective-permute-done), channel_id=1, source_target_pairs={{0,8},{8,16},{16,24},{24,0},{1,9},{9,17},{17,25},{25,1},{2,10},{10... | collective-permute-start | bytes 3145736 | tf_op jit(solution)/shard_map/ppermute | solution.py:132
  72.6 25.6 %collective-permute-start.2 = (bf16[256,2048]{1,0:T(8,128)(2,1)}, bf16[256,2048]{1,0:T(8,128)(2,1)}, u32[]{:S(2)}, u32[]{:S(2)}) collective-permute-start(bf16[256,2048]{1,0:T(8,128)(2,1)} %collective-permute-done.1), channel_id=1, source_target_pairs={{0,8},{8,16},{16,24},{24,0},{1,9},{9,17},{17,25},{25,1},{2,10},{10... | collective-permute-start | bytes 3145736 | tf_op jit(solution)/shard_map/ppermute | solution.py:132
  100.6 30.4 %collective-permute-start.3 = (bf16[256,2048]{1,0:T(8,128)(2,1)}, bf16[256,2048]{1,0:T(8,128)(2,1)}, u32[]{:S(2)}, u32[]{:S(2)}) collective-permute-start(bf16[256,2048]{1,0:T(8,128)(2,1)} %param.19), channel_id=1, source_target_pairs={{0,8},{8,16},{16,24},{24,0},{1,9},{9,17},{17,25},{25,1},{2,10},{10... | collective-permute-start | bytes 3145736 | tf_op jit(solution)/shard_map/ppermute | solution.py:132
  133.7 25.3 %collective-permute-start.4 = (bf16[256,2048]{1,0:T(8,128)(2,1)}, bf16[256,2048]{1,0:T(8,128)(2,1)}, u32[]{:S(2)}, u32[]{:S(2)}) collective-permute-start(bf16[256,2048]{1,0:T(8,128)(2,1)} %collective-permute-done.3), channel_id=1, source_target_pairs={{0,8},{8,16},{16,24},{24,0},{1,9},{9,17},{17,25},{25,1},{2,10},{10... | collective-permute-start | bytes 3145736 | tf_op jit(solution)/shard_map/ppermute | solution.py:132
  159.0 24.0 %collective-permute-start.5 = (bf16[256,2048]{1,0:T(8,128)(2,1)}, bf16[256,2048]{1,0:T(8,128)(2,1)}, u32[]{:S(2)}, u32[]{:S(2)}) collective-permute-start(bf16[256,2048]{1,0:T(8,128)(2,1)} %collective-permute-done.4), channel_id=1, source_target_pairs={{0,8},{8,16},{16,24},{24,0},{1,9},{9,17},{17,25},{25,1},{2,10},{10... | collective-permute-start | bytes 3145736 | tf_op jit(solution)/shard_map/ppermute | solution.py:132
  276.2 23.5 %collective-permute-start.10 = (bf16[256,2048]{1,0:T(8,128)(2,1)}, bf16[256,2048]{1,0:T(8,128)(2,1)}, u32[]{:S(2)}, u32[]{:S(2)}) collective-permute-start(bf16[256,2048]{1,0:T(8,128)(2,1)} %collective-permute-done.9), channel_id=1, source_target_pairs={{0,8},{8,16},{16,24},{24,0},{1,9},{9,17},{17,25},{25,1},{2,10},{10... | collective-permute-start | bytes 3145736 | tf_op jit(solution)/shard_map/ppermute | solution.py:132
  299.7 30.8 %collective-permute-start.11 = (bf16[256,2048]{1,0:T(8,128)(2,1)}, bf16[256,2048]{1,0:T(8,128)(2,1)}, u32[]{:S(2)}, u32[]{:S(2)}) collective-permute-start(bf16[256,2048]{1,0:T(8,128)(2,1)} %collective-permute-done.10), channel_id=1, source_target_pairs={{0,8},{8,16},{16,24},{24,0},{1,9},{9,17},{17,25},{25,1},{2,10},{10... | collective-permute-start | bytes 3145736 | tf_op jit(solution)/shard_map/ppermute | solution.py:132
  313.9 57.1 %collective-permute-start.12 = (bf16[256,2048]{1,0:T(8,128)(2,1)}, bf16[256,2048]{1,0:T(8,128)(2,1)}, u32[]{:S(2)}, u32[]{:S(2)}) collective-permute-start(bf16[256,2048]{1,0:T(8,128)(2,1)} %convolution_convert_fusion.7), channel_id=1, source_target_pairs={{0,8},{8,16},{16,24},{24,0},{1,9},{9,17},{17,25},{25,1},{2,10},{10... | collective-permute-start | bytes 3145736 | tf_op jit(solution)/shard_map/ppermute | solution.py:164
  371.0 263.6 %reduce-scatter.7.cloned.1.call-start = ((), (), s32[]{:S(2)}) async-start(), calls=%async_computation.9 | async-start | bytes 18874368 | tf_op jit(solution)/shard_map/reduce_scatter | solution.py:224
  432.6 28.7 %collective-permute-start.15 = (bf16[256,2048]{1,0:T(8,128)(2,1)}, bf16[256,2048]{1,0:T(8,128)(2,1)S(1)}, u32[]{:S(2)}, u32[]{:S(2)}) collective-permute-start(bf16[256,2048]{1,0:T(8,128)(2,1)} %get-tuple-element.219), channel_id=1, source_target_pairs={{0,8},{8,16},{16,24},{24,0},{1,9},{9,17},{17,25},{25,1},{2,10},{10... | collective-permute-start | bytes 3145736 | tf_op jit(solution)/shard_map/ppermute | solution.py:132
  462.3 233.5 %reduce-scatter.11.cloned.1.call-start = ((), (), s32[]{:S(2)}) async-start(), calls=%async_computation.11 | async-start | bytes 2359296 | tf_op jit(solution)/shard_map/reduce_scatter | solution.py:224
  464.0 25.4 %collective-permute-start.16 = (bf16[256,2048]{1,0:T(8,128)(2,1)}, bf16[256,2048]{1,0:T(8,128)(2,1)S(1)}, u32[]{:S(2)}, u32[]{:S(2)}) collective-permute-start(bf16[256,2048]{1,0:T(8,128)(2,1)} %copy-done.49), channel_id=1, source_target_pairs={{0,8},{8,16},{16,24},{24,0},{1,9},{9,17},{17,25},{25,1},{2,10},{10... | collective-permute-start | bytes 3145736 | tf_op jit(solution)/shard_map/ppermute | solution.py:132
  489.4 25.8 %collective-permute-start.17 = (bf16[256,2048]{1,0:T(8,128)(2,1)S(1)}, bf16[256,2048]{1,0:T(8,128)(2,1)S(1)}, u32[]{:S(2)}, u32[]{:S(2)}) collective-permute-start(bf16[256,2048]{1,0:T(8,128)(2,1)S(1)} %collective-permute-done.16), channel_id=1, source_target_pairs={{0,8},{8,16},{16,24},{24,0},{1,9},{9,17},{17,25},{25,1},{2,10},{10... | collective-permute-start | bytes 3145736 | tf_op jit(solution)/shard_map/ppermute | solution.py:132
  516.3 74.7 %collective-permute-start.18 = (bf16[256,2048]{1,0:T(8,128)(2,1)}, bf16[256,2048]{1,0:T(8,128)(2,1)}, u32[]{:S(2)}, u32[]{:S(2)}) collective-permute-start(bf16[256,2048]{1,0:T(8,128)(2,1)} %convolution_convert_fusion.10), channel_id=1, source_target_pairs={{0,8},{8,16},{16,24},{24,0},{1,9},{9,17},{17,25},{25,1},{2,10},{10... | collective-permute-start | bytes 3145736 | tf_op jit(solution)/shard_map/ppermute | solution.py:164
  579.9 117.7 %reduce-scatter.9.cloned.1.call-start = ((), (), s32[]{:S(2)}) async-start(), calls=%async_computation.10 | async-start | bytes 7077888 | tf_op jit(solution)/shard_map/reduce_scatter | solution.py:224
  598.6 24.9 %collective-permute-start.19 = (bf16[256,2048]{1,0:T(8,128)(2,1)S(1)}, bf16[256,2048]{1,0:T(8,128)(2,1)S(1)}, u32[]{:S(2)}, u32[]{:S(2)}) collective-permute-start(bf16[256,2048]{1,0:T(8,128)(2,1)S(1)} %add_convert_fusion.6), channel_id=1, source_target_pairs={{0,8},{8,16},{16,24},{24,0},{1,9},{9,17},{17,25},{25,1},{2,10},{10... | collective-permute-start | bytes 3145736 | tf_op jit(solution)/shard_map/ppermute | solution.py:164
  640.8 41.8 %collective-permute-start.20 = (bf16[256,2048]{1,0:T(8,128)(2,1)S(1)}, bf16[256,2048]{1,0:T(8,128)(2,1)S(1)}, u32[]{:S(2)}, u32[]{:S(2)}) collective-permute-start(bf16[256,2048]{1,0:T(8,128)(2,1)S(1)} %add_convert_fusion.3), channel_id=1, source_target_pairs={{0,8},{8,16},{16,24},{24,0},{1,9},{9,17},{17,25},{25,1},{2,10},{10... | collective-permute-start | bytes 3145736 | tf_op jit(solution)/shard_map/ppermute | solution.py:164
  662.4 31.4 %collective-permute-start.22 = (bf16[256,2048]{1,0:T(8,128)(2,1)S(1)}, bf16[256,2048]{1,0:T(8,128)(2,1)S(1)}, u32[]{:S(2)}, u32[]{:S(2)}) collective-permute-start(bf16[256,2048]{1,0:T(8,128)(2,1)S(1)} %add_convert_fusion.1), channel_id=1, source_target_pairs={{0,8},{8,16},{16,24},{24,0},{1,9},{9,17},{17,25},{25,1},{2,10},{10... | collective-permute-start | bytes 3145736 | tf_op jit(solution)/shard_map/ppermute | solution.py:164
  (88 other events, 1161.1 us)
Sparse Core Ops, SparseCore 0:
  10.5 48.1 all-gather.4
  60.5 28.0 all-gather.6
  90.5 55.8 all-gather.8
  148.7 89.7 all-gather.10
  371.2 72.0 reduce-scatter.4
  462.4 115.8 reduce-scatter.6
  582.1 41.0 reduce-scatter.10
  634.7 61.3 reduce-scatter.8
